TPU v7x, 32 devices: a whole 2x2x4 slice. The times are simulated.
32 devices in a mesh: seq: 8 (over z, x), ep: 4 (over y, core).
Axes of the slice: x: 2, y: 2, z: 4, core: 2. Of those that a mesh axis runs over, the one named last changes fastest.
Arguments:
- queries: bfloat16 [4, 1024, 2048], P('ep', 'seq'), may hold values from -6 to 6
- key_rows: bfloat16 [4, 1024, 2048], P('ep', 'seq'), may hold values from -6 to 6
- value_rows: bfloat16 [4, 1024, 2048], P('ep', 'seq'), may hold values from -6 to 6
- residual: bfloat16 [4, 1024, 2048], P('ep', 'seq'), may hold values from -6 to 6
- state_start: float32 [4, 16, 128, 128], P('ep'), may hold values from -96 to 96
- head_gain: float32 [2048], replicated, may hold values from 0.25 to 1.75
- ffn_gain: float32 [2048], replicated, may hold values from 0.25 to 1.75
- routes: int32 [4, 1024, 6], P('ep', 'seq'), may hold values from 0 to 15, all different within a row; in each aligned block of 128 rows (0 to 127, 128 to 255, ..., all dimensions but the last counted through in order) at most 50 rows name the same one
- route_gates: float32 [4, 1024, 6], P('ep', 'seq'), may hold values from 0.1 to 1
- gate_weight: bfloat16 [16, 2048, 704], P('ep', 'seq'), may hold values from -0.125 to 0.125
- up_weight: bfloat16 [16, 2048, 704], P('ep', 'seq'), may hold values from -0.125 to 0.125
- down_weight: bfloat16 [16, 704, 2048], P('ep', None, 'seq'), may hold values from -0.21875 to 0.21875
Outputs:
- layer_out: bfloat16 [4, 1024, 2048], P('ep', 'seq')
Inputs may be any that keep to these rules, and one draw needn't show every extreme that they name: `routes`: each position names 6 different experts. Among the positions of one device (aligned blocks of 128 positions) no expert is named more than 50 times, a bound that some block reaches.
All inputs are finite; a program needn't handle non-finite values.
Results may differ from a plain program's by a relative error of at most 0.015.
Values may be sent and summed in bfloat16 or wider, within the bound.
No kernel may reach another device: no remote copies, remote signals or barrier semaphores. Data moves between devices by JAX's collectives and lax.ppermute only.
A program may use at most 128 MiB of HBM per device.

v0:
```python
import jax
import jax.numpy as jnp
from jax import lax
from jax.sharding import PartitionSpec as P

D = 2048
HEADS = 16
HEAD_DIM = 128
EXPERTS = 16
TOP = 6
CAP = 50


def carried_in(array, axis, join, neutral):
    place = lax.axis_index(axis)
    gathered = lax.all_gather(array.astype(jnp.bfloat16), axis)
    state = jnp.zeros_like(array) + jnp.asarray(neutral, array.dtype)

    def one(turn, state):
        return join(state, lax.dynamic_index_in_dim(gathered, turn, 0, False).astype(array.dtype))

    return lax.fori_loop(0, place, one, state)


def route_slots(block_routes):
    chosen = (block_routes[:, None] == jnp.arange(EXPERTS, dtype=jnp.int32)[None, :]).astype(
        jnp.int32
    )
    counts = jnp.cumsum(chosen, axis=0) - 1
    return jnp.sum(chosen * counts, axis=1)


def silu_gate(gate_sum, up_sum):
    return gate_sum / (1.0 + jnp.exp(-gate_sum)) * up_sum


def add_states(earlier, later):
    return earlier + later


def shards(
    queries,
    key_rows,
    value_rows,
    residual,
    state_start,
    head_gain,
    ffn_gain,
    routes,
    route_gates,
    gate_weight,
    up_weight,
    down_weight,
):
    tokens = queries.shape[1]
    query_heads = queries[0].reshape(tokens, HEADS, HEAD_DIM)
    key_heads = key_rows[0].reshape(tokens, HEADS, HEAD_DIM)
    value_heads = value_rows[0].reshape(tokens, HEADS, HEAD_DIM)
    local_state = jnp.einsum(
        "thd,the->hde", key_heads, value_heads, preferred_element_type=jnp.float32
    )
    earlier = carried_in(local_state, "seq", add_states, jnp.zeros_like(local_state))
    state_before = state_start[0] + earlier
    causal = (
        jnp.arange(tokens, dtype=jnp.int32)[:, None] >= jnp.arange(tokens, dtype=jnp.int32)[None, :]
    )
    scores = jnp.einsum("thd,shd->hts", query_heads, key_heads, preferred_element_type=jnp.float32)
    scores = jnp.where(causal[None], scores, 0.0).astype(jnp.bfloat16)
    in_block = jnp.einsum("hts,she->the", scores, value_heads, preferred_element_type=jnp.float32)
    from_state = jnp.einsum(
        "thd,hde->the",
        query_heads.astype(jnp.float32),
        state_before,
        precision=lax.Precision.HIGHEST,
    )
    attended = from_state + in_block
    head_scale = lax.rsqrt(jnp.mean(attended * attended, axis=-1, keepdims=True) + 1e-05)
    head_normed = (attended * head_scale).reshape(tokens, D) * head_gain
    mixed_rows = (residual[0].astype(jnp.float32) + head_normed).astype(jnp.bfloat16)
    mixed_rows = lax.optimization_barrier(mixed_rows)
    mixed_wide = mixed_rows.astype(jnp.float32)
    row_scale = lax.rsqrt(jnp.mean(mixed_wide * mixed_wide, axis=-1, keepdims=True) + 1e-05)
    ffn_in = (mixed_wide * row_scale * ffn_gain).astype(jnp.bfloat16)
    flat_routes = routes[0].reshape(-1)
    slot_rank = route_slots(flat_routes)
    position = flat_routes * CAP + slot_rank
    token_index = jnp.arange(tokens * TOP, dtype=jnp.int32) // TOP
    source = jnp.zeros((EXPERTS * CAP,), jnp.int32).at[position].set(token_index)
    filled = jnp.zeros((EXPERTS * CAP,), jnp.bool_).at[position].set(True)
    outgoing = jnp.where(filled[:, None], ffn_in[source], jnp.zeros((), jnp.bfloat16)).reshape(
        EXPERTS, CAP, D
    )
    arrived = lax.all_to_all(outgoing, "ep", split_axis=0, concat_axis=1, tiled=True)
    whole_gate, whole_up = (
        lax.all_gather(gate_weight, "seq", axis=1, tiled=True),
        lax.all_gather(up_weight, "seq", axis=1, tiled=True),
    )
    gate_sum = jnp.einsum("erd,edh->erh", arrived, whole_gate, preferred_element_type=jnp.float32)
    up_sum = jnp.einsum("erd,edh->erh", arrived, whole_up, preferred_element_type=jnp.float32)
    hidden = silu_gate(gate_sum, up_sum).astype(jnp.bfloat16)
    expert_rows = jnp.einsum(
        "erh,ehd->erd",
        hidden,
        lax.all_gather(down_weight, "seq", axis=2, tiled=True),
        preferred_element_type=jnp.float32,
    ).astype(jnp.bfloat16)
    returned = lax.all_to_all(expert_rows, "ep", split_axis=1, concat_axis=0, tiled=True)
    picked = returned.reshape(EXPERTS * CAP, D)[position].reshape(tokens, TOP, D)
    expert_mix = jnp.sum(route_gates[0][:, :, None] * picked.astype(jnp.float32), axis=1)
    return (mixed_wide + expert_mix).astype(jnp.bfloat16)[None]


def solution(mesh):
    placed = (
        P("ep", "seq", None),
        P("ep", "seq", None),
        P("ep", "seq", None),
        P("ep", "seq", None),
        P("ep", None, None, None),
        P(),
        P(),
        P("ep", "seq", None),
        P("ep", "seq", None),
        P("ep", "seq", None),
        P("ep", "seq", None),
        P("ep", None, "seq"),
    )
    return jax.shard_map(
        shards, mesh=mesh, in_specs=placed, out_specs=P("ep", "seq", None), check_vma=False
    )
```

profile of v0, /device:TPU:16, one launch (start us, length us, event | category | flops | bytes accessed | tf_op | source)
XLA Modules:
  0.0 669.2 jit_solution(3793156813557923093)
XLA Ops:
  6.5 1.3 copy.60
  7.9 1.1 copy.62
  9.0 1.3 convolution_convert_fusion.1
  10.4 0.7 all-gather.6.cloned.1.call-update
  11.2 0.7 all-gather.10.cloned.1.call-update
  11.9 0.5 all-gather.8.cloned.1.call-update
  12.4 0.1 copy.47
  12.6 0.1 eq.29
  12.7 0.1 eq.25
  13.0 1.7 reduce-window.6
  14.7 0.3 slice_reduce_fusion
  15.0 0.1 copy.46
  15.1 0.1 mul.79
  15.4 3.4 scatter_custom_fusion.1
  18.8 3.4 scatter_custom_fusion
  22.3 61.9 %all-gather.12.cloned.1.call-done = bf16[128,128,128]{2,1,0:T(8,128)(2,1)} async-done(((bf16[16,128,128]{2,1,0:T(8,128)(2,1)}), bf16[128,128,128]{2,1,0:T(8,128)(2,1)}) %all-gather.12.cloned.1.call-update) | async-done | bytes 4194320 | tf_op jit(solution)/shard_map/all_gather | solution.py:16
  84.3 5.2 while.10
  84.3 1.3 convert_add_fusion.4
  85.6 1.3 convert_add_fusion.4
  86.9 1.3 convert_add_fusion.4
  88.2 1.3 convert_add_fusion.4
  89.5 3.2 convolution_bitcast_fusion.1
  92.8 2.3 multiply_reduce_fusion.1
  95.2 0.3 copy.44
  95.6 0.1 fusion.15
  95.7 0.2 fusion.11
  95.9 0.6 copy-done
  96.5 0.2 fusion.13
  96.7 4.8 gather_fusion
  101.5 4.7 gather.9
  106.2 2.4 broadcast_select_fusion
  108.6 45.1 %all_to_all.33 = bf16[16,50,2048]{2,1,0:T(8,128)(2,1)S(1)} all-to-all(bf16[16,50,2048]{2,1,0:T(8,128)(2,1)S(1)} %broadcast_select_fusion), channel_id=1, replica_groups=mesh['seq'=8,'ep'=4] {'ep'}, dimensions={0} | all-to-all | bytes 6553600 | tf_op jit(solution)/shard_map/all_to_all | solution.py:93
  153.7 2.5 copy.59
  156.2 92.0 %all-gather.6.cloned.1.call-done = bf16[4,2048,704]{1,2,0:T(8,128)(2,1)} async-done(((bf16[4,256,704]{1,2,0:T(8,128)(2,1)}), bf16[4,2048,704]{1,2,0:T(8,128)(2,1)}) %all-gather.6.cloned.1.call-update) | async-done | bytes 11534352 | tf_op jit(solution)/shard_map/all_gather | solution.py:95
  248.2 11.3 %fusion.2 = f32[4,200,704]{2,1,0:T(8,128)} fusion(bf16[4,2048,704]{1,2,0:T(8,128)(2,1)} %all-gather.6.cloned.1.call-done, bf16[4,200,2048]{2,0,1:T(4,128)(2,1)S(1)} %bitcast.67), kind=kOutput, calls=%fused_computation.10 | convolution fusion | flops 2306867200 | bytes 17063936 | tf_op jit(solution)/shard_map/erd,edh->erh/dot_general | solution.py:98
  259.6 152.7 %all-gather.10.cloned.1.call-done = bf16[4,704,2048]{2,1,0:T(8,128)(2,1)} async-done(((bf16[4,704,256]{2,1,0:T(8,128)(2,1)}), bf16[4,704,2048]{2,1,0:T(8,128)(2,1)}) %all-gather.10.cloned.1.call-update) | async-done | bytes 11534352 | tf_op jit(solution)/shard_map/all_gather | solution.py:104
  412.3 163.9 %all-gather.8.cloned.1.call-done = bf16[4,2048,704]{1,2,0:T(8,128)(2,1)} async-done(((bf16[4,256,704]{1,2,0:T(8,128)(2,1)}), bf16[4,2048,704]{1,2,0:T(8,128)(2,1)}) %all-gather.8.cloned.1.call-update) | async-done | bytes 11534352 | tf_op jit(solution)/shard_map/all_gather | solution.py:96
  576.2 14.9 %convolution_convert_fusion = bf16[4,200,2048]{2,1,0:T(8,128)(2,1)S(1)} fusion(bf16[4,704,2048]{2,1,0:T(8,128)(2,1)} %all-gather.10.cloned.1.call-done, f32[4,200,704]{2,1,0:T(8,128)} %fusion.2, bf16[4,2048,704]{1,2,0:T(8,128)(2,1)} %all-gather.8.cloned.1.call-done, bf16[4,200,2048]{2,0,1:T(4,128)(2,1)} %bitcast.68), kind=kOutput, calls=%fused_computation.7 | convolution fusion | flops 4618188800 | bytes 31875072 | tf_op jit(solution)/shard_map/erh,ehd->erd/dot_general | solution.py:101
  591.0 4.2 copy.54
  595.3 4.1 all-to-all-start.1
  599.4 0.1 copy.57
  599.5 37.9 %all-to-all-done.1 = bf16[4,200,2048]{2,0,1:T(4,128)(2,1)S(1)} async-done(((bf16[4,200,2048]{2,0,1:T(4,128)(2,1)}), bf16[4,200,2048]{2,0,1:T(4,128)(2,1)S(1)}, u32[]{:S(2)}, u32[]{:S(2)}) %all-to-all-start.1) | async-done | bytes 3276832 | tf_op jit(solution)/shard_map/all_to_all | solution.py:107
  637.4 3.6 copy.55
  641.1 3.2 reshape.102
  644.2 4.3 gather_fusion.1
  648.6 6.6 reshape.105
  655.1 6.7 multiply_reduce_fusion
  661.8 0.9 fusion.16
  (39 shorter events, 0.8 us)
Async XLA Ops:
  6.5 77.6 %all-gather.12.cloned.1.call-start = ((), (), s32[]{:S(2)}) async-start(), calls=%async_computation.5 | async-start | bytes 4718592 | tf_op jit(solution)/shard_map/all_gather | solution.py:16
  9.0 3.4 copy-start.5
  9.0 3.8 copy-start.3
  10.4 237.8 %all-gather.6.cloned.1.call-start = ((), (), s32[]{:S(2)}) async-start(), calls=%async_computation.2 | async-start | bytes 12976128 | tf_op jit(solution)/shard_map/all_gather | solution.py:95
  11.1 401.1 %all-gather.10.cloned.1.call-start = ((), (), s32[]{:S(2)}) async-start(), calls=%async_computation.4 | async-start | bytes 12976128 | tf_op jit(solution)/shard_map/all_gather | solution.py:104
  11.9 564.3 %all-gather.8.cloned.1.call-start = ((), (), s32[]{:S(2)}) async-start(), calls=%async_computation.3 | async-start | bytes 12976128 | tf_op jit(solution)/shard_map/all_gather | solution.py:96
  92.8 2.8 copy-start.4
  92.8 2.8 copy-start.6
  95.1 1.4 copy-start.7
  95.7 0.8 copy-start
  156.2 103.4 %copy-start.2 = (bf16[4,4,50,2048]{3,1,2,0:T(4,128)(2,1)}, bf16[4,4,50,2048]{3,1,2,0:T(4,128)(2,1)S(1)}, u32[]{:S(2)}) copy-start(bf16[4,4,50,2048]{3,1,2,0:T(4,128)(2,1)S(1)} %copy.59) | copy-start | bytes 9830404
  595.3 4.1 copy-start.8
  595.3 42.2 %all-to-all-start.1 = ((bf16[4,200,2048]{2,0,1:T(4,128)(2,1)}), bf16[4,200,2048]{2,0,1:T(4,128)(2,1)S(1)}, u32[]{:S(2)}, u32[]{:S(2)}) async-start(bf16[4,200,2048]{2,0,1:T(4,128)(2,1)} %copy.54), calls=%async_computation.1 | async-start | bytes 6553600 | tf_op jit(solution)/shard_map/all_to_all | solution.py:107
  655.1 6.7 copy-start.1
Sparse Core Ops, SparseCore 0:
  10.5 73.6 all-gather.11
  86.2 161.9 all-gather.5
  250.3 161.9 all-gather.9
  414.2 161.9 all-gather.7
where the time goes:
time: 673 us; the launch traced here: 669 us
  waiting for transfers between devices  510 us (76%)
  local copies, waits for them, and re-layouts  45.4 us (7%)
  blocking collectives  45.1 us (7%)
  matrix products  33.1 us (5%)
  other arithmetic  17.6 us (3%)
  between operations  13.5 us (2%)
    all_gather x1, waiting for transfers between devices, shards(): lax.all_gather(up_weight, 'seq', axis=1, tiled=True)  164 us
    all_gather x1, waiting for transfers between devices, shards(): lax.all_gather(down_weight, 'seq', axis=2, tiled=True)  153 us
    all_gather x1, waiting for transfers between devices, shards(): lax.all_gather(gate_weight, 'seq', axis=1, tiled=True)  92 us
    all_gather x1, waiting for transfers between devices, carried_in(): gathered = lax.all_gather(array.astype(jnp.bfloat16), axis)  61.9 us
    all_to_all x1, blocking collectives, shards(): lax.all_to_all(outgoing, 'ep', split_axis=0, concat_axis=1, tiled=True)  45.1 us
    all_to_all x1, waiting for transfers between devices, shards(): lax.all_to_all(expert_rows, 'ep', split_axis=1, concat_axis=0, tiled=True)  37.9 us
    dot_general x1, matrix products, shards(): jnp.einsum('erh,ehd->erd', hidden, lax.all_gather(down_weight, 'seq', axi...  14.9 us
  transfers between devices with their start and end apart: 5, of which 5 were waited for; matrix products, arithmetic and copies ran while one was open for 7% of the time, Pallas kernels for 0%

commit v1 on v0

v1 whole, which is shorter than its diff:
```python
import jax
import jax.numpy as jnp
from jax import lax
from jax.sharding import PartitionSpec as P

D = 2048
HEADS = 16
HEAD_DIM = 128
EXPERTS = 16
TOP = 6
CAP = 50


def carried_in(array, axis, join, neutral):
    place = lax.axis_index(axis)
    gathered = lax.all_gather(array.astype(jnp.bfloat16), axis)
    state = jnp.zeros_like(array) + jnp.asarray(neutral, array.dtype)

    def one(turn, state):
        return join(state, lax.dynamic_index_in_dim(gathered, turn, 0, False).astype(array.dtype))

    return lax.fori_loop(0, place, one, state)


def route_slots(block_routes):
    chosen = (block_routes[:, None] == jnp.arange(EXPERTS, dtype=jnp.int32)[None, :]).astype(
        jnp.int32
    )
    counts = jnp.cumsum(chosen, axis=0) - 1
    return jnp.sum(chosen * counts, axis=1)


def silu_gate(gate_sum, up_sum):
    return gate_sum / (1.0 + jnp.exp(-gate_sum)) * up_sum


def add_states(earlier, later):
    return earlier + later


def make_shards(n_ep, n_seq):
    n_dev = n_ep * n_seq

    def shards(
        queries,
        key_rows,
        value_rows,
        residual,
        state_start,
        head_gain,
        ffn_gain,
        routes,
        route_gates,
        gate_weight,
        up_weight,
        down_weight,
    ):
        local_experts = gate_weight.shape[0]
        per = n_seq // local_experts
        chunk = -(-CAP // per)
        capp = chunk * per

        seq_place = lax.axis_index("seq")
        wanted = jnp.arange(n_seq, dtype=jnp.int32) // per
        whole_gate = lax.all_to_all(gate_weight[wanted], "seq", 0, 0, tiled=True)
        whole_up = lax.all_to_all(up_weight[wanted], "seq", 0, 0, tiled=True)
        whole_down = lax.all_to_all(down_weight[wanted], "seq", 0, 0, tiled=True)
        whole_gate = whole_gate.reshape(-1, whole_gate.shape[-1])
        whole_up = whole_up.reshape(-1, whole_up.shape[-1])

        tokens = queries.shape[1]
        query_heads = queries[0].reshape(tokens, HEADS, HEAD_DIM)
        key_heads = key_rows[0].reshape(tokens, HEADS, HEAD_DIM)
        value_heads = value_rows[0].reshape(tokens, HEADS, HEAD_DIM)
        local_state = jnp.einsum(
            "thd,the->hde", key_heads, value_heads, preferred_element_type=jnp.float32
        )
        earlier = carried_in(local_state, "seq", add_states, jnp.zeros_like(local_state))
        state_before = state_start[0] + earlier
        causal = (
            jnp.arange(tokens, dtype=jnp.int32)[:, None]
            >= jnp.arange(tokens, dtype=jnp.int32)[None, :]
        )
        scores = jnp.einsum(
            "thd,shd->hts", query_heads, key_heads, preferred_element_type=jnp.float32
        )
        scores = jnp.where(causal[None], scores, 0.0).astype(jnp.bfloat16)
        in_block = jnp.einsum(
            "hts,she->the", scores, value_heads, preferred_element_type=jnp.float32
        )
        from_state = jnp.einsum(
            "thd,hde->the",
            query_heads.astype(jnp.float32),
            state_before,
            precision=lax.Precision.HIGHEST,
        )
        attended = from_state + in_block
        head_scale = lax.rsqrt(jnp.mean(attended * attended, axis=-1, keepdims=True) + 1e-05)
        head_normed = (attended * head_scale).reshape(tokens, D) * head_gain
        mixed_rows = (residual[0].astype(jnp.float32) + head_normed).astype(jnp.bfloat16)
        mixed_rows = lax.optimization_barrier(mixed_rows)
        mixed_wide = mixed_rows.astype(jnp.float32)
        row_scale = lax.rsqrt(jnp.mean(mixed_wide * mixed_wide, axis=-1, keepdims=True) + 1e-05)
        ffn_in = (mixed_wide * row_scale * ffn_gain).astype(jnp.bfloat16)
        flat_routes = routes[0].reshape(-1)
        slot_rank = route_slots(flat_routes)
        position = flat_routes * capp + slot_rank
        token_index = jnp.arange(tokens * TOP, dtype=jnp.int32) // TOP
        source = jnp.zeros((EXPERTS * capp,), jnp.int32).at[position].set(token_index)
        filled = jnp.zeros((EXPERTS * capp,), jnp.bool_).at[position].set(True)
        outgoing = jnp.where(filled[:, None], ffn_in[source], jnp.zeros((), jnp.bfloat16))
        outgoing = outgoing.reshape(EXPERTS * per, chunk, D)
        arrived = lax.all_to_all(outgoing, ("ep", "seq"), 0, 0, tiled=True)
        arrived = arrived.reshape(n_dev * chunk, D)
        gate_sum = jnp.dot(arrived, whole_gate, preferred_element_type=jnp.float32)
        up_sum = jnp.dot(arrived, whole_up, preferred_element_type=jnp.float32)
        hidden = silu_gate(gate_sum, up_sum).astype(jnp.bfloat16)
        expert_rows = jnp.einsum(
            "rh,shd->rsd", hidden, whole_down, preferred_element_type=jnp.float32
        ).astype(jnp.bfloat16)
        expert_rows = expert_rows.reshape(n_dev, chunk, D)
        returned = lax.all_to_all(expert_rows, ("ep", "seq"), 0, 0, tiled=True)
        picked = returned.reshape(EXPERTS * capp, D)[position].reshape(tokens, TOP, D)
        expert_mix = jnp.sum(route_gates[0][:, :, None] * picked.astype(jnp.float32), axis=1)
        del seq_place
        return (mixed_wide + expert_mix).astype(jnp.bfloat16)[None]

    return shards


def solution(mesh):
    placed = (
        P("ep", "seq", None),
        P("ep", "seq", None),
        P("ep", "seq", None),
        P("ep", "seq", None),
        P("ep", None, None, None),
        P(),
        P(),
        P("ep", "seq", None),
        P("ep", "seq", None),
        P("ep", "seq", None),
        P("ep", "seq", None),
        P("ep", None, "seq"),
    )
    shards = make_shards(mesh.shape["ep"], mesh.shape["seq"])
    return jax.shard_map(
        shards, mesh=mesh, in_specs=placed, out_specs=P("ep", "seq", None), check_vma=False
    )
```

time: 673 us -> 519 us (0.77)
  waiting for transfers between devices: 510 us -> 354 us
  blocking collectives: 45.1 us -> 0 us
  starting transfers between devices: 4.22 us -> 36.7 us
  local copies, waits for them, and re-layouts: 45.4 us -> 61.9 us
  matrix products: 33.1 us -> 23.8 us
    all_gather x3 -> x0, waiting for transfers between devices: 409 us -> none  [the longest x1 164 us: shards(): lax.all_gather(up_weight, 'seq', axis=1, tiled=True)]
    all_to_all x1 -> x5, waiting for transfers between devices: 37.9 us -> 354 us  [the longest x1 104 us: shards(): whole_gate = lax.all_to_all(gate_weight[wanted], 'seq', 0, 0, tiled=True)]
    all_gather x1, waiting for transfers between devices: 61.9 us -> 0.02 us  [carried_in(): gathered = lax.all_gather(array.astype(jnp.bfloat16), axis)]
    all_to_all x1 -> x0, blocking collectives: 45.1 us -> none  [shards(): lax.all_to_all(outgoing, 'ep', split_axis=0, concat_axis=1, tiled=True)]
    all_to_all x1 -> x5, starting transfers between devices: 4.1 us -> 36.6 us  [the longest x1 9.09 us: shards(): whole_down = lax.all_to_all(down_weight[wanted], 'seq', 0, 0, tiled=True)]
    reshape x1 -> x5, local copies, waits for them, and re-layouts: 3.17 us -> 15.9 us  [the longest x1 3.89 us: shards(): whole_up = whole_up.reshape(-1, whole_up.shape[-1])]
    dot_general x2, matrix products: 26.2 us -> 17.2 us  [the longest x1 11.1 us: shards(): jnp.einsum('rh,shd->rsd', hidden, whole_down, preferred_element_type=jnp....]
    gather x1 -> x4, local copies, waits for them, and re-layouts: 4.34 us -> 12.7 us  [the longest x1 4.32 us: shards(): returned.reshape(EXPERTS * capp, D)[position].reshape(tokens, TOP, D)]
  transfers between devices with their start and end apart: 5 -> 6, of which waited for: 5 -> 5; matrix products, arithmetic and copies ran while one was open for 7% -> 12% of each run, Pallas kernels for 0% -> 0%
where the time goes in v1:
time: 519 us; the launch traced here: 512 us
  waiting for transfers between devices  354 us (68%)
  local copies, waits for them, and re-layouts  61.9 us (12%)
  starting transfers between devices  36.7 us (7%)
  matrix products  23.8 us (5%)
  other arithmetic  21.9 us (4%)
  between operations  13.7 us (3%)
    all_to_all x1, waiting for transfers between devices, shards(): whole_gate = lax.all_to_all(gate_weight[wanted], 'seq', 0, 0, tiled=True)  104 us
    all_to_all x1, waiting for transfers between devices, shards(): returned = lax.all_to_all(expert_rows, ('ep', 'seq'), 0, 0, tiled=True)  91.8 us
    all_to_all x1, waiting for transfers between devices, shards(): arrived = lax.all_to_all(outgoing, ('ep', 'seq'), 0, 0, tiled=True)  88.4 us
    all_to_all x1, waiting for transfers between devices, shards(): whole_down = lax.all_to_all(down_weight[wanted], 'seq', 0, 0, tiled=True)  46.6 us
    all_to_all x1, waiting for transfers between devices, shards(): whole_up = lax.all_to_all(up_weight[wanted], 'seq', 0, 0, tiled=True)  23.8 us
    dot_general x1, matrix products, shards(): jnp.einsum('rh,shd->rsd', hidden, whole_down, preferred_element_type=jnp....  11.1 us
  transfers between devices with their start and end apart: 6, of which 5 were waited for; matrix products, arithmetic and copies ran while one was open for 12% of the time, Pallas kernels for 0%

profile of v1, /device:TPU:16, one launch (start us, length us, event | category | flops | bytes accessed | tf_op | source)
XLA Modules:
  0.0 512.5 jit_solution(7256690485836384607)
XLA Ops:
  6.5 1.4 copy.52
  8.0 1.1 copy.56
  9.1 1.3 convolution_convert_fusion.1
  10.5 2.3 gather_fusion.1
  12.8 6.3 %all-to-all-start.1 = ((bf16[8,256,704]{1,2,0:T(8,128)(2,1)}), bf16[8,256,704]{1,2,0:T(8,128)(2,1)S(1)}, u32[]{:S(2)}, u32[]{:S(2)}) async-start(bf16[8,256,704]{1,2,0:T(8,128)(2,1)} %gather_fusion.1), calls=%async_computation.1 | async-start | bytes 5767168 | tf_op jit(solution)/shard_map/all_to_all | solution.py:65
  19.4 3.7 gather_fusion.2
  23.1 0.6 fusion.19
  23.7 3.2 reduce-window.6
  26.9 103.7 %all-to-all-done.1 = bf16[8,256,704]{1,2,0:T(8,128)(2,1)S(1)} async-done(((bf16[8,256,704]{1,2,0:T(8,128)(2,1)}), bf16[8,256,704]{1,2,0:T(8,128)(2,1)S(1)}, u32[]{:S(2)}, u32[]{:S(2)}) %all-to-all-start.1) | async-done | bytes 2883616 | tf_op jit(solution)/shard_map/all_to_all | solution.py:65
  130.7 7.7 %all-to-all-start.2 = ((bf16[8,256,704]{1,2,0:T(8,128)(2,1)}), bf16[8,256,704]{1,2,0:T(8,128)(2,1)}, u32[]{:S(2)}, u32[]{:S(2)}) async-start(bf16[8,256,704]{1,2,0:T(8,128)(2,1)} %gather_fusion.2), calls=%async_computation.2 | async-start | bytes 5767168 | tf_op jit(solution)/shard_map/all_to_all | solution.py:66
  138.4 0.2 slice_reduce_fusion
  138.8 1.1 copy.57
  140.3 3.4 scatter_custom_fusion.1
  143.7 3.4 scatter_custom_fusion
  147.4 5.2 %while.10 = (s32[]{:T(128)}, f32[16,128,128]{2,1,0:T(8,128)S(1)}, s32[]{:T(128)}, bf16[8,16,128,128]{3,2,1,0:T(8,128)(2,1)}, s32[]{:T(128)}, /*index=5*/s32[]{:T(128)}, s32[]{:T(128)}) while((s32[]{:T(128)}, f32[16,128,128]{2,1,0:T(8,128)S(1)}, s32[]{:T(128)}, bf16[8,16,128,128]{3,2,1,0:T(8,128)(2,1)}, s32[]{:T(128)}, /*index=5*/s32[]{:T(128)}, ...), condition=%wide.region_1.2_spmd, body=%wide.region_0.1_spmd.sunk | while | flops 524293 | bytes 2621555 | solution.py:22
  147.4 1.3 convert_add_fusion.4
  148.8 1.3 convert_add_fusion.4
  150.1 1.3 convert_add_fusion.4
  151.4 1.3 convert_add_fusion.4
  152.7 3.3 convolution_bitcast_fusion.1
  156.0 2.1 multiply_reduce_fusion.1
  158.2 0.3 copy.41
  158.5 0.6 copy-done.9
  159.4 0.6 copy-done.4
  160.0 0.2 fusion.5
  160.2 4.9 gather_fusion
  165.1 4.9 gather.18
  170.0 4.5 broadcast_select_fusion
  174.5 23.8 %all-to-all-done.2 = bf16[8,256,704]{1,2,0:T(8,128)(2,1)} async-done(((bf16[8,256,704]{1,2,0:T(8,128)(2,1)}), bf16[8,256,704]{1,2,0:T(8,128)(2,1)}, u32[]{:S(2)}, u32[]{:S(2)}) %all-to-all-start.2) | async-done | bytes 2883616 | tf_op jit(solution)/shard_map/all_to_all | solution.py:66
  198.3 6.9 %all-to-all-start = ((bf16[32,25,2048]{2,1,0:T(8,128)(2,1)}), bf16[32,25,2048]{2,1,0:T(8,128)(2,1)}, u32[]{:S(2)}, u32[]{:S(2)}) async-start(bf16[32,25,2048]{2,1,0:T(8,128)(2,1)} %broadcast_select_fusion), calls=%async_computation | async-start | bytes 8388608 | tf_op jit(solution)/shard_map/all_to_all | solution.py:113
  205.2 2.3 gather_fusion.3
  207.4 88.4 %all-to-all-done = bf16[32,25,2048]{2,1,0:T(8,128)(2,1)} async-done(((bf16[32,25,2048]{2,1,0:T(8,128)(2,1)}), bf16[32,25,2048]{2,1,0:T(8,128)(2,1)}, u32[]{:S(2)}, u32[]{:S(2)}) %all-to-all-start) | async-done | bytes 3276832 | tf_op jit(solution)/shard_map/all_to_all | solution.py:113
  295.9 9.1 %all-to-all-start.3 = ((bf16[8,704,256]{2,1,0:T(8,128)(2,1)}), bf16[8,704,256]{2,1,0:T(8,128)(2,1)}, u32[]{:S(2)}, u32[]{:S(2)}) async-start(bf16[8,704,256]{2,1,0:T(8,128)(2,1)} %gather_fusion.3), calls=%async_computation.3 | async-start | bytes 5767168 | tf_op jit(solution)/shard_map/all_to_all | solution.py:67
  305.0 2.0 copy.54
  306.9 3.9 copy.55
  310.8 3.4 reshape.156
  314.3 6.0 %fusion.35 = f32[800,704]{1,0:T(8,128)} fusion(bf16[800,2048]{1,0:T(8,128)(2,1)S(1)} %reshape.156, bf16[2048,704]{0,1:T(8,128)(2,1)} %bitcast.71), kind=kOutput, calls=%fused_computation.75 | convolution fusion | flops 2306867200 | bytes 8413184 | tf_op jit(solution)/shard_map/dot_general | solution.py:115
  320.3 46.6 %all-to-all-done.3 = bf16[8,704,256]{2,1,0:T(8,128)(2,1)} async-done(((bf16[8,704,256]{2,1,0:T(8,128)(2,1)}), bf16[8,704,256]{2,1,0:T(8,128)(2,1)}, u32[]{:S(2)}, u32[]{:S(2)}) %all-to-all-start.3) | async-done | bytes 2883616 | tf_op jit(solution)/shard_map/all_to_all | solution.py:67
  366.9 11.1 %convolution_convert_fusion = bf16[800,8,256]{2,0,1:T(8,128)(2,1)} fusion(bf16[8,704,256]{2,1,0:T(8,128)(2,1)} %all-to-all-done.3, bf16[800,2048]{1,0:T(8,128)(2,1)S(1)} %reshape.156, bf16[2048,704]{0,1:T(8,128)(2,1)} %bitcast.70, f32[800,704]{1,0:T(8,128)} %fusion.35), kind=kOutput, calls=%fused_computation.11 | convolution fusion | flops 4618188800 | bytes 14573568 | tf_op jit(solution)/shard_map/rh,shd->rsd/dot_general | solution.py:118
  378.0 3.8 copy.49
  381.8 3.2 reshape.159
  385.0 6.7 %all-to-all-start.4 = ((bf16[32,25,2048]{2,1,0:T(8,128)(2,1)}), bf16[32,25,2048]{2,1,0:T(8,128)(2,1)}, u32[]{:S(2)}, u32[]{:S(2)}) async-start(bf16[32,25,2048]{2,1,0:T(8,128)(2,1)} %reshape.159), calls=%async_computation.4 | async-start | bytes 8388608 | tf_op jit(solution)/shard_map/all_to_all | solution.py:122
  391.9 91.8 %all-to-all-done.4 = bf16[32,25,2048]{2,1,0:T(8,128)(2,1)} async-done(((bf16[32,25,2048]{2,1,0:T(8,128)(2,1)}), bf16[32,25,2048]{2,1,0:T(8,128)(2,1)}, u32[]{:S(2)}, u32[]{:S(2)}) %all-to-all-start.4) | async-done | bytes 3276832 | tf_op jit(solution)/shard_map/all_to_all | solution.py:122
  483.7 3.4 reshape.160
  487.1 4.3 gather_fusion.4
  491.4 6.6 %reshape.163 = f32[128,6,2048]{2,1,0:T(8,128)} reshape(bf16[768,2048]{1,0:T(8,128)(2,1)} %gather_fusion.4) | data formatting | bytes 9437184 | tf_op jit(solution)/shard_map/convert_element_type | solution.py:124
  498.0 6.8 %multiply_reduce_fusion = f32[128,2048]{1,0:T(8,128)S(1)} fusion(f32[128,6,2048]{2,1,0:T(8,128)} %reshape.163, f32[128,6]{1,0:T(8,128)S(1)} %bitcast.75), kind=kLoop, calls=%fused_computation.8 | loop fusion | flops 2883584 | bytes 7343104 | tf_op jit(solution)/shard_map/reduce_sum | solution.py:124
  504.7 0.9 fusion.8
  (54 shorter events, 1.7 us)
Async XLA Ops:
  6.5 4.0 copy-start
  6.5 140.8 %all-gather.3.cloned.1.call-start = ((), (), s32[]{:S(2)}) async-start(), calls=%async_computation.5 | async-start | bytes 4718592 | tf_op jit(solution)/shard_map/all_gather | solution.py:16
  9.1 3.7 copy-start.7
  12.8 6.3 %copy-start.10 = (s32[1,128,6]{1,0,2:T(1,128)S(1)}, s32[1,128,6]{1,0,2:T(1,128)}, u32[]{:S(2)}) copy-start(s32[1,128,6]{1,0,2:T(1,128)} %param.21) | copy-start | bytes 9220
  12.8 117.8 %all-to-all-start.1 = ((bf16[8,256,704]{1,2,0:T(8,128)(2,1)}), bf16[8,256,704]{1,2,0:T(8,128)(2,1)S(1)}, u32[]{:S(2)}, u32[]{:S(2)}) async-start(bf16[8,256,704]{1,2,0:T(8,128)(2,1)} %gather_fusion.1), calls=%async_computation.1 | async-start | bytes 5767168 | tf_op jit(solution)/shard_map/all_to_all | solution.py:65
  130.7 7.9 %copy-start.2 = (bf16[8,256,704]{1,2,0:T(8,128)(2,1)}, bf16[8,256,704]{1,2,0:T(8,128)(2,1)S(1)}, u32[]{:S(2)}) copy-start(bf16[8,256,704]{1,2,0:T(8,128)(2,1)S(1)} %all-to-all-done.1) | copy-start | bytes 8650756
  130.7 67.6 %all-to-all-start.2 = ((bf16[8,256,704]{1,2,0:T(8,128)(2,1)}), bf16[8,256,704]{1,2,0:T(8,128)(2,1)}, u32[]{:S(2)}, u32[]{:S(2)}) async-start(bf16[8,256,704]{1,2,0:T(8,128)(2,1)} %gather_fusion.2), calls=%async_computation.2 | async-start | bytes 5767168 | tf_op jit(solution)/shard_map/all_to_all | solution.py:66
  152.7 3.3 copy-start.8
  158.0 1.0 copy-start.9
  158.1 1.0 copy-start.11
  158.2 1.9 copy-start.12
  159.2 0.8 copy-start.4
  174.5 30.7 %copy-start.6 = (bf16[4,704,256]{2,1,0:T(8,128)(2,1)S(1)}, bf16[4,704,256]{2,1,0:T(8,128)(2,1)}, u32[]{:S(2)}) copy-start(bf16[4,704,256]{2,1,0:T(8,128)(2,1)} %param.25) | copy-start | bytes 4325380
  198.3 97.6 %all-to-all-start = ((bf16[32,25,2048]{2,1,0:T(8,128)(2,1)}), bf16[32,25,2048]{2,1,0:T(8,128)(2,1)}, u32[]{:S(2)}, u32[]{:S(2)}) async-start(bf16[32,25,2048]{2,1,0:T(8,128)(2,1)} %broadcast_select_fusion), calls=%async_computation | async-start | bytes 8388608 | tf_op jit(solution)/shard_map/all_to_all | solution.py:113
  207.4 97.5 %copy-start.3 = (bf16[8,256,704]{1,2,0:T(8,128)(2,1)S(1)}, bf16[8,256,704]{1,2,0:T(8,128)(2,1)}, u32[]{:S(2)}) copy-start(bf16[8,256,704]{1,2,0:T(8,128)(2,1)} %copy-done.2) | copy-start | bytes 8650756
  295.9 71.0 %all-to-all-start.3 = ((bf16[8,704,256]{2,1,0:T(8,128)(2,1)}), bf16[8,704,256]{2,1,0:T(8,128)(2,1)}, u32[]{:S(2)}, u32[]{:S(2)}) async-start(bf16[8,704,256]{2,1,0:T(8,128)(2,1)} %gather_fusion.3), calls=%async_computation.3 | async-start | bytes 5767168 | tf_op jit(solution)/shard_map/all_to_all | solution.py:67
  385.0 6.7 %copy-start.13 = (f32[1,128,6]{1,0,2:T(1,128)S(1)}, f32[1,128,6]{1,0,2:T(1,128)}, u32[]{:S(2)}) copy-start(f32[1,128,6]{1,0,2:T(1,128)} %param.22) | copy-start | bytes 9220
  385.0 98.6 %all-to-all-start.4 = ((bf16[32,25,2048]{2,1,0:T(8,128)(2,1)}), bf16[32,25,2048]{2,1,0:T(8,128)(2,1)}, u32[]{:S(2)}, u32[]{:S(2)}) async-start(bf16[32,25,2048]{2,1,0:T(8,128)(2,1)} %reshape.159), calls=%async_computation.4 | async-start | bytes 8388608 | tf_op jit(solution)/shard_map/all_to_all | solution.py:122
  498.0 6.8 %copy-start.5 = (bf16[128,2048]{1,0:T(8,128)(2,1)S(1)}, bf16[128,2048]{1,0:T(8,128)(2,1)}, u32[]{:S(2)}) copy-start(bf16[128,2048]{1,0:T(8,128)(2,1)} %copy-done.4) | copy-start | bytes 1572868
  498.0 7.7 %copy-start.1 = (bf16[4,256,704]{1,2,0:T(8,128)(2,1)S(1)}, bf16[4,256,704]{1,2,0:T(8,128)(2,1)}, u32[]{:S(2)}) copy-start(bf16[4,256,704]{1,2,0:T(8,128)(2,1)} %param.23) | copy-start | bytes 4325380
Sparse Core Ops, SparseCore 0:
  10.6 122.1 all-gather.2

commit v2 on v1

--- a/solution.py
+++ b/solution.py
@@ -61,12 +61,30 @@
         capp = chunk * per
 
         seq_place = lax.axis_index("seq")
-        wanted = jnp.arange(n_seq, dtype=jnp.int32) // per
-        whole_gate = lax.all_to_all(gate_weight[wanted], "seq", 0, 0, tiled=True)
-        whole_up = lax.all_to_all(up_weight[wanted], "seq", 0, 0, tiled=True)
-        whole_down = lax.all_to_all(down_weight[wanted], "seq", 0, 0, tiled=True)
-        whole_gate = whole_gate.reshape(-1, whole_gate.shape[-1])
-        whole_up = whole_up.reshape(-1, whole_up.shape[-1])
+        slice_rows, hid = gate_weight.shape[1], gate_weight.shape[2]
+        part = slice_rows * hid
+        packed = jnp.concatenate(
+            [
+                gate_weight.reshape(local_experts, part),
+                up_weight.reshape(local_experts, part),
+                down_weight.reshape(local_experts, part),
+            ],
+            axis=1,
+        )
+        pieces = [lax.dynamic_index_in_dim(packed, seq_place // per, 0, False)]
+        for turn in range(1, n_seq):
+            target = (seq_place - turn) % n_seq
+            pieces.append(
+                lax.ppermute(
+                    lax.dynamic_index_in_dim(packed, target // per, 0, False),
+                    "seq",
+                    [(i, (i - turn) % n_seq) for i in range(n_seq)],
+                )
+            )
+        whole = jnp.roll(jnp.stack(pieces), seq_place, axis=0)
+        whole_gate = whole[:, :part].reshape(n_seq * slice_rows, hid)
+        whole_up = whole[:, part : 2 * part].reshape(n_seq * slice_rows, hid)
+        whole_down = whole[:, 2 * part :].reshape(n_seq, hid, slice_rows)
 
         tokens = queries.shape[1]
         query_heads = queries[0].reshape(tokens, HEADS, HEAD_DIM)

time: 519 us -> 722 us (1.39)
  the two profiles are of different devices: /device:TPU:16 before, /device:TPU:0 now
where the time goes in v2:
time: 722 us; the launch traced here: 710 us
  local copies, waits for them, and re-layouts  339 us (47%)
  waiting for transfers between devices  305 us (42%)
  starting transfers between devices  19.6 us (3%)
  matrix products  17.4 us (2%)
  other arithmetic  14.6 us (2%)
  between operations  14.1 us (2%)
    ppermute x7, waiting for transfers between devices, shards(): lax.ppermute(lax.dynamic_index_in_dim(packed, target // per, 0, False), '...  136 us
    all_to_all x1, waiting for transfers between devices, shards(): returned = lax.all_to_all(expert_rows, ('ep', 'seq'), 0, 0, tiled=True)  95 us
    concatenate x1, local copies, waits for them, and re-layouts, shards(): whole = jnp.roll(jnp.stack(pieces), seq_place, axis=0)  88 us
    dynamic_slice x1, local copies, waits for them, and re-layouts, shards(): lax.dynamic_index_in_dim(packed, target // per, 0, False)  87.5 us
    another operation x7, local copies, waits for them, and re-layouts, shards(): whole = jnp.roll(jnp.stack(pieces), seq_place, axis=0)  82.6 us
    all_to_all x1, waiting for transfers between devices, shards(): arrived = lax.all_to_all(outgoing, ('ep', 'seq'), 0, 0, tiled=True)  73.8 us
    unnamed x38, local copies, waits for them, and re-layouts  21.3 us
  transfers between devices with their start and end apart: 10, of which 5 were waited for; matrix products, arithmetic and copies ran while one was open for 43% of the time, Pallas kernels for 0%

profile of v2, /device:TPU:0, one launch (start us, length us, event | category | flops | bytes accessed | tf_op | source)
XLA Modules:
  0.0 709.9 jit_solution(4153354773832022908)
XLA Ops:
  6.5 1.4 copy.52
  12.0 1.9 reshape.185
  14.4 1.4 constant_dynamic-update-slice_fusion.2
  16.8 1.9 reshape.187
  19.2 2.5 copy.56
  21.6 1.4 constant_dynamic-update-slice_fusion.1
  23.1 1.4 constant_dynamic-update-slice_fusion
  24.4 87.5 %dynamic-slice_reduce_fusion = (bf16[540672]{0:T(1024)(128)(2,1)}, bf16[540672]{0:T(1024)(128)(2,1)}, bf16[540672]{0:T(1024)(128)(2,1)}, bf16[540672]{0:T(1024)(...) fusion(bf16[4,540672]{1,0:T(4,128)(2,1)} %constant_dynamic-upda, ...), kind=kLoop, calls=%fused_computation.12 | loop fusion | bytes 17301536 | tf_op jit(solution)/shard_map/jit(dynamic_index_in_dim)/dynamic_slice | solution.py:79
  112.0 6.1 collective-permute-start
  118.5 3.0 collective-permute-start.3
  123.1 1.7 reduce-window.6
  124.8 17.6 %collective-permute-done = bf16[540672]{0:T(1024)(128)(2,1)} collective-permute-done((bf16[540672]{0:T(1024)(128)(2,1)S(1)}, bf16[540672]{0:T(1024)(128)(2,1)}, u32[]{:S(2)}, u32[]{:S(2)}) %collective-permute-start) | collective-permute-done | bytes 1081376 | tf_op jit(solution)/shard_map/ppermute | solution.py:78
  142.4 23.2 %collective-permute-done.1 = bf16[540672]{0:T(1024)(128)(2,1)} collective-permute-done((bf16[540672]{0:T(1024)(128)(2,1)S(1)}, bf16[540672]{0:T(1024)(128)(2,1)}, u32[]{:S(2)}, u32[]{:S(2)}) %collective-permute-start.1) | collective-permute-done | bytes 1081376 | tf_op jit(solution)/shard_map/ppermute | solution.py:78
  166.2 3.4 scatter_custom_fusion.1
  169.6 3.4 scatter_custom_fusion
  173.2 11.1 %stack.23 = bf16[1,540672]{1,0:T(2,128)(2,1)S(1)} reshape(bf16[540672]{0:T(1024)(128)(2,1)} %collective-permute-done) | data formatting | bytes 2162688 | tf_op jit(solution)/shard_map/stack | solution.py:84
  184.3 11.9 %stack.24 = bf16[1,540672]{1,0:T(2,128)(2,1)} reshape(bf16[540672]{0:T(1024)(128)(2,1)} %collective-permute-done.1) | data formatting | bytes 2162688 | tf_op jit(solution)/shard_map/stack | solution.py:84
  196.1 11.8 %stack.25 = bf16[1,540672]{1,0:T(2,128)(2,1)} reshape(bf16[540672]{0:T(1024)(128)(2,1)} %collective-permute-done.2) | data formatting | bytes 2162688 | tf_op jit(solution)/shard_map/stack | solution.py:84
  208.0 95.3 %collective-permute-done.3 = bf16[540672]{0:T(1024)(128)(2,1)} collective-permute-done((bf16[540672]{0:T(1024)(128)(2,1)}, bf16[540672]{0:T(1024)(128)(2,1)}, u32[]{:S(2)}, u32[]{:S(2)}) %collective-permute-start.3) | collective-permute-done | bytes 1081376 | tf_op jit(solution)/shard_map/ppermute | solution.py:78
  303.3 11.9 %stack.26 = bf16[1,540672]{1,0:T(2,128)(2,1)} reshape(bf16[540672]{0:T(1024)(128)(2,1)} %collective-permute-done.3) | data formatting | bytes 2162688 | tf_op jit(solution)/shard_map/stack | solution.py:84
  315.2 11.8 %stack.27 = bf16[1,540672]{1,0:T(2,128)(2,1)} reshape(bf16[540672]{0:T(1024)(128)(2,1)} %collective-permute-done.4) | data formatting | bytes 2162688 | tf_op jit(solution)/shard_map/stack | solution.py:84
  327.0 12.2 %stack.28 = bf16[1,540672]{1,0:T(2,128)(2,1)} reshape(bf16[540672]{0:T(1024)(128)(2,1)} %collective-permute-done.5) | data formatting | bytes 2162688 | tf_op jit(solution)/shard_map/stack | solution.py:84
  339.3 11.8 %stack.29 = bf16[1,540672]{1,0:T(2,128)(2,1)} reshape(bf16[540672]{0:T(1024)(128)(2,1)} %collective-permute-done.6) | data formatting | bytes 2162688 | tf_op jit(solution)/shard_map/stack | solution.py:84
  351.1 88.0 %concatenate.9 = bf16[16,540672]{1,0:T(8,128)(2,1)} concatenate(bf16[1,540672]{1,0:T(2,128)(2,1)} %get-tuple-element.47, bf16[1,540672]{1,0:T(2,128)(2,1)S(1)} %stack.23, bf16[1,540672]{1,0:T(2,128)(2,1)} %stack.24, bf16[1,540672]{1,0:T(2,128)(2,1)} %stack.25, bf16[1,540672]{1,0:T(2,128)(2,1)} %stack.26, bf16[1,540672]{1,0:T(2,128)(2,1)} %stack.27, bf16[1,540672]{1,0:T(2,128)(2,1)} %stack.28, ...), dimensions={0} | concatenate | bytes 34603008 | tf_op jit(solution)/shard_map/jit(_roll_dynamic)/concatenate | solution.py:84
  439.2 3.3 convolution_bitcast_fusion.1
  442.5 2.1 multiply_reduce_fusion.1
  446.8 4.8 gather_fusion
  451.6 5.0 gather.9
  456.6 4.6 broadcast_select_fusion
  461.1 6.4 all-to-all-start
  467.6 7.4 %fusion.35 = (bf16[8,180224]{1,0:T(8,128)(2,1)}, bf16[8,180224]{1,0:T(8,128)(2,1)}, bf16[8,180224]{1,0:T(8,128)(2,1)}) fusion(bf16[16,540672]{1,0:T(8,128)(2,1)} %concatenate.9, s32[]{:T(128)S(6)} %select_n.155, s32[]{:T(128)S(6)} %add.195, s32[]{:T(128)S(6)} %add.194), kind=kLoop, calls=%fused_computation.79 | loop fusion | bytes 17301516 | tf_op jit(solution)/shard_map/slice | solution.py:87
  474.9 3.1 reshape.191
  478.0 3.9 reshape.129
  481.9 3.1 reshape.189
  485.0 3.9 reshape.130
  488.9 73.8 %all-to-all-done = bf16[32,25,2048]{2,1,0:T(8,128)(2,1)} async-done(((bf16[32,25,2048]{2,1,0:T(8,128)(2,1)}), bf16[32,25,2048]{2,1,0:T(8,128)(2,1)}, u32[]{:S(2)}, u32[]{:S(2)}) %all-to-all-start) | async-done | bytes 3276832 | tf_op jit(solution)/shard_map/all_to_all | solution.py:131
  562.7 3.4 reshape.125
  566.1 4.7 fusion.40
  570.9 2.9 fusion.6
  573.8 3.2 fusion.3
  577.0 1.9 copy.49
  578.8 3.2 reshape.132
  582.1 3.7 all-to-all-start.1
  585.9 95.0 %all-to-all-done.1 = bf16[32,25,2048]{2,1,0:T(8,128)(2,1)} async-done(((bf16[32,25,2048]{2,1,0:T(8,128)(2,1)}), bf16[32,25,2048]{2,1,0:T(8,128)(2,1)}, u32[]{:S(2)}, u32[]{:S(2)}) %all-to-all-start.1) | async-done | bytes 3276832 | tf_op jit(solution)/shard_map/all_to_all | solution.py:140
  680.9 3.4 reshape.133
  684.4 4.3 gather_fusion.1
  688.7 6.6 reshape.136
  695.3 6.7 multiply_reduce_fusion
  (74 shorter events, 12.0 us)
Async XLA Ops:
  6.5 4.7 copy-start.6
  6.5 432.6 %all-gather.3.cloned.1.call-start = ((), (), s32[]{:S(2)}) async-start(), calls=%async_computation.2 | async-start | bytes 4718592 | tf_op jit(solution)/shard_map/all_gather | solution.py:16
  9.1 0.8 copy-start.2
  14.4 1.7 copy-start.7
  24.4 97.1 %copy-start.9 = (s32[1,128,6]{1,0,2:T(1,128)S(1)}, s32[1,128,6]{1,0,2:T(1,128)}, u32[]{:S(2)}) copy-start(s32[1,128,6]{1,0,2:T(1,128)} %param.21) | copy-start | bytes 9220
  112.0 30.4 %collective-permute-start = (bf16[540672]{0:T(1024)(128)(2,1)S(1)}, bf16[540672]{0:T(1024)(128)(2,1)}, u32[]{:S(2)}, u32[]{:S(2)}) collective-permute-start(bf16[540672]{0:T(1024)(128)(2,1)S(1)} %get-tuple-element.35), channel_id=1, source_target_pairs={{0,28},{4,0},{8,4},{12,8},{16,12},{20,16},{24,20},{28,24},{1,29},{... | collective-permute-start | bytes 3244040 | tf_op jit(solution)/shard_map/ppermute | solution.py:78
  118.0 47.5 %collective-permute-start.1 = (bf16[540672]{0:T(1024)(128)(2,1)S(1)}, bf16[540672]{0:T(1024)(128)(2,1)}, u32[]{:S(2)}, u32[]{:S(2)}) collective-permute-start(bf16[540672]{0:T(1024)(128)(2,1)S(1)} %get-tuple-element.34), channel_id=1, source_target_pairs={{0,24},{4,28},{8,0},{12,4},{16,8},{20,12},{24,16},{28,20},{1,25},{... | collective-permute-start | bytes 3244040 | tf_op jit(solution)/shard_map/ppermute | solution.py:78
  118.5 77.7 %collective-permute-start.2 = (bf16[540672]{0:T(1024)(128)(2,1)}, bf16[540672]{0:T(1024)(128)(2,1)}, u32[]{:S(2)}, u32[]{:S(2)}) collective-permute-start(bf16[540672]{0:T(1024)(128)(2,1)} %get-tuple-element.33), channel_id=1, source_target_pairs={{0,20},{4,24},{8,28},{12,0},{16,4},{20,8},{24,12},{28,16},{1,21},{... | collective-permute-start | bytes 3244040 | tf_op jit(solution)/shard_map/ppermute | solution.py:78
  118.5 184.9 %collective-permute-start.3 = (bf16[540672]{0:T(1024)(128)(2,1)}, bf16[540672]{0:T(1024)(128)(2,1)}, u32[]{:S(2)}, u32[]{:S(2)}) collective-permute-start(bf16[540672]{0:T(1024)(128)(2,1)} %get-tuple-element.32), channel_id=1, source_target_pairs={{0,16},{4,20},{8,24},{12,28},{16,0},{20,4},{24,8},{28,12},{1,17},{... | collective-permute-start | bytes 3244040 | tf_op jit(solution)/shard_map/ppermute | solution.py:78
  121.5 193.7 %collective-permute-start.4 = (bf16[540672]{0:T(1024)(128)(2,1)}, bf16[540672]{0:T(1024)(128)(2,1)}, u32[]{:S(2)}, u32[]{:S(2)}) collective-permute-start(bf16[540672]{0:T(1024)(128)(2,1)} %get-tuple-element.31), channel_id=1, source_target_pairs={{0,12},{4,16},{8,20},{12,24},{16,28},{20,0},{24,4},{28,8},{1,13},{... | collective-permute-start | bytes 3244040 | tf_op jit(solution)/shard_map/ppermute | solution.py:78
  142.4 184.7 %collective-permute-start.5 = (bf16[540672]{0:T(1024)(128)(2,1)}, bf16[540672]{0:T(1024)(128)(2,1)}, u32[]{:S(2)}, u32[]{:S(2)}) collective-permute-start(bf16[540672]{0:T(1024)(128)(2,1)} %get-tuple-element.30), channel_id=1, source_target_pairs={{0,8},{4,12},{8,16},{12,20},{16,24},{20,28},{24,0},{28,4},{1,9},{5... | collective-permute-start | bytes 3244040 | tf_op jit(solution)/shard_map/ppermute | solution.py:78
  165.5 173.7 %collective-permute-start.6 = (bf16[540672]{0:T(1024)(128)(2,1)}, bf16[540672]{0:T(1024)(128)(2,1)}, u32[]{:S(2)}, u32[]{:S(2)}) collective-permute-start(bf16[540672]{0:T(1024)(128)(2,1)} %get-tuple-element.29), channel_id=1, source_target_pairs={{0,4},{4,8},{8,12},{12,16},{16,20},{20,24},{24,28},{28,0},{1,5},{5... | collective-permute-start | bytes 3244040 | tf_op jit(solution)/shard_map/ppermute | solution.py:78
  439.2 3.3 copy-start.3
  444.6 1.0 copy-start.8
  444.6 1.0 copy-start.10
  444.7 1.9 copy-start.11
  445.8 0.8 copy-start
  461.1 101.5 %all-to-all-start = ((bf16[32,25,2048]{2,1,0:T(8,128)(2,1)}), bf16[32,25,2048]{2,1,0:T(8,128)(2,1)}, u32[]{:S(2)}, u32[]{:S(2)}) async-start(bf16[32,25,2048]{2,1,0:T(8,128)(2,1)} %broadcast_select_fusion), calls=%async_computation | async-start | bytes 8388608 | tf_op jit(solution)/shard_map/all_to_all | solution.py:131
  566.1 4.8 copy-start.4
  570.9 2.9 copy-start.5
  582.1 3.7 copy-start.12
  582.1 98.9 %all-to-all-start.1 = ((bf16[32,25,2048]{2,1,0:T(8,128)(2,1)}), bf16[32,25,2048]{2,1,0:T(8,128)(2,1)}, u32[]{:S(2)}, u32[]{:S(2)}) async-start(bf16[32,25,2048]{2,1,0:T(8,128)(2,1)} %reshape.132), calls=%async_computation.1 | async-start | bytes 8388608 | tf_op jit(solution)/shard_map/all_to_all | solution.py:140
  695.3 6.7 copy-start.1
Sparse Core Ops, SparseCore 0:
  11.4 76.0 all-gather.2

commit v3 on v1

--- a/solution.py
+++ b/solution.py
@@ -1,7 +1,7 @@
 import jax
 import jax.numpy as jnp
 from jax import lax
-from jax.sharding import PartitionSpec as P
+from jax.sharding import Mesh, PartitionSpec as P
 
 D = 2048
 HEADS = 16
@@ -38,7 +38,8 @@
     return earlier + later
 
 
-def make_shards(n_ep, n_seq):
+def make_shards(n_ep, n_outer, n_inner):
+    n_seq = n_outer * n_inner
     n_dev = n_ep * n_seq
 
     def shards(
@@ -60,11 +61,16 @@
         chunk = -(-CAP // per)
         capp = chunk * per
 
-        seq_place = lax.axis_index("seq")
-        wanted = jnp.arange(n_seq, dtype=jnp.int32) // per
-        whole_gate = lax.all_to_all(gate_weight[wanted], "seq", 0, 0, tiled=True)
-        whole_up = lax.all_to_all(up_weight[wanted], "seq", 0, 0, tiled=True)
-        whole_down = lax.all_to_all(down_weight[wanted], "seq", 0, 0, tiled=True)
+        per_outer = n_outer // local_experts
+        wanted = jnp.arange(n_outer, dtype=jnp.int32) // per_outer
+
+        def collect(weight):
+            mine = lax.all_to_all(weight[wanted], "seq_outer", 0, 0, tiled=True)
+            return lax.all_gather(mine, "seq_inner", axis=0, tiled=False)
+
+        whole_gate = collect(gate_weight)
+        whole_up = collect(up_weight)
+        whole_down = collect(down_weight)
         whole_gate = whole_gate.reshape(-1, whole_gate.shape[-1])
         whole_up = whole_up.reshape(-1, whole_up.shape[-1])
 
@@ -75,7 +81,7 @@
         local_state = jnp.einsum(
             "thd,the->hde", key_heads, value_heads, preferred_element_type=jnp.float32
         )
-        earlier = carried_in(local_state, "seq", add_states, jnp.zeros_like(local_state))
+        earlier = carried_in(local_state, ("seq_outer", "seq_inner"), add_states, jnp.zeros_like(local_state))
         state_before = state_start[0] + earlier
         causal = (
             jnp.arange(tokens, dtype=jnp.int32)[:, None]
@@ -110,40 +116,51 @@
         filled = jnp.zeros((EXPERTS * capp,), jnp.bool_).at[position].set(True)
         outgoing = jnp.where(filled[:, None], ffn_in[source], jnp.zeros((), jnp.bfloat16))
         outgoing = outgoing.reshape(EXPERTS * per, chunk, D)
-        arrived = lax.all_to_all(outgoing, ("ep", "seq"), 0, 0, tiled=True)
-        arrived = arrived.reshape(n_dev * chunk, D)
+        arrived = lax.all_to_all(outgoing, ("ep", "seq_outer", "seq_inner"), 0, 0, tiled=True)
+        arrived = arrived.reshape(n_dev * chunk, n_outer, n_inner, D // n_seq)
+        arrived = arrived.transpose(0, 2, 1, 3).reshape(n_dev * chunk, D)
         gate_sum = jnp.dot(arrived, whole_gate, preferred_element_type=jnp.float32)
         up_sum = jnp.dot(arrived, whole_up, preferred_element_type=jnp.float32)
         hidden = silu_gate(gate_sum, up_sum).astype(jnp.bfloat16)
         expert_rows = jnp.einsum(
-            "rh,shd->rsd", hidden, whole_down, preferred_element_type=jnp.float32
+            "rh,xzhd->rzxd", hidden, whole_down, preferred_element_type=jnp.float32
         ).astype(jnp.bfloat16)
         expert_rows = expert_rows.reshape(n_dev, chunk, D)
-        returned = lax.all_to_all(expert_rows, ("ep", "seq"), 0, 0, tiled=True)
+        returned = lax.all_to_all(expert_rows, ("ep", "seq_outer", "seq_inner"), 0, 0, tiled=True)
         picked = returned.reshape(EXPERTS * capp, D)[position].reshape(tokens, TOP, D)
         expert_mix = jnp.sum(route_gates[0][:, :, None] * picked.astype(jnp.float32), axis=1)
-        del seq_place
         return (mixed_wide + expert_mix).astype(jnp.bfloat16)[None]
 
     return shards
 
 
 def solution(mesh):
+    seq = ("seq_outer", "seq_inner")
     placed = (
-        P("ep", "seq", None),
-        P("ep", "seq", None),
-        P("ep", "seq", None),
-        P("ep", "seq", None),
+        P("ep", seq, None),
+        P("ep", seq, None),
+        P("ep", seq, None),
+        P("ep", seq, None),
         P("ep", None, None, None),
         P(),
         P(),
-        P("ep", "seq", None),
-        P("ep", "seq", None),
-        P("ep", "seq", None),
-        P("ep", "seq", None),
-        P("ep", None, "seq"),
+        P("ep", seq, None),
+        P("ep", seq, None),
+        P("ep", seq, None),
+        P("ep", seq, None),
+        P("ep", None, seq),
     )
-    shards = make_shards(mesh.shape["ep"], mesh.shape["seq"])
+    n_seq, n_ep = mesh.shape["seq"], mesh.shape["ep"]
+    n_inner = 2 if n_seq % 2 == 0 else 1
+    names = list(mesh.axis_names)
+    shape = []
+    for name in names:
+        shape += [n_seq // n_inner, n_inner] if name == "seq" else [mesh.shape[name]]
+    split_names = []
+    for name in names:
+        split_names += list(seq) if name == "seq" else [name]
+    split = Mesh(mesh.devices.reshape(shape), tuple(split_names))
+    shards = make_shards(n_ep, n_seq // n_inner, n_inner)
     return jax.shard_map(
-        shards, mesh=mesh, in_specs=placed, out_specs=P("ep", "seq", None), check_vma=False
+        shards, mesh=split, in_specs=placed, out_specs=P("ep", seq, None), check_vma=False
     )

time: 519 us -> 471 us (0.908)
  waiting for transfers between devices: 354 us -> 302 us
    all_to_all x5, waiting for transfers between devices: 354 us -> 223 us  [the longest x1 90.6 us: shards(): lax.all_to_all(expert_rows, ('ep', 'seq_outer', 'seq_inner'), 0, 0, tiled...]
    all_gather x1, waiting for transfers between devices: 0.02 us -> 60.5 us  [carried_in(): gathered = lax.all_gather(array.astype(jnp.bfloat16), axis)]
    all_gather x0 -> x3, waiting for transfers between devices: none -> 17.2 us  [collect(): return lax.all_gather(mine, 'seq_inner', axis=0, tiled=False)]
  transfers between devices with their start and end apart: 6 -> 9, of which waited for: 5 -> 6; matrix products, arithmetic and copies ran while one was open for 12% -> 14% of each run, Pallas kernels for 0% -> 0%
where the time goes in v3:
time: 471 us; the launch traced here: 464 us
  waiting for transfers between devices  302 us (64%)
  local copies, waits for them, and re-layouts  64.3 us (14%)
  starting transfers between devices  37.7 us (8%)
  matrix products  24.8 us (5%)
  other arithmetic  21.5 us (5%)
  between operations  13.5 us (3%)
    all_to_all x1, waiting for transfers between devices, shards(): lax.all_to_all(expert_rows, ('ep', 'seq_outer', 'seq_inner'), 0, 0, tiled...  90.6 us
    all_to_all x1, waiting for transfers between devices, shards(): lax.all_to_all(outgoing, ('ep', 'seq_outer', 'seq_inner'), 0, 0, tiled=True)  89.4 us
    all_gather x1, waiting for transfers between devices, carried_in(): gathered = lax.all_gather(array.astype(jnp.bfloat16), axis)  60.5 us
    all_to_all x3, waiting for transfers between devices, collect(): mine = lax.all_to_all(weight[wanted], 'seq_outer', 0, 0, tiled=True)  43.2 us
    all_to_all x3, starting transfers between devices, collect(): mine = lax.all_to_all(weight[wanted], 'seq_outer', 0, 0, tiled=True)  22 us
    all_gather x3, waiting for transfers between devices, collect(): return lax.all_gather(mine, 'seq_inner', axis=0, tiled=False)  17.2 us
    dot_general x1, matrix products, shards(): jnp.einsum('rh,xzhd->rzxd', hidden, whole_down, preferred_element_type=jn...  11.2 us
    gather x2, local copies, waits for them, and re-layouts, shards(): ffn_in[source]  9.77 us
  transfers between devices with their start and end apart: 9, of which 6 were waited for; matrix products, arithmetic and copies ran while one was open for 14% of the time, Pallas kernels for 0%

profile of v3, /device:TPU:16, one launch (start us, length us, event | category | flops | bytes accessed | tf_op | source)
XLA Modules:
  0.0 463.9 jit_solution(11184702969502416443)
XLA Ops:
  6.5 1.4 copy.53
  8.0 1.1 copy.55
  9.1 1.3 convolution_convert_fusion
  10.5 1.8 gather_fusion.2
  12.3 5.3 %all-to-all-start.2 = ((bf16[4,256,704]{1,2,0:T(8,128)(2,1)}), bf16[4,256,704]{1,2,0:T(8,128)(2,1)S(1)}, u32[]{:S(2)}, u32[]{:S(2)}) async-start(bf16[4,256,704]{1,2,0:T(8,128)(2,1)} %gather_fusion.2), calls=%async_computation.2 | async-start | bytes 2883584 | tf_op jit(solution)/shard_map/all_to_all | solution.py:68
  18.0 0.9 copy.56
  18.9 1.7 reduce-window.6
  21.3 3.4 scatter_custom_fusion.1
  24.7 3.4 scatter_custom_fusion
  28.1 0.7 broadcast_in_dim.58
  28.8 3.2 gather_fusion.3
  32.0 3.1 gather_fusion
  35.1 30.2 %all-to-all-done.2 = bf16[4,256,704]{1,2,0:T(8,128)(2,1)S(1)} async-done(((bf16[4,256,704]{1,2,0:T(8,128)(2,1)}), bf16[4,256,704]{1,2,0:T(8,128)(2,1)S(1)}, u32[]{:S(2)}, u32[]{:S(2)}) %all-to-all-start.2) | async-done | bytes 1441824 | tf_op jit(solution)/shard_map/all_to_all | solution.py:68
  65.4 7.6 %all-to-all-start.3 = ((bf16[4,256,704]{1,2,0:T(8,128)(2,1)}), bf16[4,256,704]{1,2,0:T(8,128)(2,1)}, u32[]{:S(2)}, u32[]{:S(2)}) async-start(bf16[4,256,704]{1,2,0:T(8,128)(2,1)} %gather_fusion.3), calls=%async_computation.3 | async-start | bytes 2883584 | tf_op jit(solution)/shard_map/all_to_all | solution.py:68
  72.9 0.6 pad_clamp_fusion.2
  73.7 60.5 %all-gather.9.cloned.1.call-done = bf16[128,128,128]{2,1,0:T(8,128)(2,1)} async-done(((bf16[16,128,128]{2,1,0:T(8,128)(2,1)}), bf16[128,128,128]{2,1,0:T(8,128)(2,1)}) %all-gather.9.cloned.1.call-update) | async-done | bytes 4194320 | tf_op jit(solution)/shard_map/all_gather | solution.py:16
  134.2 5.3 %while.10 = (s32[]{:T(128)}, f32[16,128,128]{2,1,0:T(8,128)S(1)}, s32[]{:T(128)}, bf16[8,16,128,128]{3,2,1,0:T(8,128)(2,1)}, s32[]{:T(128)}, /*index=5*/s32[]{:T(128)}, s32[]{:T(128)}) while((s32[]{:T(128)}, f32[16,128,128]{2,1,0:T(8,128)S(1)}, s32[]{:T(128)}, bf16[8,16,128,128]{3,2,1,0:T(8,128)(2,1)}, s32[]{:T(128)}, /*index=5*/s32[]{:T(128)}, ...), condition=%wide.region_1.2_spmd, body=%wide.region_0.1_spmd.sunk | while | flops 524293 | bytes 2621555 | solution.py:22
  134.3 1.3 convert_add_fusion.4
  135.6 1.3 convert_add_fusion.4
  136.9 1.3 convert_add_fusion.4
  138.2 1.3 convert_add_fusion.4
  139.5 3.2 convolution_bitcast_fusion.1
  142.8 3.1 multiply_reduce_fusion.1
  145.9 9.1 %all-to-all-start = ((bf16[4,704,256]{2,1,0:T(8,128)(2,1)}), bf16[4,704,256]{2,1,0:T(8,128)(2,1)S(1)}, u32[]{:S(2)}, u32[]{:S(2)}) async-start(bf16[4,704,256]{2,1,0:T(8,128)(2,1)} %gather_fusion), calls=%async_computation | async-start | bytes 2883584 | tf_op jit(solution)/shard_map/all_to_all | solution.py:68
  155.0 1.1 broadcast_multiply_fusion
  156.1 1.6 copy.40
  158.1 0.6 copy-done.2
  158.9 4.8 %gather_fusion.1 = bf16[800,2048]{1,0:T(8,128)(2,1)} fusion(bf16[128,2048]{1,0:T(8,128)(2,1)S(1)} %fusion.18, s32[1024]{0:T(1024)S(1)} %copy-done.13), kind=kCustom, calls=%fused_computation.1 | custom fusion | bytes 6556800 | tf_op jit(solution)/shard_map/gather | solution.py:117
  163.7 4.9 %gather.19 = bf16[32,25,2048]{2,1,0:T(8,128)(2,1)} reshape(bf16[800,2048]{1,0:T(8,128)(2,1)} %gather_fusion.1) | data formatting | bytes 6553600 | tf_op jit(solution)/shard_map/gather | solution.py:117
  168.6 4.5 broadcast_select_fusion
  173.1 13.0 %all-to-all-done = bf16[4,704,256]{2,1,0:T(8,128)(2,1)S(1)} async-done(((bf16[4,704,256]{2,1,0:T(8,128)(2,1)}), bf16[4,704,256]{2,1,0:T(8,128)(2,1)S(1)}, u32[]{:S(2)}, u32[]{:S(2)}) %all-to-all-start) | async-done | bytes 1441824 | tf_op jit(solution)/shard_map/all_to_all | solution.py:68
  186.1 1.1 copy-done.5
  187.2 8.4 %all-to-all-start.1 = ((bf16[32,25,2048]{2,1,0:T(8,128)(2,1)}), bf16[32,25,2048]{2,1,0:T(8,128)(2,1)}, u32[]{:S(2)}, u32[]{:S(2)}) async-start(bf16[32,25,2048]{2,1,0:T(8,128)(2,1)} %broadcast_select_fusion), calls=%async_computation.1 | async-start | bytes 8388608 | tf_op jit(solution)/shard_map/all_to_all | solution.py:119
  195.6 0.7 all-gather.15.cloned.1.call-update
  196.9 89.4 %all-to-all-done.1 = bf16[32,25,2048]{2,1,0:T(8,128)(2,1)} async-done(((bf16[32,25,2048]{2,1,0:T(8,128)(2,1)}), bf16[32,25,2048]{2,1,0:T(8,128)(2,1)}, u32[]{:S(2)}, u32[]{:S(2)}) %all-to-all-start.1) | async-done | bytes 3276832 | tf_op jit(solution)/shard_map/all_to_all | solution.py:119
  286.3 7.7 %reshape.111 = bf16[800,4,2,256]{3,2,1,0:T(2,128)(2,1)S(1)} reshape(bf16[32,25,2048]{2,1,0:T(8,128)(2,1)} %all-to-all-done.1) | data formatting | bytes 6553600 | tf_op jit(solution)/shard_map/reshape | solution.py:120
  294.0 6.0 %fusion.2 = f32[800,704,1,1]{1,0,3,2:T(8,128)} fusion(bf16[2,4,256,704]{2,3,1,0:T(8,128)(2,1)} %bitcast.111, bf16[800,4,2,256]{3,2,1,0:T(2,128)(2,1)S(1)} %reshape.111), kind=kOutput, calls=%fused_computation.12 | convolution fusion | flops 2306867200 | bytes 8413184 | tf_op jit(solution)/shard_map/dot_general | solution.py:122
  300.0 17.2 %all-gather.11.cloned.1.call-done = bf16[8,704,256]{2,1,0:T(8,128)(2,1)} async-done(((bf16[4,704,256]{2,1,0:T(8,128)(2,1)}), bf16[8,704,256]{2,1,0:T(8,128)(2,1)}) %all-gather.11.cloned.1.call-update) | async-done | bytes 2883600 | tf_op jit(solution)/shard_map/all_gather | solution.py:69
  317.2 11.2 %convert_bitcast_fusion = bf16[800,4,2,256]{3,0,1,2:T(8,128)(2,1)} fusion(bf16[2,4,704,256]{3,2,1,0:T(8,128)(2,1)} %bitcast.113, bf16[2,4,256,704]{2,3,1,0:T(8,128)(2,1)} %bitcast.112, bf16[800,4,2,256]{3,2,1,0:T(2,128)(2,1)S(1)} %reshape.111, f32[800,704,1,1]{1,0,3,2:T(8,128)} %fusion.2), kind=kOutput, calls=%fused_computation.14 | convolution fusion | flops 4618188800 | bytes 14573568 | tf_op jit(solution)/shard_map/rh,xzhd->rzxd/dot_general | solution.py:125
  328.4 5.3 %copy.47 = bf16[800,4,2,256]{3,2,1,0:T(2,128)(2,1)S(1)} copy(bf16[800,4,2,256]{3,0,1,2:T(8,128)(2,1)} %convert_bitcast_fusion) | data formatting | bytes 6553600 | tf_op jit(solution)/shard_map/convert_element_type | solution.py:127
  333.7 3.8 reshape.112
  337.5 7.1 %all-to-all-start.4 = ((bf16[32,25,2048]{2,1,0:T(8,128)(2,1)}), bf16[32,25,2048]{2,1,0:T(8,128)(2,1)}, u32[]{:S(2)}, u32[]{:S(2)}) async-start(bf16[32,25,2048]{2,1,0:T(8,128)(2,1)} %reshape.112), calls=%async_computation.4 | async-start | bytes 8388608 | tf_op jit(solution)/shard_map/all_to_all | solution.py:129
  344.8 90.6 %all-to-all-done.4 = bf16[32,25,2048]{2,1,0:T(8,128)(2,1)} async-done(((bf16[32,25,2048]{2,1,0:T(8,128)(2,1)}), bf16[32,25,2048]{2,1,0:T(8,128)(2,1)}, u32[]{:S(2)}, u32[]{:S(2)}) %all-to-all-start.4) | async-done | bytes 3276832 | tf_op jit(solution)/shard_map/all_to_all | solution.py:129
  435.3 3.4 reshape.113
  438.8 4.3 gather_fusion.4
  443.1 6.5 %reshape.116 = f32[128,6,2048]{2,1,0:T(8,128)} reshape(bf16[768,2048]{1,0:T(8,128)(2,1)} %gather_fusion.4) | data formatting | bytes 9437184 | tf_op jit(solution)/shard_map/convert_element_type | solution.py:131
  449.7 6.8 %multiply_reduce_fusion = f32[128,2048]{1,0:T(8,128)S(1)} fusion(f32[128,6,2048]{2,1,0:T(8,128)} %reshape.116, f32[128,6]{1,0:T(8,128)S(1)} %bitcast.109), kind=kLoop, calls=%fused_computation.8 | loop fusion | flops 2883584 | bytes 7343104 | tf_op jit(solution)/shard_map/reduce_sum | solution.py:131
  456.4 0.9 fusion.23
  (69 shorter events, 2.7 us)
Async XLA Ops:
  6.5 4.0 copy-start
  6.5 127.6 %all-gather.9.cloned.1.call-start = ((), (), s32[]{:S(2)}) async-start(), calls=%async_computation.5 | async-start | bytes 4718592 | tf_op jit(solution)/shard_map/all_gather | solution.py:16
  10.5 7.1 %copy-start.14 = (s32[1,128,6]{1,0,2:T(1,128)S(1)}, s32[1,128,6]{1,0,2:T(1,128)}, u32[]{:S(2)}) copy-start(s32[1,128,6]{1,0,2:T(1,128)} %param.21) | copy-start | bytes 9220
  12.3 5.7 %copy-start.8 = (bf16[1,128,2048]{2,1,0:T(8,128)(2,1)S(1)}, bf16[1,128,2048]{2,1,0:T(8,128)(2,1)}, u32[]{:S(2)}) copy-start(bf16[1,128,2048]{2,1,0:T(8,128)(2,1)} %param.14) | copy-start | bytes 1572868
  12.3 53.1 %all-to-all-start.2 = ((bf16[4,256,704]{1,2,0:T(8,128)(2,1)}), bf16[4,256,704]{1,2,0:T(8,128)(2,1)S(1)}, u32[]{:S(2)}, u32[]{:S(2)}) async-start(bf16[4,256,704]{1,2,0:T(8,128)(2,1)} %gather_fusion.2), calls=%async_computation.2 | async-start | bytes 2883584 | tf_op jit(solution)/shard_map/all_to_all | solution.py:68
  21.3 13.8 %copy-start.11 = (s32[768]{0:T(1024)}, s32[768]{0:T(1024)S(1)}, u32[]{:S(2)}) copy-start(s32[768]{0:T(1024)S(1)} %fusion.38) | copy-start | bytes 9220
  65.4 8.2 %copy-start.4 = (bf16[4,256,704]{1,2,0:T(8,128)(2,1)}, bf16[4,256,704]{1,2,0:T(8,128)(2,1)S(1)}, u32[]{:S(2)}) copy-start(bf16[4,256,704]{1,2,0:T(8,128)(2,1)S(1)} %all-to-all-done.2) | copy-start | bytes 4325380
  65.4 80.5 %all-to-all-start.3 = ((bf16[4,256,704]{1,2,0:T(8,128)(2,1)}), bf16[4,256,704]{1,2,0:T(8,128)(2,1)}, u32[]{:S(2)}, u32[]{:S(2)}) async-start(bf16[4,256,704]{1,2,0:T(8,128)(2,1)} %gather_fusion.3), calls=%async_computation.3 | async-start | bytes 2883584 | tf_op jit(solution)/shard_map/all_to_all | solution.py:68
  72.9 221.0 %all-gather.13.cloned.1.call-start = ((), (), s32[]{:S(2)}) async-start(), calls=%async_computation.7 | async-start | bytes 4325376 | tf_op jit(solution)/shard_map/all_gather | solution.py:69
  134.2 5.3 %copy-start.6 = (bf16[16,8,16,128]{3,2,1,0:T(8,128)(2,1)S(1)}, bf16[16,8,16,128]{3,2,1,0:T(8,128)(2,1)}, u32[]{:S(2)}) copy-start(bf16[16,8,16,128]{3,2,1,0:T(8,128)(2,1)} %copy.56) | copy-start | bytes 1572868
  145.8 9.1 %copy-start.7 = (f32[128,16,128]{0,2,1:T(8,128)S(1)}, f32[128,16,128]{0,2,1:T(8,128)}, u32[]{:S(2)}) copy-start(f32[128,16,128]{0,2,1:T(8,128)} %get-tuple-element.38) | copy-start | bytes 3145732
  145.9 11.8 %copy-start.9 = (bf16[1,128,2048]{2,1,0:T(8,128)(2,1)S(1)}, bf16[1,128,2048]{2,1,0:T(8,128)(2,1)}, u32[]{:S(2)}) copy-start(bf16[1,128,2048]{2,1,0:T(8,128)(2,1)} %param.17) | copy-start | bytes 1572868
  145.9 11.8 %copy-start.15 = (f32[2048]{0:T(1024)S(1)}, f32[2048]{0:T(1024)}, u32[]{:S(2)}) copy-start(f32[2048]{0:T(1024)} %param.19) | copy-start | bytes 24580
  145.9 40.2 %all-to-all-start = ((bf16[4,704,256]{2,1,0:T(8,128)(2,1)}), bf16[4,704,256]{2,1,0:T(8,128)(2,1)S(1)}, u32[]{:S(2)}, u32[]{:S(2)}) async-start(bf16[4,704,256]{2,1,0:T(8,128)(2,1)} %gather_fusion), calls=%async_computation | async-start | bytes 2883584 | tf_op jit(solution)/shard_map/all_to_all | solution.py:68
  156.1 2.5 copy-start.16
  156.1 2.7 copy-start.13
  157.8 0.8 copy-start.2
  163.7 4.9 %copy-start.10 = (pred[32,25]{1,0:T(8,128)(4,1)S(1)}, pred[32,25]{1,0:T(8,128)(4,1)}, u32[]{:S(2)}) copy-start(pred[32,25]{1,0:T(8,128)(4,1)} %broadcast_in_dim.58) | copy-start | bytes 2404
  186.1 1.1 copy-start.5
  187.2 99.0 %all-to-all-start.1 = ((bf16[32,25,2048]{2,1,0:T(8,128)(2,1)}), bf16[32,25,2048]{2,1,0:T(8,128)(2,1)}, u32[]{:S(2)}, u32[]{:S(2)}) async-start(bf16[32,25,2048]{2,1,0:T(8,128)(2,1)} %broadcast_select_fusion), calls=%async_computation.1 | async-start | bytes 8388608 | tf_op jit(solution)/shard_map/all_to_all | solution.py:119
  195.6 104.4 %all-gather.15.cloned.1.call-start = ((), (), s32[]{:S(2)}) async-start(), calls=%async_computation.8 | async-start | bytes 4325376 | tf_op jit(solution)/shard_map/all_gather | solution.py:69
  196.3 120.9 %all-gather.11.cloned.1.call-start = ((), (), s32[]{:S(2)}) async-start(), calls=%async_computation.6 | async-start | bytes 4325376 | tf_op jit(solution)/shard_map/all_gather | solution.py:69
  337.5 7.1 %copy-start.17 = (f32[1,128,6]{1,0,2:T(1,128)S(1)}, f32[1,128,6]{1,0,2:T(1,128)}, u32[]{:S(2)}) copy-start(f32[1,128,6]{1,0,2:T(1,128)} %param.22) | copy-start | bytes 9220
  337.5 7.3 %copy-start.12 = (s32[768]{0:T(1024)S(1)}, s32[768]{0:T(1024)}, u32[]{:S(2)}) copy-start(s32[768]{0:T(1024)} %copy-done.11) | copy-start | bytes 9220
  337.5 97.8 %all-to-all-start.4 = ((bf16[32,25,2048]{2,1,0:T(8,128)(2,1)}), bf16[32,25,2048]{2,1,0:T(8,128)(2,1)}, u32[]{:S(2)}, u32[]{:S(2)}) async-start(bf16[32,25,2048]{2,1,0:T(8,128)(2,1)} %reshape.112), calls=%async_computation.4 | async-start | bytes 8388608 | tf_op jit(solution)/shard_map/all_to_all | solution.py:129
  449.7 6.8 %copy-start.3 = (bf16[128,2048]{1,0:T(8,128)(2,1)S(1)}, bf16[128,2048]{1,0:T(8,128)(2,1)}, u32[]{:S(2)}) copy-start(bf16[128,2048]{1,0:T(8,128)(2,1)} %copy-done.2) | copy-start | bytes 1572868
  449.7 7.7 %copy-start.1 = (bf16[4,256,704]{1,2,0:T(8,128)(2,1)S(1)}, bf16[4,256,704]{1,2,0:T(8,128)(2,1)}, u32[]{:S(2)}) copy-start(bf16[4,256,704]{1,2,0:T(8,128)(2,1)} %param.23) | copy-start | bytes 4325380
Sparse Core Ops, SparseCore 0:
  10.6 123.4 all-gather.8
  135.7 44.1 all-gather.12
  198.0 76.1 all-gather.14
  275.6 41.5 all-gather.10

commit v4 on v3

--- a/solution.py
+++ b/solution.py
@@ -11,15 +11,14 @@
 CAP = 50
 
 
-def carried_in(array, axis, join, neutral):
-    place = lax.axis_index(axis)
-    gathered = lax.all_gather(array.astype(jnp.bfloat16), axis)
-    state = jnp.zeros_like(array) + jnp.asarray(neutral, array.dtype)
-
-    def one(turn, state):
-        return join(state, lax.dynamic_index_in_dim(gathered, turn, 0, False).astype(array.dtype))
-
-    return lax.fori_loop(0, place, one, state)
+def carried_in(array, axis, count):
+    total = array
+    shift = 1
+    while shift < count:
+        moved = lax.ppermute(total, axis, [(i, i + shift) for i in range(count - shift)])
+        total = total + moved
+        shift *= 2
+    return total - array
 
 
 def route_slots(block_routes):
@@ -32,10 +31,6 @@
 
 def silu_gate(gate_sum, up_sum):
     return gate_sum / (1.0 + jnp.exp(-gate_sum)) * up_sum
-
-
-def add_states(earlier, later):
-    return earlier + later
 
 
 def make_shards(n_ep, n_outer, n_inner):
@@ -81,7 +76,7 @@
         local_state = jnp.einsum(
             "thd,the->hde", key_heads, value_heads, preferred_element_type=jnp.float32
         )
-        earlier = carried_in(local_state, ("seq_outer", "seq_inner"), add_states, jnp.zeros_like(local_state))
+        earlier = carried_in(local_state, ("seq_outer", "seq_inner"), n_seq)
         state_before = state_start[0] + earlier
         causal = (
             jnp.arange(tokens, dtype=jnp.int32)[:, None]

time: 471 us -> 495 us (1.051)
  starting transfers between devices: 37.7 us -> 61.9 us
  waiting for transfers between devices: 302 us -> 296 us
    ppermute x0 -> x3, waiting for transfers between devices: none -> 88.4 us  [carried_in(): lax.ppermute(total, axis, [(i, i + shift) for i in range(count - shift)])]
    all_gather x1 -> x0, waiting for transfers between devices: 60.5 us -> none  [carried_in(): gathered = lax.all_gather(array.astype(jnp.bfloat16), axis)]
    all_to_all x3, waiting for transfers between devices: 43.2 us -> 9.5 us  [collect(): mine = lax.all_to_all(weight[wanted], 'seq_outer', 0, 0, tiled=True)]
    all_to_all x3, starting transfers between devices: 22 us -> 41.4 us  [collect(): mine = lax.all_to_all(weight[wanted], 'seq_outer', 0, 0, tiled=True)]
    ppermute x0 -> x3, starting transfers between devices: none -> 6.58 us  [carried_in(): lax.ppermute(total, axis, [(i, i + shift) for i in range(count - shift)])]
  transfers between devices with their start and end apart: 9 -> 11, of which waited for: 6 -> 7; matrix products, arithmetic and copies ran while one was open for 14% -> 14% of each run, Pallas kernels for 0% -> 0%
where the time goes in v4:
time: 495 us; the launch traced here: 487 us
  waiting for transfers between devices  296 us (60%)
  local copies, waits for them, and re-layouts  68.2 us (14%)
  starting transfers between devices  61.9 us (13%)
  other arithmetic  23.9 us (5%)
  matrix products  23.8 us (5%)
  between operations  13.4 us (3%)
    all_to_all x1, waiting for transfers between devices, shards(): lax.all_to_all(expert_rows, ('ep', 'seq_outer', 'seq_inner'), 0, 0, tiled...  90.6 us
    all_to_all x1, waiting for transfers between devices, shards(): lax.all_to_all(outgoing, ('ep', 'seq_outer', 'seq_inner'), 0, 0, tiled=True)  89.4 us
    ppermute x3, waiting for transfers between devices, carried_in(): lax.ppermute(total, axis, [(i, i + shift) for i in range(count - shift)])  88.4 us
    all_to_all x3, starting transfers between devices, collect(): mine = lax.all_to_all(weight[wanted], 'seq_outer', 0, 0, tiled=True)  41.4 us
    all_gather x3, waiting for transfers between devices, collect(): return lax.all_gather(mine, 'seq_inner', axis=0, tiled=False)  17 us
    dot_general x1, matrix products, shards(): jnp.einsum('rh,xzhd->rzxd', hidden, whole_down, preferred_element_type=jn...  11.2 us
  transfers between devices with their start and end apart: 11, of which 7 were waited for; matrix products, arithmetic and copies ran while one was open for 14% of the time, Pallas kernels for 0%

profile of v4, /device:TPU:16, one launch (start us, length us, event | category | flops | bytes accessed | tf_op | source)
XLA Modules:
  0.0 487.2 jit_solution(172861357103157620)
XLA Ops:
  6.5 1.3 copy-done
  7.9 1.8 gather_fusion.2
  9.7 5.3 %all-to-all-start.2 = ((bf16[4,256,704]{1,2,0:T(8,128)(2,1)}), bf16[4,256,704]{1,2,0:T(8,128)(2,1)S(1)}, u32[]{:S(2)}, u32[]{:S(2)}) async-start(bf16[4,256,704]{1,2,0:T(8,128)(2,1)} %gather_fusion.2), calls=%async_computation.2 | async-start | bytes 2883584 | tf_op jit(solution)/shard_map/all_to_all | solution.py:63
  15.9 3.4 collective-permute-start
  19.3 50.9 %collective-permute-done = f32[16,128,128]{2,1,0:T(8,128)S(1)} collective-permute-done((f32[16,128,128]{2,1,0:T(8,128)S(1)}, f32[16,128,128]{2,1,0:T(8,128)S(1)}, u32[]{:S(2)}, u32[]{:S(2)}) %collective-permute-start) | collective-permute-done | bytes 1048608 | tf_op jit(solution)/shard_map/ppermute | solution.py:18
  70.2 1.1 add.87
  71.3 1.9 collective-permute-start.1
  74.0 1.0 eq.29
  75.0 1.0 eq.25
  75.9 2.0 copy.56
  77.9 3.1 gather_fusion.3
  81.0 4.7 all-to-all-start.3
  86.4 4.1 reduce-window.6
  90.5 1.0 slice_reduce_fusion
  92.3 1.0 mul.79
  93.3 33.0 %collective-permute-done.1 = f32[16,128,128]{2,1,0:T(8,128)} collective-permute-done((f32[16,128,128]{2,1,0:T(8,128)}, f32[16,128,128]{2,1,0:T(8,128)}, u32[]{:S(2)}, u32[]{:S(2)}) %collective-permute-start.1) | collective-permute-done | bytes 1048608 | tf_op jit(solution)/shard_map/ppermute | solution.py:18
  126.3 2.6 add.88
  128.9 1.3 collective-permute-start.2
  130.4 3.4 scatter_custom_fusion.1
  133.8 3.4 scatter_custom_fusion
  137.3 3.2 gather_fusion
  140.6 1.8 convolution_bitcast_fusion
  142.4 4.5 collective-permute-done.2
  146.9 4.2 multiply_reduce_fusion.1
  151.2 31.4 %all-to-all-start = ((bf16[4,704,256]{2,1,0:T(8,128)(2,1)}), bf16[4,704,256]{2,1,0:T(8,128)(2,1)S(1)}, u32[]{:S(2)}, u32[]{:S(2)}) async-start(bf16[4,704,256]{2,1,0:T(8,128)(2,1)} %gather_fusion), calls=%async_computation | async-start | bytes 2883584 | tf_op jit(solution)/shard_map/all_to_all | solution.py:63
  182.6 1.3 broadcast_multiply_fusion
  183.9 1.3 copy.40
  185.2 1.4 fusion.20
  187.6 4.8 gather_fusion.1
  192.4 4.9 %gather.19 = bf16[32,25,2048]{2,1,0:T(8,128)(2,1)} reshape(bf16[800,2048]{1,0:T(8,128)(2,1)} %gather_fusion.1) | data formatting | bytes 6553600 | tf_op jit(solution)/shard_map/gather | solution.py:112
  197.3 4.5 broadcast_select_fusion
  201.8 9.5 %all-to-all-done = bf16[4,704,256]{2,1,0:T(8,128)(2,1)S(1)} async-done(((bf16[4,704,256]{2,1,0:T(8,128)(2,1)}), bf16[4,704,256]{2,1,0:T(8,128)(2,1)S(1)}, u32[]{:S(2)}, u32[]{:S(2)}) %all-to-all-start) | async-done | bytes 1441824 | tf_op jit(solution)/shard_map/all_to_all | solution.py:63
  211.3 1.1 copy-done.5
  212.4 6.5 %all-to-all-start.1 = ((bf16[32,25,2048]{2,1,0:T(8,128)(2,1)}), bf16[32,25,2048]{2,1,0:T(8,128)(2,1)}, u32[]{:S(2)}, u32[]{:S(2)}) async-start(bf16[32,25,2048]{2,1,0:T(8,128)(2,1)} %broadcast_select_fusion), calls=%async_computation.1 | async-start | bytes 8388608 | tf_op jit(solution)/shard_map/all_to_all | solution.py:114
  220.4 89.4 %all-to-all-done.1 = bf16[32,25,2048]{2,1,0:T(8,128)(2,1)} async-done(((bf16[32,25,2048]{2,1,0:T(8,128)(2,1)}), bf16[32,25,2048]{2,1,0:T(8,128)(2,1)}, u32[]{:S(2)}, u32[]{:S(2)}) %all-to-all-start.1) | async-done | bytes 3276832 | tf_op jit(solution)/shard_map/all_to_all | solution.py:114
  309.8 7.7 %reshape.109 = bf16[800,4,2,256]{3,2,1,0:T(2,128)(2,1)S(1)} reshape(bf16[32,25,2048]{2,1,0:T(8,128)(2,1)} %all-to-all-done.1) | data formatting | bytes 6553600 | tf_op jit(solution)/shard_map/reshape | solution.py:115
  317.5 6.0 %fusion.2 = f32[800,704,1,1]{1,0,3,2:T(8,128)} fusion(bf16[2,4,256,704]{2,3,1,0:T(8,128)(2,1)} %bitcast.106, bf16[800,4,2,256]{3,2,1,0:T(2,128)(2,1)S(1)} %reshape.109), kind=kOutput, calls=%fused_computation.11 | convolution fusion | flops 2306867200 | bytes 8413184 | tf_op jit(solution)/shard_map/dot_general | solution.py:117
  323.5 17.0 %all-gather.7.cloned.1.call-done = bf16[8,704,256]{2,1,0:T(8,128)(2,1)} async-done(((bf16[4,704,256]{2,1,0:T(8,128)(2,1)}), bf16[8,704,256]{2,1,0:T(8,128)(2,1)}) %all-gather.7.cloned.1.call-update) | async-done | bytes 2883600 | tf_op jit(solution)/shard_map/all_gather | solution.py:64
  340.5 11.2 %convert_bitcast_fusion = bf16[800,4,2,256]{3,0,1,2:T(8,128)(2,1)} fusion(bf16[2,4,704,256]{3,2,1,0:T(8,128)(2,1)} %bitcast.108, bf16[2,4,256,704]{2,3,1,0:T(8,128)(2,1)} %bitcast.107, bf16[800,4,2,256]{3,2,1,0:T(2,128)(2,1)S(1)} %reshape.109, f32[800,704,1,1]{1,0,3,2:T(8,128)} %fusion.2), kind=kOutput, calls=%fused_computation.13 | convolution fusion | flops 4618188800 | bytes 14573568 | tf_op jit(solution)/shard_map/rh,xzhd->rzxd/dot_general | solution.py:120
  351.7 5.3 %copy.47 = bf16[800,4,2,256]{3,2,1,0:T(2,128)(2,1)S(1)} copy(bf16[800,4,2,256]{3,0,1,2:T(8,128)(2,1)} %convert_bitcast_fusion) | data formatting | bytes 6553600 | tf_op jit(solution)/shard_map/convert_element_type | solution.py:122
  357.0 3.8 reshape.110
  360.8 7.1 %all-to-all-start.4 = ((bf16[32,25,2048]{2,1,0:T(8,128)(2,1)}), bf16[32,25,2048]{2,1,0:T(8,128)(2,1)}, u32[]{:S(2)}, u32[]{:S(2)}) async-start(bf16[32,25,2048]{2,1,0:T(8,128)(2,1)} %reshape.110), calls=%async_computation.4 | async-start | bytes 8388608 | tf_op jit(solution)/shard_map/all_to_all | solution.py:124
  368.1 90.6 %all-to-all-done.4 = bf16[32,25,2048]{2,1,0:T(8,128)(2,1)} async-done(((bf16[32,25,2048]{2,1,0:T(8,128)(2,1)}), bf16[32,25,2048]{2,1,0:T(8,128)(2,1)}, u32[]{:S(2)}, u32[]{:S(2)}) %all-to-all-start.4) | async-done | bytes 3276832 | tf_op jit(solution)/shard_map/all_to_all | solution.py:124
  458.7 3.4 reshape.111
  462.1 4.3 gather_fusion.4
  466.4 6.6 %reshape.113 = f32[128,6,2048]{2,1,0:T(8,128)} reshape(bf16[768,2048]{1,0:T(8,128)(2,1)} %gather_fusion.4) | data formatting | bytes 9437184 | tf_op jit(solution)/shard_map/convert_element_type | solution.py:126
  473.0 6.8 %multiply_reduce_fusion = f32[128,2048]{1,0:T(8,128)S(1)} fusion(f32[128,6,2048]{2,1,0:T(8,128)} %reshape.113, f32[128,6]{1,0:T(8,128)S(1)} %bitcast.104), kind=kLoop, calls=%fused_computation.7 | loop fusion | flops 2883584 | bytes 7343104 | tf_op jit(solution)/shard_map/reduce_sum | solution.py:126
  479.8 0.9 fusion.25
  (64 shorter events, 6.0 us)
Async XLA Ops:
  6.5 1.4 copy-start
  7.9 70.0 %copy-start.14 = (s32[1024]{0:T(1024)}, s32[1024]{0:T(1024)S(1)}, u32[]{:S(2)}) copy-start(s32[1024]{0:T(1024)S(1)} %pad_clamp_fusion.1) | copy-start | bytes 12292
  7.9 7.1 %copy-start.7 = (bf16[1,128,2048]{2,1,0:T(8,128)(2,1)S(1)}, bf16[1,128,2048]{2,1,0:T(8,128)(2,1)}, u32[]{:S(2)}) copy-start(bf16[1,128,2048]{2,1,0:T(8,128)(2,1)} %param.14) | copy-start | bytes 1572868
  9.7 5.6 %copy-start.8 = (bf16[1,128,2048]{2,1,0:T(8,128)(2,1)S(1)}, bf16[1,128,2048]{2,1,0:T(8,128)(2,1)}, u32[]{:S(2)}) copy-start(bf16[1,128,2048]{2,1,0:T(8,128)(2,1)} %param.13) | copy-start | bytes 1572868
  9.7 71.4 %all-to-all-start.2 = ((bf16[4,256,704]{1,2,0:T(8,128)(2,1)}), bf16[4,256,704]{1,2,0:T(8,128)(2,1)S(1)}, u32[]{:S(2)}, u32[]{:S(2)}) async-start(bf16[4,256,704]{1,2,0:T(8,128)(2,1)} %gather_fusion.2), calls=%async_computation.2 | async-start | bytes 2883584 | tf_op jit(solution)/shard_map/all_to_all | solution.py:63
  15.4 57.8 %copy-start.11 = (s32[1,128,6]{1,0,2:T(1,128)S(1)}, s32[1,128,6]{1,0,2:T(1,128)}, u32[]{:S(2)}) copy-start(s32[1,128,6]{1,0,2:T(1,128)} %param.19) | copy-start | bytes 9220
  15.9 54.3 %collective-permute-start = (f32[16,128,128]{2,1,0:T(8,128)S(1)}, f32[16,128,128]{2,1,0:T(8,128)S(1)}, u32[]{:S(2)}, u32[]{:S(2)}) collective-permute-start(f32[16,128,128]{2,1,0:T(8,128)S(1)} %fusion.28), channel_id=1, source_target_pairs={{0,4},{4,8},{8,12},{12,16},{16,20},{20,24},{24,28},{1,5},{5,9},{9,... | collective-permute-start | bytes 3145736 | tf_op jit(solution)/shard_map/ppermute | solution.py:18
  71.3 55.0 %collective-permute-start.1 = (f32[16,128,128]{2,1,0:T(8,128)}, f32[16,128,128]{2,1,0:T(8,128)}, u32[]{:S(2)}, u32[]{:S(2)}) collective-permute-start(f32[16,128,128]{2,1,0:T(8,128)} %add.87), channel_id=1, source_target_pairs={{0,8},{4,12},{8,16},{12,20},{16,24},{20,28},{1,9},{5,13},{9,17},{1... | collective-permute-start | bytes 3145736 | tf_op jit(solution)/shard_map/ppermute | solution.py:18
  81.0 47.9 %copy-start.4 = (bf16[4,256,704]{1,2,0:T(8,128)(2,1)}, bf16[4,256,704]{1,2,0:T(8,128)(2,1)S(1)}, u32[]{:S(2)}) copy-start(bf16[4,256,704]{1,2,0:T(8,128)(2,1)S(1)} %all-to-all-done.2) | copy-start | bytes 4325380
  81.0 70.1 %all-to-all-start.3 = ((bf16[4,256,704]{1,2,0:T(8,128)(2,1)}), bf16[4,256,704]{1,2,0:T(8,128)(2,1)}, u32[]{:S(2)}, u32[]{:S(2)}) async-start(bf16[4,256,704]{1,2,0:T(8,128)(2,1)} %gather_fusion.3), calls=%async_computation.3 | async-start | bytes 2883584 | tf_op jit(solution)/shard_map/all_to_all | solution.py:63
  85.8 231.7 %all-gather.9.cloned.1.call-start = ((), (), s32[]{:S(2)}) async-start(), calls=%async_computation.6 | async-start | bytes 4325376 | tf_op jit(solution)/shard_map/all_gather | solution.py:64
  93.3 37.0 %copy-start.10 = (s32[16,6,128]{2,0,1:T(8,128)S(1)}, s32[16,6,128]{2,0,1:T(8,128)}, u32[]{:S(2)}) copy-start(s32[16,6,128]{2,0,1:T(8,128)} %reduce-window.6) | copy-start | bytes 147460
  128.9 18.0 %collective-permute-start.2 = (f32[16,128,128]{2,1,0:T(8,128)}, f32[16,128,128]{2,1,0:T(8,128)}, u32[]{:S(2)}, u32[]{:S(2)}) collective-permute-start(f32[16,128,128]{2,1,0:T(8,128)} %add.88), channel_id=1, source_target_pairs={{0,16},{4,20},{8,24},{12,28},{1,17},{5,21},{9,25},{13,29},{2,18},{... | collective-permute-start | bytes 3145736 | tf_op jit(solution)/shard_map/ppermute | solution.py:18
  130.2 10.3 %copy-start.6 = (bf16[16,8,16,128]{3,2,1,0:T(8,128)(2,1)S(1)}, bf16[16,8,16,128]{3,2,1,0:T(8,128)(2,1)}, u32[]{:S(2)}) copy-start(bf16[16,8,16,128]{3,2,1,0:T(8,128)(2,1)} %copy.56) | copy-start | bytes 1572868
  151.2 34.0 %copy-start.9 = (bf16[1,128,2048]{2,1,0:T(8,128)(2,1)S(1)}, bf16[1,128,2048]{2,1,0:T(8,128)(2,1)}, u32[]{:S(2)}) copy-start(bf16[1,128,2048]{2,1,0:T(8,128)(2,1)} %param.15) | copy-start | bytes 1572868
  151.2 34.0 %copy-start.12 = (f32[2048]{0:T(1024)S(1)}, f32[2048]{0:T(1024)}, u32[]{:S(2)}) copy-start(f32[2048]{0:T(1024)} %param.17) | copy-start | bytes 24580
  151.2 60.1 %all-to-all-start = ((bf16[4,704,256]{2,1,0:T(8,128)(2,1)}), bf16[4,704,256]{2,1,0:T(8,128)(2,1)S(1)}, u32[]{:S(2)}, u32[]{:S(2)}) async-start(bf16[4,704,256]{2,1,0:T(8,128)(2,1)} %gather_fusion), calls=%async_computation | async-start | bytes 2883584 | tf_op jit(solution)/shard_map/all_to_all | solution.py:63
  183.9 3.5 copy-start.13
  186.6 0.8 copy-start.2
  211.3 1.1 copy-start.5
  212.4 97.4 %all-to-all-start.1 = ((bf16[32,25,2048]{2,1,0:T(8,128)(2,1)}), bf16[32,25,2048]{2,1,0:T(8,128)(2,1)}, u32[]{:S(2)}, u32[]{:S(2)}) async-start(bf16[32,25,2048]{2,1,0:T(8,128)(2,1)} %broadcast_select_fusion), calls=%async_computation.1 | async-start | bytes 8388608 | tf_op jit(solution)/shard_map/all_to_all | solution.py:114
  218.9 104.6 %all-gather.11.cloned.1.call-start = ((), (), s32[]{:S(2)}) async-start(), calls=%async_computation.7 | async-start | bytes 4325376 | tf_op jit(solution)/shard_map/all_gather | solution.py:64
  219.7 120.8 %all-gather.7.cloned.1.call-start = ((), (), s32[]{:S(2)}) async-start(), calls=%async_computation.5 | async-start | bytes 4325376 | tf_op jit(solution)/shard_map/all_gather | solution.py:64
  360.8 7.1 %copy-start.15 = (f32[1,128,6]{1,0,2:T(1,128)S(1)}, f32[1,128,6]{1,0,2:T(1,128)}, u32[]{:S(2)}) copy-start(f32[1,128,6]{1,0,2:T(1,128)} %param.20) | copy-start | bytes 9220
  360.8 97.8 %all-to-all-start.4 = ((bf16[32,25,2048]{2,1,0:T(8,128)(2,1)}), bf16[32,25,2048]{2,1,0:T(8,128)(2,1)}, u32[]{:S(2)}, u32[]{:S(2)}) async-start(bf16[32,25,2048]{2,1,0:T(8,128)(2,1)} %reshape.110), calls=%async_computation.4 | async-start | bytes 8388608 | tf_op jit(solution)/shard_map/all_to_all | solution.py:124
  473.0 6.8 %copy-start.3 = (bf16[128,2048]{1,0:T(8,128)(2,1)S(1)}, bf16[128,2048]{1,0:T(8,128)(2,1)}, u32[]{:S(2)}) copy-start(bf16[128,2048]{1,0:T(8,128)(2,1)} %copy-done.2) | copy-start | bytes 1572868
  473.0 7.7 %copy-start.1 = (bf16[4,256,704]{1,2,0:T(8,128)(2,1)S(1)}, bf16[4,256,704]{1,2,0:T(8,128)(2,1)}, u32[]{:S(2)}) copy-start(bf16[4,256,704]{1,2,0:T(8,128)(2,1)} %param.21) | copy-start | bytes 4325380
Sparse Core Ops, SparseCore 0:
  142.5 43.2 all-gather.8
  221.3 76.1 all-gather.10
  299.1 41.3 all-gather.6

commit v5 on v4

--- a/solution.py
+++ b/solution.py
@@ -56,19 +56,6 @@
         chunk = -(-CAP // per)
         capp = chunk * per
 
-        per_outer = n_outer // local_experts
-        wanted = jnp.arange(n_outer, dtype=jnp.int32) // per_outer
-
-        def collect(weight):
-            mine = lax.all_to_all(weight[wanted], "seq_outer", 0, 0, tiled=True)
-            return lax.all_gather(mine, "seq_inner", axis=0, tiled=False)
-
-        whole_gate = collect(gate_weight)
-        whole_up = collect(up_weight)
-        whole_down = collect(down_weight)
-        whole_gate = whole_gate.reshape(-1, whole_gate.shape[-1])
-        whole_up = whole_up.reshape(-1, whole_up.shape[-1])
-
         tokens = queries.shape[1]
         query_heads = queries[0].reshape(tokens, HEADS, HEAD_DIM)
         key_heads = key_rows[0].reshape(tokens, HEADS, HEAD_DIM)
@@ -111,6 +98,22 @@
         filled = jnp.zeros((EXPERTS * capp,), jnp.bool_).at[position].set(True)
         outgoing = jnp.where(filled[:, None], ffn_in[source], jnp.zeros((), jnp.bfloat16))
         outgoing = outgoing.reshape(EXPERTS * per, chunk, D)
+        outgoing, gate_weight, up_weight, down_weight = lax.optimization_barrier(
+            (outgoing, gate_weight, up_weight, down_weight)
+        )
+        per_outer = n_outer // local_experts
+        wanted = jnp.arange(n_outer, dtype=jnp.int32) // per_outer
+
+        def collect(weight):
+            mine = lax.all_to_all(weight[wanted], "seq_outer", 0, 0, tiled=True)
+            return lax.all_gather(mine, "seq_inner", axis=0, tiled=False)
+
+        whole_gate = collect(gate_weight)
+        whole_up = collect(up_weight)
+        whole_down = collect(down_weight)
+        whole_gate = whole_gate.reshape(-1, whole_gate.shape[-1])
+        whole_up = whole_up.reshape(-1, whole_up.shape[-1])
+
         arrived = lax.all_to_all(outgoing, ("ep", "seq_outer", "seq_inner"), 0, 0, tiled=True)
         arrived = arrived.reshape(n_dev * chunk, n_outer, n_inner, D // n_seq)
         arrived = arrived.transpose(0, 2, 1, 3).reshape(n_dev * chunk, D)

time: 495 us -> 548 us (1.11)
  waiting for transfers between devices: 296 us -> 349 us
    all_to_all x3, waiting for transfers between devices: 9.5 us -> 85.9 us  [collect(): mine = lax.all_to_all(weight[wanted], 'seq_outer', 0, 0, tiled=True)]
    ppermute x3, waiting for transfers between devices: 88.4 us -> 47.3 us  [carried_in(): lax.ppermute(total, axis, [(i, i + shift) for i in range(count - shift)])]
    all_gather x3, waiting for transfers between devices: 17 us -> 33.9 us  [collect(): return lax.all_gather(mine, 'seq_inner', axis=0, tiled=False)]
  transfers between devices with their start and end apart: 11 -> 11, of which waited for: 7 -> 9; matrix products, arithmetic and copies ran while one was open for 14% -> 8% of each run, Pallas kernels for 0% -> 0%
where the time goes in v5:
time: 548 us; the launch traced here: 541 us
  waiting for transfers between devices  349 us (64%)
  local copies, waits for them, and re-layouts  68 us (12%)
  starting transfers between devices  60.9 us (11%)
  other arithmetic  25.2 us (5%)
  matrix products  24.1 us (4%)
  between operations  13.4 us (2%)
    all_to_all x1, waiting for transfers between devices, shards(): lax.all_to_all(expert_rows, ('ep', 'seq_outer', 'seq_inner'), 0, 0, tiled...  90.6 us
    all_to_all x1, waiting for transfers between devices, shards(): lax.all_to_all(outgoing, ('ep', 'seq_outer', 'seq_inner'), 0, 0, tiled=True)  89.4 us
    all_to_all x3, waiting for transfers between devices, collect(): mine = lax.all_to_all(weight[wanted], 'seq_outer', 0, 0, tiled=True)  85.9 us
    ppermute x3, waiting for transfers between devices, carried_in(): lax.ppermute(total, axis, [(i, i + shift) for i in range(count - shift)])  47.3 us
    all_to_all x3, starting transfers between devices, collect(): mine = lax.all_to_all(weight[wanted], 'seq_outer', 0, 0, tiled=True)  41.1 us
    all_gather x3, waiting for transfers between devices, collect(): return lax.all_gather(mine, 'seq_inner', axis=0, tiled=False)  33.9 us
    dot_general x1, matrix products, shards(): jnp.einsum('rh,xzhd->rzxd', hidden, whole_down, preferred_element_type=jn...  11.2 us
  transfers between devices with their start and end apart: 11, of which 9 were waited for; matrix products, arithmetic and copies ran while one was open for 8% of the time, Pallas kernels for 0%

profile of v5, /device:TPU:16, one launch (start us, length us, event | category | flops | bytes accessed | tf_op | source)
XLA Modules:
  0.0 540.6 jit_solution(17741339476611903665)
XLA Ops:
  6.5 1.4 copy.53
  8.0 1.1 copy.55
  9.6 3.4 collective-permute-start
  13.0 24.3 %collective-permute-done = f32[16,128,128]{2,1,0:T(8,128)S(1)} collective-permute-done((f32[16,128,128]{2,1,0:T(8,128)S(1)}, f32[16,128,128]{2,1,0:T(8,128)S(1)}, u32[]{:S(2)}, u32[]{:S(2)}) %collective-permute-start) | collective-permute-done | bytes 1048608 | tf_op jit(solution)/shard_map/ppermute | solution.py:18
  37.3 1.1 add.87
  38.5 3.5 collective-permute-start.1
  42.7 1.0 eq.29
  43.7 1.0 eq.25
  44.6 2.0 copy.56
  47.2 4.1 reduce-window.6
  51.4 1.0 slice_reduce_fusion
  53.2 1.0 mul.79
  55.1 9.6 %collective-permute-done.1 = f32[16,128,128]{2,1,0:T(8,128)} collective-permute-done((f32[16,128,128]{2,1,0:T(8,128)}, f32[16,128,128]{2,1,0:T(8,128)}, u32[]{:S(2)}, u32[]{:S(2)}) %collective-permute-start.1) | collective-permute-done | bytes 1048608 | tf_op jit(solution)/shard_map/ppermute | solution.py:18
  64.7 2.7 add.88
  67.4 1.3 collective-permute-start.2
  68.7 3.4 scatter_custom_fusion.1
  72.1 3.4 scatter_custom_fusion
  77.4 2.9 convolution_bitcast_fusion
  80.3 13.4 %collective-permute-done.2 = f32[16,128,128]{2,1,0:T(8,128)} collective-permute-done((f32[16,128,128]{2,1,0:T(8,128)}, f32[16,128,128]{2,1,0:T(8,128)}, u32[]{:S(2)}, u32[]{:S(2)}) %collective-permute-start.2) | collective-permute-done | bytes 1048608 | tf_op jit(solution)/shard_map/ppermute | solution.py:18
  93.7 3.4 multiply_reduce_fusion.1
  97.8 1.2 fusion.20
  100.7 4.9 gather_fusion
  105.6 4.9 gather.18
  110.5 4.5 broadcast_select_fusion
  115.0 2.0 gather_fusion.2
  117.0 27.5 %all-to-all-start.2 = ((bf16[4,256,704]{1,2,0:T(8,128)(2,1)}), bf16[4,256,704]{1,2,0:T(8,128)(2,1)S(1)}, u32[]{:S(2)}, u32[]{:S(2)}) async-start(bf16[4,256,704]{1,2,0:T(8,128)(2,1)} %gather_fusion.2), calls=%async_computation.2 | async-start | bytes 2883584 | tf_op jit(solution)/shard_map/all_to_all | solution.py:108
  144.5 1.9 gather_fusion.3
  146.4 29.2 %all-to-all-done.2 = bf16[4,256,704]{1,2,0:T(8,128)(2,1)S(1)} async-done(((bf16[4,256,704]{1,2,0:T(8,128)(2,1)}), bf16[4,256,704]{1,2,0:T(8,128)(2,1)S(1)}, u32[]{:S(2)}, u32[]{:S(2)}) %all-to-all-start.2) | async-done | bytes 1441824 | tf_op jit(solution)/shard_map/all_to_all | solution.py:108
  175.5 6.8 %all-to-all-start.3 = ((bf16[4,256,704]{1,2,0:T(8,128)(2,1)}), bf16[4,256,704]{1,2,0:T(8,128)(2,1)S(1)}, u32[]{:S(2)}, u32[]{:S(2)}) async-start(bf16[4,256,704]{1,2,0:T(8,128)(2,1)} %gather_fusion.3), calls=%async_computation.3 | async-start | bytes 2883584 | tf_op jit(solution)/shard_map/all_to_all | solution.py:108
  182.3 3.3 gather_fusion.1
  185.6 27.1 %all-to-all-done.3 = bf16[4,256,704]{1,2,0:T(8,128)(2,1)S(1)} async-done(((bf16[4,256,704]{1,2,0:T(8,128)(2,1)}), bf16[4,256,704]{1,2,0:T(8,128)(2,1)S(1)}, u32[]{:S(2)}, u32[]{:S(2)}) %all-to-all-start.3) | async-done | bytes 1441824 | tf_op jit(solution)/shard_map/all_to_all | solution.py:108
  212.7 6.8 %all-to-all-start = ((bf16[4,704,256]{2,1,0:T(8,128)(2,1)}), bf16[4,704,256]{2,1,0:T(8,128)(2,1)S(1)}, u32[]{:S(2)}, u32[]{:S(2)}) async-start(bf16[4,704,256]{2,1,0:T(8,128)(2,1)} %gather_fusion.1), calls=%async_computation | async-start | bytes 2883584 | tf_op jit(solution)/shard_map/all_to_all | solution.py:108
  220.3 29.6 %all-to-all-done = bf16[4,704,256]{2,1,0:T(8,128)(2,1)S(1)} async-done(((bf16[4,704,256]{2,1,0:T(8,128)(2,1)}), bf16[4,704,256]{2,1,0:T(8,128)(2,1)S(1)}, u32[]{:S(2)}, u32[]{:S(2)}) %all-to-all-start) | async-done | bytes 1441824 | tf_op jit(solution)/shard_map/all_to_all | solution.py:108
  249.9 1.1 copy-done.6
  251.0 6.5 %all-to-all-start.1 = ((bf16[32,25,2048]{2,1,0:T(8,128)(2,1)}), bf16[32,25,2048]{2,1,0:T(8,128)(2,1)}, u32[]{:S(2)}, u32[]{:S(2)}) async-start(bf16[32,25,2048]{2,1,0:T(8,128)(2,1)} %broadcast_select_fusion), calls=%async_computation.1 | async-start | bytes 8388608 | tf_op jit(solution)/shard_map/all_to_all | solution.py:117
  259.0 89.4 %all-to-all-done.1 = bf16[32,25,2048]{2,1,0:T(8,128)(2,1)} async-done(((bf16[32,25,2048]{2,1,0:T(8,128)(2,1)}), bf16[32,25,2048]{2,1,0:T(8,128)(2,1)}, u32[]{:S(2)}, u32[]{:S(2)}) %all-to-all-start.1) | async-done | bytes 3276832 | tf_op jit(solution)/shard_map/all_to_all | solution.py:117
  348.4 7.7 %reshape.109 = bf16[800,4,2,256]{3,2,1,0:T(2,128)(2,1)S(1)} reshape(bf16[32,25,2048]{2,1,0:T(8,128)(2,1)} %all-to-all-done.1) | data formatting | bytes 6553600 | tf_op jit(solution)/shard_map/reshape | solution.py:118
  356.1 6.0 %fusion.2 = f32[800,704,1,1]{1,0,3,2:T(8,128)} fusion(bf16[2,4,256,704]{2,3,1,0:T(8,128)(2,1)} %bitcast.106, bf16[800,4,2,256]{3,2,1,0:T(2,128)(2,1)S(1)} %reshape.109), kind=kOutput, calls=%fused_computation.11 | convolution fusion | flops 2306867200 | bytes 8413184 | tf_op jit(solution)/shard_map/dot_general | solution.py:120
  362.2 33.9 %all-gather.7.cloned.1.call-done = bf16[8,704,256]{2,1,0:T(8,128)(2,1)} async-done(((bf16[4,704,256]{2,1,0:T(8,128)(2,1)}), bf16[8,704,256]{2,1,0:T(8,128)(2,1)}) %all-gather.7.cloned.1.call-update) | async-done | bytes 2883600 | tf_op jit(solution)/shard_map/all_gather | solution.py:109
  396.0 11.2 %convert_bitcast_fusion = bf16[800,4,2,256]{3,0,1,2:T(8,128)(2,1)} fusion(bf16[2,4,704,256]{3,2,1,0:T(8,128)(2,1)} %bitcast.108, bf16[2,4,256,704]{2,3,1,0:T(8,128)(2,1)} %bitcast.107, bf16[800,4,2,256]{3,2,1,0:T(2,128)(2,1)S(1)} %reshape.109, f32[800,704,1,1]{1,0,3,2:T(8,128)} %fusion.2), kind=kOutput, calls=%fused_computation.13 | convolution fusion | flops 4618188800 | bytes 14573568 | tf_op jit(solution)/shard_map/rh,xzhd->rzxd/dot_general | solution.py:123
  407.3 5.3 copy.47
  412.6 3.8 reshape.110
  416.4 4.9 all-to-all-start.4
  421.4 90.6 %all-to-all-done.4 = bf16[32,25,2048]{2,1,0:T(8,128)(2,1)} async-done(((bf16[32,25,2048]{2,1,0:T(8,128)(2,1)}), bf16[32,25,2048]{2,1,0:T(8,128)(2,1)}, u32[]{:S(2)}, u32[]{:S(2)}) %all-to-all-start.4) | async-done | bytes 3276832 | tf_op jit(solution)/shard_map/all_to_all | solution.py:127
  512.0 3.4 reshape.111
  515.4 4.4 gather_fusion.4
  519.8 6.6 %reshape.113 = f32[128,6,2048]{2,1,0:T(8,128)} reshape(bf16[768,2048]{1,0:T(8,128)(2,1)} %gather_fusion.4) | data formatting | bytes 9437184 | tf_op jit(solution)/shard_map/convert_element_type | solution.py:129
  526.4 6.8 %multiply_reduce_fusion = f32[128,2048]{1,0:T(8,128)S(1)} fusion(f32[128,6,2048]{2,1,0:T(8,128)} %reshape.113, f32[128,6]{1,0:T(8,128)S(1)} %bitcast.104), kind=kLoop, calls=%fused_computation.7 | loop fusion | flops 2883584 | bytes 7343104 | tf_op jit(solution)/shard_map/reduce_sum | solution.py:129
  (62 shorter events, 11.1 us)
Async XLA Ops:
  6.5 108.5 %copy-start = (bf16[4,256,704]{1,2,0:T(8,128)(2,1)S(1)}, bf16[4,256,704]{1,2,0:T(8,128)(2,1)}, u32[]{:S(2)}) copy-start(bf16[4,256,704]{1,2,0:T(8,128)(2,1)} %param.21) | copy-start | bytes 4325380
  9.1 32.8 %copy-start.12 = (s32[1,128,6]{1,0,2:T(1,128)S(1)}, s32[1,128,6]{1,0,2:T(1,128)}, u32[]{:S(2)}) copy-start(s32[1,128,6]{1,0,2:T(1,128)} %param.19) | copy-start | bytes 9220
  9.6 27.7 %collective-permute-start = (f32[16,128,128]{2,1,0:T(8,128)S(1)}, f32[16,128,128]{2,1,0:T(8,128)S(1)}, u32[]{:S(2)}, u32[]{:S(2)}) collective-permute-start(f32[16,128,128]{2,1,0:T(8,128)S(1)} %fusion.28), channel_id=1, source_target_pairs={{0,4},{4,8},{8,12},{12,16},{16,20},{20,24},{24,28},{1,5},{5,9},{9,... | collective-permute-start | bytes 3145736 | tf_op jit(solution)/shard_map/ppermute | solution.py:18
  38.5 26.2 %collective-permute-start.1 = (f32[16,128,128]{2,1,0:T(8,128)}, f32[16,128,128]{2,1,0:T(8,128)}, u32[]{:S(2)}, u32[]{:S(2)}) collective-permute-start(f32[16,128,128]{2,1,0:T(8,128)} %add.87), channel_id=1, source_target_pairs={{0,8},{4,12},{8,16},{12,20},{16,24},{20,28},{1,9},{5,13},{9,17},{1... | collective-permute-start | bytes 3145736 | tf_op jit(solution)/shard_map/ppermute | solution.py:18
  67.4 26.3 %collective-permute-start.2 = (f32[16,128,128]{2,1,0:T(8,128)}, f32[16,128,128]{2,1,0:T(8,128)}, u32[]{:S(2)}, u32[]{:S(2)}) collective-permute-start(f32[16,128,128]{2,1,0:T(8,128)} %add.88), channel_id=1, source_target_pairs={{0,16},{4,20},{8,24},{12,28},{1,17},{5,21},{9,25},{13,29},{2,18},{... | collective-permute-start | bytes 3145736 | tf_op jit(solution)/shard_map/ppermute | solution.py:18
  68.7 8.1 %copy-start.9 = (s32[768]{0:T(1024)}, s32[768]{0:T(1024)S(1)}, u32[]{:S(2)}) copy-start(s32[768]{0:T(1024)S(1)} %fusion.41) | copy-start | bytes 9220
  97.1 0.7 copy-start.13
  97.2 3.5 copy-start.11
  99.0 0.8 copy-start.2
  105.6 4.9 copy-start.8
  115.0 29.5 %copy-start.7 = (bf16[4,256,704]{1,2,0:T(8,128)(2,1)S(1)}, bf16[4,256,704]{1,2,0:T(8,128)(2,1)}, u32[]{:S(2)}) copy-start(bf16[4,256,704]{1,2,0:T(8,128)(2,1)} %param.22) | copy-start | bytes 4325380
  117.0 58.5 %all-to-all-start.2 = ((bf16[4,256,704]{1,2,0:T(8,128)(2,1)}), bf16[4,256,704]{1,2,0:T(8,128)(2,1)S(1)}, u32[]{:S(2)}, u32[]{:S(2)}) async-start(bf16[4,256,704]{1,2,0:T(8,128)(2,1)} %gather_fusion.2), calls=%async_computation.2 | async-start | bytes 2883584 | tf_op jit(solution)/shard_map/all_to_all | solution.py:108
  175.5 10.1 %copy-start.4 = (bf16[4,256,704]{1,2,0:T(8,128)(2,1)}, bf16[4,256,704]{1,2,0:T(8,128)(2,1)S(1)}, u32[]{:S(2)}) copy-start(bf16[4,256,704]{1,2,0:T(8,128)(2,1)S(1)} %all-to-all-done.2) | copy-start | bytes 4325380
  175.5 37.2 %all-to-all-start.3 = ((bf16[4,256,704]{1,2,0:T(8,128)(2,1)}), bf16[4,256,704]{1,2,0:T(8,128)(2,1)S(1)}, u32[]{:S(2)}, u32[]{:S(2)}) async-start(bf16[4,256,704]{1,2,0:T(8,128)(2,1)} %gather_fusion.3), calls=%async_computation.3 | async-start | bytes 2883584 | tf_op jit(solution)/shard_map/all_to_all | solution.py:108
  212.7 37.2 %copy-start.5 = (bf16[4,256,704]{1,2,0:T(8,128)(2,1)}, bf16[4,256,704]{1,2,0:T(8,128)(2,1)S(1)}, u32[]{:S(2)}) copy-start(bf16[4,256,704]{1,2,0:T(8,128)(2,1)S(1)} %all-to-all-done.3) | copy-start | bytes 4325380
  212.7 37.2 %all-to-all-start = ((bf16[4,704,256]{2,1,0:T(8,128)(2,1)}), bf16[4,704,256]{2,1,0:T(8,128)(2,1)S(1)}, u32[]{:S(2)}, u32[]{:S(2)}) async-start(bf16[4,704,256]{2,1,0:T(8,128)(2,1)} %gather_fusion.1), calls=%async_computation | async-start | bytes 2883584 | tf_op jit(solution)/shard_map/all_to_all | solution.py:108
  219.5 136.6 %all-gather.9.cloned.1.call-start = ((), (), s32[]{:S(2)}) async-start(), calls=%async_computation.6 | async-start | bytes 4325376 | tf_op jit(solution)/shard_map/all_gather | solution.py:109
  249.9 1.1 copy-start.6
  251.0 97.4 %all-to-all-start.1 = ((bf16[32,25,2048]{2,1,0:T(8,128)(2,1)}), bf16[32,25,2048]{2,1,0:T(8,128)(2,1)}, u32[]{:S(2)}, u32[]{:S(2)}) async-start(bf16[32,25,2048]{2,1,0:T(8,128)(2,1)} %broadcast_select_fusion), calls=%async_computation.1 | async-start | bytes 8388608 | tf_op jit(solution)/shard_map/all_to_all | solution.py:117
  257.5 104.6 %all-gather.11.cloned.1.call-start = ((), (), s32[]{:S(2)}) async-start(), calls=%async_computation.7 | async-start | bytes 4325376 | tf_op jit(solution)/shard_map/all_gather | solution.py:109
  258.3 137.8 %all-gather.7.cloned.1.call-start = ((), (), s32[]{:S(2)}) async-start(), calls=%async_computation.5 | async-start | bytes 4325376 | tf_op jit(solution)/shard_map/all_gather | solution.py:109
  416.4 4.9 copy-start.14
  416.4 5.1 copy-start.10
  416.4 95.6 %all-to-all-start.4 = ((bf16[32,25,2048]{2,1,0:T(8,128)(2,1)}), bf16[32,25,2048]{2,1,0:T(8,128)(2,1)}, u32[]{:S(2)}, u32[]{:S(2)}) async-start(bf16[32,25,2048]{2,1,0:T(8,128)(2,1)} %reshape.110), calls=%async_computation.4 | async-start | bytes 8388608 | tf_op jit(solution)/shard_map/all_to_all | solution.py:127
  526.4 6.8 %copy-start.3 = (bf16[128,2048]{1,0:T(8,128)(2,1)S(1)}, bf16[128,2048]{1,0:T(8,128)(2,1)}, u32[]{:S(2)}) copy-start(bf16[128,2048]{1,0:T(8,128)(2,1)} %copy-done.2) | copy-start | bytes 1572868
  526.4 7.7 %copy-start.1 = (bf16[4,256,704]{1,2,0:T(8,128)(2,1)S(1)}, bf16[4,256,704]{1,2,0:T(8,128)(2,1)}, u32[]{:S(2)}) copy-start(bf16[4,256,704]{1,2,0:T(8,128)(2,1)} %param.21) | copy-start | bytes 4325380
Sparse Core Ops, SparseCore 0:
  221.9 54.2 all-gather.8
  277.7 72.4 all-gather.10
  351.8 44.2 all-gather.6

commit v6 on v4

--- a/solution.py
+++ b/solution.py
@@ -33,9 +33,9 @@
     return gate_sum / (1.0 + jnp.exp(-gate_sum)) * up_sum
 
 
-def make_shards(n_ep, n_outer, n_inner):
-    n_seq = n_outer * n_inner
-    n_dev = n_ep * n_seq
+def make_shards(n_seq):
+    seq = ("seq_hi", "seq_lo")
+    group = ("ep", "seq_lo")
 
     def shards(
         queries,
@@ -51,17 +51,9 @@
         up_weight,
         down_weight,
     ):
-        local_experts = gate_weight.shape[0]
-        per = n_seq // local_experts
-        chunk = -(-CAP // per)
-        capp = chunk * per
-
-        per_outer = n_outer // local_experts
-        wanted = jnp.arange(n_outer, dtype=jnp.int32) // per_outer
-
         def collect(weight):
-            mine = lax.all_to_all(weight[wanted], "seq_outer", 0, 0, tiled=True)
-            return lax.all_gather(mine, "seq_inner", axis=0, tiled=False)
+            mine = lax.all_to_all(weight, "seq_lo", 0, 0, tiled=False)
+            return lax.all_gather(mine, "seq_hi", axis=0, tiled=False)
 
         whole_gate = collect(gate_weight)
         whole_up = collect(up_weight)
@@ -76,7 +68,7 @@
         local_state = jnp.einsum(
             "thd,the->hde", key_heads, value_heads, preferred_element_type=jnp.float32
         )
-        earlier = carried_in(local_state, ("seq_outer", "seq_inner"), n_seq)
+        earlier = carried_in(local_state, seq, n_seq)
         state_before = state_start[0] + earlier
         causal = (
             jnp.arange(tokens, dtype=jnp.int32)[:, None]
@@ -105,24 +97,23 @@
         ffn_in = (mixed_wide * row_scale * ffn_gain).astype(jnp.bfloat16)
         flat_routes = routes[0].reshape(-1)
         slot_rank = route_slots(flat_routes)
-        position = flat_routes * capp + slot_rank
+        position = flat_routes * CAP + slot_rank
         token_index = jnp.arange(tokens * TOP, dtype=jnp.int32) // TOP
-        source = jnp.zeros((EXPERTS * capp,), jnp.int32).at[position].set(token_index)
-        filled = jnp.zeros((EXPERTS * capp,), jnp.bool_).at[position].set(True)
+        source = jnp.zeros((EXPERTS * CAP,), jnp.int32).at[position].set(token_index)
+        filled = jnp.zeros((EXPERTS * CAP,), jnp.bool_).at[position].set(True)
         outgoing = jnp.where(filled[:, None], ffn_in[source], jnp.zeros((), jnp.bfloat16))
-        outgoing = outgoing.reshape(EXPERTS * per, chunk, D)
-        arrived = lax.all_to_all(outgoing, ("ep", "seq_outer", "seq_inner"), 0, 0, tiled=True)
-        arrived = arrived.reshape(n_dev * chunk, n_outer, n_inner, D // n_seq)
-        arrived = arrived.transpose(0, 2, 1, 3).reshape(n_dev * chunk, D)
+        outgoing = outgoing.reshape(EXPERTS, CAP, D)
+        arrived = lax.all_to_all(outgoing, group, 0, 0, tiled=True)
+        arrived = arrived.reshape(EXPERTS * CAP, D)
         gate_sum = jnp.dot(arrived, whole_gate, preferred_element_type=jnp.float32)
         up_sum = jnp.dot(arrived, whole_up, preferred_element_type=jnp.float32)
         hidden = silu_gate(gate_sum, up_sum).astype(jnp.bfloat16)
         expert_rows = jnp.einsum(
-            "rh,xzhd->rzxd", hidden, whole_down, preferred_element_type=jnp.float32
+            "rh,abhd->rabd", hidden, whole_down, preferred_element_type=jnp.float32
         ).astype(jnp.bfloat16)
-        expert_rows = expert_rows.reshape(n_dev, chunk, D)
-        returned = lax.all_to_all(expert_rows, ("ep", "seq_outer", "seq_inner"), 0, 0, tiled=True)
-        picked = returned.reshape(EXPERTS * capp, D)[position].reshape(tokens, TOP, D)
+        expert_rows = expert_rows.reshape(EXPERTS, CAP, D)
+        returned = lax.all_to_all(expert_rows, group, 0, 0, tiled=True)
+        picked = returned.reshape(EXPERTS * CAP, D)[position].reshape(tokens, TOP, D)
         expert_mix = jnp.sum(route_gates[0][:, :, None] * picked.astype(jnp.float32), axis=1)
         return (mixed_wide + expert_mix).astype(jnp.bfloat16)[None]
 
@@ -130,7 +121,7 @@
 
 
 def solution(mesh):
-    seq = ("seq_outer", "seq_inner")
+    seq = ("seq_hi", "seq_lo")
     placed = (
         P("ep", seq, None),
         P("ep", seq, None),
@@ -146,16 +137,14 @@
         P("ep", None, seq),
     )
     n_seq, n_ep = mesh.shape["seq"], mesh.shape["ep"]
-    n_inner = 2 if n_seq % 2 == 0 else 1
+    n_lo = EXPERTS // n_ep
     names = list(mesh.axis_names)
-    shape = []
+    shape, split_names = [], []
     for name in names:
-        shape += [n_seq // n_inner, n_inner] if name == "seq" else [mesh.shape[name]]
-    split_names = []
-    for name in names:
+        shape += [n_seq // n_lo, n_lo] if name == "seq" else [mesh.shape[name]]
         split_names += list(seq) if name == "seq" else [name]
     split = Mesh(mesh.devices.reshape(shape), tuple(split_names))
-    shards = make_shards(n_ep, n_seq // n_inner, n_inner)
     return jax.shard_map(
-        shards, mesh=split, in_specs=placed, out_specs=P("ep", seq, None), check_vma=False
+        make_shards(n_seq), mesh=split, in_specs=placed, out_specs=P("ep", seq, None),
+        check_vma=False,
     )

time: 495 us -> 467 us (0.943)
  waiting for transfers between devices: 296 us -> 253 us
  starting transfers between devices: 61.9 us -> 87.5 us
  local copies, waits for them, and re-layouts: 68.2 us -> 60.1 us
    all_to_all x5, waiting for transfers between devices: 189 us -> 46.3 us  [the longest x1 46.3 us: shards(): returned = lax.all_to_all(expert_rows, group, 0, 0, tiled=True)]
    all_gather x3, waiting for transfers between devices: 17 us -> 131 us  [collect(): return lax.all_gather(mine, 'seq_hi', axis=0, tiled=False)]
    all_to_all x5, starting transfers between devices: 55 us -> 76.4 us  [the longest x3 63.6 us: collect(): mine = lax.all_to_all(weight, 'seq_lo', 0, 0, tiled=False)]
    ppermute x3, waiting for transfers between devices: 88.4 us -> 74.6 us  [carried_in(): lax.ppermute(total, axis, [(i, i + shift) for i in range(count - shift)])]
    gather x4 -> x1, local copies, waits for them, and re-layouts: 12.5 us -> 4.33 us  [shards(): returned.reshape(EXPERTS * CAP, D)[position].reshape(tokens, TOP, D)]
    reshape x3 -> x5, local copies, waits for them, and re-layouts: 14.9 us -> 17.4 us  [the longest x1 3.83 us: shards(): whole_up = whole_up.reshape(-1, whole_up.shape[-1])]
  transfers between devices with their start and end apart: 11 -> 11, of which waited for: 7 -> 6; matrix products, arithmetic and copies ran while one was open for 14% -> 14% of each run, Pallas kernels for 0% -> 0%
where the time goes in v6:
time: 467 us; the launch traced here: 462 us
  waiting for transfers between devices  253 us (54%)
  starting transfers between devices  87.5 us (19%)
  local copies, waits for them, and re-layouts  60.1 us (13%)
  matrix products  24.8 us (5%)
  other arithmetic  23.5 us (5%)
  between operations  13.4 us (3%)
    all_gather x3, waiting for transfers between devices, collect(): return lax.all_gather(mine, 'seq_hi', axis=0, tiled=False)  131 us
    ppermute x3, waiting for transfers between devices, carried_in(): lax.ppermute(total, axis, [(i, i + shift) for i in range(count - shift)])  74.6 us
    all_to_all x3, starting transfers between devices, collect(): mine = lax.all_to_all(weight, 'seq_lo', 0, 0, tiled=False)  63.6 us
    all_to_all x1, waiting for transfers between devices, shards(): returned = lax.all_to_all(expert_rows, group, 0, 0, tiled=True)  46.3 us
    dot_general x1, matrix products, shards(): jnp.einsum('rh,abhd->rabd', hidden, whole_down, preferred_element_type=jn...  11.1 us
    ppermute x3, starting transfers between devices, carried_in(): lax.ppermute(total, axis, [(i, i + shift) for i in range(count - shift)])  10.8 us
    gather x2, local copies, waits for them, and re-layouts, shards(): ffn_in[source]  9.56 us
  transfers between devices with their start and end apart: 11, of which 6 were waited for; matrix products, arithmetic and copies ran while one was open for 14% of the time, Pallas kernels for 0%

profile of v6, /device:TPU:16, one launch (start us, length us, event | category | flops | bytes accessed | tf_op | source)
XLA Modules:
  0.0 462.1 jit_solution(938071313608475263)
XLA Ops:
  6.5 3.9 all-to-all-start.1
  11.4 3.9 collective-permute-start
  15.3 33.3 %collective-permute-done = f32[16,128,128]{2,1,0:T(8,128)S(1)} collective-permute-done((f32[16,128,128]{2,1,0:T(8,128)S(1)}, f32[16,128,128]{2,1,0:T(8,128)S(1)}, u32[]{:S(2)}, u32[]{:S(2)}) %collective-permute-start) | collective-permute-done | bytes 1048608 | tf_op jit(solution)/shard_map/ppermute | solution.py:18
  48.6 1.1 add.81
  49.6 5.6 %collective-permute-start.1 = (f32[16,128,128]{2,1,0:T(8,128)}, f32[16,128,128]{2,1,0:T(8,128)}, u32[]{:S(2)}, u32[]{:S(2)}) collective-permute-start(f32[16,128,128]{2,1,0:T(8,128)} %add.81), channel_id=1, source_target_pairs={{0,8},{4,12},{8,16},{12,20},{16,24},{20,28},{1,9},{5,13},{9,17},{1... | collective-permute-start | bytes 3145736 | tf_op jit(solution)/shard_map/ppermute | solution.py:18
  55.2 0.7 copy.44
  56.0 1.0 eq.29
  57.0 1.0 eq.25
  57.9 2.0 copy.58
  59.9 4.3 all-to-all-start.2
  64.9 4.1 reduce-window.6
  69.0 1.0 slice_reduce_fusion
  70.1 0.8 copy.43
  70.9 1.0 mul.79
  71.9 7.3 %collective-permute-done.1 = f32[16,128,128]{2,1,0:T(8,128)} collective-permute-done((f32[16,128,128]{2,1,0:T(8,128)}, f32[16,128,128]{2,1,0:T(8,128)}, u32[]{:S(2)}, u32[]{:S(2)}) %collective-permute-start.1) | collective-permute-done | bytes 1048608 | tf_op jit(solution)/shard_map/ppermute | solution.py:18
  79.1 2.6 add.82
  81.8 1.3 collective-permute-start.2
  83.2 3.4 scatter_custom_fusion.1
  86.6 3.4 scatter_custom_fusion
  90.2 2.9 convolution_bitcast_fusion
  93.1 34.1 %collective-permute-done.2 = f32[16,128,128]{2,1,0:T(8,128)} collective-permute-done((f32[16,128,128]{2,1,0:T(8,128)}, f32[16,128,128]{2,1,0:T(8,128)}, u32[]{:S(2)}, u32[]{:S(2)}) %collective-permute-start.2) | collective-permute-done | bytes 1048608 | tf_op jit(solution)/shard_map/ppermute | solution.py:18
  127.1 4.2 multiply_reduce_fusion.1
  131.4 55.4 %all-to-all-start.3 = ((bf16[4,704,256]{2,1,0:T(8,128)(2,1)}), bf16[4,704,256]{2,1,0:T(8,128)(2,1)S(1)}, u32[]{:S(2)}, u32[]{:S(2)}) async-start(bf16[4,704,256]{2,1,0:T(8,128)(2,1)} %param.23), calls=%async_computation.3 | async-start | bytes 2883584 | tf_op jit(solution)/shard_map/all_to_all | solution.py:55
  186.8 1.3 broadcast_multiply_fusion
  188.1 1.3 copy.41
  189.4 1.4 fusion.7
  191.8 4.9 %gather_fusion = bf16[800,2048]{1,0:T(8,128)(2,1)} fusion(bf16[128,2048]{1,0:T(8,128)(2,1)S(1)} %fusion.5, s32[1024]{0:T(1024)S(1)} %pad_clamp_fusion.1), kind=kCustom, calls=%fused_computation | custom fusion | bytes 6556800 | tf_op jit(solution)/shard_map/gather | solution.py:104
  196.7 4.7 %gather.9 = bf16[16,50,2048]{2,1,0:T(8,128)(2,1)} reshape(bf16[800,2048]{1,0:T(8,128)(2,1)} %gather_fusion) | data formatting | bytes 6553600 | tf_op jit(solution)/shard_map/gather | solution.py:104
  201.3 4.2 broadcast_select_fusion
  205.5 1.1 copy-done.3
  206.6 6.8 %all-to-all-start = ((bf16[16,50,2048]{2,1,0:T(8,128)(2,1)}), bf16[16,50,2048]{2,1,0:T(8,128)(2,1)}, u32[]{:S(2)}, u32[]{:S(2)}) async-start(bf16[16,50,2048]{2,1,0:T(8,128)(2,1)} %broadcast_select_fusion), calls=%async_computation | async-start | bytes 7340032 | tf_op jit(solution)/shard_map/all_to_all | solution.py:106
  213.5 0.7 all-gather.9.cloned.1.call-update
  215.0 3.8 copy.55
  218.8 68.2 %all-gather.9.cloned.1.call-done = bf16[8,256,704]{1,2,0:T(8,128)(2,1)} async-done(((bf16[4,256,704]{1,2,0:T(8,128)(2,1)}), bf16[8,256,704]{1,2,0:T(8,128)(2,1)}) %all-gather.9.cloned.1.call-update) | async-done | bytes 2883600 | tf_op jit(solution)/shard_map/all_gather | solution.py:56
  286.9 3.8 copy.56
  290.8 3.2 reshape.111
  294.0 6.0 %fusion.33 = f32[800,704]{1,0:T(8,128)} fusion(bf16[800,2048]{1,0:T(8,128)(2,1)S(1)} %reshape.111, bf16[2048,704]{0,1:T(8,128)(2,1)} %bitcast.69), kind=kOutput, calls=%fused_computation.66 | convolution fusion | flops 2306867200 | bytes 8413184 | tf_op jit(solution)/shard_map/dot_general | solution.py:108
  300.0 62.4 %all-gather.11.cloned.1.call-done = bf16[8,704,256]{2,1,0:T(8,128)(2,1)} async-done(((bf16[4,704,256]{2,1,0:T(8,128)(2,1)}), bf16[8,704,256]{2,1,0:T(8,128)(2,1)}) %all-gather.11.cloned.1.call-update) | async-done | bytes 2883600 | tf_op jit(solution)/shard_map/all_gather | solution.py:56
  362.4 11.1 %convolution_convert_fusion = bf16[800,2,4,256]{3,0,2,1:T(8,128)(2,1)} fusion(bf16[2,4,704,256]{3,2,1,0:T(8,128)(2,1)} %bitcast.74, bf16[800,2048]{1,0:T(8,128)(2,1)S(1)} %reshape.111, bf16[2048,704]{0,1:T(8,128)(2,1)} %bitcast.68, f32[800,704]{1,0:T(8,128)} %fusion.33), kind=kOutput, calls=%fused_computation.7 | convolution fusion | flops 4618188800 | bytes 14573568 | tf_op jit(solution)/shard_map/rh,abhd->rabd/dot_general | solution.py:111
  373.6 4.5 copy.49
  378.0 3.5 reshape.114
  381.5 6.0 %all-to-all-start.4 = ((bf16[16,50,2048]{2,1,0:T(8,128)(2,1)}), bf16[16,50,2048]{2,1,0:T(8,128)(2,1)}, u32[]{:S(2)}, u32[]{:S(2)}) async-start(bf16[16,50,2048]{2,1,0:T(8,128)(2,1)} %reshape.114), calls=%async_computation.4 | async-start | bytes 7340032 | tf_op jit(solution)/shard_map/all_to_all | solution.py:115
  387.6 46.3 %all-to-all-done.4 = bf16[16,50,2048]{2,1,0:T(8,128)(2,1)} async-done(((bf16[16,50,2048]{2,1,0:T(8,128)(2,1)}), bf16[16,50,2048]{2,1,0:T(8,128)(2,1)}, u32[]{:S(2)}, u32[]{:S(2)}) %all-to-all-start.4) | async-done | bytes 3276832 | tf_op jit(solution)/shard_map/all_to_all | solution.py:115
  433.9 3.2 reshape.115
  437.1 4.3 gather_fusion.1
  441.4 6.5 %reshape.117 = f32[128,6,2048]{2,1,0:T(8,128)} reshape(bf16[768,2048]{1,0:T(8,128)(2,1)} %gather_fusion.1) | data formatting | bytes 9437184 | tf_op jit(solution)/shard_map/convert_element_type | solution.py:117
  447.9 6.7 %multiply_reduce_fusion = f32[128,2048]{1,0:T(8,128)S(1)} fusion(f32[128,6,2048]{2,1,0:T(8,128)} %reshape.117, f32[128,6]{1,0:T(8,128)S(1)} %bitcast.72), kind=kLoop, calls=%fused_computation.4 | loop fusion | flops 2883584 | bytes 7343104 | tf_op jit(solution)/shard_map/reduce_sum | solution.py:117
  454.6 0.9 fusion.10
  (55 shorter events, 3.8 us)
Async XLA Ops:
  6.5 3.9 copy-start.5
  6.5 4.2 copy-start.6
  6.5 53.4 %all-to-all-start.1 = ((bf16[4,256,704]{1,2,0:T(8,128)(2,1)}), bf16[4,256,704]{1,2,0:T(8,128)(2,1)S(1)}, u32[]{:S(2)}, u32[]{:S(2)}) async-start(bf16[4,256,704]{1,2,0:T(8,128)(2,1)} %param.21), calls=%async_computation.1 | async-start | bytes 2883584 | tf_op jit(solution)/shard_map/all_to_all | solution.py:55
  10.8 44.4 %copy-start.9 = (s32[1,128,6]{1,0,2:T(1,128)S(1)}, s32[1,128,6]{1,0,2:T(1,128)}, u32[]{:S(2)}) copy-start(s32[1,128,6]{1,0,2:T(1,128)} %param.19) | copy-start | bytes 9220
  11.4 37.2 %collective-permute-start = (f32[16,128,128]{2,1,0:T(8,128)S(1)}, f32[16,128,128]{2,1,0:T(8,128)S(1)}, u32[]{:S(2)}, u32[]{:S(2)}) collective-permute-start(f32[16,128,128]{2,1,0:T(8,128)S(1)} %fusion.13), channel_id=1, source_target_pairs={{0,4},{4,8},{8,12},{12,16},{16,20},{20,24},{24,28},{1,5},{5,9},{9,... | collective-permute-start | bytes 3145736 | tf_op jit(solution)/shard_map/ppermute | solution.py:18
  49.6 29.5 %collective-permute-start.1 = (f32[16,128,128]{2,1,0:T(8,128)}, f32[16,128,128]{2,1,0:T(8,128)}, u32[]{:S(2)}, u32[]{:S(2)}) collective-permute-start(f32[16,128,128]{2,1,0:T(8,128)} %add.81), channel_id=1, source_target_pairs={{0,8},{4,12},{8,16},{12,20},{16,24},{20,28},{1,9},{5,13},{9,17},{1... | collective-permute-start | bytes 3145736 | tf_op jit(solution)/shard_map/ppermute | solution.py:18
  59.9 21.9 %copy-start.2 = (bf16[4,256,704]{1,2,0:T(8,128)(2,1)}, bf16[4,256,704]{1,2,0:T(8,128)(2,1)S(1)}, u32[]{:S(2)}) copy-start(bf16[4,256,704]{1,2,0:T(8,128)(2,1)S(1)} %all-to-all-done.1) | copy-start | bytes 4325380
  59.9 71.5 %all-to-all-start.2 = ((bf16[4,256,704]{1,2,0:T(8,128)(2,1)}), bf16[4,256,704]{1,2,0:T(8,128)(2,1)}, u32[]{:S(2)}, u32[]{:S(2)}) async-start(bf16[4,256,704]{1,2,0:T(8,128)(2,1)} %param.22), calls=%async_computation.2 | async-start | bytes 2883584 | tf_op jit(solution)/shard_map/all_to_all | solution.py:55
  64.2 150.8 %all-gather.7.cloned.1.call-start = ((), (), s32[]{:S(2)}) async-start(), calls=%async_computation.5 | async-start | bytes 4325376 | tf_op jit(solution)/shard_map/all_gather | solution.py:56
  71.8 11.3 %copy-start.8 = (s32[16,6,128]{2,0,1:T(8,128)S(1)}, s32[16,6,128]{2,0,1:T(8,128)}, u32[]{:S(2)}) copy-start(s32[16,6,128]{2,0,1:T(8,128)} %reduce-window.6) | copy-start | bytes 147460
  81.8 45.3 %collective-permute-start.2 = (f32[16,128,128]{2,1,0:T(8,128)}, f32[16,128,128]{2,1,0:T(8,128)}, u32[]{:S(2)}, u32[]{:S(2)}) collective-permute-start(f32[16,128,128]{2,1,0:T(8,128)} %add.82), channel_id=1, source_target_pairs={{0,16},{4,20},{8,24},{12,28},{1,17},{5,21},{9,25},{13,29},{2,18},{... | collective-permute-start | bytes 3145736 | tf_op jit(solution)/shard_map/ppermute | solution.py:18
  83.1 44.1 %copy-start.4 = (bf16[16,8,16,128]{3,2,1,0:T(8,128)(2,1)S(1)}, bf16[16,8,16,128]{3,2,1,0:T(8,128)(2,1)}, u32[]{:S(2)}) copy-start(bf16[16,8,16,128]{3,2,1,0:T(8,128)(2,1)} %copy.58) | copy-start | bytes 1572868
  131.4 58.0 %copy-start.7 = (bf16[1,128,2048]{2,1,0:T(8,128)(2,1)S(1)}, bf16[1,128,2048]{2,1,0:T(8,128)(2,1)}, u32[]{:S(2)}) copy-start(bf16[1,128,2048]{2,1,0:T(8,128)(2,1)} %param.15) | copy-start | bytes 1572868
  131.4 58.0 %copy-start.10 = (f32[2048]{0:T(1024)S(1)}, f32[2048]{0:T(1024)}, u32[]{:S(2)}) copy-start(f32[2048]{0:T(1024)} %param.17) | copy-start | bytes 24580
  131.4 74.1 %all-to-all-start.3 = ((bf16[4,704,256]{2,1,0:T(8,128)(2,1)}), bf16[4,704,256]{2,1,0:T(8,128)(2,1)S(1)}, u32[]{:S(2)}, u32[]{:S(2)}) async-start(bf16[4,704,256]{2,1,0:T(8,128)(2,1)} %param.23), calls=%async_computation.3 | async-start | bytes 2883584 | tf_op jit(solution)/shard_map/all_to_all | solution.py:55
  188.1 3.5 copy-start.11
  190.8 0.8 copy-start
  205.5 1.1 copy-start.3
  206.6 84.1 %all-to-all-start = ((bf16[16,50,2048]{2,1,0:T(8,128)(2,1)}), bf16[16,50,2048]{2,1,0:T(8,128)(2,1)}, u32[]{:S(2)}, u32[]{:S(2)}) async-start(bf16[16,50,2048]{2,1,0:T(8,128)(2,1)} %broadcast_select_fusion), calls=%async_computation | async-start | bytes 7340032 | tf_op jit(solution)/shard_map/all_to_all | solution.py:106
  213.5 73.4 %all-gather.9.cloned.1.call-start = ((), (), s32[]{:S(2)}) async-start(), calls=%async_computation.6 | async-start | bytes 4325376 | tf_op jit(solution)/shard_map/all_gather | solution.py:56
  214.2 148.2 %all-gather.11.cloned.1.call-start = ((), (), s32[]{:S(2)}) async-start(), calls=%async_computation.7 | async-start | bytes 4325376 | tf_op jit(solution)/shard_map/all_gather | solution.py:56
  381.5 6.0 %copy-start.12 = (f32[1,128,6]{1,0,2:T(1,128)S(1)}, f32[1,128,6]{1,0,2:T(1,128)}, u32[]{:S(2)}) copy-start(f32[1,128,6]{1,0,2:T(1,128)} %param.20) | copy-start | bytes 9220
  381.5 52.4 %all-to-all-start.4 = ((bf16[16,50,2048]{2,1,0:T(8,128)(2,1)}), bf16[16,50,2048]{2,1,0:T(8,128)(2,1)}, u32[]{:S(2)}, u32[]{:S(2)}) async-start(bf16[16,50,2048]{2,1,0:T(8,128)(2,1)} %reshape.114), calls=%async_computation.4 | async-start | bytes 7340032 | tf_op jit(solution)/shard_map/all_to_all | solution.py:115
  447.9 6.7 %copy-start.1 = (bf16[128,2048]{1,0:T(8,128)(2,1)S(1)}, bf16[128,2048]{1,0:T(8,128)(2,1)}, u32[]{:S(2)}) copy-start(bf16[128,2048]{1,0:T(8,128)(2,1)} %copy-done) | copy-start | bytes 1572868
Sparse Core Ops, SparseCore 0:
  93.2 73.9 all-gather.6
  215.9 71.0 all-gather.8
  288.5 73.9 all-gather.10

commit v7 on v6

--- a/solution.py
+++ b/solution.py
@@ -11,14 +11,30 @@
 CAP = 50
 
 
-def carried_in(array, axis, count):
+def scanned(array, axis, count):
     total = array
     shift = 1
     while shift < count:
         moved = lax.ppermute(total, axis, [(i, i + shift) for i in range(count - shift)])
         total = total + moved
         shift *= 2
-    return total - array
+    return total
+
+
+def summed(array, axis, count):
+    total = array
+    shift = 1
+    while shift < count:
+        total = total + lax.ppermute(total, axis, [(i, i ^ shift) for i in range(count)])
+        shift *= 2
+    return total
+
+
+def carried_in(array, n_hi, n_lo):
+    within = scanned(array, "seq_lo", n_lo) - array
+    group_total = summed(array, "seq_lo", n_lo)
+    before = scanned(group_total, "seq_hi", n_hi) - group_total
+    return within + before
 
 
 def route_slots(block_routes):
@@ -33,7 +49,7 @@
     return gate_sum / (1.0 + jnp.exp(-gate_sum)) * up_sum
 
 
-def make_shards(n_seq):
+def make_shards(n_seq, n_lo):
     seq = ("seq_hi", "seq_lo")
     group = ("ep", "seq_lo")
 
@@ -52,8 +68,8 @@
         down_weight,
     ):
         def collect(weight):
-            mine = lax.all_to_all(weight, "seq_lo", 0, 0, tiled=False)
-            return lax.all_gather(mine, "seq_hi", axis=0, tiled=False)
+            across = lax.all_gather(weight, "seq_hi", axis=0, tiled=False)
+            return lax.all_to_all(across, "seq_lo", 1, 1, tiled=False)
 
         whole_gate = collect(gate_weight)
         whole_up = collect(up_weight)
@@ -68,7 +84,7 @@
         local_state = jnp.einsum(
             "thd,the->hde", key_heads, value_heads, preferred_element_type=jnp.float32
         )
-        earlier = carried_in(local_state, seq, n_seq)
+        earlier = carried_in(local_state, n_seq // n_lo, n_lo)
         state_before = state_start[0] + earlier
         causal = (
             jnp.arange(tokens, dtype=jnp.int32)[:, None]
@@ -145,6 +161,6 @@
         split_names += list(seq) if name == "seq" else [name]
     split = Mesh(mesh.devices.reshape(shape), tuple(split_names))
     return jax.shard_map(
-        make_shards(n_seq), mesh=split, in_specs=placed, out_specs=P("ep", seq, None),
+        make_shards(n_seq, n_lo), mesh=split, in_specs=placed, out_specs=P("ep", seq, None),
         check_vma=False,
     )

time: 467 us -> 540 us (1.16)
  the two profiles are of different devices: /device:TPU:16 before, /device:TPU:0 now
where the time goes in v7:
time: 540 us; the launch traced here: 531 us
  waiting for transfers between devices  337 us (62%)
  local copies, waits for them, and re-layouts  86.5 us (16%)
  starting transfers between devices  48.3 us (9%)
  matrix products  25.1 us (5%)
  other arithmetic  20.8 us (4%)
  between operations  13.9 us (3%)
    all_gather x3, waiting for transfers between devices, collect(): across = lax.all_gather(weight, 'seq_hi', axis=0, tiled=False)  155 us
    ppermute x3, waiting for transfers between devices, scanned(): lax.ppermute(total, axis, [(i, i + shift) for i in range(count - shift)])  102 us
    all_to_all x1, waiting for transfers between devices, shards(): returned = lax.all_to_all(expert_rows, group, 0, 0, tiled=True)  46.2 us
    ppermute x2, waiting for transfers between devices, summed(): lax.ppermute(total, axis, [(i, i ^ shift) for i in range(count)])  26.3 us
    all_gather x3, local copies, waits for them, and re-layouts, collect(): across = lax.all_gather(weight, 'seq_hi', axis=0, tiled=False)  16.4 us
    ppermute x2, starting transfers between devices, summed(): lax.ppermute(total, axis, [(i, i ^ shift) for i in range(count)])  13.6 us
    all_to_all x3, starting transfers between devices, collect(): return lax.all_to_all(across, 'seq_lo', 1, 1, tiled=False)  13.1 us
    ppermute x3, starting transfers between devices, scanned(): lax.ppermute(total, axis, [(i, i + shift) for i in range(count - shift)])  12.2 us
  transfers between devices with their start and end apart: 13, of which 9 were waited for; matrix products, arithmetic and copies ran while one was open for 16% of the time, Pallas kernels for 0%

profile of v7, /device:TPU:0, one launch (start us, length us, event | category | flops | bytes accessed | tf_op | source)
XLA Modules:
  0.0 531.3 jit_solution(2251021210988835212)
XLA Ops:
  7.3 78.2 %all-gather.7.cloned.1.call-done = bf16[8,256,704]{1,2,0:T(8,128)(2,1)} async-done(((bf16[4,256,704]{1,2,0:T(8,128)(2,1)}), bf16[8,256,704]{1,2,0:T(8,128)(2,1)}) %all-gather.7.cloned.1.call-update) | async-done | bytes 2883600 | tf_op jit(solution)/shard_map/all_gather | solution.py:71
  85.4 6.4 %copy.47 = bf16[2,4,256,704]{2,0,3,1:T(2,128)(2,1)} copy(bf16[2,4,256,704]{2,3,1,0:T(8,128)(2,1)} %bitcast.70) | data formatting | bytes 5767168 | tf_op jit(solution)/shard_map/all_gather | solution.py:71
  91.8 3.7 all-to-all-start.1
  97.6 1.3 copy.59
  99.5 3.9 collective-permute-start
  103.4 1.5 collective-permute-start.2
  104.9 45.2 %collective-permute-done = f32[16,128,128]{2,1,0:T(8,128)S(1)} collective-permute-done((f32[16,128,128]{2,1,0:T(8,128)S(1)}, f32[16,128,128]{2,1,0:T(8,128)S(1)}, u32[]{:S(2)}, u32[]{:S(2)}) %collective-permute-start) | collective-permute-done | bytes 1048608 | tf_op jit(solution)/shard_map/ppermute | solution.py:18
  150.1 21.6 %collective-permute-done.2 = f32[16,128,128]{2,1,0:T(8,128)S(1)} collective-permute-done((f32[16,128,128]{2,1,0:T(8,128)S(1)}, f32[16,128,128]{2,1,0:T(8,128)S(1)}, u32[]{:S(2)}, u32[]{:S(2)}) %collective-permute-start.2) | collective-permute-done | bytes 1048608 | tf_op jit(solution)/shard_map/ppermute | solution.py:28
  171.8 1.6 fusion.42
  173.4 12.1 %collective-permute-start.3 = (f32[16,128,128]{2,1,0:T(8,128)}, f32[16,128,128]{2,1,0:T(8,128)}, u32[]{:S(2)}, u32[]{:S(2)}) collective-permute-start(f32[16,128,128]{2,1,0:T(8,128)} %get-tuple-element.6), channel_id=1, source_target_pairs={{0,8},{4,12},{8,0},{12,4},{1,9},{5,13},{9,1},{13,5},{2,10},{6,14},... | collective-permute-start | bytes 3145736 | tf_op jit(solution)/shard_map/ppermute | solution.py:28
  187.0 1.7 reduce-window.6
  188.8 6.4 %copy.49 = bf16[2,4,256,704]{2,0,3,1:T(2,128)(2,1)} copy(bf16[2,4,256,704]{2,3,1,0:T(8,128)(2,1)} %bitcast.69) | data formatting | bytes 5767168 | tf_op jit(solution)/shard_map/all_gather | solution.py:71
  195.2 4.6 all-to-all-start.2
  200.3 4.9 collective-permute-start.1
  205.2 4.7 collective-permute-done.3
  209.9 2.6 add.93
  212.5 3.3 collective-permute-start.4
  216.0 3.6 scatter_custom_fusion.1
  219.5 3.4 scatter_custom_fusion
  223.1 3.1 convolution_bitcast_fusion
  226.2 36.6 %collective-permute-done.1 = f32[16,128,128]{2,1,0:T(8,128)} collective-permute-done((f32[16,128,128]{2,1,0:T(8,128)}, f32[16,128,128]{2,1,0:T(8,128)}, u32[]{:S(2)}, u32[]{:S(2)}) %collective-permute-start.1) | collective-permute-done | bytes 1048608 | tf_op jit(solution)/shard_map/ppermute | solution.py:18
  262.8 20.4 %collective-permute-done.4 = f32[16,128,128]{2,1,0:T(8,128)} collective-permute-done((f32[16,128,128]{2,1,0:T(8,128)}, f32[16,128,128]{2,1,0:T(8,128)}, u32[]{:S(2)}, u32[]{:S(2)}) %collective-permute-start.4) | collective-permute-done | bytes 1048608 | tf_op jit(solution)/shard_map/ppermute | solution.py:18
  283.2 4.3 multiply_reduce_fusion.1
  288.7 2.6 copy.41
  291.2 1.4 fusion.15
  293.6 4.8 gather_fusion
  298.4 4.7 gather.9
  303.1 4.2 broadcast_select_fusion
  307.4 4.5 all-to-all-start
  312.6 76.7 %all-gather.11.cloned.1.call-done = bf16[8,704,256]{2,1,0:T(8,128)(2,1)} async-done(((bf16[4,704,256]{2,1,0:T(8,128)(2,1)}), bf16[8,704,256]{2,1,0:T(8,128)(2,1)}) %all-gather.11.cloned.1.call-update) | async-done | bytes 2883600 | tf_op jit(solution)/shard_map/all_gather | solution.py:71
  389.3 3.6 copy.51
  393.0 4.8 all-to-all-start.3
  397.8 5.3 copy.48
  403.0 6.1 %reshape.112 = bf16[2048,704]{0,1:T(8,128)(2,1)} reshape(bf16[2,4,256,704]{2,1,0,3:T(4,128)(2,1)} %copy.48) | data formatting | bytes 5767168 | tf_op jit(solution)/shard_map/reshape | solution.py:77
  409.1 5.5 %copy.50 = bf16[2,4,256,704]{2,1,0,3:T(4,128)(2,1)S(1)} copy(bf16[2,4,256,704]{2,0,3,1:T(2,128)(2,1)} %all-to-all-done.2) | data formatting | bytes 5767168 | tf_op jit(solution)/shard_map/all_to_all | solution.py:72
  414.6 3.3 reshape.113
  417.9 3.4 reshape.111
  421.4 6.0 %fusion.43 = f32[800,704]{1,0:T(8,128)} fusion(bf16[800,2048]{1,0:T(8,128)(2,1)S(1)} %reshape.111, bf16[2048,704]{0,1:T(8,128)(2,1)} %reshape.112), kind=kOutput, calls=%fused_computation.72 | convolution fusion | flops 2306867200 | bytes 8413184 | tf_op jit(solution)/shard_map/dot_general | solution.py:124
  427.4 4.9 all-to-all-done.3
  432.2 11.2 %fusion.2 = bf16[800,2,4,256]{3,0,2,1:T(8,128)(2,1)} fusion(bf16[2,4,704,256]{3,2,0,1:T(8,128)(2,1)} %all-to-all-done.3, bf16[800,2048]{1,0:T(8,128)(2,1)S(1)} %reshape.111, bf16[2048,704]{0,1:T(8,128)(2,1)} %reshape.113, f32[800,704]{1,0:T(8,128)} %fusion.43), kind=kOutput, calls=%fused_computation.9 | convolution fusion | flops 4618188800 | bytes 14573568 | tf_op jit(solution)/shard_map/rh,abhd->rabd/dot_general | solution.py:127
  443.4 4.5 copy.53
  447.9 3.5 reshape.114
  451.3 4.9 all-to-all-start.4
  456.4 46.2 %all-to-all-done.4 = bf16[16,50,2048]{2,1,0:T(8,128)(2,1)} async-done(((bf16[16,50,2048]{2,1,0:T(8,128)(2,1)}), bf16[16,50,2048]{2,1,0:T(8,128)(2,1)}, u32[]{:S(2)}, u32[]{:S(2)}) %all-to-all-start.4) | async-done | bytes 3276832 | tf_op jit(solution)/shard_map/all_to_all | solution.py:131
  502.6 3.2 reshape.115
  505.8 4.3 gather_fusion.1
  510.1 6.5 %reshape.117 = f32[128,6,2048]{2,1,0:T(8,128)} reshape(bf16[768,2048]{1,0:T(8,128)(2,1)} %gather_fusion.1) | data formatting | bytes 9437184 | tf_op jit(solution)/shard_map/convert_element_type | solution.py:133
  516.7 6.7 %multiply_reduce_fusion = f32[128,2048]{1,0:T(8,128)S(1)} fusion(f32[128,6,2048]{2,1,0:T(8,128)} %reshape.117, f32[128,6]{1,0:T(8,128)S(1)} %bitcast.74), kind=kLoop, calls=%fused_computation.4 | loop fusion | flops 2883584 | bytes 7343104 | tf_op jit(solution)/shard_map/reduce_sum | solution.py:133
  (58 shorter events, 9.4 us)
Async XLA Ops:
  6.5 78.9 %all-gather.7.cloned.1.call-start = ((), (), s32[]{:S(2)}) async-start(), calls=%async_computation.5 | async-start | bytes 4325376 | tf_op jit(solution)/shard_map/all_gather | solution.py:71
  91.8 103.3 %all-to-all-start.1 = ((bf16[2,4,256,704]{2,0,3,1:T(2,128)(2,1)}), bf16[2,4,256,704]{2,0,3,1:T(2,128)(2,1)S(1)}, u32[]{:S(2)}, u32[]{:S(2)}) async-start(bf16[2,4,256,704]{2,0,3,1:T(2,128)(2,1)} %copy.47), calls=%async_computation.1 | async-start | bytes 5767168 | tf_op jit(solution)/shard_map/all_to_all | solution.py:72
  95.5 93.3 %all-gather.9.cloned.1.call-start = ((), (), s32[]{:S(2)}) async-start(), calls=%async_computation.6 | async-start | bytes 4325376 | tf_op jit(solution)/shard_map/all_gather | solution.py:71
  97.6 75.8 %copy-start.3 = (bf16[1,128,2048]{1,2,0:T(8,128)(2,1)}, bf16[1,128,2048]{1,2,0:T(8,128)(2,1)S(1)}, u32[]{:S(2)}) copy-start(bf16[1,128,2048]{1,2,0:T(8,128)(2,1)S(1)} %copy.57) | copy-start | bytes 1572868
  98.9 51.2 %copy-start.4 = (bf16[16,8,16,128]{3,2,1,0:T(8,128)(2,1)}, bf16[16,8,16,128]{3,2,1,0:T(8,128)(2,1)S(1)}, u32[]{:S(2)}) copy-start(bf16[16,8,16,128]{3,2,1,0:T(8,128)(2,1)S(1)} %copy.59) | copy-start | bytes 1572868
  99.5 72.3 %copy-start = (f32[16,128,128]{2,1,0:T(8,128)}, f32[16,128,128]{2,1,0:T(8,128)S(1)}, u32[]{:S(2)}) copy-start(f32[16,128,128]{2,1,0:T(8,128)S(1)} %fusion.22) | copy-start | bytes 3145732
  99.5 86.0 %copy-start.6 = (s32[1,128,6]{1,0,2:T(1,128)S(1)}, s32[1,128,6]{1,0,2:T(1,128)}, u32[]{:S(2)}) copy-start(s32[1,128,6]{1,0,2:T(1,128)} %param.19) | copy-start | bytes 9220
  99.5 50.6 %collective-permute-start = (f32[16,128,128]{2,1,0:T(8,128)S(1)}, f32[16,128,128]{2,1,0:T(8,128)S(1)}, u32[]{:S(2)}, u32[]{:S(2)}) collective-permute-start(f32[16,128,128]{2,1,0:T(8,128)S(1)} %fusion.22), channel_id=1, source_target_pairs={{0,4},{4,8},{8,12},{1,5},{5,9},{9,13},{2,6},{6,10},{10,14},{3,7},{... | collective-permute-start | bytes 3145736 | tf_op jit(solution)/shard_map/ppermute | solution.py:18
  103.4 68.3 %collective-permute-start.2 = (f32[16,128,128]{2,1,0:T(8,128)S(1)}, f32[16,128,128]{2,1,0:T(8,128)S(1)}, u32[]{:S(2)}, u32[]{:S(2)}) collective-permute-start(f32[16,128,128]{2,1,0:T(8,128)S(1)} %fusion.22), channel_id=1, source_target_pairs={{0,4},{4,0},{8,12},{12,8},{1,5},{5,1},{9,13},{13,9},{2,6},{6,2},{1... | collective-permute-start | bytes 3145736 | tf_op jit(solution)/shard_map/ppermute | solution.py:28
  173.4 36.5 %collective-permute-start.3 = (f32[16,128,128]{2,1,0:T(8,128)}, f32[16,128,128]{2,1,0:T(8,128)}, u32[]{:S(2)}, u32[]{:S(2)}) collective-permute-start(f32[16,128,128]{2,1,0:T(8,128)} %get-tuple-element.6), channel_id=1, source_target_pairs={{0,8},{4,12},{8,0},{12,4},{1,9},{5,13},{9,1},{13,5},{2,10},{6,14},... | collective-permute-start | bytes 3145736 | tf_op jit(solution)/shard_map/ppermute | solution.py:28
  195.2 112.2 %all-to-all-start.2 = ((bf16[2,4,256,704]{2,0,3,1:T(2,128)(2,1)}), bf16[2,4,256,704]{2,0,3,1:T(2,128)(2,1)}, u32[]{:S(2)}, u32[]{:S(2)}) async-start(bf16[2,4,256,704]{2,0,3,1:T(2,128)(2,1)} %copy.49), calls=%async_computation.2 | async-start | bytes 5767168 | tf_op jit(solution)/shard_map/all_to_all | solution.py:72
  200.3 62.5 %collective-permute-start.1 = (f32[16,128,128]{2,1,0:T(8,128)}, f32[16,128,128]{2,1,0:T(8,128)}, u32[]{:S(2)}, u32[]{:S(2)}) collective-permute-start(f32[16,128,128]{2,1,0:T(8,128)} %get-tuple-element.5), channel_id=1, source_target_pairs={{0,8},{4,12},{1,9},{5,13},{2,10},{6,14},{3,11},{7,15},{16,24},{20,... | collective-permute-start | bytes 3145736 | tf_op jit(solution)/shard_map/ppermute | solution.py:18
  212.5 70.7 %collective-permute-start.4 = (f32[16,128,128]{2,1,0:T(8,128)}, f32[16,128,128]{2,1,0:T(8,128)}, u32[]{:S(2)}, u32[]{:S(2)}) collective-permute-start(f32[16,128,128]{2,1,0:T(8,128)} %add.93), channel_id=1, source_target_pairs={{0,16},{1,17},{2,18},{3,19},{4,20},{5,21},{6,22},{7,23},{8,24},{9,... | collective-permute-start | bytes 3145736 | tf_op jit(solution)/shard_map/ppermute | solution.py:18
  287.5 3.7 copy-start.5
  287.6 3.7 copy-start.7
  288.7 4.7 copy-start.8
  292.6 0.8 copy-start.1
  307.4 85.6 %all-to-all-start = ((bf16[16,50,2048]{2,1,0:T(8,128)(2,1)}), bf16[16,50,2048]{2,1,0:T(8,128)(2,1)}, u32[]{:S(2)}, u32[]{:S(2)}) async-start(bf16[16,50,2048]{2,1,0:T(8,128)(2,1)} %broadcast_select_fusion), calls=%async_computation | async-start | bytes 7340032 | tf_op jit(solution)/shard_map/all_to_all | solution.py:122
  311.9 77.5 %all-gather.11.cloned.1.call-start = ((), (), s32[]{:S(2)}) async-start(), calls=%async_computation.7 | async-start | bytes 4325376 | tf_op jit(solution)/shard_map/all_gather | solution.py:71
  393.0 39.3 %all-to-all-start.3 = ((bf16[2,4,704,256]{3,2,0,1:T(8,128)(2,1)}), bf16[2,4,704,256]{3,2,0,1:T(8,128)(2,1)}, u32[]{:S(2)}, u32[]{:S(2)}) async-start(bf16[2,4,704,256]{3,2,0,1:T(8,128)(2,1)} %copy.51), calls=%async_computation.3 | async-start | bytes 5767168 | tf_op jit(solution)/shard_map/all_to_all | solution.py:72
  451.3 4.9 copy-start.9
  451.3 51.3 %all-to-all-start.4 = ((bf16[16,50,2048]{2,1,0:T(8,128)(2,1)}), bf16[16,50,2048]{2,1,0:T(8,128)(2,1)}, u32[]{:S(2)}, u32[]{:S(2)}) async-start(bf16[16,50,2048]{2,1,0:T(8,128)(2,1)} %reshape.114), calls=%async_computation.4 | async-start | bytes 7340032 | tf_op jit(solution)/shard_map/all_to_all | solution.py:131
  516.7 6.7 %copy-start.2 = (bf16[128,2048]{1,0:T(8,128)(2,1)S(1)}, bf16[128,2048]{1,0:T(8,128)(2,1)}, u32[]{:S(2)}) copy-start(bf16[128,2048]{1,0:T(8,128)(2,1)} %copy-done.1) | copy-start | bytes 1572868
Sparse Core Ops, SparseCore 0:
  8.9 76.4 all-gather.6
  97.9 73.3 all-gather.8
  314.3 75.0 all-gather.10

commit v8 on v7

--- a/solution.py
+++ b/solution.py
@@ -67,13 +67,17 @@
         up_weight,
         down_weight,
     ):
-        def collect(weight):
-            across = lax.all_gather(weight, "seq_hi", axis=0, tiled=False)
-            return lax.all_to_all(across, "seq_lo", 1, 1, tiled=False)
-
-        whole_gate = collect(gate_weight)
-        whole_up = collect(up_weight)
-        whole_down = collect(down_weight)
+        mine = [
+            lax.all_to_all(weight, "seq_lo", 0, 0, tiled=False)
+            for weight in (gate_weight, up_weight, down_weight)
+        ]
+        *mine, key_rows = lax.optimization_barrier((*mine, key_rows))
+        whole_gate, whole_up, whole_down = [
+            lax.all_gather(part, "seq_hi", axis=0, tiled=False) for part in mine
+        ]
+        whole_gate, key_rows, value_rows = lax.optimization_barrier(
+            (whole_gate, key_rows, value_rows)
+        )
         whole_gate = whole_gate.reshape(-1, whole_gate.shape[-1])
         whole_up = whole_up.reshape(-1, whole_up.shape[-1])
 
@@ -119,6 +123,9 @@
         filled = jnp.zeros((EXPERTS * CAP,), jnp.bool_).at[position].set(True)
         outgoing = jnp.where(filled[:, None], ffn_in[source], jnp.zeros((), jnp.bfloat16))
         outgoing = outgoing.reshape(EXPERTS, CAP, D)
+        outgoing, whole_up, whole_down = lax.optimization_barrier(
+            (outgoing, whole_up, whole_down)
+        )
         arrived = lax.all_to_all(outgoing, group, 0, 0, tiled=True)
         arrived = arrived.reshape(EXPERTS * CAP, D)
         gate_sum = jnp.dot(arrived, whole_gate, preferred_element_type=jnp.float32)

time: 540 us -> 526 us (0.974)
  the two profiles are of different devices: /device:TPU:0 before, /device:TPU:16 now
where the time goes in v8:
time: 526 us; the launch traced here: 525 us
  waiting for transfers between devices  284 us (54%)
  starting transfers between devices  64.8 us (12%)
  blocking collectives  62.8 us (12%)
  local copies, waits for them, and re-layouts  55.7 us (11%)
  matrix products  23.3 us (4%)
  other arithmetic  20 us (4%)
  between operations  13.4 us (3%)
    all_gather x3, waiting for transfers between devices, shards(): lax.all_gather(part, 'seq_hi', axis=0, tiled=False)  97.3 us
    all_to_all x3, blocking collectives, shards(): lax.all_to_all(weight, 'seq_lo', 0, 0, tiled=False)  62.8 us
    ppermute x2, waiting for transfers between devices, summed(): lax.ppermute(total, axis, [(i, i ^ shift) for i in range(count)])  59 us
    all_to_all x1, waiting for transfers between devices, shards(): returned = lax.all_to_all(expert_rows, group, 0, 0, tiled=True)  45.9 us
    all_to_all x1, starting transfers between devices, shards(): arrived = lax.all_to_all(outgoing, group, 0, 0, tiled=True)  45.3 us
    ppermute x3, waiting for transfers between devices, scanned(): lax.ppermute(total, axis, [(i, i + shift) for i in range(count - shift)])  43.2 us
    all_to_all x1, waiting for transfers between devices, shards(): arrived = lax.all_to_all(outgoing, group, 0, 0, tiled=True)  39 us
    dot_general x1, matrix products, shards(): jnp.einsum('rh,abhd->rabd', hidden, whole_down, preferred_element_type=jn...  11.1 us
  transfers between devices with their start and end apart: 10, of which 9 were waited for; matrix products, arithmetic and copies ran while one was open for 9% of the time, Pallas kernels for 0%

profile of v8, /device:TPU:16, one launch (start us, length us, event | category | flops | bytes accessed | tf_op | source)
XLA Modules:
  0.0 524.6 jit_solution(140234720175148413)
XLA Ops:
  6.5 23.3 %all_to_all.25 = bf16[4,256,704]{1,2,0:T(8,128)(2,1)} all-to-all(bf16[4,256,704]{1,2,0:T(8,128)(2,1)} %param.21), channel_id=1, replica_groups=mesh['seq_hi'=2,'seq_lo'=4,'ep'=4] {'seq_lo'}, dimensions={0} | all-to-all | bytes 2883584 | tf_op jit(solution)/shard_map/all_to_all | solution.py:71
  29.9 20.4 %all_to_all.26 = bf16[4,256,704]{1,2,0:T(8,128)(2,1)} all-to-all(bf16[4,256,704]{1,2,0:T(8,128)(2,1)S(1)} %copy-done.2), channel_id=1, replica_groups=mesh['seq_hi'=2,'seq_lo'=4,'ep'=4] {'seq_lo'}, dimensions={0} | all-to-all | bytes 2883584 | tf_op jit(solution)/shard_map/all_to_all | solution.py:71
  50.3 19.1 %all_to_all.27 = bf16[4,704,256]{2,1,0:T(8,128)(2,1)} all-to-all(bf16[4,704,256]{2,1,0:T(8,128)(2,1)S(1)} %copy-done.3), channel_id=1, replica_groups=mesh['seq_hi'=2,'seq_lo'=4,'ep'=4] {'seq_lo'}, dimensions={0} | all-to-all | bytes 2883584 | tf_op jit(solution)/shard_map/all_to_all | solution.py:71
  69.5 70.4 %all-gather.7.cloned.1.call-done = bf16[8,256,704]{1,2,0:T(8,128)(2,1)} async-done(((bf16[4,256,704]{1,2,0:T(8,128)(2,1)}), bf16[8,256,704]{1,2,0:T(8,128)(2,1)}) %all-gather.7.cloned.1.call-update) | async-done | bytes 2883600 | tf_op jit(solution)/shard_map/all_gather | solution.py:76
  139.9 0.3 copy.55
  140.3 0.5 fusion.19
  140.8 4.4 collective-permute-start
  145.2 1.4 collective-permute-start.2
  146.7 21.1 %collective-permute-done = f32[16,128,128]{2,1,0:T(8,128)} collective-permute-done((f32[16,128,128]{2,1,0:T(8,128)S(1)}, f32[16,128,128]{2,1,0:T(8,128)}, u32[]{:S(2)}, u32[]{:S(2)}) %collective-permute-start) | collective-permute-done | bytes 1048608 | tf_op jit(solution)/shard_map/ppermute | solution.py:18
  167.7 21.3 %collective-permute-done.2 = f32[16,128,128]{2,1,0:T(8,128)} collective-permute-done((f32[16,128,128]{2,1,0:T(8,128)S(1)}, f32[16,128,128]{2,1,0:T(8,128)}, u32[]{:S(2)}, u32[]{:S(2)}) %collective-permute-start.2) | collective-permute-done | bytes 1048608 | tf_op jit(solution)/shard_map/ppermute | solution.py:28
  189.1 3.1 fusion.39
  192.2 4.5 collective-permute-start.3
  197.3 1.7 reduce-window.6
  199.0 0.3 slice_reduce_fusion
  199.5 2.9 collective-permute-start.1
  202.5 37.7 %collective-permute-done.3 = f32[16,128,128]{2,1,0:T(8,128)} collective-permute-done((f32[16,128,128]{2,1,0:T(8,128)}, f32[16,128,128]{2,1,0:T(8,128)}, u32[]{:S(2)}, u32[]{:S(2)}) %collective-permute-start.3) | collective-permute-done | bytes 1048608 | tf_op jit(solution)/shard_map/ppermute | solution.py:28
  240.1 2.6 add.96
  242.8 1.3 collective-permute-start.4
  244.2 3.4 scatter_custom_fusion.1
  247.6 3.4 scatter_custom_fusion
  251.2 3.8 copy.57
  254.9 1.6 fusion.4
  256.5 6.1 %collective-permute-done.1 = f32[16,128,128]{2,1,0:T(8,128)} collective-permute-done((f32[16,128,128]{2,1,0:T(8,128)}, f32[16,128,128]{2,1,0:T(8,128)}, u32[]{:S(2)}, u32[]{:S(2)}) %collective-permute-start.1) | collective-permute-done | bytes 1048608 | tf_op jit(solution)/shard_map/ppermute | solution.py:18
  262.6 16.1 %collective-permute-done.4 = f32[16,128,128]{2,1,0:T(8,128)} collective-permute-done((f32[16,128,128]{2,1,0:T(8,128)}, f32[16,128,128]{2,1,0:T(8,128)}, u32[]{:S(2)}, u32[]{:S(2)}) %collective-permute-start.4) | collective-permute-done | bytes 1048608 | tf_op jit(solution)/shard_map/ppermute | solution.py:18
  278.7 4.0 multiply_reduce_fusion.1
  282.9 0.3 copy.42
  283.2 0.6 copy-done.7
  284.1 0.6 copy-done
  284.9 4.9 gather_fusion
  289.8 4.7 gather.9
  294.4 4.2 broadcast_select_fusion
  298.6 26.9 %all-gather.11.cloned.1.call-done = bf16[8,704,256]{2,1,0:T(8,128)(2,1)} async-done(((bf16[4,704,256]{2,1,0:T(8,128)(2,1)}), bf16[8,704,256]{2,1,0:T(8,128)(2,1)}) %all-gather.11.cloned.1.call-update) | async-done | bytes 2883600 | tf_op jit(solution)/shard_map/all_gather | solution.py:76
  325.5 45.3 %all-to-all-start.3 = ((bf16[16,50,2048]{2,1,0:T(8,128)(2,1)}), bf16[16,50,2048]{2,1,0:T(8,128)(2,1)}, u32[]{:S(2)}, u32[]{:S(2)}) async-start(bf16[16,50,2048]{2,1,0:T(8,128)(2,1)} %broadcast_select_fusion), calls=%async_computation.3 | async-start | bytes 7340032 | tf_op jit(solution)/shard_map/all_to_all | solution.py:129
  370.8 4.0 copy.49
  374.9 3.4 reshape.113
  378.3 39.0 %all-to-all-done.3 = bf16[16,50,2048]{2,1,0:T(8,128)(2,1)} async-done(((bf16[16,50,2048]{2,1,0:T(8,128)(2,1)}), bf16[16,50,2048]{2,1,0:T(8,128)(2,1)}, u32[]{:S(2)}, u32[]{:S(2)}) %all-to-all-start.3) | async-done | bytes 3276832 | tf_op jit(solution)/shard_map/all_to_all | solution.py:129
  417.2 3.2 reshape.112
  420.4 6.0 %fusion.40 = f32[800,704]{1,0:T(8,128)} fusion(bf16[800,2048]{1,0:T(8,128)(2,1)S(1)} %reshape.112, bf16[2048,704]{0,1:T(8,128)(2,1)} %reshape.113), kind=kOutput, calls=%fused_computation.71 | convolution fusion | flops 2306867200 | bytes 8413184 | tf_op jit(solution)/shard_map/dot_general | solution.py:131
  426.5 11.1 %convolution_convert_fusion = bf16[800,2,4,256]{3,0,2,1:T(8,128)(2,1)} fusion(bf16[2,4,704,256]{3,2,1,0:T(8,128)(2,1)} %bitcast.80, bf16[800,2048]{1,0:T(8,128)(2,1)S(1)} %reshape.112, bf16[2048,704]{0,1:T(8,128)(2,1)} %bitcast.75, f32[800,704]{1,0:T(8,128)} %fusion.40), kind=kOutput, calls=%fused_computation.7 | convolution fusion | flops 4618188800 | bytes 14573568 | tf_op jit(solution)/shard_map/rh,abhd->rabd/dot_general | solution.py:134
  437.6 4.5 copy.50
  442.0 3.4 reshape.114
  445.5 4.9 all-to-all-start.4
  450.5 45.9 %all-to-all-done.4 = bf16[16,50,2048]{2,1,0:T(8,128)(2,1)} async-done(((bf16[16,50,2048]{2,1,0:T(8,128)(2,1)}), bf16[16,50,2048]{2,1,0:T(8,128)(2,1)}, u32[]{:S(2)}, u32[]{:S(2)}) %all-to-all-start.4) | async-done | bytes 3276832 | tf_op jit(solution)/shard_map/all_to_all | solution.py:138
  496.4 3.2 reshape.115
  499.6 4.3 gather_fusion.1
  503.9 6.6 %reshape.117 = f32[128,6,2048]{2,1,0:T(8,128)} reshape(bf16[768,2048]{1,0:T(8,128)(2,1)} %gather_fusion.1) | data formatting | bytes 9437184 | tf_op jit(solution)/shard_map/convert_element_type | solution.py:140
  510.5 6.7 %multiply_reduce_fusion = f32[128,2048]{1,0:T(8,128)S(1)} fusion(f32[128,6,2048]{2,1,0:T(8,128)} %reshape.117, f32[128,6]{1,0:T(8,128)S(1)} %bitcast.78), kind=kLoop, calls=%fused_computation.4 | loop fusion | flops 2883584 | bytes 7343104 | tf_op jit(solution)/shard_map/reduce_sum | solution.py:140
  517.1 0.9 fusion.16
  (55 shorter events, 2.1 us)
Async XLA Ops:
  6.5 23.3 %copy-start.2 = (bf16[4,256,704]{1,2,0:T(8,128)(2,1)S(1)}, bf16[4,256,704]{1,2,0:T(8,128)(2,1)}, u32[]{:S(2)}) copy-start(bf16[4,256,704]{1,2,0:T(8,128)(2,1)} %param.22) | copy-start | bytes 4325380
  6.5 43.7 %copy-start.3 = (bf16[4,704,256]{2,1,0:T(8,128)(2,1)S(1)}, bf16[4,704,256]{2,1,0:T(8,128)(2,1)}, u32[]{:S(2)}) copy-start(bf16[4,704,256]{2,1,0:T(8,128)(2,1)} %param.23) | copy-start | bytes 4325380
  6.5 133.3 %all-gather.7.cloned.1.call-start = ((), (), s32[]{:S(2)}) async-start(), calls=%async_computation.5 | async-start | bytes 4325376 | tf_op jit(solution)/shard_map/all_gather | solution.py:76
  50.3 89.6 %copy-start.4 = (bf16[1,128,2048]{2,1,0:T(8,128)(2,1)S(1)}, bf16[1,128,2048]{2,1,0:T(8,128)(2,1)}, u32[]{:S(2)}) copy-start(bf16[1,128,2048]{2,1,0:T(8,128)(2,1)} %param.14) | copy-start | bytes 1572868
  50.3 89.9 %copy-start.5 = (bf16[1,128,2048]{2,1,0:T(8,128)(2,1)S(1)}, bf16[1,128,2048]{2,1,0:T(8,128)(2,1)}, u32[]{:S(2)}) copy-start(bf16[1,128,2048]{2,1,0:T(8,128)(2,1)} %param.13) | copy-start | bytes 1572868
  69.4 181.7 %all-gather.9.cloned.1.call-start = ((), (), s32[]{:S(2)}) async-start(), calls=%async_computation.6 | async-start | bytes 4325376 | tf_op jit(solution)/shard_map/all_gather | solution.py:76
  140.8 26.9 %collective-permute-start = (f32[16,128,128]{2,1,0:T(8,128)S(1)}, f32[16,128,128]{2,1,0:T(8,128)}, u32[]{:S(2)}, u32[]{:S(2)}) collective-permute-start(f32[16,128,128]{2,1,0:T(8,128)S(1)} %fusion.19), channel_id=1, source_target_pairs={{0,4},{4,8},{8,12},{1,5},{5,9},{9,13},{2,6},{6,10},{10,14},{3,7},{... | collective-permute-start | bytes 3145736 | tf_op jit(solution)/shard_map/ppermute | solution.py:18
  145.2 43.9 %collective-permute-start.2 = (f32[16,128,128]{2,1,0:T(8,128)S(1)}, f32[16,128,128]{2,1,0:T(8,128)}, u32[]{:S(2)}, u32[]{:S(2)}) collective-permute-start(f32[16,128,128]{2,1,0:T(8,128)S(1)} %fusion.19), channel_id=1, source_target_pairs={{0,4},{4,0},{8,12},{12,8},{1,5},{5,1},{9,13},{13,9},{2,6},{6,2},{1... | collective-permute-start | bytes 3145736 | tf_op jit(solution)/shard_map/ppermute | solution.py:28
  146.6 50.1 %copy-start.8 = (s32[1,128,6]{1,0,2:T(1,128)S(1)}, s32[1,128,6]{1,0,2:T(1,128)}, u32[]{:S(2)}) copy-start(s32[1,128,6]{1,0,2:T(1,128)} %param.19) | copy-start | bytes 9220
  146.6 50.5 %copy-start.6 = (bf16[1,128,2048]{2,1,0:T(8,128)(2,1)S(1)}, bf16[1,128,2048]{2,1,0:T(8,128)(2,1)}, u32[]{:S(2)}) copy-start(bf16[1,128,2048]{2,1,0:T(8,128)(2,1)} %param.12) | copy-start | bytes 1572868
  146.6 178.9 %all-gather.11.cloned.1.call-start = ((), (), s32[]{:S(2)}) async-start(), calls=%async_computation.7 | async-start | bytes 4325376 | tf_op jit(solution)/shard_map/all_gather | solution.py:76
  192.2 47.9 %collective-permute-start.3 = (f32[16,128,128]{2,1,0:T(8,128)}, f32[16,128,128]{2,1,0:T(8,128)}, u32[]{:S(2)}, u32[]{:S(2)}) collective-permute-start(f32[16,128,128]{2,1,0:T(8,128)} %get-tuple-element.26), channel_id=1, source_target_pairs={{0,8},{4,12},{8,0},{12,4},{1,9},{5,13},{9,1},{13,5},{2,10},{6,14},... | collective-permute-start | bytes 3145736 | tf_op jit(solution)/shard_map/ppermute | solution.py:28
  199.5 63.1 %collective-permute-start.1 = (f32[16,128,128]{2,1,0:T(8,128)}, f32[16,128,128]{2,1,0:T(8,128)}, u32[]{:S(2)}, u32[]{:S(2)}) collective-permute-start(f32[16,128,128]{2,1,0:T(8,128)} %get-tuple-element.25), channel_id=1, source_target_pairs={{0,8},{4,12},{1,9},{5,13},{2,10},{6,14},{3,11},{7,15},{16,24},{20,... | collective-permute-start | bytes 3145736 | tf_op jit(solution)/shard_map/ppermute | solution.py:18
  242.8 36.0 %collective-permute-start.4 = (f32[16,128,128]{2,1,0:T(8,128)}, f32[16,128,128]{2,1,0:T(8,128)}, u32[]{:S(2)}, u32[]{:S(2)}) collective-permute-start(f32[16,128,128]{2,1,0:T(8,128)} %add.96), channel_id=1, source_target_pairs={{0,16},{1,17},{2,18},{3,19},{4,20},{5,21},{6,22},{7,23},{8,24},{9,... | collective-permute-start | bytes 3145736 | tf_op jit(solution)/shard_map/ppermute | solution.py:18
  282.7 1.0 copy-start.7
  282.7 1.0 copy-start.9
  282.9 1.9 copy-start.10
  283.9 0.8 copy-start
  325.5 91.7 %all-to-all-start.3 = ((bf16[16,50,2048]{2,1,0:T(8,128)(2,1)}), bf16[16,50,2048]{2,1,0:T(8,128)(2,1)}, u32[]{:S(2)}, u32[]{:S(2)}) async-start(bf16[16,50,2048]{2,1,0:T(8,128)(2,1)} %broadcast_select_fusion), calls=%async_computation.3 | async-start | bytes 7340032 | tf_op jit(solution)/shard_map/all_to_all | solution.py:129
  445.5 4.9 copy-start.11
  445.5 50.9 %all-to-all-start.4 = ((bf16[16,50,2048]{2,1,0:T(8,128)(2,1)}), bf16[16,50,2048]{2,1,0:T(8,128)(2,1)}, u32[]{:S(2)}, u32[]{:S(2)}) async-start(bf16[16,50,2048]{2,1,0:T(8,128)(2,1)} %reshape.114), calls=%async_computation.4 | async-start | bytes 7340032 | tf_op jit(solution)/shard_map/all_to_all | solution.py:138
  510.5 6.7 %copy-start.1 = (bf16[128,2048]{1,0:T(8,128)(2,1)S(1)}, bf16[128,2048]{1,0:T(8,128)(2,1)}, u32[]{:S(2)}) copy-start(bf16[128,2048]{1,0:T(8,128)(2,1)} %copy-done) | copy-start | bytes 1572868
Sparse Core Ops, SparseCore 0:
  69.5 70.2 all-gather.6
  146.7 71.1 all-gather.8
  251.3 74.2 all-gather.10

commit v9 on v6

--- a/solution.py
+++ b/solution.py
@@ -51,15 +51,15 @@
         up_weight,
         down_weight,
     ):
-        def collect(weight):
-            mine = lax.all_to_all(weight, "seq_lo", 0, 0, tiled=False)
-            return lax.all_gather(mine, "seq_hi", axis=0, tiled=False)
-
-        whole_gate = collect(gate_weight)
-        whole_up = collect(up_weight)
-        whole_down = collect(down_weight)
-        whole_gate = whole_gate.reshape(-1, whole_gate.shape[-1])
-        whole_up = whole_up.reshape(-1, whole_up.shape[-1])
+        slice_rows = gate_weight.shape[1]
+        packed = jnp.concatenate(
+            [gate_weight, up_weight, jnp.swapaxes(down_weight, 1, 2)], axis=1
+        )
+        packed = lax.all_to_all(packed, "seq_lo", 0, 0, tiled=False)
+        packed = lax.all_gather(packed, "seq_hi", axis=0, tiled=False)
+        whole_gate = packed[:, :, :slice_rows]
+        whole_up = packed[:, :, slice_rows : 2 * slice_rows]
+        whole_down = packed[:, :, 2 * slice_rows :]
 
         tokens = queries.shape[1]
         query_heads = queries[0].reshape(tokens, HEADS, HEAD_DIM)
@@ -104,12 +104,16 @@
         outgoing = jnp.where(filled[:, None], ffn_in[source], jnp.zeros((), jnp.bfloat16))
         outgoing = outgoing.reshape(EXPERTS, CAP, D)
         arrived = lax.all_to_all(outgoing, group, 0, 0, tiled=True)
-        arrived = arrived.reshape(EXPERTS * CAP, D)
-        gate_sum = jnp.dot(arrived, whole_gate, preferred_element_type=jnp.float32)
-        up_sum = jnp.dot(arrived, whole_up, preferred_element_type=jnp.float32)
+        arrived = arrived.reshape(EXPERTS * CAP, *whole_gate.shape[:3])
+        gate_sum = jnp.einsum(
+            "rabd,abdh->rh", arrived, whole_gate, preferred_element_type=jnp.float32
+        )
+        up_sum = jnp.einsum(
+            "rabd,abdh->rh", arrived, whole_up, preferred_element_type=jnp.float32
+        )
         hidden = silu_gate(gate_sum, up_sum).astype(jnp.bfloat16)
         expert_rows = jnp.einsum(
-            "rh,abhd->rabd", hidden, whole_down, preferred_element_type=jnp.float32
+            "rh,abdh->rabd", hidden, whole_down, preferred_element_type=jnp.float32
         ).astype(jnp.bfloat16)
         expert_rows = expert_rows.reshape(EXPERTS, CAP, D)
         returned = lax.all_to_all(expert_rows, group, 0, 0, tiled=True)

time: 467 us -> 503 us (1.077)
  blocking collectives: 0 us -> 228 us
  waiting for transfers between devices: 253 us -> 146 us
  starting transfers between devices: 87.5 us -> 22.6 us
  local copies, waits for them, and re-layouts: 60.1 us -> 48 us
    all_to_all x0 -> x1, blocking collectives: none -> 228 us  [shards(): arrived = lax.all_to_all(outgoing, group, 0, 0, tiled=True)]
    all_gather x3 -> x1, waiting for transfers between devices: 131 us -> 0.02 us  [shards(): packed = lax.all_gather(packed, 'seq_hi', axis=0, tiled=False)]
    all_to_all x4 -> x1, starting transfers between devices: 70.4 us -> 5.07 us  [shards(): packed = lax.all_to_all(packed, 'seq_lo', 0, 0, tiled=False)]
    ppermute x3, waiting for transfers between devices: 74.6 us -> 99.7 us  [carried_in(): lax.ppermute(total, axis, [(i, i + shift) for i in range(count - shift)])]
    reshape x3 -> x1, local copies, waits for them, and re-layouts: 10.8 us -> 6.52 us  [shards(): arrived = arrived.reshape(EXPERTS * CAP, *whole_gate.shape[:3])]
  transfers between devices with their start and end apart: 11 -> 6, of which waited for: 6 -> 4; matrix products, arithmetic and copies ran while one was open for 14% -> 8% of each run, Pallas kernels for 0% -> 0%
where the time goes in v9:
time: 503 us; the launch traced here: 502 us
  blocking collectives  228 us (45%)
  waiting for transfers between devices  146 us (29%)
  local copies, waits for them, and re-layouts  48 us (10%)
  matrix products  23.2 us (5%)
  starting transfers between devices  22.6 us (4%)
  other arithmetic  19.9 us (4%)
  between operations  13.8 us (3%)
    all_to_all x1, blocking collectives, shards(): arrived = lax.all_to_all(outgoing, group, 0, 0, tiled=True)  228 us
    ppermute x3, waiting for transfers between devices, carried_in(): lax.ppermute(total, axis, [(i, i + shift) for i in range(count - shift)])  99.7 us
    all_to_all x1, waiting for transfers between devices, shards(): returned = lax.all_to_all(expert_rows, group, 0, 0, tiled=True)  46.3 us
    dot_general x1, matrix products, shards(): jnp.einsum('rh,abdh->rabd', hidden, whole_down, preferred_element_type=jn...  11.3 us
    ppermute x3, starting transfers between devices, carried_in(): lax.ppermute(total, axis, [(i, i + shift) for i in range(count - shift)])  10.7 us
  transfers between devices with their start and end apart: 6, of which 4 were waited for; matrix products, arithmetic and copies ran while one was open for 8% of the time, Pallas kernels for 0%

profile of v9, /device:TPU:16, one launch (start us, length us, event | category | flops | bytes accessed | tf_op | source)
XLA Modules:
  0.0 501.9 jit_solution(14938240984582697478)
XLA Ops:
  6.5 3.7 pad_maximum_fusion
  10.2 5.1 %all-to-all-start.1 = ((bf16[4,768,704]{1,2,0:T(8,128)(2,1)}), bf16[4,768,704]{1,2,0:T(8,128)(2,1)}, u32[]{:S(2)}, u32[]{:S(2)}) async-start(bf16[4,768,704]{1,2,0:T(8,128)(2,1)} %pad_maximum_fusion), calls=%async_computation.1 | async-start | bytes 8650752 | tf_op jit(solution)/shard_map/all_to_all | solution.py:58
  15.3 0.3 copy.54
  15.7 0.1 copy.56
  15.8 0.5 fusion.39
  16.3 3.8 collective-permute-start
  20.1 64.4 %collective-permute-done = f32[16,128,128]{2,1,0:T(8,128)S(1)} collective-permute-done((f32[16,128,128]{2,1,0:T(8,128)S(1)}, f32[16,128,128]{2,1,0:T(8,128)S(1)}, u32[]{:S(2)}, u32[]{:S(2)}) %collective-permute-start) | collective-permute-done | bytes 1048608 | tf_op jit(solution)/shard_map/ppermute | solution.py:18
  84.5 1.1 add.81
  85.6 5.6 %collective-permute-start.1 = (f32[16,128,128]{2,1,0:T(8,128)}, f32[16,128,128]{2,1,0:T(8,128)}, u32[]{:S(2)}, u32[]{:S(2)}) collective-permute-start(f32[16,128,128]{2,1,0:T(8,128)} %add.81), channel_id=1, source_target_pairs={{0,8},{4,12},{8,16},{12,20},{16,24},{20,28},{1,9},{5,13},{9,17},{1... | collective-permute-start | bytes 3145736 | tf_op jit(solution)/shard_map/ppermute | solution.py:18
  91.2 0.1 copy.43
  91.3 0.1 eq.29
  91.5 0.1 eq.25
  91.6 0.1 copy.57
  91.8 1.7 reduce-window.6
  93.5 0.3 slice_reduce_fusion
  93.8 0.1 copy.42
  93.9 0.1 mul.79
  94.0 19.0 %collective-permute-done.1 = f32[16,128,128]{2,1,0:T(8,128)} collective-permute-done((f32[16,128,128]{2,1,0:T(8,128)}, f32[16,128,128]{2,1,0:T(8,128)}, u32[]{:S(2)}, u32[]{:S(2)}) %collective-permute-start.1) | collective-permute-done | bytes 1048608 | tf_op jit(solution)/shard_map/ppermute | solution.py:18
  113.1 2.7 add.82
  115.7 1.3 collective-permute-start.2
  117.1 3.4 scatter_custom_fusion.1
  120.5 3.4 scatter_custom_fusion
  124.1 1.8 convolution_bitcast_fusion
  125.9 16.3 %collective-permute-done.2 = f32[16,128,128]{2,1,0:T(8,128)} collective-permute-done((f32[16,128,128]{2,1,0:T(8,128)}, f32[16,128,128]{2,1,0:T(8,128)}, u32[]{:S(2)}, u32[]{:S(2)}) %collective-permute-start.2) | collective-permute-done | bytes 1048608 | tf_op jit(solution)/shard_map/ppermute | solution.py:18
  142.3 3.3 multiply_reduce_fusion.1
  145.7 0.3 copy.40
  146.1 0.6 copy-done.6
  146.7 0.1 fusion.33
  146.8 0.2 fusion.29
  147.0 0.6 copy-done
  147.6 0.2 fusion.31
  147.8 4.8 gather_fusion
  152.7 4.7 gather.9
  157.4 2.4 broadcast_select_fusion
  159.8 228.5 %all_to_all.15 = bf16[16,50,2048]{2,1,0:T(8,128)(2,1)} all-to-all(bf16[16,50,2048]{2,1,0:T(8,128)(2,1)S(1)} %broadcast_select_fusion), channel_id=1, replica_groups=mesh['seq_hi'=2,'seq_lo'=4,'ep'=4] {'ep','seq_lo'}, dimensions={0} | all-to-all | bytes 6553600 | tf_op jit(solution)/shard_map/all_to_all | solution.py:106
  388.2 6.5 %reshape.105 = bf16[800,2,4,256]{3,2,1,0:T(4,128)(2,1)S(1)} reshape(bf16[16,50,2048]{2,1,0:T(8,128)(2,1)} %all_to_all.15) | data formatting | bytes 6553600 | tf_op jit(solution)/shard_map/reshape | solution.py:107
  394.8 6.3 %fusion.2 = f32[800,704,1,1]{1,0,3,2:T(8,128)} fusion(bf16[800,2,4,256]{3,2,1,0:T(4,128)(2,1)S(1)} %reshape.105, bf16[2,4,768,704]{2,3,1,0:T(8,128)(2,1)} %bitcast.90), kind=kOutput, calls=%fused_computation.9 | convolution fusion | flops 2306867200 | bytes 8413184 | tf_op jit(solution)/shard_map/rabd,abdh->rh/dot_general | solution.py:108
  401.1 11.3 %fusion.11 = bf16[800,2,4,256]{3,0,2,1:T(8,128)(2,1)} fusion(bf16[2,4,768,704]{2,3,1,0:T(8,128)(2,1)} %bitcast.91, bf16[800,2,4,256]{3,2,1,0:T(4,128)(2,1)S(1)} %reshape.105, f32[800,704,1,1]{1,0,3,2:T(8,128)} %fusion.2), kind=kOutput, calls=%fused_computation.21 | convolution fusion | flops 4618188800 | bytes 14778368 | tf_op jit(solution)/shard_map/rh,abdh->rabd/dot_general | solution.py:115
  412.3 4.5 copy.48
  416.8 3.4 reshape.106
  420.2 6.8 %all-to-all-start.2 = ((bf16[16,50,2048]{2,1,0:T(8,128)(2,1)}), bf16[16,50,2048]{2,1,0:T(8,128)(2,1)}, u32[]{:S(2)}, u32[]{:S(2)}) async-start(bf16[16,50,2048]{2,1,0:T(8,128)(2,1)} %reshape.106), calls=%async_computation.2 | async-start | bytes 7340032 | tf_op jit(solution)/shard_map/all_to_all | solution.py:119
  427.0 0.1 copy.53
  427.1 46.3 %all-to-all-done.2 = bf16[16,50,2048]{2,1,0:T(8,128)(2,1)} async-done(((bf16[16,50,2048]{2,1,0:T(8,128)(2,1)}), bf16[16,50,2048]{2,1,0:T(8,128)(2,1)}, u32[]{:S(2)}, u32[]{:S(2)}) %all-to-all-start.2) | async-done | bytes 3276832 | tf_op jit(solution)/shard_map/all_to_all | solution.py:119
  473.4 3.2 reshape.107
  476.6 4.3 gather_fusion.1
  480.9 6.6 %reshape.109 = f32[128,6,2048]{2,1,0:T(8,128)} reshape(bf16[768,2048]{1,0:T(8,128)(2,1)} %gather_fusion.1) | data formatting | bytes 9437184 | tf_op jit(solution)/shard_map/convert_element_type | solution.py:121
  487.5 6.7 %multiply_reduce_fusion = f32[128,2048]{1,0:T(8,128)S(1)} fusion(f32[128,6,2048]{2,1,0:T(8,128)} %reshape.109, f32[128,6]{1,0:T(8,128)S(1)} %bitcast.88), kind=kLoop, calls=%fused_computation.4 | loop fusion | flops 2883584 | bytes 7343104 | tf_op jit(solution)/shard_map/reduce_sum | solution.py:121
  494.1 0.9 fusion.36
  (39 shorter events, 0.5 us)
Async XLA Ops:
  10.2 5.1 %copy-start.3 = (bf16[1,128,2048]{2,1,0:T(8,128)(2,1)S(1)}, bf16[1,128,2048]{2,1,0:T(8,128)(2,1)}, u32[]{:S(2)}) copy-start(bf16[1,128,2048]{2,1,0:T(8,128)(2,1)} %param.14) | copy-start | bytes 1572868
  10.2 5.4 %copy-start.4 = (bf16[1,128,2048]{2,1,0:T(8,128)(2,1)S(1)}, bf16[1,128,2048]{2,1,0:T(8,128)(2,1)}, u32[]{:S(2)}) copy-start(bf16[1,128,2048]{2,1,0:T(8,128)(2,1)} %param.13) | copy-start | bytes 1572868
  10.2 115.7 %all-to-all-start.1 = ((bf16[4,768,704]{1,2,0:T(8,128)(2,1)}), bf16[4,768,704]{1,2,0:T(8,128)(2,1)}, u32[]{:S(2)}, u32[]{:S(2)}) async-start(bf16[4,768,704]{1,2,0:T(8,128)(2,1)} %pad_maximum_fusion), calls=%async_computation.1 | async-start | bytes 8650752 | tf_op jit(solution)/shard_map/all_to_all | solution.py:58
  15.3 379.5 %all-gather.3.cloned.1.call-start = ((), (), s32[]{:S(2)}) async-start(), calls=%async_computation.3 | async-start | bytes 12976128 | tf_op jit(solution)/shard_map/all_gather | solution.py:59
  15.6 75.6 %copy-start.7 = (s32[1,128,6]{1,0,2:T(1,128)S(1)}, s32[1,128,6]{1,0,2:T(1,128)}, u32[]{:S(2)}) copy-start(s32[1,128,6]{1,0,2:T(1,128)} %param.19) | copy-start | bytes 9220
  15.6 76.0 %copy-start.5 = (bf16[1,128,2048]{2,1,0:T(8,128)(2,1)S(1)}, bf16[1,128,2048]{2,1,0:T(8,128)(2,1)}, u32[]{:S(2)}) copy-start(bf16[1,128,2048]{2,1,0:T(8,128)(2,1)} %param.12) | copy-start | bytes 1572868
  16.3 68.2 %collective-permute-start = (f32[16,128,128]{2,1,0:T(8,128)S(1)}, f32[16,128,128]{2,1,0:T(8,128)S(1)}, u32[]{:S(2)}, u32[]{:S(2)}) collective-permute-start(f32[16,128,128]{2,1,0:T(8,128)S(1)} %fusion.39), channel_id=1, source_target_pairs={{0,4},{4,8},{8,12},{12,16},{16,20},{20,24},{24,28},{1,5},{5,9},{9,... | collective-permute-start | bytes 3145736 | tf_op jit(solution)/shard_map/ppermute | solution.py:18
  85.6 27.4 %collective-permute-start.1 = (f32[16,128,128]{2,1,0:T(8,128)}, f32[16,128,128]{2,1,0:T(8,128)}, u32[]{:S(2)}, u32[]{:S(2)}) collective-permute-start(f32[16,128,128]{2,1,0:T(8,128)} %add.81), channel_id=1, source_target_pairs={{0,8},{4,12},{8,16},{12,20},{16,24},{20,28},{1,9},{5,13},{9,17},{1... | collective-permute-start | bytes 3145736 | tf_op jit(solution)/shard_map/ppermute | solution.py:18
  115.7 26.5 %collective-permute-start.2 = (f32[16,128,128]{2,1,0:T(8,128)}, f32[16,128,128]{2,1,0:T(8,128)}, u32[]{:S(2)}, u32[]{:S(2)}) collective-permute-start(f32[16,128,128]{2,1,0:T(8,128)} %add.82), channel_id=1, source_target_pairs={{0,16},{4,20},{8,24},{12,28},{1,17},{5,21},{9,25},{13,29},{2,18},{... | collective-permute-start | bytes 3145736 | tf_op jit(solution)/shard_map/ppermute | solution.py:18
  125.9 16.3 %copy-start.2 = (f32[128,16,128]{0,2,1:T(8,128)S(1)}, f32[128,16,128]{0,2,1:T(8,128)}, u32[]{:S(2)}) copy-start(f32[128,16,128]{0,2,1:T(8,128)} %convolution_bitcast_fusion) | copy-start | bytes 3145732
  145.6 1.1 copy-start.6
  145.6 1.1 copy-start.8
  145.6 2.0 copy-start.9
  146.8 0.8 copy-start
  420.2 6.8 %copy-start.10 = (f32[1,128,6]{1,0,2:T(1,128)S(1)}, f32[1,128,6]{1,0,2:T(1,128)}, u32[]{:S(2)}) copy-start(f32[1,128,6]{1,0,2:T(1,128)} %param.20) | copy-start | bytes 9220
  420.2 53.2 %all-to-all-start.2 = ((bf16[16,50,2048]{2,1,0:T(8,128)(2,1)}), bf16[16,50,2048]{2,1,0:T(8,128)(2,1)}, u32[]{:S(2)}, u32[]{:S(2)}) async-start(bf16[16,50,2048]{2,1,0:T(8,128)(2,1)} %reshape.106), calls=%async_computation.2 | async-start | bytes 7340032 | tf_op jit(solution)/shard_map/all_to_all | solution.py:119
  487.5 6.7 %copy-start.1 = (bf16[128,2048]{1,0:T(8,128)(2,1)S(1)}, bf16[128,2048]{1,0:T(8,128)(2,1)}, u32[]{:S(2)}) copy-start(bf16[128,2048]{1,0:T(8,128)(2,1)} %copy-done) | copy-start | bytes 1572868
Sparse Core Ops, SparseCore 0:
  126.1 204.0 all-gather.2

commit v10 on v9

--- a/solution.py
+++ b/solution.py
@@ -56,6 +56,7 @@
             [gate_weight, up_weight, jnp.swapaxes(down_weight, 1, 2)], axis=1
         )
         packed = lax.all_to_all(packed, "seq_lo", 0, 0, tiled=False)
+        packed, key_rows, value_rows = lax.optimization_barrier((packed, key_rows, value_rows))
         packed = lax.all_gather(packed, "seq_hi", axis=0, tiled=False)
         whole_gate = packed[:, :, :slice_rows]
         whole_up = packed[:, :, slice_rows : 2 * slice_rows]

time: 503 us -> 501 us (level)
  blocking collectives: 228 us -> 281 us
  waiting for transfers between devices: 146 us -> 103 us
  starting transfers between devices: 22.6 us -> 12.8 us
    all_to_all x0 -> x1, blocking collectives: none -> 53.2 us  [shards(): packed = lax.all_to_all(packed, 'seq_lo', 0, 0, tiled=False)]
    ppermute x3, waiting for transfers between devices: 99.7 us -> 56.5 us  [carried_in(): lax.ppermute(total, axis, [(i, i + shift) for i in range(count - shift)])]
    all_to_all x1 -> x0, starting transfers between devices: 5.07 us -> none  [shards(): packed = lax.all_to_all(packed, 'seq_lo', 0, 0, tiled=False)]
  transfers between devices with their start and end apart: 6 -> 5, of which waited for: 4 -> 4; matrix products, arithmetic and copies ran while one was open for 8% -> 7% of each run, Pallas kernels for 0% -> 0%
where the time goes in v10:
time: 501 us
  blocking collectives  281 us (56%)
  waiting for transfers between devices  103 us (21%)
  local copies, waits for them, and re-layouts  48 us (10%)
  matrix products  23.2 us (5%)
  other arithmetic  18.6 us (4%)
  between operations  13.8 us (3%)
  starting transfers between devices  12.8 us (3%)
    all_to_all x1, blocking collectives, shards(): arrived = lax.all_to_all(outgoing, group, 0, 0, tiled=True)  228 us
    ppermute x3, waiting for transfers between devices, carried_in(): lax.ppermute(total, axis, [(i, i + shift) for i in range(count - shift)])  56.5 us
    all_to_all x1, blocking collectives, shards(): packed = lax.all_to_all(packed, 'seq_lo', 0, 0, tiled=False)  53.2 us
    all_to_all x1, waiting for transfers between devices, shards(): returned = lax.all_to_all(expert_rows, group, 0, 0, tiled=True)  46.3 us
    dot_general x1, matrix products, shards(): jnp.einsum('rh,abdh->rabd', hidden, whole_down, preferred_element_type=jn...  11.3 us
  transfers between devices with their start and end apart: 5, of which 4 were waited for; matrix products, arithmetic and copies ran while one was open for 7% of the time, Pallas kernels for 0%

profile of v10, /device:TPU:16, one launch (start us, length us, event | category | flops | bytes accessed | tf_op | source)
XLA Modules:
  0.0 500.6 jit_solution(17262102450175498203)
XLA Ops:
  6.5 2.4 pad_maximum_fusion
  8.9 53.2 %all_to_all.15 = bf16[4,768,704]{1,2,0:T(8,128)(2,1)} all-to-all(bf16[4,768,704]{1,2,0:T(8,128)(2,1)S(1)} %pad_maximum_fusion), channel_id=1, replica_groups=mesh['seq_hi'=2,'seq_lo'=4,'ep'=4] {'seq_lo'}, dimensions={0} | all-to-all | bytes 8650752 | tf_op jit(solution)/shard_map/all_to_all | solution.py:58
  62.1 0.3 copy.56
  62.4 0.1 copy.58
  62.5 0.5 fusion.41
  63.0 2.8 collective-permute-start
  65.9 23.3 %collective-permute-done = f32[16,128,128]{2,1,0:T(8,128)S(1)} collective-permute-done((f32[16,128,128]{2,1,0:T(8,128)S(1)}, f32[16,128,128]{2,1,0:T(8,128)S(1)}, u32[]{:S(2)}, u32[]{:S(2)}) %collective-permute-start) | collective-permute-done | bytes 1048608 | tf_op jit(solution)/shard_map/ppermute | solution.py:18
  89.2 1.1 add.84
  90.3 3.3 collective-permute-start.1
  93.6 0.1 copy.44
  93.7 0.1 eq.29
  93.9 0.1 eq.25
  94.0 0.1 copy.59
  94.2 1.7 reduce-window.6
  95.9 0.3 slice_reduce_fusion
  96.2 0.1 copy.43
  96.3 0.1 mul.79
  96.4 18.5 %collective-permute-done.1 = f32[16,128,128]{2,1,0:T(8,128)} collective-permute-done((f32[16,128,128]{2,1,0:T(8,128)}, f32[16,128,128]{2,1,0:T(8,128)}, u32[]{:S(2)}, u32[]{:S(2)}) %collective-permute-start.1) | collective-permute-done | bytes 1048608 | tf_op jit(solution)/shard_map/ppermute | solution.py:18
  114.9 2.7 add.85
  117.6 1.3 collective-permute-start.2
  119.0 3.4 scatter_custom_fusion.1
  122.4 3.4 scatter_custom_fusion
  126.0 1.6 fusion.26
  127.6 14.7 %collective-permute-done.2 = f32[16,128,128]{2,1,0:T(8,128)} collective-permute-done((f32[16,128,128]{2,1,0:T(8,128)}, f32[16,128,128]{2,1,0:T(8,128)}, u32[]{:S(2)}, u32[]{:S(2)}) %collective-permute-start.2) | collective-permute-done | bytes 1048608 | tf_op jit(solution)/shard_map/ppermute | solution.py:18
  142.3 3.5 multiply_reduce_fusion.1
  146.0 0.3 copy.41
  146.4 0.6 copy-done.5
  147.0 0.1 fusion.35
  147.1 0.2 fusion.31
  147.3 0.6 copy-done
  147.9 0.2 fusion.33
  148.1 4.8 gather_fusion
  153.0 4.7 gather.9
  157.7 2.4 broadcast_select_fusion
  160.1 228.2 %all_to_all.16 = bf16[16,50,2048]{2,1,0:T(8,128)(2,1)} all-to-all(bf16[16,50,2048]{2,1,0:T(8,128)(2,1)S(1)} %broadcast_select_fusion), channel_id=1, replica_groups=mesh['seq_hi'=2,'seq_lo'=4,'ep'=4] {'ep','seq_lo'}, dimensions={0} | all-to-all | bytes 6553600 | tf_op jit(solution)/shard_map/all_to_all | solution.py:107
  388.3 6.5 %reshape.105 = bf16[800,2,4,256]{3,2,1,0:T(4,128)(2,1)S(1)} reshape(bf16[16,50,2048]{2,1,0:T(8,128)(2,1)} %all_to_all.16) | data formatting | bytes 6553600 | tf_op jit(solution)/shard_map/reshape | solution.py:108
  394.9 6.3 %fusion.2 = f32[800,704,1,1]{1,0,3,2:T(8,128)} fusion(bf16[800,2,4,256]{3,2,1,0:T(4,128)(2,1)S(1)} %reshape.105, bf16[2,4,768,704]{2,3,1,0:T(8,128)(2,1)} %bitcast.94), kind=kOutput, calls=%fused_computation.9 | convolution fusion | flops 2306867200 | bytes 8413184 | tf_op jit(solution)/shard_map/rabd,abdh->rh/dot_general | solution.py:109
  401.1 11.3 %fusion.11 = bf16[800,2,4,256]{3,0,2,1:T(8,128)(2,1)} fusion(bf16[2,4,768,704]{2,3,1,0:T(8,128)(2,1)} %bitcast.95, bf16[800,2,4,256]{3,2,1,0:T(4,128)(2,1)S(1)} %reshape.105, f32[800,704,1,1]{1,0,3,2:T(8,128)} %fusion.2), kind=kOutput, calls=%fused_computation.21 | convolution fusion | flops 4618188800 | bytes 14778368 | tf_op jit(solution)/shard_map/rh,abdh->rabd/dot_general | solution.py:116
  412.4 4.5 copy.49
  416.9 3.4 reshape.106
  420.3 5.4 %all-to-all-start.2 = ((bf16[16,50,2048]{2,1,0:T(8,128)(2,1)}), bf16[16,50,2048]{2,1,0:T(8,128)(2,1)}, u32[]{:S(2)}, u32[]{:S(2)}) async-start(bf16[16,50,2048]{2,1,0:T(8,128)(2,1)} %reshape.106), calls=%async_computation.2 | async-start | bytes 7340032 | tf_op jit(solution)/shard_map/all_to_all | solution.py:120
  425.7 0.1 copy.55
  425.8 46.3 %all-to-all-done.2 = bf16[16,50,2048]{2,1,0:T(8,128)(2,1)} async-done(((bf16[16,50,2048]{2,1,0:T(8,128)(2,1)}), bf16[16,50,2048]{2,1,0:T(8,128)(2,1)}, u32[]{:S(2)}, u32[]{:S(2)}) %all-to-all-start.2) | async-done | bytes 3276832 | tf_op jit(solution)/shard_map/all_to_all | solution.py:120
  472.1 3.2 reshape.107
  475.3 4.3 gather_fusion.1
  479.6 6.6 %reshape.109 = f32[128,6,2048]{2,1,0:T(8,128)} reshape(bf16[768,2048]{1,0:T(8,128)(2,1)} %gather_fusion.1) | data formatting | bytes 9437184 | tf_op jit(solution)/shard_map/convert_element_type | solution.py:122
  486.2 6.7 %multiply_reduce_fusion = f32[128,2048]{1,0:T(8,128)S(1)} fusion(f32[128,6,2048]{2,1,0:T(8,128)} %reshape.109, f32[128,6]{1,0:T(8,128)S(1)} %bitcast.92), kind=kLoop, calls=%fused_computation.4 | loop fusion | flops 2883584 | bytes 7343104 | tf_op jit(solution)/shard_map/reduce_sum | solution.py:122
  492.9 0.9 fusion.38
  (36 shorter events, 0.5 us)
Async XLA Ops:
  6.5 388.3 %all-gather.3.cloned.1.call-start = ((), (), s32[]{:S(2)}) async-start(), calls=%async_computation.3 | async-start | bytes 12976128 | tf_op jit(solution)/shard_map/all_gather | solution.py:60
  8.9 53.2 %copy-start.2 = (bf16[1,128,2048]{2,1,0:T(8,128)(2,1)S(1)}, bf16[1,128,2048]{2,1,0:T(8,128)(2,1)}, u32[]{:S(2)}) copy-start(bf16[1,128,2048]{2,1,0:T(8,128)(2,1)} %param.14) | copy-start | bytes 1572868
  8.9 53.5 %copy-start.3 = (bf16[1,128,2048]{2,1,0:T(8,128)(2,1)S(1)}, bf16[1,128,2048]{2,1,0:T(8,128)(2,1)}, u32[]{:S(2)}) copy-start(bf16[1,128,2048]{2,1,0:T(8,128)(2,1)} %param.13) | copy-start | bytes 1572868
  62.4 31.3 %copy-start.6 = (s32[1,128,6]{1,0,2:T(1,128)S(1)}, s32[1,128,6]{1,0,2:T(1,128)}, u32[]{:S(2)}) copy-start(s32[1,128,6]{1,0,2:T(1,128)} %param.19) | copy-start | bytes 9220
  62.4 31.6 %copy-start.4 = (bf16[1,128,2048]{2,1,0:T(8,128)(2,1)S(1)}, bf16[1,128,2048]{2,1,0:T(8,128)(2,1)}, u32[]{:S(2)}) copy-start(bf16[1,128,2048]{2,1,0:T(8,128)(2,1)} %param.12) | copy-start | bytes 1572868
  63.0 26.2 %collective-permute-start = (f32[16,128,128]{2,1,0:T(8,128)S(1)}, f32[16,128,128]{2,1,0:T(8,128)S(1)}, u32[]{:S(2)}, u32[]{:S(2)}) collective-permute-start(f32[16,128,128]{2,1,0:T(8,128)S(1)} %fusion.41), channel_id=1, source_target_pairs={{0,4},{4,8},{8,12},{12,16},{16,20},{20,24},{24,28},{1,5},{5,9},{9,... | collective-permute-start | bytes 3145736 | tf_op jit(solution)/shard_map/ppermute | solution.py:18
  90.3 24.6 %collective-permute-start.1 = (f32[16,128,128]{2,1,0:T(8,128)}, f32[16,128,128]{2,1,0:T(8,128)}, u32[]{:S(2)}, u32[]{:S(2)}) collective-permute-start(f32[16,128,128]{2,1,0:T(8,128)} %add.84), channel_id=1, source_target_pairs={{0,8},{4,12},{8,16},{12,20},{16,24},{20,28},{1,9},{5,13},{9,17},{1... | collective-permute-start | bytes 3145736 | tf_op jit(solution)/shard_map/ppermute | solution.py:18
  117.6 24.7 %collective-permute-start.2 = (f32[16,128,128]{2,1,0:T(8,128)}, f32[16,128,128]{2,1,0:T(8,128)}, u32[]{:S(2)}, u32[]{:S(2)}) collective-permute-start(f32[16,128,128]{2,1,0:T(8,128)} %add.85), channel_id=1, source_target_pairs={{0,16},{4,20},{8,24},{12,28},{1,17},{5,21},{9,25},{13,29},{2,18},{... | collective-permute-start | bytes 3145736 | tf_op jit(solution)/shard_map/ppermute | solution.py:18
  145.9 1.1 copy-start.5
  145.9 1.1 copy-start.7
  145.9 2.0 copy-start.8
  147.1 0.8 copy-start
  420.3 5.4 %copy-start.9 = (f32[1,128,6]{1,0,2:T(1,128)S(1)}, f32[1,128,6]{1,0,2:T(1,128)}, u32[]{:S(2)}) copy-start(f32[1,128,6]{1,0,2:T(1,128)} %param.20) | copy-start | bytes 9220
  420.3 51.8 %all-to-all-start.2 = ((bf16[16,50,2048]{2,1,0:T(8,128)(2,1)}), bf16[16,50,2048]{2,1,0:T(8,128)(2,1)}, u32[]{:S(2)}, u32[]{:S(2)}) async-start(bf16[16,50,2048]{2,1,0:T(8,128)(2,1)} %reshape.106), calls=%async_computation.2 | async-start | bytes 7340032 | tf_op jit(solution)/shard_map/all_to_all | solution.py:120
  486.2 6.7 %copy-start.1 = (bf16[128,2048]{1,0:T(8,128)(2,1)S(1)}, bf16[128,2048]{1,0:T(8,128)(2,1)}, u32[]{:S(2)}) copy-start(bf16[128,2048]{1,0:T(8,128)(2,1)} %copy-done) | copy-start | bytes 1572868
Sparse Core Ops, SparseCore 0:
  126.1 202.7 all-gather.2

commit v11 on v9

--- a/solution.py
+++ b/solution.py
@@ -51,6 +51,17 @@
         up_weight,
         down_weight,
     ):
+        tokens = queries.shape[1]
+        query_heads = queries[0].reshape(tokens, HEADS, HEAD_DIM)
+        key_heads = key_rows[0].reshape(tokens, HEADS, HEAD_DIM)
+        value_heads = value_rows[0].reshape(tokens, HEADS, HEAD_DIM)
+        local_state = jnp.einsum(
+            "thd,the->hde", key_heads, value_heads, preferred_element_type=jnp.float32
+        )
+        earlier = carried_in(local_state, seq, n_seq)
+        earlier, gate_weight, up_weight, down_weight = lax.optimization_barrier(
+            (earlier, gate_weight, up_weight, down_weight)
+        )
         slice_rows = gate_weight.shape[1]
         packed = jnp.concatenate(
             [gate_weight, up_weight, jnp.swapaxes(down_weight, 1, 2)], axis=1
@@ -61,14 +72,6 @@
         whole_up = packed[:, :, slice_rows : 2 * slice_rows]
         whole_down = packed[:, :, 2 * slice_rows :]
 
-        tokens = queries.shape[1]
-        query_heads = queries[0].reshape(tokens, HEADS, HEAD_DIM)
-        key_heads = key_rows[0].reshape(tokens, HEADS, HEAD_DIM)
-        value_heads = value_rows[0].reshape(tokens, HEADS, HEAD_DIM)
-        local_state = jnp.einsum(
-            "thd,the->hde", key_heads, value_heads, preferred_element_type=jnp.float32
-        )
-        earlier = carried_in(local_state, seq, n_seq)
         state_before = state_start[0] + earlier
         causal = (
             jnp.arange(tokens, dtype=jnp.int32)[:, None]

time: 503 us -> 479 us (0.952)
  blocking collectives: 228 us -> 85.8 us
  waiting for transfers between devices: 146 us -> 246 us
  starting transfers between devices: 22.6 us -> 39.7 us
    all_to_all x1, blocking collectives: 228 us -> 85.8 us  [shards(): arrived = lax.all_to_all(outgoing, group, 0, 0, tiled=True)]
    all_gather x1, waiting for transfers between devices: 0.02 us -> 89.7 us  [shards(): packed = lax.all_gather(packed, 'seq_hi', axis=0, tiled=False)]
    all_to_all x1, waiting for transfers between devices: 0.01 us -> 38.7 us  [shards(): packed = lax.all_to_all(packed, 'seq_lo', 0, 0, tiled=False)]
    ppermute x3, waiting for transfers between devices: 99.7 us -> 71.4 us  [carried_in(): lax.ppermute(total, axis, [(i, i + shift) for i in range(count - shift)])]
    all_to_all x1, starting transfers between devices: 5.07 us -> 25.3 us  [shards(): packed = lax.all_to_all(packed, 'seq_lo', 0, 0, tiled=False)]
  transfers between devices with their start and end apart: 6 -> 6, of which waited for: 4 -> 6; matrix products, arithmetic and copies ran while one was open for 8% -> 7% of each run, Pallas kernels for 0% -> 0%
where the time goes in v11:
time: 479 us; the launch traced here: 475 us
  waiting for transfers between devices  246 us (51%)
  blocking collectives  85.8 us (18%)
  local copies, waits for them, and re-layouts  49.7 us (10%)
  starting transfers between devices  39.7 us (8%)
  matrix products  22.5 us (5%)
  other arithmetic  17.6 us (4%)
  between operations  13.7 us (3%)
    all_gather x1, waiting for transfers between devices, shards(): packed = lax.all_gather(packed, 'seq_hi', axis=0, tiled=False)  89.7 us
    all_to_all x1, blocking collectives, shards(): arrived = lax.all_to_all(outgoing, group, 0, 0, tiled=True)  85.8 us
    ppermute x3, waiting for transfers between devices, carried_in(): lax.ppermute(total, axis, [(i, i + shift) for i in range(count - shift)])  71.4 us
    all_to_all x1, waiting for transfers between devices, shards(): returned = lax.all_to_all(expert_rows, group, 0, 0, tiled=True)  46.3 us
    all_to_all x1, waiting for transfers between devices, shards(): packed = lax.all_to_all(packed, 'seq_lo', 0, 0, tiled=False)  38.7 us
    all_to_all x1, starting transfers between devices, shards(): packed = lax.all_to_all(packed, 'seq_lo', 0, 0, tiled=False)  25.3 us
    dot_general x1, matrix products, shards(): jnp.einsum('rh,abdh->rabd', hidden, whole_down, preferred_element_type=jn...  11.3 us
    gather x2, local copies, waits for them, and re-layouts, shards(): ffn_in[source]  9.84 us
  transfers between devices with their start and end apart: 6, of which 6 were waited for; matrix products, arithmetic and copies ran while one was open for 7% of the time, Pallas kernels for 0%

profile of v11, /device:TPU:16, one launch (start us, length us, event | category | flops | bytes accessed | tf_op | source)
XLA Modules:
  0.0 475.0 jit_solution(5315081367141907928)
XLA Ops:
  6.5 1.3 copy.54
  7.8 1.1 copy.56
  9.0 0.5 fusion.37
  9.5 3.4 collective-permute-start
  12.9 24.3 %collective-permute-done = f32[16,128,128]{2,1,0:T(8,128)S(1)} collective-permute-done((f32[16,128,128]{2,1,0:T(8,128)S(1)}, f32[16,128,128]{2,1,0:T(8,128)S(1)}, u32[]{:S(2)}, u32[]{:S(2)}) %collective-permute-start) | collective-permute-done | bytes 1048608 | tf_op jit(solution)/shard_map/ppermute | solution.py:18
  37.2 0.2 add.81
  37.4 3.7 collective-permute-start.1
  41.2 22.4 %collective-permute-done.1 = f32[16,128,128]{2,1,0:T(8,128)S(1)} collective-permute-done((f32[16,128,128]{2,1,0:T(8,128)S(1)}, f32[16,128,128]{2,1,0:T(8,128)S(1)}, u32[]{:S(2)}, u32[]{:S(2)}) %collective-permute-start.1) | collective-permute-done | bytes 1048608 | tf_op jit(solution)/shard_map/ppermute | solution.py:18
  63.6 0.1 add.82
  63.7 1.3 collective-permute-start.2
  65.0 24.7 %collective-permute-done.2 = f32[16,128,128]{2,1,0:T(8,128)S(1)} collective-permute-done((f32[16,128,128]{2,1,0:T(8,128)S(1)}, f32[16,128,128]{2,1,0:T(8,128)S(1)}, u32[]{:S(2)}, u32[]{:S(2)}) %collective-permute-start.2) | collective-permute-done | bytes 1048608 | tf_op jit(solution)/shard_map/ppermute | solution.py:18
  89.7 1.1 add_subtract_fusion
  90.8 2.1 pad_maximum_fusion
  93.0 25.3 %all-to-all-start.1 = ((bf16[4,768,704]{1,2,0:T(8,128)(2,1)}), bf16[4,768,704]{1,2,0:T(8,128)(2,1)}, u32[]{:S(2)}, u32[]{:S(2)}) async-start(bf16[4,768,704]{1,2,0:T(8,128)(2,1)} %pad_maximum_fusion), calls=%async_computation.1 | async-start | bytes 8650752 | tf_op jit(solution)/shard_map/all_to_all | solution.py:69
  118.4 0.1 eq.29
  118.5 0.1 eq.25
  118.8 1.7 reduce-window.6
  120.5 0.3 slice_reduce_fusion
  120.8 0.1 copy.42
  120.9 0.1 mul.79
  121.2 3.4 scatter_custom_fusion.1
  124.6 3.4 scatter_custom_fusion
  128.1 2.5 convolution_bitcast_fusion.1
  130.7 38.7 %all-to-all-done.1 = bf16[4,768,704]{1,2,0:T(8,128)(2,1)} async-done(((bf16[4,768,704]{1,2,0:T(8,128)(2,1)}), bf16[4,768,704]{1,2,0:T(8,128)(2,1)}, u32[]{:S(2)}, u32[]{:S(2)}) %all-to-all-start.1) | async-done | bytes 4325408 | tf_op jit(solution)/shard_map/all_to_all | solution.py:69
  169.4 1.9 multiply_reduce_fusion.1
  171.3 1.3 broadcast_multiply_fusion
  172.6 0.3 copy.40
  173.0 0.1 fusion.33
  173.2 0.2 fusion.29
  173.4 0.6 copy-done
  173.9 0.2 fusion.31
  174.1 4.8 %gather_fusion = bf16[800,2048]{1,0:T(8,128)(2,1)} fusion(bf16[128,2048]{1,0:T(8,128)(2,1)S(1)} %fusion.31, s32[1024]{0:T(1024)S(1)} %pad_clamp_fusion.1), kind=kCustom, calls=%fused_computation | custom fusion | bytes 6556800 | tf_op jit(solution)/shard_map/gather | solution.py:107
  179.0 5.0 %gather.9 = bf16[16,50,2048]{2,1,0:T(8,128)(2,1)} reshape(bf16[800,2048]{1,0:T(8,128)(2,1)} %gather_fusion) | data formatting | bytes 6553600 | tf_op jit(solution)/shard_map/gather | solution.py:107
  184.0 2.7 broadcast_select_fusion
  186.7 85.8 %all_to_all.15 = bf16[16,50,2048]{2,1,0:T(8,128)(2,1)} all-to-all(bf16[16,50,2048]{2,1,0:T(8,128)(2,1)S(1)} %broadcast_select_fusion), channel_id=1, replica_groups=mesh['seq_hi'=2,'seq_lo'=4,'ep'=4] {'ep','seq_lo'}, dimensions={0} | all-to-all | bytes 6553600 | tf_op jit(solution)/shard_map/all_to_all | solution.py:109
  272.5 6.5 %reshape.105 = bf16[800,2,4,256]{3,2,1,0:T(4,128)(2,1)S(1)} reshape(bf16[16,50,2048]{2,1,0:T(8,128)(2,1)} %all_to_all.15) | data formatting | bytes 6553600 | tf_op jit(solution)/shard_map/reshape | solution.py:110
  279.1 89.7 %all-gather.3.cloned.1.call-done = bf16[8,768,704]{1,2,0:T(8,128)(2,1)} async-done(((bf16[4,768,704]{1,2,0:T(8,128)(2,1)}), bf16[8,768,704]{1,2,0:T(8,128)(2,1)}) %all-gather.3.cloned.1.call-update) | async-done | bytes 8650768 | tf_op jit(solution)/shard_map/all_gather | solution.py:70
  368.7 6.3 %fusion.2 = f32[800,704,1,1]{1,0,3,2:T(8,128)} fusion(bf16[800,2,4,256]{3,2,1,0:T(4,128)(2,1)S(1)} %reshape.105, bf16[2,4,768,704]{2,3,1,0:T(8,128)(2,1)} %bitcast.88), kind=kOutput, calls=%fused_computation.9 | convolution fusion | flops 2306867200 | bytes 8413184 | tf_op jit(solution)/shard_map/rabd,abdh->rh/dot_general | solution.py:111
  375.0 11.3 %fusion.11 = bf16[800,2,4,256]{3,0,2,1:T(8,128)(2,1)} fusion(bf16[2,4,768,704]{2,3,1,0:T(8,128)(2,1)} %bitcast.89, bf16[800,2,4,256]{3,2,1,0:T(4,128)(2,1)S(1)} %reshape.105, f32[800,704,1,1]{1,0,3,2:T(8,128)} %fusion.2), kind=kOutput, calls=%fused_computation.21 | convolution fusion | flops 4618188800 | bytes 14778368 | tf_op jit(solution)/shard_map/rh,abdh->rabd/dot_general | solution.py:118
  386.3 4.5 copy.48
  390.7 3.4 reshape.106
  394.2 6.0 %all-to-all-start.2 = ((bf16[16,50,2048]{2,1,0:T(8,128)(2,1)}), bf16[16,50,2048]{2,1,0:T(8,128)(2,1)}, u32[]{:S(2)}, u32[]{:S(2)}) async-start(bf16[16,50,2048]{2,1,0:T(8,128)(2,1)} %reshape.106), calls=%async_computation.2 | async-start | bytes 7340032 | tf_op jit(solution)/shard_map/all_to_all | solution.py:122
  400.2 46.3 %all-to-all-done.2 = bf16[16,50,2048]{2,1,0:T(8,128)(2,1)} async-done(((bf16[16,50,2048]{2,1,0:T(8,128)(2,1)}), bf16[16,50,2048]{2,1,0:T(8,128)(2,1)}, u32[]{:S(2)}, u32[]{:S(2)}) %all-to-all-start.2) | async-done | bytes 3276832 | tf_op jit(solution)/shard_map/all_to_all | solution.py:122
  446.5 3.2 reshape.107
  449.7 4.3 gather_fusion.1
  454.0 6.6 %reshape.109 = f32[128,6,2048]{2,1,0:T(8,128)} reshape(bf16[768,2048]{1,0:T(8,128)(2,1)} %gather_fusion.1) | data formatting | bytes 9437184 | tf_op jit(solution)/shard_map/convert_element_type | solution.py:124
  460.6 6.7 %multiply_reduce_fusion = f32[128,2048]{1,0:T(8,128)S(1)} fusion(f32[128,6,2048]{2,1,0:T(8,128)} %reshape.109, f32[128,6]{1,0:T(8,128)S(1)} %bitcast.86), kind=kLoop, calls=%fused_computation.4 | loop fusion | flops 2883584 | bytes 7343104 | tf_op jit(solution)/shard_map/reduce_sum | solution.py:124
  467.3 0.9 fusion.34
  (40 shorter events, 0.7 us)
Async XLA Ops:
  9.5 27.7 %collective-permute-start = (f32[16,128,128]{2,1,0:T(8,128)S(1)}, f32[16,128,128]{2,1,0:T(8,128)S(1)}, u32[]{:S(2)}, u32[]{:S(2)}) collective-permute-start(f32[16,128,128]{2,1,0:T(8,128)S(1)} %fusion.37), channel_id=1, source_target_pairs={{0,4},{4,8},{8,12},{12,16},{16,20},{20,24},{24,28},{1,5},{5,9},{9,... | collective-permute-start | bytes 3145736 | tf_op jit(solution)/shard_map/ppermute | solution.py:18
  37.4 53.5 %copy-start.2 = (bf16[4,704,256]{2,1,0:T(8,128)(2,1)S(1)}, bf16[4,704,256]{2,1,0:T(8,128)(2,1)}, u32[]{:S(2)}) copy-start(bf16[4,704,256]{2,1,0:T(8,128)(2,1)} %param.23) | copy-start | bytes 4325380
  37.4 53.5 %copy-start.3 = (bf16[4,256,704]{1,2,0:T(8,128)(2,1)S(1)}, bf16[4,256,704]{1,2,0:T(8,128)(2,1)}, u32[]{:S(2)}) copy-start(bf16[4,256,704]{1,2,0:T(8,128)(2,1)} %param.22) | copy-start | bytes 4325380
  37.4 53.4 %copy-start.4 = (bf16[4,256,704]{1,2,0:T(8,128)(2,1)S(1)}, bf16[4,256,704]{1,2,0:T(8,128)(2,1)}, u32[]{:S(2)}) copy-start(bf16[4,256,704]{1,2,0:T(8,128)(2,1)} %param.21) | copy-start | bytes 4325380
  37.4 26.2 %collective-permute-start.1 = (f32[16,128,128]{2,1,0:T(8,128)S(1)}, f32[16,128,128]{2,1,0:T(8,128)S(1)}, u32[]{:S(2)}, u32[]{:S(2)}) collective-permute-start(f32[16,128,128]{2,1,0:T(8,128)S(1)} %add.81), channel_id=1, source_target_pairs={{0,8},{4,12},{8,16},{12,20},{16,24},{20,28},{1,9},{5,13},{9,17},{1... | collective-permute-start | bytes 3145736 | tf_op jit(solution)/shard_map/ppermute | solution.py:18
  63.7 26.0 %collective-permute-start.2 = (f32[16,128,128]{2,1,0:T(8,128)S(1)}, f32[16,128,128]{2,1,0:T(8,128)S(1)}, u32[]{:S(2)}, u32[]{:S(2)}) collective-permute-start(f32[16,128,128]{2,1,0:T(8,128)S(1)} %add.82), channel_id=1, source_target_pairs={{0,16},{4,20},{8,24},{12,28},{1,17},{5,21},{9,25},{13,29},{2,18},{... | collective-permute-start | bytes 3145736 | tf_op jit(solution)/shard_map/ppermute | solution.py:18
  93.0 25.3 %copy-start.7 = (s32[1,128,6]{1,0,2:T(1,128)S(1)}, s32[1,128,6]{1,0,2:T(1,128)}, u32[]{:S(2)}) copy-start(s32[1,128,6]{1,0,2:T(1,128)} %param.19) | copy-start | bytes 9220
  93.0 25.7 %copy-start.5 = (bf16[1,128,2048]{2,1,0:T(8,128)(2,1)S(1)}, bf16[1,128,2048]{2,1,0:T(8,128)(2,1)}, u32[]{:S(2)}) copy-start(bf16[1,128,2048]{2,1,0:T(8,128)(2,1)} %param.12) | copy-start | bytes 1572868
  93.0 76.4 %all-to-all-start.1 = ((bf16[4,768,704]{1,2,0:T(8,128)(2,1)}), bf16[4,768,704]{1,2,0:T(8,128)(2,1)}, u32[]{:S(2)}, u32[]{:S(2)}) async-start(bf16[4,768,704]{1,2,0:T(8,128)(2,1)} %pad_maximum_fusion), calls=%async_computation.1 | async-start | bytes 8650752 | tf_op jit(solution)/shard_map/all_to_all | solution.py:69
  118.3 250.5 %all-gather.3.cloned.1.call-start = ((), (), s32[]{:S(2)}) async-start(), calls=%async_computation.3 | async-start | bytes 12976128 | tf_op jit(solution)/shard_map/all_gather | solution.py:70
  169.4 3.6 copy-start.6
  169.4 3.6 copy-start.8
  171.3 2.6 copy-start.9
  173.1 0.8 copy-start
  394.2 6.0 %copy-start.10 = (f32[1,128,6]{1,0,2:T(1,128)S(1)}, f32[1,128,6]{1,0,2:T(1,128)}, u32[]{:S(2)}) copy-start(f32[1,128,6]{1,0,2:T(1,128)} %param.20) | copy-start | bytes 9220
  394.2 52.4 %all-to-all-start.2 = ((bf16[16,50,2048]{2,1,0:T(8,128)(2,1)}), bf16[16,50,2048]{2,1,0:T(8,128)(2,1)}, u32[]{:S(2)}, u32[]{:S(2)}) async-start(bf16[16,50,2048]{2,1,0:T(8,128)(2,1)} %reshape.106), calls=%async_computation.2 | async-start | bytes 7340032 | tf_op jit(solution)/shard_map/all_to_all | solution.py:122
  460.6 6.7 %copy-start.1 = (bf16[128,2048]{1,0:T(8,128)(2,1)S(1)}, bf16[128,2048]{1,0:T(8,128)(2,1)}, u32[]{:S(2)}) copy-start(bf16[128,2048]{1,0:T(8,128)(2,1)} %copy-done) | copy-start | bytes 1572868
Sparse Core Ops, SparseCore 0:
  169.5 199.1 all-gather.2

commit v12 on v9

--- a/solution.py
+++ b/solution.py
@@ -55,11 +55,7 @@
         packed = jnp.concatenate(
             [gate_weight, up_weight, jnp.swapaxes(down_weight, 1, 2)], axis=1
         )
-        packed = lax.all_to_all(packed, "seq_lo", 0, 0, tiled=False)
-        packed = lax.all_gather(packed, "seq_hi", axis=0, tiled=False)
-        whole_gate = packed[:, :, :slice_rows]
-        whole_up = packed[:, :, slice_rows : 2 * slice_rows]
-        whole_down = packed[:, :, 2 * slice_rows :]
+        across = lax.all_gather(packed, "seq_hi", axis=0, tiled=False)
 
         tokens = queries.shape[1]
         query_heads = queries[0].reshape(tokens, HEADS, HEAD_DIM)
@@ -104,6 +100,11 @@
         outgoing = jnp.where(filled[:, None], ffn_in[source], jnp.zeros((), jnp.bfloat16))
         outgoing = outgoing.reshape(EXPERTS, CAP, D)
         arrived = lax.all_to_all(outgoing, group, 0, 0, tiled=True)
+        across, arrived = lax.optimization_barrier((across, arrived))
+        packed = lax.all_to_all(across, "seq_lo", 1, 1, tiled=False)
+        whole_gate = packed[:, :, :slice_rows]
+        whole_up = packed[:, :, slice_rows : 2 * slice_rows]
+        whole_down = packed[:, :, 2 * slice_rows :]
         arrived = arrived.reshape(EXPERTS * CAP, *whole_gate.shape[:3])
         gate_sum = jnp.einsum(
             "rabd,abdh->rh", arrived, whole_gate, preferred_element_type=jnp.float32

time: 503 us -> 552 us (1.097)
  blocking collectives: 228 us -> 0 us
  waiting for transfers between devices: 146 us -> 365 us
  starting transfers between devices: 22.6 us -> 66.6 us
  local copies, waits for them, and re-layouts: 48 us -> 64.6 us
    all_to_all x1 -> x0, blocking collectives: 228 us -> none  [shards(): arrived = lax.all_to_all(outgoing, group, 0, 0, tiled=True)]
    all_to_all x1 -> x2, waiting for transfers between devices: 0.01 us -> 167 us  [the longest x1 89.9 us: shards(): packed = lax.all_to_all(across, 'seq_lo', 1, 1, tiled=False)]
    ppermute x3, waiting for transfers between devices: 99.7 us -> 152 us  [carried_in(): lax.ppermute(total, axis, [(i, i + shift) for i in range(count - shift)])]
    all_to_all x1 -> x2, starting transfers between devices: 5.07 us -> 53.5 us  [the longest x1 47.6 us: shards(): arrived = lax.all_to_all(outgoing, group, 0, 0, tiled=True)]
    optimization_barrier x0 -> x1, local copies, waits for them, and re-layouts: none -> 7.32 us  [shards(): across, arrived = lax.optimization_barrier((across, arrived))]
    slice x1 -> x2, local copies, waits for them, and re-layouts: 0.25 us -> 5.81 us  [the longest x1 5.56 us: shards(): whole_gate = packed[:, :, :slice_rows]]
  transfers between devices with their start and end apart: 6 -> 7, of which waited for: 4 -> 6; matrix products, arithmetic and copies ran while one was open for 8% -> 8% of each run, Pallas kernels for 0% -> 0%
where the time goes in v12:
time: 552 us; the launch traced here: 551 us
  waiting for transfers between devices  365 us (66%)
  starting transfers between devices  66.6 us (12%)
  local copies, waits for them, and re-layouts  64.6 us (12%)
  matrix products  21.3 us (4%)
  other arithmetic  18.9 us (3%)
  between operations  13.8 us (2%)
    ppermute x3, waiting for transfers between devices, carried_in(): lax.ppermute(total, axis, [(i, i + shift) for i in range(count - shift)])  152 us
    all_to_all x1, waiting for transfers between devices, shards(): packed = lax.all_to_all(across, 'seq_lo', 1, 1, tiled=False)  89.9 us
    all_to_all x1, waiting for transfers between devices, shards(): arrived = lax.all_to_all(outgoing, group, 0, 0, tiled=True)  77.3 us
    all_to_all x1, starting transfers between devices, shards(): arrived = lax.all_to_all(outgoing, group, 0, 0, tiled=True)  47.6 us
    all_to_all x1, waiting for transfers between devices, shards(): returned = lax.all_to_all(expert_rows, group, 0, 0, tiled=True)  46.2 us
    dot_general x1, matrix products, shards(): jnp.einsum('rh,abdh->rabd', hidden, whole_down, preferred_element_type=jn...  11.2 us
  transfers between devices with their start and end apart: 7, of which 6 were waited for; matrix products, arithmetic and copies ran while one was open for 8% of the time, Pallas kernels for 0%

profile of v12, /device:TPU:16, one launch (start us, length us, event | category | flops | bytes accessed | tf_op | source)
XLA Modules:
  0.0 550.5 jit_solution(3312125212321383432)
XLA Ops:
  6.5 1.1 copy.63
  7.7 1.3 copy.61
  9.0 0.5 fusion.39
  9.6 3.5 collective-permute-start
  13.1 24.3 %collective-permute-done = f32[16,128,128]{2,1,0:T(8,128)S(1)} collective-permute-done((f32[16,128,128]{2,1,0:T(8,128)S(1)}, f32[16,128,128]{2,1,0:T(8,128)S(1)}, u32[]{:S(2)}, u32[]{:S(2)}) %collective-permute-start) | collective-permute-done | bytes 1048608 | tf_op jit(solution)/shard_map/ppermute | solution.py:18
  37.5 3.5 collective-permute-start.1
  41.0 2.2 pad_maximum_fusion
  43.2 0.7 copy-done.6
  44.0 0.1 eq.29
  44.4 0.1 mul.79
  44.6 1.7 reduce-window.6
  46.3 0.3 slice_reduce_fusion
  46.6 117.6 %collective-permute-done.1 = f32[16,128,128]{2,1,0:T(8,128)} collective-permute-done((f32[16,128,128]{2,1,0:T(8,128)S(1)}, f32[16,128,128]{2,1,0:T(8,128)}, u32[]{:S(2)}, u32[]{:S(2)}) %collective-permute-start.1) | collective-permute-done | bytes 1048608 | tf_op jit(solution)/shard_map/ppermute | solution.py:18
  164.2 2.3 add.82
  166.5 1.3 collective-permute-start.2
  167.9 3.4 scatter_custom_fusion.1
  171.3 3.4 scatter_custom_fusion
  174.8 1.1 copy.64
  176.0 1.9 convolution_bitcast_fusion
  177.9 10.1 %collective-permute-done.2 = f32[16,128,128]{2,1,0:T(8,128)} collective-permute-done((f32[16,128,128]{2,1,0:T(8,128)}, f32[16,128,128]{2,1,0:T(8,128)}, u32[]{:S(2)}, u32[]{:S(2)}) %collective-permute-start.2) | collective-permute-done | bytes 1048608 | tf_op jit(solution)/shard_map/ppermute | solution.py:18
  188.0 3.3 multiply_reduce_fusion.1
  191.4 0.3 copy.40
  191.8 0.6 copy-done.5
  192.3 0.1 fusion.29
  192.5 0.2 fusion.25
  192.7 0.6 copy-done
  193.3 0.2 fusion.27
  193.5 4.8 gather_fusion
  198.3 4.7 gather.9
  203.1 4.1 broadcast_select_fusion
  207.2 47.6 %all-to-all-start = ((bf16[16,50,2048]{2,1,0:T(8,128)(2,1)}), bf16[16,50,2048]{2,1,0:T(8,128)(2,1)}, u32[]{:S(2)}, u32[]{:S(2)}) async-start(bf16[16,50,2048]{2,1,0:T(8,128)(2,1)} %broadcast_select_fusion), calls=%async_computation | async-start | bytes 7340032 | tf_op jit(solution)/shard_map/all_to_all | solution.py:102
  254.9 77.3 %all-to-all-done = bf16[16,50,2048]{2,1,0:T(8,128)(2,1)} async-done(((bf16[16,50,2048]{2,1,0:T(8,128)(2,1)}), bf16[16,50,2048]{2,1,0:T(8,128)(2,1)}, u32[]{:S(2)}, u32[]{:S(2)}) %all-to-all-start) | async-done | bytes 3276832 | tf_op jit(solution)/shard_map/all_to_all | solution.py:102
  332.2 7.3 %copy.46 = bf16[2,4,768,704]{2,3,0,1:T(8,128)(2,1)} copy(bf16[2,4,768,704]{2,3,1,0:T(8,128)(2,1)} %bitcast.80) | data formatting | bytes 17301504 | tf_op jit(solution)/shard_map/optimization_barrier | solution.py:103
  339.5 5.9 %all-to-all-start.1 = ((bf16[2,4,768,704]{2,3,0,1:T(8,128)(2,1)}), bf16[2,4,768,704]{2,3,0,1:T(8,128)(2,1)}, u32[]{:S(2)}, u32[]{:S(2)}) async-start(bf16[2,4,768,704]{2,3,0,1:T(8,128)(2,1)} %copy.46), calls=%async_computation.1 | async-start | bytes 17301504 | tf_op jit(solution)/shard_map/all_to_all | solution.py:104
  345.4 6.5 %reshape.105 = bf16[800,2,4,256]{3,2,1,0:T(4,128)(2,1)S(1)} reshape(bf16[16,50,2048]{2,1,0:T(8,128)(2,1)} %all-to-all-done) | data formatting | bytes 6553600 | tf_op jit(solution)/shard_map/reshape | solution.py:108
  351.9 89.9 %all-to-all-done.1 = bf16[2,4,768,704]{2,3,0,1:T(8,128)(2,1)} async-done(((bf16[2,4,768,704]{2,3,0,1:T(8,128)(2,1)}), bf16[2,4,768,704]{2,3,0,1:T(8,128)(2,1)}, u32[]{:S(2)}, u32[]{:S(2)}) %all-to-all-start.1) | async-done | bytes 8650784 | tf_op jit(solution)/shard_map/all_to_all | solution.py:104
  441.8 5.6 %fusion.59 = (bf16[2,4,256,704]{2,3,0,1:T(8,128)(2,1)S(1)}, bf16[2,4,256,704]{2,3,0,1:T(8,128)(2,1)}, bf16[2,4,256,704]{2,3,0,1:T(8,128)(2,1)}) fusion(bf16[2,4,768,704]{2,3,0,1:T(8,128)(2,1)} %all-to-all-done.1), kind=kLoop, calls=%fused_computation.80 | loop fusion | bytes 17301504 | tf_op jit(solution)/shard_map/slice | solution.py:105
  447.4 4.5 fusion.2
  451.8 11.2 %fusion.11 = bf16[800,2,4,256]{3,0,2,1:T(8,128)(2,1)} fusion(bf16[2,4,256,704]{2,3,0,1:T(8,128)(2,1)} %get-tuple-element.11, bf16[2,4,256,704]{2,3,0,1:T(8,128)(2,1)} %get-tuple-element.10, bf16[800,2,4,256]{3,2,1,0:T(4,128)(2,1)S(1)} %reshape.105, f32[800,704,1,1]{1,0,3,2:T(8,128)} %fusion.2), kind=kOutput, calls=%fused_computation.21 | convolution fusion | flops 4618188800 | bytes 14573568 | tf_op jit(solution)/shard_map/rh,abdh->rabd/dot_general | solution.py:116
  463.0 4.5 copy.52
  467.5 3.4 reshape.106
  470.9 4.8 all-to-all-start.2
  475.9 46.2 %all-to-all-done.2 = bf16[16,50,2048]{2,1,0:T(8,128)(2,1)} async-done(((bf16[16,50,2048]{2,1,0:T(8,128)(2,1)}), bf16[16,50,2048]{2,1,0:T(8,128)(2,1)}, u32[]{:S(2)}, u32[]{:S(2)}) %all-to-all-start.2) | async-done | bytes 3276832 | tf_op jit(solution)/shard_map/all_to_all | solution.py:120
  522.0 3.2 reshape.107
  525.2 4.3 gather_fusion.1
  529.6 6.6 %reshape.109 = f32[128,6,2048]{2,1,0:T(8,128)} reshape(bf16[768,2048]{1,0:T(8,128)(2,1)} %gather_fusion.1) | data formatting | bytes 9437184 | tf_op jit(solution)/shard_map/convert_element_type | solution.py:122
  536.1 6.7 %multiply_reduce_fusion = f32[128,2048]{1,0:T(8,128)S(1)} fusion(f32[128,6,2048]{2,1,0:T(8,128)} %reshape.109, f32[128,6]{1,0:T(8,128)S(1)} %bitcast.91), kind=kLoop, calls=%fused_computation.4 | loop fusion | flops 2883584 | bytes 7343104 | tf_op jit(solution)/shard_map/reduce_sum | solution.py:122
  542.8 0.9 fusion.36
  (40 shorter events, 1.1 us)
Async XLA Ops:
  6.5 248.3 %all-gather.3.cloned.1.call-start = ((), (), s32[]{:S(2)}) async-start(), calls=%async_computation.3 | async-start | bytes 12976128 | tf_op jit(solution)/shard_map/all_gather | solution.py:58
  9.0 32.0 %copy-start.2 = (bf16[4,704,256]{2,1,0:T(8,128)(2,1)S(1)}, bf16[4,704,256]{2,1,0:T(8,128)(2,1)}, u32[]{:S(2)}) copy-start(bf16[4,704,256]{2,1,0:T(8,128)(2,1)} %param.23) | copy-start | bytes 4325380
  9.0 32.0 %copy-start.3 = (bf16[4,256,704]{1,2,0:T(8,128)(2,1)S(1)}, bf16[4,256,704]{1,2,0:T(8,128)(2,1)}, u32[]{:S(2)}) copy-start(bf16[4,256,704]{1,2,0:T(8,128)(2,1)} %param.22) | copy-start | bytes 4325380
  9.0 32.0 %copy-start.4 = (bf16[4,256,704]{1,2,0:T(8,128)(2,1)S(1)}, bf16[4,256,704]{1,2,0:T(8,128)(2,1)}, u32[]{:S(2)}) copy-start(bf16[4,256,704]{1,2,0:T(8,128)(2,1)} %param.21) | copy-start | bytes 4325380
  9.6 27.8 %collective-permute-start = (f32[16,128,128]{2,1,0:T(8,128)S(1)}, f32[16,128,128]{2,1,0:T(8,128)S(1)}, u32[]{:S(2)}, u32[]{:S(2)}) collective-permute-start(f32[16,128,128]{2,1,0:T(8,128)S(1)} %fusion.39), channel_id=1, source_target_pairs={{0,4},{4,8},{8,12},{12,16},{16,20},{20,24},{24,28},{1,5},{5,9},{9,... | collective-permute-start | bytes 3145736 | tf_op jit(solution)/shard_map/ppermute | solution.py:18
  37.5 126.7 %collective-permute-start.1 = (f32[16,128,128]{2,1,0:T(8,128)S(1)}, f32[16,128,128]{2,1,0:T(8,128)}, u32[]{:S(2)}, u32[]{:S(2)}) collective-permute-start(f32[16,128,128]{2,1,0:T(8,128)S(1)} %add.81), channel_id=1, source_target_pairs={{0,8},{4,12},{8,16},{12,20},{16,24},{20,28},{1,9},{5,13},{9,17},{1... | collective-permute-start | bytes 3145736 | tf_op jit(solution)/shard_map/ppermute | solution.py:18
  43.2 0.7 copy-start.6
  166.5 21.5 %collective-permute-start.2 = (f32[16,128,128]{2,1,0:T(8,128)}, f32[16,128,128]{2,1,0:T(8,128)}, u32[]{:S(2)}, u32[]{:S(2)}) collective-permute-start(f32[16,128,128]{2,1,0:T(8,128)} %add.82), channel_id=1, source_target_pairs={{0,16},{4,20},{8,24},{12,28},{1,17},{5,21},{9,25},{13,29},{2,18},{... | collective-permute-start | bytes 3145736 | tf_op jit(solution)/shard_map/ppermute | solution.py:18
  191.3 1.0 copy-start.5
  191.3 1.0 copy-start.7
  191.3 1.9 copy-start.8
  192.5 0.8 copy-start
  207.2 125.0 %all-to-all-start = ((bf16[16,50,2048]{2,1,0:T(8,128)(2,1)}), bf16[16,50,2048]{2,1,0:T(8,128)(2,1)}, u32[]{:S(2)}, u32[]{:S(2)}) async-start(bf16[16,50,2048]{2,1,0:T(8,128)(2,1)} %broadcast_select_fusion), calls=%async_computation | async-start | bytes 7340032 | tf_op jit(solution)/shard_map/all_to_all | solution.py:102
  339.5 102.3 %all-to-all-start.1 = ((bf16[2,4,768,704]{2,3,0,1:T(8,128)(2,1)}), bf16[2,4,768,704]{2,3,0,1:T(8,128)(2,1)}, u32[]{:S(2)}, u32[]{:S(2)}) async-start(bf16[2,4,768,704]{2,3,0,1:T(8,128)(2,1)} %copy.46), calls=%async_computation.1 | async-start | bytes 17301504 | tf_op jit(solution)/shard_map/all_to_all | solution.py:104
  470.9 4.9 copy-start.9
  470.9 51.1 %all-to-all-start.2 = ((bf16[16,50,2048]{2,1,0:T(8,128)(2,1)}), bf16[16,50,2048]{2,1,0:T(8,128)(2,1)}, u32[]{:S(2)}, u32[]{:S(2)}) async-start(bf16[16,50,2048]{2,1,0:T(8,128)(2,1)} %reshape.106), calls=%async_computation.2 | async-start | bytes 7340032 | tf_op jit(solution)/shard_map/all_to_all | solution.py:120
  536.1 6.7 %copy-start.1 = (bf16[128,2048]{1,0:T(8,128)(2,1)S(1)}, bf16[128,2048]{1,0:T(8,128)(2,1)}, u32[]{:S(2)}) copy-start(bf16[128,2048]{1,0:T(8,128)(2,1)} %copy-done) | copy-start | bytes 1572868
Sparse Core Ops, SparseCore 0:
  43.4 199.2 all-gather.2

commit v13 on v6

--- a/solution.py
+++ b/solution.py
@@ -51,6 +51,17 @@
         up_weight,
         down_weight,
     ):
+        tokens = queries.shape[1]
+        query_heads = queries[0].reshape(tokens, HEADS, HEAD_DIM)
+        key_heads = key_rows[0].reshape(tokens, HEADS, HEAD_DIM)
+        value_heads = value_rows[0].reshape(tokens, HEADS, HEAD_DIM)
+        local_state = jnp.einsum(
+            "thd,the->hde", key_heads, value_heads, preferred_element_type=jnp.float32
+        )
+        earlier = carried_in(local_state, seq, n_seq)
+        earlier, gate_weight, up_weight, down_weight = lax.optimization_barrier(
+            (earlier, gate_weight, up_weight, down_weight)
+        )
         def collect(weight):
             mine = lax.all_to_all(weight, "seq_lo", 0, 0, tiled=False)
             return lax.all_gather(mine, "seq_hi", axis=0, tiled=False)
@@ -61,14 +72,6 @@
         whole_gate = whole_gate.reshape(-1, whole_gate.shape[-1])
         whole_up = whole_up.reshape(-1, whole_up.shape[-1])
 
-        tokens = queries.shape[1]
-        query_heads = queries[0].reshape(tokens, HEADS, HEAD_DIM)
-        key_heads = key_rows[0].reshape(tokens, HEADS, HEAD_DIM)
-        value_heads = value_rows[0].reshape(tokens, HEADS, HEAD_DIM)
-        local_state = jnp.einsum(
-            "thd,the->hde", key_heads, value_heads, preferred_element_type=jnp.float32
-        )
-        earlier = carried_in(local_state, seq, n_seq)
         state_before = state_start[0] + earlier
         causal = (
             jnp.arange(tokens, dtype=jnp.int32)[:, None]

time: 467 us -> 491 us (1.051)
  waiting for transfers between devices: 253 us -> 319 us
  starting transfers between devices: 87.5 us -> 51.9 us
    all_gather x3, waiting for transfers between devices: 131 us -> 180 us  [collect(): return lax.all_gather(mine, 'seq_hi', axis=0, tiled=False)]
    all_to_all x3, starting transfers between devices: 63.6 us -> 32.2 us  [collect(): mine = lax.all_to_all(weight, 'seq_lo', 0, 0, tiled=False)]
    all_to_all x3, waiting for transfers between devices: 0.01 us -> 19.8 us  [collect(): mine = lax.all_to_all(weight, 'seq_lo', 0, 0, tiled=False)]
  transfers between devices with their start and end apart: 11 -> 11, of which waited for: 6 -> 9; matrix products, arithmetic and copies ran while one was open for 14% -> 11% of each run, Pallas kernels for 0% -> 0%
where the time goes in v13:
time: 491 us; the launch traced here: 486 us
  waiting for transfers between devices  319 us (65%)
  local copies, waits for them, and re-layouts  58.2 us (12%)
  starting transfers between devices  51.9 us (11%)
  matrix products  24.6 us (5%)
  other arithmetic  19.3 us (4%)
  between operations  13.5 us (3%)
    all_gather x3, waiting for transfers between devices, collect(): return lax.all_gather(mine, 'seq_hi', axis=0, tiled=False)  180 us
    ppermute x3, waiting for transfers between devices, carried_in(): lax.ppermute(total, axis, [(i, i + shift) for i in range(count - shift)])  71.4 us
    all_to_all x1, waiting for transfers between devices, shards(): returned = lax.all_to_all(expert_rows, group, 0, 0, tiled=True)  46.3 us
    all_to_all x3, starting transfers between devices, collect(): mine = lax.all_to_all(weight, 'seq_lo', 0, 0, tiled=False)  32.2 us
    all_to_all x3, waiting for transfers between devices, collect(): mine = lax.all_to_all(weight, 'seq_lo', 0, 0, tiled=False)  19.8 us
    dot_general x1, matrix products, shards(): jnp.einsum('rh,abhd->rabd', hidden, whole_down, preferred_element_type=jn...  11.1 us
  transfers between devices with their start and end apart: 11, of which 9 were waited for; matrix products, arithmetic and copies ran while one was open for 11% of the time, Pallas kernels for 0%

profile of v13, /device:TPU:16, one launch (start us, length us, event | category | flops | bytes accessed | tf_op | source)
XLA Modules:
  0.0 486.3 jit_solution(9097645365593717049)
XLA Ops:
  6.5 1.3 copy.53
  7.9 1.3 copy.57
  9.2 0.8 copy-done.6
  10.0 0.5 fusion.11
  10.6 3.4 collective-permute-start
  14.0 24.3 %collective-permute-done = f32[16,128,128]{2,1,0:T(8,128)S(1)} collective-permute-done((f32[16,128,128]{2,1,0:T(8,128)S(1)}, f32[16,128,128]{2,1,0:T(8,128)S(1)}, u32[]{:S(2)}, u32[]{:S(2)}) %collective-permute-start) | collective-permute-done | bytes 1048608 | tf_op jit(solution)/shard_map/ppermute | solution.py:18
  38.4 3.5 collective-permute-start.1
  41.9 22.4 %collective-permute-done.1 = f32[16,128,128]{2,1,0:T(8,128)S(1)} collective-permute-done((f32[16,128,128]{2,1,0:T(8,128)S(1)}, f32[16,128,128]{2,1,0:T(8,128)S(1)}, u32[]{:S(2)}, u32[]{:S(2)}) %collective-permute-start.1) | collective-permute-done | bytes 1048608 | tf_op jit(solution)/shard_map/ppermute | solution.py:18
  64.5 1.4 collective-permute-start.2
  65.9 24.7 %collective-permute-done.2 = f32[16,128,128]{2,1,0:T(8,128)S(1)} collective-permute-done((f32[16,128,128]{2,1,0:T(8,128)S(1)}, f32[16,128,128]{2,1,0:T(8,128)S(1)}, u32[]{:S(2)}, u32[]{:S(2)}) %collective-permute-start.2) | collective-permute-done | bytes 1048608 | tf_op jit(solution)/shard_map/ppermute | solution.py:18
  90.6 1.1 add_subtract_fusion
  91.7 25.1 %all-to-all-start.1 = ((bf16[4,256,704]{1,2,0:T(8,128)(2,1)}), bf16[4,256,704]{1,2,0:T(8,128)(2,1)S(1)}, u32[]{:S(2)}, u32[]{:S(2)}) async-start(bf16[4,256,704]{1,2,0:T(8,128)(2,1)} %param.21), calls=%async_computation.1 | async-start | bytes 2883584 | tf_op jit(solution)/shard_map/all_to_all | solution.py:66
  117.4 18.3 %all-to-all-done.1 = bf16[4,256,704]{1,2,0:T(8,128)(2,1)S(1)} async-done(((bf16[4,256,704]{1,2,0:T(8,128)(2,1)}), bf16[4,256,704]{1,2,0:T(8,128)(2,1)S(1)}, u32[]{:S(2)}, u32[]{:S(2)}) %all-to-all-start.1) | async-done | bytes 1441824 | tf_op jit(solution)/shard_map/all_to_all | solution.py:66
  135.7 3.6 all-to-all-start.2
  139.3 1.7 reduce-window.6
  141.7 3.4 scatter_custom_fusion.1
  145.1 3.4 scatter_custom_fusion
  148.6 3.5 convolution_bitcast_fusion.1
  152.1 3.4 multiply_reduce_fusion.1
  155.5 1.5 all-to-all-done.2
  157.0 3.6 all-to-all-start.3
  160.6 2.4 broadcast_multiply_fusion
  163.0 2.5 copy.41
  165.6 1.4 fusion.7
  167.2 0.6 copy-done
  167.9 4.9 %gather_fusion = bf16[800,2048]{1,0:T(8,128)(2,1)} fusion(bf16[128,2048]{1,0:T(8,128)(2,1)S(1)} %fusion.5, s32[1024]{0:T(1024)S(1)} %pad_clamp_fusion.1), kind=kCustom, calls=%fused_computation | custom fusion | bytes 6556800 | tf_op jit(solution)/shard_map/gather | solution.py:107
  172.8 4.9 %gather.9 = bf16[16,50,2048]{2,1,0:T(8,128)(2,1)} reshape(bf16[800,2048]{1,0:T(8,128)(2,1)} %gather_fusion) | data formatting | bytes 6553600 | tf_op jit(solution)/shard_map/gather | solution.py:107
  177.7 4.3 broadcast_select_fusion
  182.0 1.1 copy-done.4
  183.1 5.1 %all-to-all-start = ((bf16[16,50,2048]{2,1,0:T(8,128)(2,1)}), bf16[16,50,2048]{2,1,0:T(8,128)(2,1)}, u32[]{:S(2)}, u32[]{:S(2)}) async-start(bf16[16,50,2048]{2,1,0:T(8,128)(2,1)} %broadcast_select_fusion), calls=%async_computation | async-start | bytes 7340032 | tf_op jit(solution)/shard_map/all_to_all | solution.py:109
  188.3 0.7 all-gather.9.cloned.1.call-update
  189.7 48.2 %all-gather.7.cloned.1.call-done = bf16[8,256,704]{1,2,0:T(8,128)(2,1)} async-done(((bf16[4,256,704]{1,2,0:T(8,128)(2,1)}), bf16[8,256,704]{1,2,0:T(8,128)(2,1)}) %all-gather.7.cloned.1.call-update) | async-done | bytes 2883600 | tf_op jit(solution)/shard_map/all_gather | solution.py:67
  237.9 3.8 copy.55
  241.7 70.6 %all-gather.9.cloned.1.call-done = bf16[8,256,704]{1,2,0:T(8,128)(2,1)} async-done(((bf16[4,256,704]{1,2,0:T(8,128)(2,1)}), bf16[8,256,704]{1,2,0:T(8,128)(2,1)}) %all-gather.9.cloned.1.call-update) | async-done | bytes 2883600 | tf_op jit(solution)/shard_map/all_gather | solution.py:67
  312.3 3.8 copy.56
  316.1 3.2 reshape.111
  319.3 6.0 %fusion.35 = f32[800,704]{1,0:T(8,128)} fusion(bf16[800,2048]{1,0:T(8,128)(2,1)S(1)} %reshape.111, bf16[2048,704]{0,1:T(8,128)(2,1)} %bitcast.67), kind=kOutput, calls=%fused_computation.65 | convolution fusion | flops 2306867200 | bytes 8413184 | tf_op jit(solution)/shard_map/dot_general | solution.py:111
  325.4 61.3 %all-gather.11.cloned.1.call-done = bf16[8,704,256]{2,1,0:T(8,128)(2,1)} async-done(((bf16[4,704,256]{2,1,0:T(8,128)(2,1)}), bf16[8,704,256]{2,1,0:T(8,128)(2,1)}) %all-gather.11.cloned.1.call-update) | async-done | bytes 2883600 | tf_op jit(solution)/shard_map/all_gather | solution.py:67
  386.7 11.1 %convolution_convert_fusion = bf16[800,2,4,256]{3,0,2,1:T(8,128)(2,1)} fusion(bf16[2,4,704,256]{3,2,1,0:T(8,128)(2,1)} %bitcast.72, bf16[800,2048]{1,0:T(8,128)(2,1)S(1)} %reshape.111, bf16[2048,704]{0,1:T(8,128)(2,1)} %bitcast.66, f32[800,704]{1,0:T(8,128)} %fusion.35), kind=kOutput, calls=%fused_computation.7 | convolution fusion | flops 4618188800 | bytes 14573568 | tf_op jit(solution)/shard_map/rh,abhd->rabd/dot_general | solution.py:114
  397.9 4.5 copy.49
  402.3 3.5 reshape.114
  405.8 6.0 %all-to-all-start.4 = ((bf16[16,50,2048]{2,1,0:T(8,128)(2,1)}), bf16[16,50,2048]{2,1,0:T(8,128)(2,1)}, u32[]{:S(2)}, u32[]{:S(2)}) async-start(bf16[16,50,2048]{2,1,0:T(8,128)(2,1)} %reshape.114), calls=%async_computation.4 | async-start | bytes 7340032 | tf_op jit(solution)/shard_map/all_to_all | solution.py:118
  411.9 46.3 %all-to-all-done.4 = bf16[16,50,2048]{2,1,0:T(8,128)(2,1)} async-done(((bf16[16,50,2048]{2,1,0:T(8,128)(2,1)}), bf16[16,50,2048]{2,1,0:T(8,128)(2,1)}, u32[]{:S(2)}, u32[]{:S(2)}) %all-to-all-start.4) | async-done | bytes 3276832 | tf_op jit(solution)/shard_map/all_to_all | solution.py:118
  458.1 3.2 reshape.115
  461.3 4.3 gather_fusion.1
  465.6 6.5 %reshape.117 = f32[128,6,2048]{2,1,0:T(8,128)} reshape(bf16[768,2048]{1,0:T(8,128)(2,1)} %gather_fusion.1) | data formatting | bytes 9437184 | tf_op jit(solution)/shard_map/convert_element_type | solution.py:120
  472.2 6.7 %multiply_reduce_fusion = f32[128,2048]{1,0:T(8,128)S(1)} fusion(f32[128,6,2048]{2,1,0:T(8,128)} %reshape.117, f32[128,6]{1,0:T(8,128)S(1)} %bitcast.70), kind=kLoop, calls=%fused_computation.4 | loop fusion | flops 2883584 | bytes 7343104 | tf_op jit(solution)/shard_map/reduce_sum | solution.py:120
  478.9 0.9 fusion.8
  (56 shorter events, 2.9 us)
Async XLA Ops:
  7.8 30.5 %copy-start.5 = (bf16[1,128,2048]{1,2,0:T(8,128)(2,1)}, bf16[1,128,2048]{1,2,0:T(8,128)(2,1)S(1)}, u32[]{:S(2)}) copy-start(bf16[1,128,2048]{1,2,0:T(8,128)(2,1)S(1)} %copy.53) | copy-start | bytes 1572868
  9.2 0.8 copy-start.6
  10.6 27.7 %collective-permute-start = (f32[16,128,128]{2,1,0:T(8,128)S(1)}, f32[16,128,128]{2,1,0:T(8,128)S(1)}, u32[]{:S(2)}, u32[]{:S(2)}) collective-permute-start(f32[16,128,128]{2,1,0:T(8,128)S(1)} %fusion.11), channel_id=1, source_target_pairs={{0,4},{4,8},{8,12},{12,16},{16,20},{20,24},{24,28},{1,5},{5,9},{9,... | collective-permute-start | bytes 3145736 | tf_op jit(solution)/shard_map/ppermute | solution.py:18
  38.4 25.9 %collective-permute-start.1 = (f32[16,128,128]{2,1,0:T(8,128)S(1)}, f32[16,128,128]{2,1,0:T(8,128)S(1)}, u32[]{:S(2)}, u32[]{:S(2)}) collective-permute-start(f32[16,128,128]{2,1,0:T(8,128)S(1)} %add.81), channel_id=1, source_target_pairs={{0,8},{4,12},{8,16},{12,20},{16,24},{20,28},{1,9},{5,13},{9,17},{1... | collective-permute-start | bytes 3145736 | tf_op jit(solution)/shard_map/ppermute | solution.py:18
  64.5 52.4 %copy-start.9 = (s32[1,128,6]{1,0,2:T(1,128)S(1)}, s32[1,128,6]{1,0,2:T(1,128)}, u32[]{:S(2)}) copy-start(s32[1,128,6]{1,0,2:T(1,128)} %param.19) | copy-start | bytes 9220
  64.5 52.8 %copy-start.7 = (bf16[1,128,2048]{2,1,0:T(8,128)(2,1)S(1)}, bf16[1,128,2048]{2,1,0:T(8,128)(2,1)}, u32[]{:S(2)}) copy-start(bf16[1,128,2048]{2,1,0:T(8,128)(2,1)} %param.12) | copy-start | bytes 1572868
  64.5 26.1 %collective-permute-start.2 = (f32[16,128,128]{2,1,0:T(8,128)S(1)}, f32[16,128,128]{2,1,0:T(8,128)S(1)}, u32[]{:S(2)}, u32[]{:S(2)}) collective-permute-start(f32[16,128,128]{2,1,0:T(8,128)S(1)} %add.82), channel_id=1, source_target_pairs={{0,16},{4,20},{8,24},{12,28},{1,17},{5,21},{9,25},{13,29},{2,18},{... | collective-permute-start | bytes 3145736 | tf_op jit(solution)/shard_map/ppermute | solution.py:18
  91.7 43.9 %all-to-all-start.1 = ((bf16[4,256,704]{1,2,0:T(8,128)(2,1)}), bf16[4,256,704]{1,2,0:T(8,128)(2,1)S(1)}, u32[]{:S(2)}, u32[]{:S(2)}) async-start(bf16[4,256,704]{1,2,0:T(8,128)(2,1)} %param.21), calls=%async_computation.1 | async-start | bytes 2883584 | tf_op jit(solution)/shard_map/all_to_all | solution.py:66
  135.7 16.5 %copy-start.2 = (bf16[4,256,704]{1,2,0:T(8,128)(2,1)}, bf16[4,256,704]{1,2,0:T(8,128)(2,1)S(1)}, u32[]{:S(2)}) copy-start(bf16[4,256,704]{1,2,0:T(8,128)(2,1)S(1)} %all-to-all-done.1) | copy-start | bytes 4325380
  135.7 21.3 %all-to-all-start.2 = ((bf16[4,256,704]{1,2,0:T(8,128)(2,1)}), bf16[4,256,704]{1,2,0:T(8,128)(2,1)S(1)}, u32[]{:S(2)}, u32[]{:S(2)}) async-start(bf16[4,256,704]{1,2,0:T(8,128)(2,1)} %param.22), calls=%async_computation.2 | async-start | bytes 2883584 | tf_op jit(solution)/shard_map/all_to_all | solution.py:66
  157.0 8.5 %copy-start.3 = (bf16[4,256,704]{1,2,0:T(8,128)(2,1)}, bf16[4,256,704]{1,2,0:T(8,128)(2,1)S(1)}, u32[]{:S(2)}) copy-start(bf16[4,256,704]{1,2,0:T(8,128)(2,1)S(1)} %all-to-all-done.2) | copy-start | bytes 4325380
  157.0 25.0 %all-to-all-start.3 = ((bf16[4,704,256]{2,1,0:T(8,128)(2,1)}), bf16[4,704,256]{2,1,0:T(8,128)(2,1)S(1)}, u32[]{:S(2)}, u32[]{:S(2)}) async-start(bf16[4,704,256]{2,1,0:T(8,128)(2,1)} %param.23), calls=%async_computation.3 | async-start | bytes 2883584 | tf_op jit(solution)/shard_map/all_to_all | solution.py:66
  160.5 5.0 %copy-start.8 = (bf16[1,128,2048]{2,1,0:T(8,128)(2,1)S(1)}, bf16[1,128,2048]{2,1,0:T(8,128)(2,1)}, u32[]{:S(2)}) copy-start(bf16[1,128,2048]{2,1,0:T(8,128)(2,1)} %param.15) | copy-start | bytes 1572868
  160.6 5.0 %copy-start.10 = (f32[2048]{0:T(1024)S(1)}, f32[2048]{0:T(1024)}, u32[]{:S(2)}) copy-start(f32[2048]{0:T(1024)} %param.17) | copy-start | bytes 24580
  160.6 77.3 %all-gather.7.cloned.1.call-start = ((), (), s32[]{:S(2)}) async-start(), calls=%async_computation.5 | async-start | bytes 4325376 | tf_op jit(solution)/shard_map/all_gather | solution.py:67
  163.0 4.8 copy-start.11
  166.9 0.8 copy-start
  182.0 1.1 copy-start.4
  183.1 133.0 %all-to-all-start = ((bf16[16,50,2048]{2,1,0:T(8,128)(2,1)}), bf16[16,50,2048]{2,1,0:T(8,128)(2,1)}, u32[]{:S(2)}, u32[]{:S(2)}) async-start(bf16[16,50,2048]{2,1,0:T(8,128)(2,1)} %broadcast_select_fusion), calls=%async_computation | async-start | bytes 7340032 | tf_op jit(solution)/shard_map/all_to_all | solution.py:109
  188.2 124.1 %all-gather.9.cloned.1.call-start = ((), (), s32[]{:S(2)}) async-start(), calls=%async_computation.6 | async-start | bytes 4325376 | tf_op jit(solution)/shard_map/all_gather | solution.py:67
  189.0 197.7 %all-gather.11.cloned.1.call-start = ((), (), s32[]{:S(2)}) async-start(), calls=%async_computation.7 | async-start | bytes 4325376 | tf_op jit(solution)/shard_map/all_gather | solution.py:67
  405.8 6.0 %copy-start.12 = (f32[1,128,6]{1,0,2:T(1,128)S(1)}, f32[1,128,6]{1,0,2:T(1,128)}, u32[]{:S(2)}) copy-start(f32[1,128,6]{1,0,2:T(1,128)} %param.20) | copy-start | bytes 9220
  405.8 52.4 %all-to-all-start.4 = ((bf16[16,50,2048]{2,1,0:T(8,128)(2,1)}), bf16[16,50,2048]{2,1,0:T(8,128)(2,1)}, u32[]{:S(2)}, u32[]{:S(2)}) async-start(bf16[16,50,2048]{2,1,0:T(8,128)(2,1)} %reshape.114), calls=%async_computation.4 | async-start | bytes 7340032 | tf_op jit(solution)/shard_map/all_to_all | solution.py:118
  472.2 6.7 %copy-start.1 = (bf16[128,2048]{1,0:T(8,128)(2,1)S(1)}, bf16[128,2048]{1,0:T(8,128)(2,1)}, u32[]{:S(2)}) copy-start(bf16[128,2048]{1,0:T(8,128)(2,1)} %copy-done) | copy-start | bytes 1572868
Sparse Core Ops, SparseCore 0:
  165.7 72.1 all-gather.6
  239.5 72.8 all-gather.8
  313.9 72.7 all-gather.10

commit v14 on v6

--- a/solution.py
+++ b/solution.py
@@ -55,10 +55,9 @@
             mine = lax.all_to_all(weight, "seq_lo", 0, 0, tiled=False)
             return lax.all_gather(mine, "seq_hi", axis=0, tiled=False)
 
-        whole_gate = collect(gate_weight)
+        gate_across = lax.all_gather(gate_weight, "seq_hi", axis=0, tiled=False)
         whole_up = collect(up_weight)
         whole_down = collect(down_weight)
-        whole_gate = whole_gate.reshape(-1, whole_gate.shape[-1])
         whole_up = whole_up.reshape(-1, whole_up.shape[-1])
 
         tokens = queries.shape[1]
@@ -69,6 +68,9 @@
             "thd,the->hde", key_heads, value_heads, preferred_element_type=jnp.float32
         )
         earlier = carried_in(local_state, seq, n_seq)
+        gate_across, earlier = lax.optimization_barrier((gate_across, earlier))
+        whole_gate = lax.all_to_all(gate_across, "seq_lo", 1, 1, tiled=False)
+        whole_gate = whole_gate.reshape(-1, whole_gate.shape[-1])
         state_before = state_start[0] + earlier
         causal = (
             jnp.arange(tokens, dtype=jnp.int32)[:, None]
@@ -103,6 +105,9 @@
         filled = jnp.zeros((EXPERTS * CAP,), jnp.bool_).at[position].set(True)
         outgoing = jnp.where(filled[:, None], ffn_in[source], jnp.zeros((), jnp.bfloat16))
         outgoing = outgoing.reshape(EXPERTS, CAP, D)
+        outgoing, whole_up, whole_down = lax.optimization_barrier(
+            (outgoing, whole_up, whole_down)
+        )
         arrived = lax.all_to_all(outgoing, group, 0, 0, tiled=True)
         arrived = arrived.reshape(EXPERTS * CAP, D)
         gate_sum = jnp.dot(arrived, whole_gate, preferred_element_type=jnp.float32)

time: 467 us -> 485 us (1.039)
  waiting for transfers between devices: 253 us -> 267 us
  local copies, waits for them, and re-layouts: 60.1 us -> 70.1 us
    all_gather x3 -> x2, waiting for transfers between devices: 131 us -> 40.4 us  [collect(): return lax.all_gather(mine, 'seq_hi', axis=0, tiled=False)]
    ppermute x3, waiting for transfers between devices: 74.6 us -> 144 us  [carried_in(): lax.ppermute(total, axis, [(i, i + shift) for i in range(count - shift)])]
    all_to_all x0 -> x1, starting transfers between devices: none -> 57.9 us  [shards(): whole_gate = lax.all_to_all(gate_across, 'seq_lo', 1, 1, tiled=False)]
    all_to_all x3 -> x2, starting transfers between devices: 63.6 us -> 8.11 us  [collect(): mine = lax.all_to_all(weight, 'seq_lo', 0, 0, tiled=False)]
    all_to_all x1, waiting for transfers between devices: 0.01 us -> 35 us  [shards(): arrived = lax.all_to_all(outgoing, group, 0, 0, tiled=True)]
    optimization_barrier x0 -> x1, local copies, waits for them, and re-layouts: none -> 6.33 us  [shards(): gate_across, earlier = lax.optimization_barrier((gate_across, earlier))]
    all_to_all x0 -> x1, local copies, waits for them, and re-layouts: none -> 5.26 us  [shards(): whole_gate = lax.all_to_all(gate_across, 'seq_lo', 1, 1, tiled=False)]
where the time goes in v14:
time: 485 us; the launch traced here: 481 us
  waiting for transfers between devices  267 us (55%)
  starting transfers between devices  83.9 us (17%)
  local copies, waits for them, and re-layouts  70.1 us (14%)
  matrix products  24.5 us (5%)
  other arithmetic  22.1 us (5%)
  between operations  13.4 us (3%)
    ppermute x3, waiting for transfers between devices, carried_in(): lax.ppermute(total, axis, [(i, i + shift) for i in range(count - shift)])  144 us
    all_to_all x1, starting transfers between devices, shards(): whole_gate = lax.all_to_all(gate_across, 'seq_lo', 1, 1, tiled=False)  57.9 us
    all_to_all x1, waiting for transfers between devices, shards(): returned = lax.all_to_all(expert_rows, group, 0, 0, tiled=True)  45.9 us
    all_gather x2, waiting for transfers between devices, collect(): return lax.all_gather(mine, 'seq_hi', axis=0, tiled=False)  40.4 us
    all_to_all x1, waiting for transfers between devices, shards(): arrived = lax.all_to_all(outgoing, group, 0, 0, tiled=True)  35 us
    dot_general x1, matrix products, shards(): jnp.einsum('rh,abhd->rabd', hidden, whole_down, preferred_element_type=jn...  11.1 us
  transfers between devices with their start and end apart: 11, of which 6 were waited for; matrix products, arithmetic and copies ran while one was open for 14% of the time, Pallas kernels for 0%

profile of v14, /device:TPU:16, one launch (start us, length us, event | category | flops | bytes accessed | tf_op | source)
XLA Modules:
  0.0 480.8 jit_solution(1797326733842186821)
XLA Ops:
  6.5 0.7 all-gather.7.cloned.1.call-update
  7.3 3.8 all-to-all-start
  11.5 0.8 copy-done.4
  12.3 0.5 fusion.11
  12.8 3.9 collective-permute-start
  16.7 77.1 %collective-permute-done = f32[16,128,128]{2,1,0:T(8,128)S(1)} collective-permute-done((f32[16,128,128]{2,1,0:T(8,128)S(1)}, f32[16,128,128]{2,1,0:T(8,128)S(1)}, u32[]{:S(2)}, u32[]{:S(2)}) %collective-permute-start) | collective-permute-done | bytes 1048608 | tf_op jit(solution)/shard_map/ppermute | solution.py:18
  93.8 1.1 add.81
  95.0 1.9 collective-permute-start.1
  96.9 4.3 all-to-all-start.1
  101.3 0.7 all-gather.9.cloned.1.call-update
  102.0 20.2 %collective-permute-done.1 = f32[16,128,128]{2,1,0:T(8,128)} collective-permute-done((f32[16,128,128]{2,1,0:T(8,128)}, f32[16,128,128]{2,1,0:T(8,128)}, u32[]{:S(2)}, u32[]{:S(2)}) %collective-permute-start.1) | collective-permute-done | bytes 1048608 | tf_op jit(solution)/shard_map/ppermute | solution.py:18
  122.2 1.9 add.82
  124.1 1.3 collective-permute-start.2
  125.6 46.6 %collective-permute-done.2 = f32[16,128,128]{2,1,0:T(8,128)S(1)} collective-permute-done((f32[16,128,128]{2,1,0:T(8,128)S(1)}, f32[16,128,128]{2,1,0:T(8,128)S(1)}, u32[]{:S(2)}, u32[]{:S(2)}) %collective-permute-start.2) | collective-permute-done | bytes 1048608 | tf_op jit(solution)/shard_map/ppermute | solution.py:18
  172.3 1.2 add_subtract_fusion
  173.4 6.3 %copy.48 = bf16[2,4,256,704]{2,0,3,1:T(2,128)(2,1)} copy(bf16[2,4,256,704]{2,3,1,0:T(8,128)(2,1)} %bitcast.66) | data formatting | bytes 5767168 | tf_op jit(solution)/shard_map/optimization_barrier | solution.py:71
  179.8 57.9 %all-to-all-start.3 = ((bf16[2,4,256,704]{2,0,3,1:T(2,128)(2,1)}), bf16[2,4,256,704]{2,0,3,1:T(2,128)(2,1)S(1)}, u32[]{:S(2)}, u32[]{:S(2)}) async-start(bf16[2,4,256,704]{2,0,3,1:T(2,128)(2,1)} %copy.48), calls=%async_computation.3 | async-start | bytes 5767168 | tf_op jit(solution)/shard_map/all_to_all | solution.py:72
  237.8 1.1 copy.58
  239.0 1.7 reduce-window.6
  241.4 3.4 scatter_custom_fusion.1
  244.8 3.6 scatter_custom_fusion
  248.5 3.5 convolution_bitcast_fusion.1
  252.1 3.4 multiply_reduce_fusion.1
  255.4 2.5 broadcast_multiply_fusion
  257.9 2.7 copy.41
  260.6 1.4 fusion.7
  262.3 0.6 copy-done
  263.1 4.9 %gather_fusion = bf16[800,2048]{1,0:T(8,128)(2,1)} fusion(bf16[128,2048]{1,0:T(8,128)(2,1)S(1)} %fusion.5, s32[1024]{0:T(1024)S(1)} %pad_clamp_fusion.1), kind=kCustom, calls=%fused_computation | custom fusion | bytes 6556800 | tf_op jit(solution)/shard_map/gather | solution.py:106
  267.9 4.7 gather.9
  272.6 4.2 broadcast_select_fusion
  276.8 3.8 copy.56
  280.6 40.4 %all-gather.11.cloned.1.call-done = bf16[8,704,256]{2,1,0:T(8,128)(2,1)} async-done(((bf16[4,704,256]{2,1,0:T(8,128)(2,1)}), bf16[8,704,256]{2,1,0:T(8,128)(2,1)}) %all-gather.11.cloned.1.call-update) | async-done | bytes 2883600 | tf_op jit(solution)/shard_map/all_gather | solution.py:56
  321.0 5.8 %all-to-all-start.2 = ((bf16[16,50,2048]{2,1,0:T(8,128)(2,1)}), bf16[16,50,2048]{2,1,0:T(8,128)(2,1)}, u32[]{:S(2)}, u32[]{:S(2)}) async-start(bf16[16,50,2048]{2,1,0:T(8,128)(2,1)} %broadcast_select_fusion), calls=%async_computation.2 | async-start | bytes 7340032 | tf_op jit(solution)/shard_map/all_to_all | solution.py:111
  326.9 5.3 %copy.49 = bf16[2,4,256,704]{2,1,0,3:T(4,128)(2,1)} copy(bf16[2,4,256,704]{2,0,3,1:T(2,128)(2,1)S(1)} %all-to-all-done.3) | data formatting | bytes 5767168 | tf_op jit(solution)/shard_map/all_to_all | solution.py:72
  332.1 6.1 %reshape.113 = bf16[2048,704]{0,1:T(8,128)(2,1)} reshape(bf16[2,4,256,704]{2,1,0,3:T(4,128)(2,1)} %copy.49) | data formatting | bytes 5767168 | tf_op jit(solution)/shard_map/reshape | solution.py:73
  338.2 35.0 %all-to-all-done.2 = bf16[16,50,2048]{2,1,0:T(8,128)(2,1)} async-done(((bf16[16,50,2048]{2,1,0:T(8,128)(2,1)}), bf16[16,50,2048]{2,1,0:T(8,128)(2,1)}, u32[]{:S(2)}, u32[]{:S(2)}) %all-to-all-start.2) | async-done | bytes 3276832 | tf_op jit(solution)/shard_map/all_to_all | solution.py:111
  373.3 3.4 reshape.112
  376.7 6.0 %fusion.35 = f32[800,704]{1,0:T(8,128)} fusion(bf16[800,2048]{1,0:T(8,128)(2,1)S(1)} %reshape.112, bf16[2048,704]{0,1:T(8,128)(2,1)} %reshape.113), kind=kOutput, calls=%fused_computation.65 | convolution fusion | flops 2306867200 | bytes 8413184 | tf_op jit(solution)/shard_map/dot_general | solution.py:113
  382.7 11.1 %convolution_convert_fusion = bf16[800,2,4,256]{3,0,2,1:T(8,128)(2,1)} fusion(bf16[2,4,704,256]{3,2,1,0:T(8,128)(2,1)} %bitcast.72, bf16[800,2048]{1,0:T(8,128)(2,1)S(1)} %reshape.112, bf16[2048,704]{0,1:T(8,128)(2,1)} %bitcast.67, f32[800,704]{1,0:T(8,128)} %fusion.35), kind=kOutput, calls=%fused_computation.7 | convolution fusion | flops 4618188800 | bytes 14573568 | tf_op jit(solution)/shard_map/rh,abhd->rabd/dot_general | solution.py:116
  393.8 4.5 copy.50
  398.2 3.4 reshape.114
  401.7 4.9 %all-to-all-start.4 = ((bf16[16,50,2048]{2,1,0:T(8,128)(2,1)}), bf16[16,50,2048]{2,1,0:T(8,128)(2,1)}, u32[]{:S(2)}, u32[]{:S(2)}) async-start(bf16[16,50,2048]{2,1,0:T(8,128)(2,1)} %reshape.114), calls=%async_computation.4 | async-start | bytes 7340032 | tf_op jit(solution)/shard_map/all_to_all | solution.py:120
  406.7 45.9 %all-to-all-done.4 = bf16[16,50,2048]{2,1,0:T(8,128)(2,1)} async-done(((bf16[16,50,2048]{2,1,0:T(8,128)(2,1)}), bf16[16,50,2048]{2,1,0:T(8,128)(2,1)}, u32[]{:S(2)}, u32[]{:S(2)}) %all-to-all-start.4) | async-done | bytes 3276832 | tf_op jit(solution)/shard_map/all_to_all | solution.py:120
  452.6 3.2 reshape.115
  455.8 4.3 gather_fusion.1
  460.1 6.6 %reshape.117 = f32[128,6,2048]{2,1,0:T(8,128)} reshape(bf16[768,2048]{1,0:T(8,128)(2,1)} %gather_fusion.1) | data formatting | bytes 9437184 | tf_op jit(solution)/shard_map/convert_element_type | solution.py:122
  466.7 6.7 %multiply_reduce_fusion = f32[128,2048]{1,0:T(8,128)S(1)} fusion(f32[128,6,2048]{2,1,0:T(8,128)} %reshape.117, f32[128,6]{1,0:T(8,128)S(1)} %bitcast.70), kind=kLoop, calls=%fused_computation.4 | loop fusion | flops 2883584 | bytes 7343104 | tf_op jit(solution)/shard_map/reduce_sum | solution.py:122
  473.3 0.9 fusion.8
  (56 shorter events, 2.2 us)
Async XLA Ops:
  6.5 4.5 copy-start.5
  6.5 4.8 copy-start.6
  6.5 166.9 %all-gather.7.cloned.1.call-start = ((), (), s32[]{:S(2)}) async-start(), calls=%async_computation.5 | async-start | bytes 4325376 | tf_op jit(solution)/shard_map/all_gather | solution.py:58
  7.3 89.6 %all-to-all-start = ((bf16[4,256,704]{1,2,0:T(8,128)(2,1)}), bf16[4,256,704]{1,2,0:T(8,128)(2,1)S(1)}, u32[]{:S(2)}, u32[]{:S(2)}) async-start(bf16[4,256,704]{1,2,0:T(8,128)(2,1)} %param.22), calls=%async_computation | async-start | bytes 2883584 | tf_op jit(solution)/shard_map/all_to_all | solution.py:55
  11.3 83.6 %copy-start.3 = (bf16[1,128,2048]{1,2,0:T(8,128)(2,1)}, bf16[1,128,2048]{1,2,0:T(8,128)(2,1)S(1)}, u32[]{:S(2)}) copy-start(bf16[1,128,2048]{1,2,0:T(8,128)(2,1)S(1)} %copy.54) | copy-start | bytes 1572868
  11.5 0.8 copy-start.4
  12.8 81.0 %collective-permute-start = (f32[16,128,128]{2,1,0:T(8,128)S(1)}, f32[16,128,128]{2,1,0:T(8,128)S(1)}, u32[]{:S(2)}, u32[]{:S(2)}) collective-permute-start(f32[16,128,128]{2,1,0:T(8,128)S(1)} %fusion.11), channel_id=1, source_target_pairs={{0,4},{4,8},{8,12},{12,16},{16,20},{20,24},{24,28},{1,5},{5,9},{9,... | collective-permute-start | bytes 3145736 | tf_op jit(solution)/shard_map/ppermute | solution.py:18
  95.0 27.2 %collective-permute-start.1 = (f32[16,128,128]{2,1,0:T(8,128)}, f32[16,128,128]{2,1,0:T(8,128)}, u32[]{:S(2)}, u32[]{:S(2)}) collective-permute-start(f32[16,128,128]{2,1,0:T(8,128)} %add.81), channel_id=1, source_target_pairs={{0,8},{4,12},{8,16},{12,20},{16,24},{20,28},{1,9},{5,13},{9,17},{1... | collective-permute-start | bytes 3145736 | tf_op jit(solution)/shard_map/ppermute | solution.py:18
  96.9 4.4 copy-start.2
  96.9 82.9 %all-to-all-start.1 = ((bf16[4,704,256]{2,1,0:T(8,128)(2,1)}), bf16[4,704,256]{2,1,0:T(8,128)(2,1)}, u32[]{:S(2)}, u32[]{:S(2)}) async-start(bf16[4,704,256]{2,1,0:T(8,128)(2,1)} %param.23), calls=%async_computation.1 | async-start | bytes 2883584 | tf_op jit(solution)/shard_map/all_to_all | solution.py:55
  101.2 24.1 %copy-start.8 = (s32[1,128,6]{1,0,2:T(1,128)S(1)}, s32[1,128,6]{1,0,2:T(1,128)}, u32[]{:S(2)}) copy-start(s32[1,128,6]{1,0,2:T(1,128)} %param.19) | copy-start | bytes 9220
  101.2 175.6 %all-gather.9.cloned.1.call-start = ((), (), s32[]{:S(2)}) async-start(), calls=%async_computation.6 | async-start | bytes 4325376 | tf_op jit(solution)/shard_map/all_gather | solution.py:56
  124.1 48.2 %collective-permute-start.2 = (f32[16,128,128]{2,1,0:T(8,128)S(1)}, f32[16,128,128]{2,1,0:T(8,128)S(1)}, u32[]{:S(2)}, u32[]{:S(2)}) collective-permute-start(f32[16,128,128]{2,1,0:T(8,128)S(1)} %add.82), channel_id=1, source_target_pairs={{0,16},{4,20},{8,24},{12,28},{1,17},{5,21},{9,25},{13,29},{2,18},{... | collective-permute-start | bytes 3145736 | tf_op jit(solution)/shard_map/ppermute | solution.py:18
  179.8 141.3 %all-to-all-start.3 = ((bf16[2,4,256,704]{2,0,3,1:T(2,128)(2,1)}), bf16[2,4,256,704]{2,0,3,1:T(2,128)(2,1)S(1)}, u32[]{:S(2)}, u32[]{:S(2)}) async-start(bf16[2,4,256,704]{2,0,3,1:T(2,128)(2,1)} %copy.48), calls=%async_computation.3 | async-start | bytes 5767168 | tf_op jit(solution)/shard_map/all_to_all | solution.py:72
  237.7 83.3 %all-gather.11.cloned.1.call-start = ((), (), s32[]{:S(2)}) async-start(), calls=%async_computation.7 | async-start | bytes 4325376 | tf_op jit(solution)/shard_map/all_gather | solution.py:56
  255.4 5.2 %copy-start.7 = (bf16[1,128,2048]{2,1,0:T(8,128)(2,1)S(1)}, bf16[1,128,2048]{2,1,0:T(8,128)(2,1)}, u32[]{:S(2)}) copy-start(bf16[1,128,2048]{2,1,0:T(8,128)(2,1)} %param.15) | copy-start | bytes 1572868
  255.4 5.2 %copy-start.9 = (f32[2048]{0:T(1024)S(1)}, f32[2048]{0:T(1024)}, u32[]{:S(2)}) copy-start(f32[2048]{0:T(1024)} %param.17) | copy-start | bytes 24580
  257.9 4.9 %copy-start.10 = (f32[2048]{0:T(1024)S(1)}, f32[2048]{0:T(1024)}, u32[]{:S(2)}) copy-start(f32[2048]{0:T(1024)} %param.18) | copy-start | bytes 24580
  262.1 0.8 copy-start
  321.0 52.2 %all-to-all-start.2 = ((bf16[16,50,2048]{2,1,0:T(8,128)(2,1)}), bf16[16,50,2048]{2,1,0:T(8,128)(2,1)}, u32[]{:S(2)}, u32[]{:S(2)}) async-start(bf16[16,50,2048]{2,1,0:T(8,128)(2,1)} %broadcast_select_fusion), calls=%async_computation.2 | async-start | bytes 7340032 | tf_op jit(solution)/shard_map/all_to_all | solution.py:111
  401.7 4.9 %copy-start.11 = (f32[1,128,6]{1,0,2:T(1,128)S(1)}, f32[1,128,6]{1,0,2:T(1,128)}, u32[]{:S(2)}) copy-start(f32[1,128,6]{1,0,2:T(1,128)} %param.20) | copy-start | bytes 9220
  401.7 50.9 %all-to-all-start.4 = ((bf16[16,50,2048]{2,1,0:T(8,128)(2,1)}), bf16[16,50,2048]{2,1,0:T(8,128)(2,1)}, u32[]{:S(2)}, u32[]{:S(2)}) async-start(bf16[16,50,2048]{2,1,0:T(8,128)(2,1)} %reshape.114), calls=%async_computation.4 | async-start | bytes 7340032 | tf_op jit(solution)/shard_map/all_to_all | solution.py:120
  466.7 6.7 %copy-start.1 = (bf16[128,2048]{1,0:T(8,128)(2,1)S(1)}, bf16[128,2048]{1,0:T(8,128)(2,1)}, u32[]{:S(2)}) copy-start(bf16[128,2048]{1,0:T(8,128)(2,1)} %copy-done) | copy-start | bytes 1572868
Sparse Core Ops, SparseCore 0:
  8.9 71.9 all-gather.6
  103.6 79.9 all-gather.8
  248.7 72.3 all-gather.10

commit v15 on v6

--- a/solution.py
+++ b/solution.py
@@ -113,8 +113,20 @@
         ).astype(jnp.bfloat16)
         expert_rows = expert_rows.reshape(EXPERTS, CAP, D)
         returned = lax.all_to_all(expert_rows, group, 0, 0, tiled=True)
-        picked = returned.reshape(EXPERTS * CAP, D)[position].reshape(tokens, TOP, D)
-        expert_mix = jnp.sum(route_gates[0][:, :, None] * picked.astype(jnp.float32), axis=1)
+        slots = jnp.arange(EXPERTS * CAP, dtype=jnp.int32)
+        combine = jnp.sum(
+            jnp.where(
+                position.reshape(tokens, TOP)[:, :, None] == slots[None, None, :],
+                route_gates[0][:, :, None],
+                0.0,
+            ),
+            axis=1,
+        )
+        expert_mix = jnp.dot(
+            combine,
+            returned.reshape(EXPERTS * CAP, D).astype(jnp.float32),
+            precision=lax.Precision.HIGHEST,
+        )
         return (mixed_wide + expert_mix).astype(jnp.bfloat16)[None]
 
     return shards

time: 467 us -> 452 us (0.968)
  local copies, waits for them, and re-layouts: 60.1 us -> 48.5 us
  other arithmetic: 23.5 us -> 18.4 us
    convert_element_type x1 -> x0, local copies, waits for them, and re-layouts: 6.55 us -> none  [shards(): picked.astype(jnp.float32)]
    reduce_sum x1, other arithmetic: 6.67 us -> 1.06 us  [shards(): jnp.sum(jnp.where(position.reshape(tokens, TOP)[:, :, None] == slots[None...]
  transfers between devices with their start and end apart: 11 -> 11, of which waited for: 6 -> 6; matrix products, arithmetic and copies ran while one was open for 14% -> 15% of each run, Pallas kernels for 0% -> 0%
where the time goes in v15:
time: 452 us; the launch traced here: 447 us
  waiting for transfers between devices  251 us (56%)
  starting transfers between devices  87.5 us (19%)
  local copies, waits for them, and re-layouts  48.5 us (11%)
  matrix products  28.7 us (6%)
  other arithmetic  18.4 us (4%)
  between operations  13.4 us (3%)
    all_gather x3, waiting for transfers between devices, collect(): return lax.all_gather(mine, 'seq_hi', axis=0, tiled=False)  131 us
    ppermute x3, waiting for transfers between devices, carried_in(): lax.ppermute(total, axis, [(i, i + shift) for i in range(count - shift)])  73.9 us
    all_to_all x3, starting transfers between devices, collect(): mine = lax.all_to_all(weight, 'seq_lo', 0, 0, tiled=False)  63.6 us
    all_to_all x1, waiting for transfers between devices, shards(): returned = lax.all_to_all(expert_rows, group, 0, 0, tiled=True)  45.1 us
    dot_general x1, matrix products, shards(): jnp.einsum('rh,abhd->rabd', hidden, whole_down, preferred_element_type=jn...  11.1 us
    ppermute x3, starting transfers between devices, carried_in(): lax.ppermute(total, axis, [(i, i + shift) for i in range(count - shift)])  10.8 us
    gather x2, local copies, waits for them, and re-layouts, shards(): ffn_in[source]  9.56 us
  transfers between devices with their start and end apart: 11, of which 6 were waited for; matrix products, arithmetic and copies ran while one was open for 15% of the time, Pallas kernels for 0%

profile of v15, /device:TPU:16, one launch (start us, length us, event | category | flops | bytes accessed | tf_op | source)
XLA Modules:
  0.0 447.4 jit_solution(3711181150492119529)
XLA Ops:
  6.5 3.9 all-to-all-start.1
  11.4 3.9 collective-permute-start
  15.3 33.3 %collective-permute-done = f32[16,128,128]{2,1,0:T(8,128)S(1)} collective-permute-done((f32[16,128,128]{2,1,0:T(8,128)S(1)}, f32[16,128,128]{2,1,0:T(8,128)S(1)}, u32[]{:S(2)}, u32[]{:S(2)}) %collective-permute-start) | collective-permute-done | bytes 1048608 | tf_op jit(solution)/shard_map/ppermute | solution.py:18
  48.6 1.1 add.86
  49.6 5.6 %collective-permute-start.1 = (f32[16,128,128]{2,1,0:T(8,128)}, f32[16,128,128]{2,1,0:T(8,128)}, u32[]{:S(2)}, u32[]{:S(2)}) collective-permute-start(f32[16,128,128]{2,1,0:T(8,128)} %add.86), channel_id=1, source_target_pairs={{0,8},{4,12},{8,16},{12,20},{16,24},{20,28},{1,9},{5,13},{9,17},{1... | collective-permute-start | bytes 3145736 | tf_op jit(solution)/shard_map/ppermute | solution.py:18
  55.2 0.7 copy.59
  56.0 1.0 eq.42
  57.0 1.0 eq.38
  57.9 2.0 copy.75
  59.9 4.3 all-to-all-start.2
  64.3 0.6 fusion.22
  64.9 4.1 reduce-window.6
  69.0 1.0 slice_reduce_fusion
  70.1 1.5 broadcast_multiply_fusion.1
  71.6 1.0 mul.76
  72.6 6.6 %collective-permute-done.1 = f32[16,128,128]{2,1,0:T(8,128)} collective-permute-done((f32[16,128,128]{2,1,0:T(8,128)}, f32[16,128,128]{2,1,0:T(8,128)}, u32[]{:S(2)}, u32[]{:S(2)}) %collective-permute-start.1) | collective-permute-done | bytes 1048608 | tf_op jit(solution)/shard_map/ppermute | solution.py:18
  79.1 2.6 add.87
  81.8 1.3 collective-permute-start.2
  83.2 3.4 scatter_custom_fusion.1
  86.6 3.4 scatter_custom_fusion
  90.2 2.9 convolution_bitcast_fusion
  93.1 34.1 %collective-permute-done.2 = f32[16,128,128]{2,1,0:T(8,128)} collective-permute-done((f32[16,128,128]{2,1,0:T(8,128)}, f32[16,128,128]{2,1,0:T(8,128)}, u32[]{:S(2)}, u32[]{:S(2)}) %collective-permute-start.2) | collective-permute-done | bytes 1048608 | tf_op jit(solution)/shard_map/ppermute | solution.py:18
  127.1 4.2 multiply_reduce_fusion
  131.4 55.4 %all-to-all-start.3 = ((bf16[4,704,256]{2,1,0:T(8,128)(2,1)}), bf16[4,704,256]{2,1,0:T(8,128)(2,1)S(1)}, u32[]{:S(2)}, u32[]{:S(2)}) async-start(bf16[4,704,256]{2,1,0:T(8,128)(2,1)} %param.23), calls=%async_computation.3 | async-start | bytes 2883584 | tf_op jit(solution)/shard_map/all_to_all | solution.py:55
  186.8 1.3 broadcast_multiply_fusion
  188.1 1.3 copy.58
  189.4 1.4 fusion.8
  191.0 0.6 copy-done
  191.8 4.9 %gather_fusion = bf16[800,2048]{1,0:T(8,128)(2,1)} fusion(bf16[128,2048]{1,0:T(8,128)(2,1)S(1)} %fusion.7, s32[1024]{0:T(1024)S(1)} %pad_clamp_fusion), kind=kCustom, calls=%fused_computation | custom fusion | bytes 6556800 | tf_op jit(solution)/shard_map/gather | solution.py:104
  196.7 4.7 %gather.6 = bf16[16,50,2048]{2,1,0:T(8,128)(2,1)} reshape(bf16[800,2048]{1,0:T(8,128)(2,1)} %gather_fusion) | data formatting | bytes 6553600 | tf_op jit(solution)/shard_map/gather | solution.py:104
  201.3 4.2 broadcast_select_fusion
  205.5 1.1 copy-done.2
  206.7 6.8 %all-to-all-start = ((bf16[16,50,2048]{2,1,0:T(8,128)(2,1)}), bf16[16,50,2048]{2,1,0:T(8,128)(2,1)}, u32[]{:S(2)}, u32[]{:S(2)}) async-start(bf16[16,50,2048]{2,1,0:T(8,128)(2,1)} %broadcast_select_fusion), calls=%async_computation | async-start | bytes 7340032 | tf_op jit(solution)/shard_map/all_to_all | solution.py:106
  213.5 0.7 all-gather.9.cloned.1.call-update
  215.0 3.8 copy.72
  218.8 68.2 %all-gather.9.cloned.1.call-done = bf16[8,256,704]{1,2,0:T(8,128)(2,1)} async-done(((bf16[4,256,704]{1,2,0:T(8,128)(2,1)}), bf16[8,256,704]{1,2,0:T(8,128)(2,1)}) %all-gather.9.cloned.1.call-update) | async-done | bytes 2883600 | tf_op jit(solution)/shard_map/all_gather | solution.py:56
  286.9 3.8 copy.73
  290.8 3.2 reshape.120
  294.0 6.0 %fusion.33 = f32[800,704]{1,0:T(8,128)} fusion(bf16[800,2048]{1,0:T(8,128)(2,1)S(1)} %reshape.120, bf16[2048,704]{0,1:T(8,128)(2,1)} %bitcast.75), kind=kOutput, calls=%fused_computation.67 | convolution fusion | flops 2306867200 | bytes 8413184 | tf_op jit(solution)/shard_map/dot_general | solution.py:108
  300.0 62.4 %all-gather.11.cloned.1.call-done = bf16[8,704,256]{2,1,0:T(8,128)(2,1)} async-done(((bf16[4,704,256]{2,1,0:T(8,128)(2,1)}), bf16[8,704,256]{2,1,0:T(8,128)(2,1)}) %all-gather.11.cloned.1.call-update) | async-done | bytes 2883600 | tf_op jit(solution)/shard_map/all_gather | solution.py:56
  362.4 11.1 %convolution_convert_fusion = bf16[800,2,4,256]{3,0,2,1:T(8,128)(2,1)} fusion(bf16[2,4,704,256]{3,2,1,0:T(8,128)(2,1)} %bitcast.80, bf16[800,2048]{1,0:T(8,128)(2,1)S(1)} %reshape.120, bf16[2048,704]{0,1:T(8,128)(2,1)} %bitcast.74, f32[800,704]{1,0:T(8,128)} %fusion.33), kind=kOutput, calls=%fused_computation.10 | convolution fusion | flops 4618188800 | bytes 14573568 | tf_op jit(solution)/shard_map/rh,abhd->rabd/dot_general | solution.py:111
  373.6 4.5 copy.66
  378.0 3.5 reshape.123
  381.5 6.0 %all-to-all-start.4 = ((bf16[16,50,2048]{2,1,0:T(8,128)(2,1)}), bf16[16,50,2048]{2,1,0:T(8,128)(2,1)}, u32[]{:S(2)}, u32[]{:S(2)}) async-start(bf16[16,50,2048]{2,1,0:T(8,128)(2,1)} %reshape.123), calls=%async_computation.4 | async-start | bytes 7340032 | tf_op jit(solution)/shard_map/all_to_all | solution.py:115
  387.7 1.1 select_reduce_fusion
  388.8 45.1 %all-to-all-done.4 = bf16[16,50,2048]{2,1,0:T(8,128)(2,1)} async-done(((bf16[16,50,2048]{2,1,0:T(8,128)(2,1)}), bf16[16,50,2048]{2,1,0:T(8,128)(2,1)}, u32[]{:S(2)}, u32[]{:S(2)}) %all-to-all-start.4) | async-done | bytes 3276832 | tf_op jit(solution)/shard_map/all_to_all | solution.py:115
  433.9 3.2 reshape.124
  437.1 3.8 fusion.1
  (54 shorter events, 2.7 us)
Async XLA Ops:
  6.5 3.9 copy-start.5
  6.5 4.2 copy-start.6
  6.5 53.4 %all-to-all-start.1 = ((bf16[4,256,704]{1,2,0:T(8,128)(2,1)}), bf16[4,256,704]{1,2,0:T(8,128)(2,1)S(1)}, u32[]{:S(2)}, u32[]{:S(2)}) async-start(bf16[4,256,704]{1,2,0:T(8,128)(2,1)} %param.21), calls=%async_computation.1 | async-start | bytes 2883584 | tf_op jit(solution)/shard_map/all_to_all | solution.py:55
  10.8 44.4 %copy-start.11 = (s32[1,128,6]{1,0,2:T(1,128)S(1)}, s32[1,128,6]{1,0,2:T(1,128)}, u32[]{:S(2)}) copy-start(s32[1,128,6]{1,0,2:T(1,128)} %param.19) | copy-start | bytes 9220
  11.4 37.2 %collective-permute-start = (f32[16,128,128]{2,1,0:T(8,128)S(1)}, f32[16,128,128]{2,1,0:T(8,128)S(1)}, u32[]{:S(2)}, u32[]{:S(2)}) collective-permute-start(f32[16,128,128]{2,1,0:T(8,128)S(1)} %fusion.13), channel_id=1, source_target_pairs={{0,4},{4,8},{8,12},{12,16},{16,20},{20,24},{24,28},{1,5},{5,9},{9,... | collective-permute-start | bytes 3145736 | tf_op jit(solution)/shard_map/ppermute | solution.py:18
  49.6 29.5 %collective-permute-start.1 = (f32[16,128,128]{2,1,0:T(8,128)}, f32[16,128,128]{2,1,0:T(8,128)}, u32[]{:S(2)}, u32[]{:S(2)}) collective-permute-start(f32[16,128,128]{2,1,0:T(8,128)} %add.86), channel_id=1, source_target_pairs={{0,8},{4,12},{8,16},{12,20},{16,24},{20,28},{1,9},{5,13},{9,17},{1... | collective-permute-start | bytes 3145736 | tf_op jit(solution)/shard_map/ppermute | solution.py:18
  59.9 21.9 %copy-start.1 = (bf16[4,256,704]{1,2,0:T(8,128)(2,1)}, bf16[4,256,704]{1,2,0:T(8,128)(2,1)S(1)}, u32[]{:S(2)}) copy-start(bf16[4,256,704]{1,2,0:T(8,128)(2,1)S(1)} %all-to-all-done.1) | copy-start | bytes 4325380
  59.9 71.5 %all-to-all-start.2 = ((bf16[4,256,704]{1,2,0:T(8,128)(2,1)}), bf16[4,256,704]{1,2,0:T(8,128)(2,1)}, u32[]{:S(2)}, u32[]{:S(2)}) async-start(bf16[4,256,704]{1,2,0:T(8,128)(2,1)} %param.22), calls=%async_computation.2 | async-start | bytes 2883584 | tf_op jit(solution)/shard_map/all_to_all | solution.py:55
  64.2 150.8 %all-gather.7.cloned.1.call-start = ((), (), s32[]{:S(2)}) async-start(), calls=%async_computation.5 | async-start | bytes 4325376 | tf_op jit(solution)/shard_map/all_gather | solution.py:56
  72.6 10.5 %copy-start.8 = (s32[16,6,128]{2,0,1:T(8,128)S(1)}, s32[16,6,128]{2,0,1:T(8,128)}, u32[]{:S(2)}) copy-start(s32[16,6,128]{2,0,1:T(8,128)} %reduce-window.6) | copy-start | bytes 147460
  81.8 45.3 %collective-permute-start.2 = (f32[16,128,128]{2,1,0:T(8,128)}, f32[16,128,128]{2,1,0:T(8,128)}, u32[]{:S(2)}, u32[]{:S(2)}) collective-permute-start(f32[16,128,128]{2,1,0:T(8,128)} %add.87), channel_id=1, source_target_pairs={{0,16},{4,20},{8,24},{12,28},{1,17},{5,21},{9,25},{13,29},{2,18},{... | collective-permute-start | bytes 3145736 | tf_op jit(solution)/shard_map/ppermute | solution.py:18
  83.1 44.1 %copy-start.3 = (bf16[16,8,16,128]{3,2,1,0:T(8,128)(2,1)S(1)}, bf16[16,8,16,128]{3,2,1,0:T(8,128)(2,1)}, u32[]{:S(2)}) copy-start(bf16[16,8,16,128]{3,2,1,0:T(8,128)(2,1)} %copy.75) | copy-start | bytes 1572868
  131.4 58.0 %copy-start.7 = (bf16[1,128,2048]{2,1,0:T(8,128)(2,1)S(1)}, bf16[1,128,2048]{2,1,0:T(8,128)(2,1)}, u32[]{:S(2)}) copy-start(bf16[1,128,2048]{2,1,0:T(8,128)(2,1)} %param.15) | copy-start | bytes 1572868
  131.4 58.0 %copy-start.9 = (f32[2048]{0:T(1024)S(1)}, f32[2048]{0:T(1024)}, u32[]{:S(2)}) copy-start(f32[2048]{0:T(1024)} %param.17) | copy-start | bytes 24580
  131.4 74.1 %all-to-all-start.3 = ((bf16[4,704,256]{2,1,0:T(8,128)(2,1)}), bf16[4,704,256]{2,1,0:T(8,128)(2,1)S(1)}, u32[]{:S(2)}, u32[]{:S(2)}) async-start(bf16[4,704,256]{2,1,0:T(8,128)(2,1)} %param.23), calls=%async_computation.3 | async-start | bytes 2883584 | tf_op jit(solution)/shard_map/all_to_all | solution.py:55
  188.1 3.5 copy-start.10
  190.8 0.8 copy-start
  205.5 1.1 copy-start.2
  206.7 84.1 %all-to-all-start = ((bf16[16,50,2048]{2,1,0:T(8,128)(2,1)}), bf16[16,50,2048]{2,1,0:T(8,128)(2,1)}, u32[]{:S(2)}, u32[]{:S(2)}) async-start(bf16[16,50,2048]{2,1,0:T(8,128)(2,1)} %broadcast_select_fusion), calls=%async_computation | async-start | bytes 7340032 | tf_op jit(solution)/shard_map/all_to_all | solution.py:106
  213.5 73.4 %all-gather.9.cloned.1.call-start = ((), (), s32[]{:S(2)}) async-start(), calls=%async_computation.6 | async-start | bytes 4325376 | tf_op jit(solution)/shard_map/all_gather | solution.py:56
  214.2 148.2 %all-gather.11.cloned.1.call-start = ((), (), s32[]{:S(2)}) async-start(), calls=%async_computation.7 | async-start | bytes 4325376 | tf_op jit(solution)/shard_map/all_gather | solution.py:56
  381.5 6.1 %copy-start.4 = (s32[1,128,6]{2,1,0:T(8,128)S(1)}, s32[1,128,6]{2,1,0:T(8,128)}, u32[]{:S(2)}) copy-start(s32[1,128,6]{2,1,0:T(8,128)} %copy.59) | copy-start | bytes 9220
  381.5 6.2 %copy-start.12 = (f32[1,128,6]{1,0,2:T(1,128)S(1)}, f32[1,128,6]{1,0,2:T(1,128)}, u32[]{:S(2)}) copy-start(f32[1,128,6]{1,0,2:T(1,128)} %param.20) | copy-start | bytes 9220
  381.5 52.4 %all-to-all-start.4 = ((bf16[16,50,2048]{2,1,0:T(8,128)(2,1)}), bf16[16,50,2048]{2,1,0:T(8,128)(2,1)}, u32[]{:S(2)}, u32[]{:S(2)}) async-start(bf16[16,50,2048]{2,1,0:T(8,128)(2,1)} %reshape.123), calls=%async_computation.4 | async-start | bytes 7340032 | tf_op jit(solution)/shard_map/all_to_all | solution.py:115
Sparse Core Ops, SparseCore 0:
  93.2 73.9 all-gather.6
  215.9 71.0 all-gather.8
  288.5 73.9 all-gather.10

commit v16 on v6

--- a/solution.py
+++ b/solution.py
@@ -98,10 +98,12 @@
         flat_routes = routes[0].reshape(-1)
         slot_rank = route_slots(flat_routes)
         position = flat_routes * CAP + slot_rank
-        token_index = jnp.arange(tokens * TOP, dtype=jnp.int32) // TOP
-        source = jnp.zeros((EXPERTS * CAP,), jnp.int32).at[position].set(token_index)
-        filled = jnp.zeros((EXPERTS * CAP,), jnp.bool_).at[position].set(True)
-        outgoing = jnp.where(filled[:, None], ffn_in[source], jnp.zeros((), jnp.bfloat16))
+        slots = jnp.arange(EXPERTS * CAP, dtype=jnp.int32)
+        routed = position.reshape(tokens, TOP)[:, :, None] == slots[None, None, :]
+        chosen = jnp.any(routed, axis=1).astype(jnp.bfloat16)
+        outgoing = jnp.einsum(
+            "ts,td->sd", chosen, ffn_in, preferred_element_type=jnp.float32
+        ).astype(jnp.bfloat16)
         outgoing = outgoing.reshape(EXPERTS, CAP, D)
         arrived = lax.all_to_all(outgoing, group, 0, 0, tiled=True)
         arrived = arrived.reshape(EXPERTS * CAP, D)
@@ -113,8 +115,12 @@
         ).astype(jnp.bfloat16)
         expert_rows = expert_rows.reshape(EXPERTS, CAP, D)
         returned = lax.all_to_all(expert_rows, group, 0, 0, tiled=True)
-        picked = returned.reshape(EXPERTS * CAP, D)[position].reshape(tokens, TOP, D)
-        expert_mix = jnp.sum(route_gates[0][:, :, None] * picked.astype(jnp.float32), axis=1)
+        combine = jnp.sum(jnp.where(routed, route_gates[0][:, :, None], 0.0), axis=1)
+        expert_mix = jnp.dot(
+            combine,
+            returned.reshape(EXPERTS * CAP, D).astype(jnp.float32),
+            precision=lax.Precision.HIGHEST,
+        )
         return (mixed_wide + expert_mix).astype(jnp.bfloat16)[None]
 
     return shards

time: 467 us -> 448 us (0.959)
  local copies, waits for them, and re-layouts: 60.1 us -> 27.4 us
  starting transfers between devices: 87.5 us -> 103 us
  other arithmetic: 23.5 us -> 8.71 us
  waiting for transfers between devices: 253 us -> 264 us
    all_to_all x1, starting transfers between devices: 6.84 us -> 73.9 us  [shards(): arrived = lax.all_to_all(outgoing, group, 0, 0, tiled=True)]
    all_to_all x3, starting transfers between devices: 63.6 us -> 13.4 us  [collect(): mine = lax.all_to_all(weight, 'seq_lo', 0, 0, tiled=False)]
    all_to_all x3, waiting for transfers between devices: 0.01 us -> 35.4 us  [collect(): mine = lax.all_to_all(weight, 'seq_lo', 0, 0, tiled=False)]
    ppermute x3, waiting for transfers between devices: 74.6 us -> 51.3 us  [carried_in(): lax.ppermute(total, axis, [(i, i + shift) for i in range(count - shift)])]
    gather x3 -> x0, local copies, waits for them, and re-layouts: 13.9 us -> none  [the longest x2 9.56 us: shards(): ffn_in[source]]
    scatter x2 -> x0, local copies, waits for them, and re-layouts: 6.76 us -> none  [the longest x1 3.38 us: shards(): filled = jnp.zeros((EXPERTS * CAP,), jnp.bool_).at[position].set(True)]
    convert_element_type x1 -> x0, local copies, waits for them, and re-layouts: 6.55 us -> none  [shards(): picked.astype(jnp.float32)]
    reduce_sum x1, other arithmetic: 6.67 us -> 1.04 us  [shards(): jnp.sum(jnp.where(routed, route_gates[0][:, :, None], 0.0), axis=1)]
  transfers between devices with their start and end apart: 11 -> 11, of which waited for: 6 -> 6; matrix products, arithmetic and copies ran while one was open for 14% -> 8% of each run, Pallas kernels for 0% -> 0%
where the time goes in v16:
time: 448 us; the launch traced here: 444 us
  waiting for transfers between devices  264 us (59%)
  starting transfers between devices  103 us (23%)
  local copies, waits for them, and re-layouts  27.4 us (6%)
  matrix products  27.4 us (6%)
  between operations  13.4 us (3%)
  other arithmetic  8.71 us (2%)
    all_gather x3, waiting for transfers between devices, collect(): return lax.all_gather(mine, 'seq_hi', axis=0, tiled=False)  131 us
    all_to_all x1, starting transfers between devices, shards(): arrived = lax.all_to_all(outgoing, group, 0, 0, tiled=True)  73.9 us
    ppermute x3, waiting for transfers between devices, carried_in(): lax.ppermute(total, axis, [(i, i + shift) for i in range(count - shift)])  51.3 us
    all_to_all x1, waiting for transfers between devices, shards(): returned = lax.all_to_all(expert_rows, group, 0, 0, tiled=True)  45.3 us
    all_to_all x3, waiting for transfers between devices, collect(): mine = lax.all_to_all(weight, 'seq_lo', 0, 0, tiled=False)  35.4 us
    all_to_all x3, starting transfers between devices, collect(): mine = lax.all_to_all(weight, 'seq_lo', 0, 0, tiled=False)  13.4 us
    dot_general x1, matrix products, shards(): jnp.einsum('rh,abhd->rabd', hidden, whole_down, preferred_element_type=jn...  11.1 us
    ppermute x3, starting transfers between devices, carried_in(): lax.ppermute(total, axis, [(i, i + shift) for i in range(count - shift)])  9.07 us
  transfers between devices with their start and end apart: 11, of which 6 were waited for; matrix products, arithmetic and copies ran while one was open for 8% of the time, Pallas kernels for 0%

profile of v16, /device:TPU:16, one launch (start us, length us, event | category | flops | bytes accessed | tf_op | source)
XLA Modules:
  0.0 443.7 jit_solution(17068574951090220227)
XLA Ops:
  6.5 3.9 all-to-all-start.1
  10.4 0.3 copy.70
  10.8 0.5 fusion.17
  11.4 3.9 collective-permute-start
  15.3 35.4 %all-to-all-done.1 = bf16[4,256,704]{1,2,0:T(8,128)(2,1)S(1)} async-done(((bf16[4,256,704]{1,2,0:T(8,128)(2,1)}), bf16[4,256,704]{1,2,0:T(8,128)(2,1)S(1)}, u32[]{:S(2)}, u32[]{:S(2)}) %all-to-all-start.1) | async-done | bytes 1441824 | tf_op jit(solution)/shard_map/all_to_all | solution.py:55
  50.7 4.5 %all-to-all-start.2 = ((bf16[4,256,704]{1,2,0:T(8,128)(2,1)}), bf16[4,256,704]{1,2,0:T(8,128)(2,1)}, u32[]{:S(2)}, u32[]{:S(2)}) async-start(bf16[4,256,704]{1,2,0:T(8,128)(2,1)} %param.22), calls=%async_computation.2 | async-start | bytes 2883584 | tf_op jit(solution)/shard_map/all_to_all | solution.py:55
  55.2 2.3 add.59
  57.6 3.9 collective-permute-start.1
  61.4 0.1 copy.59
  61.6 0.1 eq.42
  61.7 31.2 %collective-permute-done.1 = f32[16,128,128]{2,1,0:T(8,128)} collective-permute-done((f32[16,128,128]{2,1,0:T(8,128)}, f32[16,128,128]{2,1,0:T(8,128)}, u32[]{:S(2)}, u32[]{:S(2)}) %collective-permute-start.1) | collective-permute-done | bytes 1048608 | tf_op jit(solution)/shard_map/ppermute | solution.py:18
  92.9 2.6 add.60
  95.6 1.3 collective-permute-start.2
  96.9 0.1 eq.38
  97.1 1.7 reduce-window.6
  98.9 0.3 slice_reduce_fusion
  99.2 0.1 reduce_sum.40
  99.5 1.8 convolution_bitcast_fusion
  101.3 5.0 %all-to-all-start.3 = ((bf16[4,704,256]{2,1,0:T(8,128)(2,1)}), bf16[4,704,256]{2,1,0:T(8,128)(2,1)}, u32[]{:S(2)}, u32[]{:S(2)}) async-start(bf16[4,704,256]{2,1,0:T(8,128)(2,1)} %param.23), calls=%async_computation.3 | async-start | bytes 2883584 | tf_op jit(solution)/shard_map/all_to_all | solution.py:55
  106.4 0.4 fusion
  106.8 0.3 all-gather.7.cloned.1.call-update
  107.1 20.1 %collective-permute-done.2 = f32[16,128,128]{2,1,0:T(8,128)} collective-permute-done((f32[16,128,128]{2,1,0:T(8,128)}, f32[16,128,128]{2,1,0:T(8,128)}, u32[]{:S(2)}, u32[]{:S(2)}) %collective-permute-start.2) | collective-permute-done | bytes 1048608 | tf_op jit(solution)/shard_map/ppermute | solution.py:18
  127.2 3.0 multiply_reduce_fusion
  130.3 0.3 copy.58
  130.6 0.6 copy-done.6
  131.2 0.1 fusion.9
  131.3 0.2 fusion.6
  131.5 0.6 copy-done
  132.1 1.1 convolution_convert_fusion
  133.2 2.7 reshape.87
  135.9 73.9 %all-to-all-start = ((bf16[16,50,2048]{2,1,0:T(8,128)(2,1)}), bf16[16,50,2048]{2,1,0:T(8,128)(2,1)}, u32[]{:S(2)}, u32[]{:S(2)}) async-start(bf16[16,50,2048]{2,1,0:T(8,128)(2,1)} %reshape.87), calls=%async_computation | async-start | bytes 7340032 | tf_op jit(solution)/shard_map/all_to_all | solution.py:108
  209.9 0.7 all-gather.9.cloned.1.call-update
  210.6 0.2 all-gather.11.cloned.1.call-start
  210.8 0.5 all-gather.11.cloned.1.call-update
  211.4 3.8 copy.72
  215.2 69.5 %all-gather.9.cloned.1.call-done = bf16[8,256,704]{1,2,0:T(8,128)(2,1)} async-done(((bf16[4,256,704]{1,2,0:T(8,128)(2,1)}), bf16[8,256,704]{1,2,0:T(8,128)(2,1)}) %all-gather.9.cloned.1.call-update) | async-done | bytes 2883600 | tf_op jit(solution)/shard_map/all_gather | solution.py:56
  284.7 3.8 copy.73
  288.5 3.2 reshape.88
  291.7 6.0 %fusion.29 = f32[800,704]{1,0:T(8,128)} fusion(bf16[800,2048]{1,0:T(8,128)(2,1)S(1)} %reshape.88, bf16[2048,704]{0,1:T(8,128)(2,1)} %bitcast.76), kind=kOutput, calls=%fused_computation.51 | convolution fusion | flops 2306867200 | bytes 8413184 | tf_op jit(solution)/shard_map/dot_general | solution.py:110
  297.7 61.1 %all-gather.11.cloned.1.call-done = bf16[8,704,256]{2,1,0:T(8,128)(2,1)} async-done(((bf16[4,704,256]{2,1,0:T(8,128)(2,1)}), bf16[8,704,256]{2,1,0:T(8,128)(2,1)}) %all-gather.11.cloned.1.call-update) | async-done | bytes 2883600 | tf_op jit(solution)/shard_map/all_gather | solution.py:56
  358.8 11.1 %convolution_convert_fusion.1 = bf16[800,2,4,256]{3,0,2,1:T(8,128)(2,1)} fusion(bf16[2,4,704,256]{3,2,1,0:T(8,128)(2,1)} %bitcast.81, bf16[800,2048]{1,0:T(8,128)(2,1)S(1)} %reshape.88, bf16[2048,704]{0,1:T(8,128)(2,1)} %bitcast.75, f32[800,704]{1,0:T(8,128)} %fusion.29), kind=kOutput, calls=%fused_computation.8 | convolution fusion | flops 4618188800 | bytes 14573568 | tf_op jit(solution)/shard_map/rh,abhd->rabd/dot_general | solution.py:113
  370.0 4.5 %copy.66 = bf16[800,2,4,256]{3,2,1,0:T(4,128)(2,1)S(1)} copy(bf16[800,2,4,256]{3,0,2,1:T(8,128)(2,1)} %convolution_convert_fusion.1) | data formatting | bytes 6553600 | tf_op jit(solution)/shard_map/convert_element_type | solution.py:115
  374.4 3.4 reshape.91
  377.9 5.9 %all-to-all-start.4 = ((bf16[16,50,2048]{2,1,0:T(8,128)(2,1)}), bf16[16,50,2048]{2,1,0:T(8,128)(2,1)}, u32[]{:S(2)}, u32[]{:S(2)}) async-start(bf16[16,50,2048]{2,1,0:T(8,128)(2,1)} %reshape.91), calls=%async_computation.4 | async-start | bytes 7340032 | tf_op jit(solution)/shard_map/all_to_all | solution.py:117
  383.8 1.0 select_reduce_fusion
  384.9 45.3 %all-to-all-done.4 = bf16[16,50,2048]{2,1,0:T(8,128)(2,1)} async-done(((bf16[16,50,2048]{2,1,0:T(8,128)(2,1)}), bf16[16,50,2048]{2,1,0:T(8,128)(2,1)}, u32[]{:S(2)}, u32[]{:S(2)}) %all-to-all-start.4) | async-done | bytes 3276832 | tf_op jit(solution)/shard_map/all_to_all | solution.py:117
  430.2 3.2 reshape.92
  433.4 3.8 fusion.2
  (39 shorter events, 0.7 us)
Async XLA Ops:
  6.5 3.9 copy-start.3
  6.5 4.2 copy-start.4
  6.5 44.2 %all-to-all-start.1 = ((bf16[4,256,704]{1,2,0:T(8,128)(2,1)}), bf16[4,256,704]{1,2,0:T(8,128)(2,1)S(1)}, u32[]{:S(2)}, u32[]{:S(2)}) async-start(bf16[4,256,704]{1,2,0:T(8,128)(2,1)} %param.21), calls=%async_computation.1 | async-start | bytes 2883584 | tf_op jit(solution)/shard_map/all_to_all | solution.py:55
  11.4 43.9 %collective-permute-start = (f32[16,128,128]{2,1,0:T(8,128)S(1)}, f32[16,128,128]{2,1,0:T(8,128)}, u32[]{:S(2)}, u32[]{:S(2)}) collective-permute-start(f32[16,128,128]{2,1,0:T(8,128)S(1)} %fusion.17), channel_id=1, source_target_pairs={{0,4},{4,8},{8,12},{12,16},{16,20},{20,24},{24,28},{1,5},{5,9},{9,... | collective-permute-start | bytes 3145736 | tf_op jit(solution)/shard_map/ppermute | solution.py:18
  50.7 6.8 %copy-start.1 = (bf16[4,256,704]{1,2,0:T(8,128)(2,1)}, bf16[4,256,704]{1,2,0:T(8,128)(2,1)S(1)}, u32[]{:S(2)}) copy-start(bf16[4,256,704]{1,2,0:T(8,128)(2,1)S(1)} %all-to-all-done.1) | copy-start | bytes 4325380
  50.7 10.7 %copy-start.9 = (s32[1,128,6]{1,0,2:T(1,128)S(1)}, s32[1,128,6]{1,0,2:T(1,128)}, u32[]{:S(2)}) copy-start(s32[1,128,6]{1,0,2:T(1,128)} %param.19) | copy-start | bytes 9220
  50.7 50.6 %all-to-all-start.2 = ((bf16[4,256,704]{1,2,0:T(8,128)(2,1)}), bf16[4,256,704]{1,2,0:T(8,128)(2,1)}, u32[]{:S(2)}, u32[]{:S(2)}) async-start(bf16[4,256,704]{1,2,0:T(8,128)(2,1)} %param.22), calls=%async_computation.2 | async-start | bytes 2883584 | tf_op jit(solution)/shard_map/all_to_all | solution.py:55
  57.6 35.4 %collective-permute-start.1 = (f32[16,128,128]{2,1,0:T(8,128)}, f32[16,128,128]{2,1,0:T(8,128)}, u32[]{:S(2)}, u32[]{:S(2)}) collective-permute-start(f32[16,128,128]{2,1,0:T(8,128)} %add.59), channel_id=1, source_target_pairs={{0,8},{4,12},{8,16},{12,20},{16,24},{20,28},{1,9},{5,13},{9,17},{1... | collective-permute-start | bytes 3145736 | tf_op jit(solution)/shard_map/ppermute | solution.py:18
  61.4 35.6 %copy-start.5 = (bf16[1,128,2048]{2,1,0:T(8,128)(2,1)S(1)}, bf16[1,128,2048]{2,1,0:T(8,128)(2,1)}, u32[]{:S(2)}) copy-start(bf16[1,128,2048]{2,1,0:T(8,128)(2,1)} %param.12) | copy-start | bytes 1572868
  95.6 31.6 %collective-permute-start.2 = (f32[16,128,128]{2,1,0:T(8,128)}, f32[16,128,128]{2,1,0:T(8,128)}, u32[]{:S(2)}, u32[]{:S(2)}) collective-permute-start(f32[16,128,128]{2,1,0:T(8,128)} %add.60), channel_id=1, source_target_pairs={{0,16},{4,20},{8,24},{12,28},{1,17},{5,21},{9,25},{13,29},{2,18},{... | collective-permute-start | bytes 3145736 | tf_op jit(solution)/shard_map/ppermute | solution.py:18
  101.3 25.8 %copy-start.2 = (f32[128,16,128]{0,2,1:T(8,128)S(1)}, f32[128,16,128]{0,2,1:T(8,128)}, u32[]{:S(2)}) copy-start(f32[128,16,128]{0,2,1:T(8,128)} %convolution_bitcast_fusion) | copy-start | bytes 3145732
  101.3 34.6 %all-to-all-start.3 = ((bf16[4,704,256]{2,1,0:T(8,128)(2,1)}), bf16[4,704,256]{2,1,0:T(8,128)(2,1)}, u32[]{:S(2)}, u32[]{:S(2)}) async-start(bf16[4,704,256]{2,1,0:T(8,128)(2,1)} %param.23), calls=%async_computation.3 | async-start | bytes 2883584 | tf_op jit(solution)/shard_map/all_to_all | solution.py:55
  106.4 105.0 %all-gather.7.cloned.1.call-start = ((), (), s32[]{:S(2)}) async-start(), calls=%async_computation.5 | async-start | bytes 4325376 | tf_op jit(solution)/shard_map/all_gather | solution.py:56
  130.1 1.0 copy-start.6
  130.1 1.0 copy-start.7
  130.3 1.9 copy-start.8
  131.3 0.8 copy-start
  135.9 152.6 %all-to-all-start = ((bf16[16,50,2048]{2,1,0:T(8,128)(2,1)}), bf16[16,50,2048]{2,1,0:T(8,128)(2,1)}, u32[]{:S(2)}, u32[]{:S(2)}) async-start(bf16[16,50,2048]{2,1,0:T(8,128)(2,1)} %reshape.87), calls=%async_computation | async-start | bytes 7340032 | tf_op jit(solution)/shard_map/all_to_all | solution.py:108
  209.9 74.8 %all-gather.9.cloned.1.call-start = ((), (), s32[]{:S(2)}) async-start(), calls=%async_computation.6 | async-start | bytes 4325376 | tf_op jit(solution)/shard_map/all_gather | solution.py:56
  210.6 148.2 %all-gather.11.cloned.1.call-start = ((), (), s32[]{:S(2)}) async-start(), calls=%async_computation.7 | async-start | bytes 4325376 | tf_op jit(solution)/shard_map/all_gather | solution.py:56
  377.9 6.0 %copy-start.10 = (f32[1,128,6]{1,0,2:T(1,128)S(1)}, f32[1,128,6]{1,0,2:T(1,128)}, u32[]{:S(2)}) copy-start(f32[1,128,6]{1,0,2:T(1,128)} %param.20) | copy-start | bytes 9220
  377.9 52.4 %all-to-all-start.4 = ((bf16[16,50,2048]{2,1,0:T(8,128)(2,1)}), bf16[16,50,2048]{2,1,0:T(8,128)(2,1)}, u32[]{:S(2)}, u32[]{:S(2)}) async-start(bf16[16,50,2048]{2,1,0:T(8,128)(2,1)} %reshape.91), calls=%async_computation.4 | async-start | bytes 7340032 | tf_op jit(solution)/shard_map/all_to_all | solution.py:117
Sparse Core Ops, SparseCore 0:
  108.7 74.6 all-gather.6
  212.3 72.3 all-gather.8
  286.2 72.5 all-gather.10

commit v17 on v16

--- a/solution.py
+++ b/solution.py
@@ -105,6 +105,9 @@
             "ts,td->sd", chosen, ffn_in, preferred_element_type=jnp.float32
         ).astype(jnp.bfloat16)
         outgoing = outgoing.reshape(EXPERTS, CAP, D)
+        outgoing, whole_gate, whole_up, whole_down = lax.optimization_barrier(
+            (outgoing, whole_gate, whole_up, whole_down)
+        )
         arrived = lax.all_to_all(outgoing, group, 0, 0, tiled=True)
         arrived = arrived.reshape(EXPERTS * CAP, D)
         gate_sum = jnp.dot(arrived, whole_gate, preferred_element_type=jnp.float32)

time: 448 us -> 467 us (1.042)
  blocking collectives: 0 us -> 104 us
  starting transfers between devices: 103 us -> 15.1 us
  waiting for transfers between devices: 264 us -> 255 us
  other arithmetic: 8.71 us -> 14 us
  local copies, waits for them, and re-layouts: 27.4 us -> 32.5 us
    all_to_all x0 -> x3, blocking collectives: none -> 104 us  [the longest x2 55.2 us: collect(): mine = lax.all_to_all(weight, 'seq_lo', 0, 0, tiled=False)]
    ppermute x3, waiting for transfers between devices: 51.3 us -> 137 us  [carried_in(): lax.ppermute(total, axis, [(i, i + shift) for i in range(count - shift)])]
    all_to_all x1 -> x0, starting transfers between devices: 73.9 us -> none  [shards(): arrived = lax.all_to_all(outgoing, group, 0, 0, tiled=True)]
    all_gather x3, waiting for transfers between devices: 131 us -> 73.6 us  [collect(): return lax.all_gather(mine, 'seq_hi', axis=0, tiled=False)]
    all_to_all x3 -> x1, waiting for transfers between devices: 35.4 us -> 0.01 us  [collect(): mine = lax.all_to_all(weight, 'seq_lo', 0, 0, tiled=False)]
    all_to_all x3 -> x1, starting transfers between devices: 13.4 us -> 3.56 us  [collect(): mine = lax.all_to_all(weight, 'seq_lo', 0, 0, tiled=False)]
  transfers between devices with their start and end apart: 11 -> 8, of which waited for: 6 -> 5; matrix products, arithmetic and copies ran while one was open for 8% -> 8% of each run, Pallas kernels for 0% -> 0%
where the time goes in v17:
time: 467 us; the launch traced here: 462 us
  waiting for transfers between devices  255 us (55%)
  blocking collectives  104 us (22%)
  local copies, waits for them, and re-layouts  32.5 us (7%)
  matrix products  27.7 us (6%)
  starting transfers between devices  15.1 us (3%)
  other arithmetic  14 us (3%)
  between operations  13.4 us (3%)
    ppermute x3, waiting for transfers between devices, carried_in(): lax.ppermute(total, axis, [(i, i + shift) for i in range(count - shift)])  137 us
    all_gather x3, waiting for transfers between devices, collect(): return lax.all_gather(mine, 'seq_hi', axis=0, tiled=False)  73.6 us
    all_to_all x2, blocking collectives, collect(): mine = lax.all_to_all(weight, 'seq_lo', 0, 0, tiled=False)  55.2 us
    all_to_all x1, blocking collectives, shards(): arrived = lax.all_to_all(outgoing, group, 0, 0, tiled=True)  49.1 us
    all_to_all x1, waiting for transfers between devices, shards(): returned = lax.all_to_all(expert_rows, group, 0, 0, tiled=True)  45 us
    dot_general x1, matrix products, shards(): jnp.einsum('rh,abhd->rabd', hidden, whole_down, preferred_element_type=jn...  11.1 us
  transfers between devices with their start and end apart: 8, of which 5 were waited for; matrix products, arithmetic and copies ran while one was open for 8% of the time, Pallas kernels for 0%

profile of v17, /device:TPU:16, one launch (start us, length us, event | category | flops | bytes accessed | tf_op | source)
XLA Modules:
  0.0 462.1 jit_solution(10886275962124659744)
XLA Ops:
  6.5 23.1 %all_to_all.25 = bf16[4,256,704]{1,2,0:T(8,128)(2,1)} all-to-all(bf16[4,256,704]{1,2,0:T(8,128)(2,1)} %param.21), channel_id=1, replica_groups=mesh['seq_hi'=2,'seq_lo'=4,'ep'=4] {'seq_lo'}, dimensions={0} | all-to-all | bytes 2883584 | tf_op jit(solution)/shard_map/all_to_all | solution.py:55
  29.8 32.1 %all_to_all.26 = bf16[4,256,704]{1,2,0:T(8,128)(2,1)} all-to-all(bf16[4,256,704]{1,2,0:T(8,128)(2,1)S(1)} %copy-done.2), channel_id=1, replica_groups=mesh['seq_hi'=2,'seq_lo'=4,'ep'=4] {'seq_lo'}, dimensions={0} | all-to-all | bytes 2883584 | tf_op jit(solution)/shard_map/all_to_all | solution.py:55
  61.9 0.3 copy.70
  62.3 0.5 fusion.17
  62.8 3.4 collective-permute-start
  66.2 3.6 all-to-all-start.2
  69.8 54.7 %collective-permute-done = f32[16,128,128]{2,1,0:T(8,128)} collective-permute-done((f32[16,128,128]{2,1,0:T(8,128)S(1)}, f32[16,128,128]{2,1,0:T(8,128)}, u32[]{:S(2)}, u32[]{:S(2)}) %collective-permute-start) | collective-permute-done | bytes 1048608 | tf_op jit(solution)/shard_map/ppermute | solution.py:18
  124.5 2.3 add.59
  126.8 1.9 collective-permute-start.1
  128.8 0.7 copy.59
  129.5 1.0 eq.42
  130.5 74.9 %collective-permute-done.1 = f32[16,128,128]{2,1,0:T(8,128)} collective-permute-done((f32[16,128,128]{2,1,0:T(8,128)}, f32[16,128,128]{2,1,0:T(8,128)}, u32[]{:S(2)}, u32[]{:S(2)}) %collective-permute-start.1) | collective-permute-done | bytes 1048608 | tf_op jit(solution)/shard_map/ppermute | solution.py:18
  205.4 2.6 add.60
  208.0 1.3 collective-permute-start.2
  209.3 0.6 fusion.26
  209.9 1.0 eq.38
  210.9 4.1 reduce-window.6
  215.0 1.0 slice_reduce_fusion
  216.1 1.1 copy-done.1
  217.2 0.9 fusion.25
  218.1 1.1 copy.75
  219.3 0.1 reduce_sum.40
  219.4 0.9 bitcast_add_fusion.2
  220.4 1.0 fusion
  221.4 1.8 convolution_bitcast_fusion
  223.2 6.9 %collective-permute-done.2 = f32[16,128,128]{2,1,0:T(8,128)} collective-permute-done((f32[16,128,128]{2,1,0:T(8,128)}, f32[16,128,128]{2,1,0:T(8,128)}, u32[]{:S(2)}, u32[]{:S(2)}) %collective-permute-start.2) | collective-permute-done | bytes 1048608 | tf_op jit(solution)/shard_map/ppermute | solution.py:18
  230.2 3.3 multiply_reduce_fusion
  233.6 0.3 copy.58
  233.9 0.6 copy-done.6
  234.5 0.1 fusion.9
  234.7 0.2 fusion.6
  234.9 0.6 copy-done
  235.5 1.1 convolution_convert_fusion
  236.5 2.7 reshape.87
  239.2 3.8 copy.72
  243.0 3.8 copy.73
  246.8 73.6 %all-gather.11.cloned.1.call-done = bf16[8,704,256]{2,1,0:T(8,128)(2,1)} async-done(((bf16[4,704,256]{2,1,0:T(8,128)(2,1)}), bf16[8,704,256]{2,1,0:T(8,128)(2,1)}) %all-gather.11.cloned.1.call-update) | async-done | bytes 2883600 | tf_op jit(solution)/shard_map/all_gather | solution.py:56
  320.3 49.1 %all_to_all.27 = bf16[16,50,2048]{2,1,0:T(8,128)(2,1)} all-to-all(bf16[16,50,2048]{2,1,0:T(8,128)(2,1)} %reshape.87), channel_id=1, replica_groups=mesh['seq_hi'=2,'seq_lo'=4,'ep'=4] {'ep','seq_lo'}, dimensions={0} | all-to-all | bytes 6553600 | tf_op jit(solution)/shard_map/all_to_all | solution.py:111
  369.4 3.2 reshape.90
  372.6 6.0 %fusion.29 = f32[800,704]{1,0:T(8,128)} fusion(bf16[800,2048]{1,0:T(8,128)(2,1)S(1)} %reshape.90, bf16[2048,704]{0,1:T(8,128)(2,1)} %bitcast.75), kind=kOutput, calls=%fused_computation.51 | convolution fusion | flops 2306867200 | bytes 8413184 | tf_op jit(solution)/shard_map/dot_general | solution.py:113
  378.7 11.1 %convolution_convert_fusion.1 = bf16[800,2,4,256]{3,0,2,1:T(8,128)(2,1)} fusion(bf16[2,4,704,256]{3,2,1,0:T(8,128)(2,1)} %bitcast.81, bf16[800,2048]{1,0:T(8,128)(2,1)S(1)} %reshape.90, bf16[2048,704]{0,1:T(8,128)(2,1)} %bitcast.76, f32[800,704]{1,0:T(8,128)} %fusion.29), kind=kOutput, calls=%fused_computation.8 | convolution fusion | flops 4618188800 | bytes 14573568 | tf_op jit(solution)/shard_map/rh,abhd->rabd/dot_general | solution.py:116
  389.8 4.5 copy.66
  394.2 3.4 reshape.91
  397.7 4.9 %all-to-all-start.4 = ((bf16[16,50,2048]{2,1,0:T(8,128)(2,1)}), bf16[16,50,2048]{2,1,0:T(8,128)(2,1)}, u32[]{:S(2)}, u32[]{:S(2)}) async-start(bf16[16,50,2048]{2,1,0:T(8,128)(2,1)} %reshape.91), calls=%async_computation.4 | async-start | bytes 7340032 | tf_op jit(solution)/shard_map/all_to_all | solution.py:120
  402.6 1.0 select_reduce_fusion
  403.6 45.0 %all-to-all-done.4 = bf16[16,50,2048]{2,1,0:T(8,128)(2,1)} async-done(((bf16[16,50,2048]{2,1,0:T(8,128)(2,1)}), bf16[16,50,2048]{2,1,0:T(8,128)(2,1)}, u32[]{:S(2)}, u32[]{:S(2)}) %all-to-all-start.4) | async-done | bytes 3276832 | tf_op jit(solution)/shard_map/all_to_all | solution.py:120
  448.6 3.2 reshape.92
  451.8 3.8 fusion.2
  (36 shorter events, 0.5 us)
Async XLA Ops:
  6.5 23.2 %copy-start.2 = (bf16[4,256,704]{1,2,0:T(8,128)(2,1)S(1)}, bf16[4,256,704]{1,2,0:T(8,128)(2,1)}, u32[]{:S(2)}) copy-start(bf16[4,256,704]{1,2,0:T(8,128)(2,1)} %param.22) | copy-start | bytes 4325380
  6.5 232.7 %all-gather.7.cloned.1.call-start = ((), (), s32[]{:S(2)}) async-start(), calls=%async_computation.5 | async-start | bytes 4325376 | tf_op jit(solution)/shard_map/all_gather | solution.py:56
  29.7 32.2 %copy-start.4 = (bf16[1,128,2048]{2,1,0:T(8,128)(2,1)S(1)}, bf16[1,128,2048]{2,1,0:T(8,128)(2,1)}, u32[]{:S(2)}) copy-start(bf16[1,128,2048]{2,1,0:T(8,128)(2,1)} %param.14) | copy-start | bytes 1572868
  29.7 32.4 %copy-start.5 = (bf16[1,128,2048]{2,1,0:T(8,128)(2,1)S(1)}, bf16[1,128,2048]{2,1,0:T(8,128)(2,1)}, u32[]{:S(2)}) copy-start(bf16[1,128,2048]{2,1,0:T(8,128)(2,1)} %param.13) | copy-start | bytes 1572868
  29.7 213.2 %all-gather.9.cloned.1.call-start = ((), (), s32[]{:S(2)}) async-start(), calls=%async_computation.6 | async-start | bytes 4325376 | tf_op jit(solution)/shard_map/all_gather | solution.py:56
  62.8 66.0 %copy-start.9 = (s32[1,128,6]{1,0,2:T(1,128)S(1)}, s32[1,128,6]{1,0,2:T(1,128)}, u32[]{:S(2)}) copy-start(s32[1,128,6]{1,0,2:T(1,128)} %param.19) | copy-start | bytes 9220
  62.8 61.7 %collective-permute-start = (f32[16,128,128]{2,1,0:T(8,128)S(1)}, f32[16,128,128]{2,1,0:T(8,128)}, u32[]{:S(2)}, u32[]{:S(2)}) collective-permute-start(f32[16,128,128]{2,1,0:T(8,128)S(1)} %fusion.17), channel_id=1, source_target_pairs={{0,4},{4,8},{8,12},{12,16},{16,20},{20,24},{24,28},{1,5},{5,9},{9,... | collective-permute-start | bytes 3145736 | tf_op jit(solution)/shard_map/ppermute | solution.py:18
  66.2 149.9 %all-to-all-start.2 = ((bf16[4,704,256]{2,1,0:T(8,128)(2,1)}), bf16[4,704,256]{2,1,0:T(8,128)(2,1)S(1)}, u32[]{:S(2)}, u32[]{:S(2)}) async-start(bf16[4,704,256]{2,1,0:T(8,128)(2,1)} %param.23), calls=%async_computation.2 | async-start | bytes 2883584 | tf_op jit(solution)/shard_map/all_to_all | solution.py:55
  69.8 250.5 %all-gather.11.cloned.1.call-start = ((), (), s32[]{:S(2)}) async-start(), calls=%async_computation.7 | async-start | bytes 4325376 | tf_op jit(solution)/shard_map/all_gather | solution.py:56
  126.8 78.5 %collective-permute-start.1 = (f32[16,128,128]{2,1,0:T(8,128)}, f32[16,128,128]{2,1,0:T(8,128)}, u32[]{:S(2)}, u32[]{:S(2)}) collective-permute-start(f32[16,128,128]{2,1,0:T(8,128)} %add.59), channel_id=1, source_target_pairs={{0,8},{4,12},{8,16},{12,20},{16,24},{20,28},{1,9},{5,13},{9,17},{1... | collective-permute-start | bytes 3145736 | tf_op jit(solution)/shard_map/ppermute | solution.py:18
  208.0 22.2 %collective-permute-start.2 = (f32[16,128,128]{2,1,0:T(8,128)}, f32[16,128,128]{2,1,0:T(8,128)}, u32[]{:S(2)}, u32[]{:S(2)}) collective-permute-start(f32[16,128,128]{2,1,0:T(8,128)} %add.60), channel_id=1, source_target_pairs={{0,16},{4,20},{8,24},{12,28},{1,17},{5,21},{9,25},{13,29},{2,18},{... | collective-permute-start | bytes 3145736 | tf_op jit(solution)/shard_map/ppermute | solution.py:18
  216.1 1.1 copy-start.1
  233.5 1.0 copy-start.6
  233.5 1.0 copy-start.7
  233.6 1.9 copy-start.3
  233.6 1.9 copy-start.8
  234.7 0.8 copy-start
  397.7 4.9 %copy-start.10 = (f32[1,128,6]{1,0,2:T(1,128)S(1)}, f32[1,128,6]{1,0,2:T(1,128)}, u32[]{:S(2)}) copy-start(f32[1,128,6]{1,0,2:T(1,128)} %param.20) | copy-start | bytes 9220
  397.7 50.9 %all-to-all-start.4 = ((bf16[16,50,2048]{2,1,0:T(8,128)(2,1)}), bf16[16,50,2048]{2,1,0:T(8,128)(2,1)}, u32[]{:S(2)}, u32[]{:S(2)}) async-start(bf16[16,50,2048]{2,1,0:T(8,128)(2,1)} %reshape.91), calls=%async_computation.4 | async-start | bytes 7340032 | tf_op jit(solution)/shard_map/all_to_all | solution.py:120
Sparse Core Ops, SparseCore 0:
  29.8 70.3 all-gather.6
  101.8 93.2 all-gather.8
  217.4 102.9 all-gather.10

commit v18 on v16

--- a/solution.py
+++ b/solution.py
@@ -110,8 +110,9 @@
         gate_sum = jnp.dot(arrived, whole_gate, preferred_element_type=jnp.float32)
         up_sum = jnp.dot(arrived, whole_up, preferred_element_type=jnp.float32)
         hidden = silu_gate(gate_sum, up_sum).astype(jnp.bfloat16)
-        expert_rows = jnp.einsum(
-            "rh,abhd->rabd", hidden, whole_down, preferred_element_type=jnp.float32
+        down_rows = jnp.transpose(whole_down, (2, 0, 1, 3)).reshape(whole_down.shape[2], D)
+        expert_rows = jnp.dot(
+            hidden, down_rows, preferred_element_type=jnp.float32
         ).astype(jnp.bfloat16)
         expert_rows = expert_rows.reshape(EXPERTS, CAP, D)
         returned = lax.all_to_all(expert_rows, group, 0, 0, tiled=True)

time: 448 us -> 459 us (1.025)
  waiting for transfers between devices: 264 us -> 278 us
  starting transfers between devices: 103 us -> 95.7 us
    ppermute x3, waiting for transfers between devices: 51.3 us -> 60.1 us  [carried_in(): lax.ppermute(total, axis, [(i, i + shift) for i in range(count - shift)])]
    all_to_all x1, starting transfers between devices: 73.9 us -> 67 us  [shards(): arrived = lax.all_to_all(outgoing, group, 0, 0, tiled=True)]
    all_gather x3, waiting for transfers between devices: 131 us -> 136 us  [collect(): return lax.all_gather(mine, 'seq_hi', axis=0, tiled=False)]
where the time goes in v18:
time: 459 us; the launch traced here: 455 us
  waiting for transfers between devices  278 us (61%)
  starting transfers between devices  95.7 us (21%)
  local copies, waits for them, and re-layouts  31.6 us (7%)
  matrix products  27.3 us (6%)
  between operations  13.4 us (3%)
  other arithmetic  8.82 us (2%)
    all_gather x3, waiting for transfers between devices, collect(): return lax.all_gather(mine, 'seq_hi', axis=0, tiled=False)  136 us
    all_to_all x1, starting transfers between devices, shards(): arrived = lax.all_to_all(outgoing, group, 0, 0, tiled=True)  67 us
    ppermute x3, waiting for transfers between devices, carried_in(): lax.ppermute(total, axis, [(i, i + shift) for i in range(count - shift)])  60.1 us
    all_to_all x1, waiting for transfers between devices, shards(): returned = lax.all_to_all(expert_rows, group, 0, 0, tiled=True)  45.3 us
    all_to_all x3, waiting for transfers between devices, collect(): mine = lax.all_to_all(weight, 'seq_lo', 0, 0, tiled=False)  35.4 us
    all_to_all x3, starting transfers between devices, collect(): mine = lax.all_to_all(weight, 'seq_lo', 0, 0, tiled=False)  13.4 us
    dot_general x1, matrix products, shards(): jnp.dot(hidden, down_rows, preferred_element_type=jnp.float32)  11.2 us
  transfers between devices with their start and end apart: 11, of which 6 were waited for; matrix products, arithmetic and copies ran while one was open for 8% of the time, Pallas kernels for 0%

profile of v18, /device:TPU:16, one launch (start us, length us, event | category | flops | bytes accessed | tf_op | source)
XLA Modules:
  0.0 455.2 jit_solution(18138249846143941738)
XLA Ops:
  6.5 3.9 all-to-all-start.1
  10.4 0.3 copy.69
  10.8 0.5 fusion.16
  11.4 3.9 collective-permute-start
  15.3 35.4 %all-to-all-done.1 = bf16[4,256,704]{1,2,0:T(8,128)(2,1)S(1)} async-done(((bf16[4,256,704]{1,2,0:T(8,128)(2,1)}), bf16[4,256,704]{1,2,0:T(8,128)(2,1)S(1)}, u32[]{:S(2)}, u32[]{:S(2)}) %all-to-all-start.1) | async-done | bytes 1441824 | tf_op jit(solution)/shard_map/all_to_all | solution.py:55
  50.7 4.5 all-to-all-start.3
  55.3 2.4 add.59
  57.7 3.8 collective-permute-start.1
  61.5 0.1 copy.59
  61.6 0.1 eq.42
  61.8 31.2 %collective-permute-done.1 = f32[16,128,128]{2,1,0:T(8,128)} collective-permute-done((f32[16,128,128]{2,1,0:T(8,128)}, f32[16,128,128]{2,1,0:T(8,128)}, u32[]{:S(2)}, u32[]{:S(2)}) %collective-permute-start.1) | collective-permute-done | bytes 1048608 | tf_op jit(solution)/shard_map/ppermute | solution.py:18
  92.9 2.7 add.60
  95.6 1.3 collective-permute-start.2
  96.9 0.1 eq.38
  97.2 1.7 reduce-window.6
  98.9 0.3 slice_reduce_fusion
  99.3 0.1 reduce_sum.40
  99.6 1.8 convolution_bitcast_fusion
  101.4 5.0 %all-to-all-start.2 = ((bf16[4,256,704]{1,2,0:T(8,128)(2,1)}), bf16[4,256,704]{1,2,0:T(8,128)(2,1)}, u32[]{:S(2)}, u32[]{:S(2)}) async-start(bf16[4,256,704]{1,2,0:T(8,128)(2,1)} %param.22), calls=%async_computation.2 | async-start | bytes 2883584 | tf_op jit(solution)/shard_map/all_to_all | solution.py:55
  106.4 0.4 fusion
  106.8 28.9 %collective-permute-done.2 = f32[16,128,128]{2,1,0:T(8,128)} collective-permute-done((f32[16,128,128]{2,1,0:T(8,128)}, f32[16,128,128]{2,1,0:T(8,128)}, u32[]{:S(2)}, u32[]{:S(2)}) %collective-permute-start.2) | collective-permute-done | bytes 1048608 | tf_op jit(solution)/shard_map/ppermute | solution.py:18
  135.8 3.0 multiply_reduce_fusion
  138.9 0.3 copy.58
  139.2 0.6 copy-done.6
  139.8 0.1 fusion.8
  139.9 0.2 fusion.5
  140.1 0.6 copy-done
  140.7 1.1 convolution_convert_fusion
  141.8 2.7 reshape.90
  144.5 67.0 %all-to-all-start = ((bf16[16,50,2048]{2,1,0:T(8,128)(2,1)}), bf16[16,50,2048]{2,1,0:T(8,128)(2,1)}, u32[]{:S(2)}, u32[]{:S(2)}) async-start(bf16[16,50,2048]{2,1,0:T(8,128)(2,1)} %reshape.90), calls=%async_computation | async-start | bytes 7340032 | tf_op jit(solution)/shard_map/all_to_all | solution.py:108
  211.6 0.7 all-gather.11.cloned.1.call-update
  212.3 0.2 all-gather.9.cloned.1.call-start
  212.5 0.5 all-gather.9.cloned.1.call-update
  213.1 3.8 copy.71
  216.9 69.4 %all-gather.11.cloned.1.call-done = bf16[8,704,256]{2,1,0:T(8,128)(2,1)} async-done(((bf16[4,704,256]{2,1,0:T(8,128)(2,1)}), bf16[8,704,256]{2,1,0:T(8,128)(2,1)}) %all-gather.11.cloned.1.call-update) | async-done | bytes 2883600 | tf_op jit(solution)/shard_map/all_gather | solution.py:56
  286.4 4.0 copy.90
  290.4 3.4 reshape.94
  293.8 66.8 %all-gather.9.cloned.1.call-done = bf16[8,256,704]{1,2,0:T(8,128)(2,1)} async-done(((bf16[4,256,704]{1,2,0:T(8,128)(2,1)}), bf16[8,256,704]{1,2,0:T(8,128)(2,1)}) %all-gather.9.cloned.1.call-update) | async-done | bytes 2883600 | tf_op jit(solution)/shard_map/all_gather | solution.py:56
  360.5 3.8 copy.72
  364.3 3.2 reshape.91
  367.5 6.0 %fusion.28 = f32[800,704]{1,0:T(8,128)} fusion(bf16[800,2048]{1,0:T(8,128)(2,1)S(1)} %reshape.91, bf16[2048,704]{0,1:T(8,128)(2,1)} %bitcast.74), kind=kOutput, calls=%fused_computation.51 | convolution fusion | flops 2306867200 | bytes 8413184 | tf_op jit(solution)/shard_map/dot_general | solution.py:110
  373.5 11.2 %convolution_convert_fusion.1 = bf16[800,2048]{1,0:T(8,128)(2,1)} fusion(bf16[704,2048]{1,0:T(8,128)(2,1)} %reshape.94, f32[800,704]{1,0:T(8,128)} %fusion.28, bf16[800,2048]{1,0:T(8,128)(2,1)S(1)} %reshape.91, bf16[2048,704]{0,1:T(8,128)(2,1)} %bitcast.75), kind=kOutput, calls=%fused_computation.1 | convolution fusion | flops 4618188800 | bytes 14573568 | tf_op jit(solution)/shard_map/dot_general | solution.py:114
  384.6 4.7 %reshape.95 = bf16[16,50,2048]{2,1,0:T(8,128)(2,1)} reshape(bf16[800,2048]{1,0:T(8,128)(2,1)} %convolution_convert_fusion.1) | data formatting | bytes 6553600 | tf_op jit(solution)/shard_map/reshape | solution.py:117
  389.3 6.0 %all-to-all-start.4 = ((bf16[16,50,2048]{2,1,0:T(8,128)(2,1)}), bf16[16,50,2048]{2,1,0:T(8,128)(2,1)}, u32[]{:S(2)}, u32[]{:S(2)}) async-start(bf16[16,50,2048]{2,1,0:T(8,128)(2,1)} %reshape.95), calls=%async_computation.4 | async-start | bytes 7340032 | tf_op jit(solution)/shard_map/all_to_all | solution.py:118
  395.3 1.0 select_reduce_fusion
  396.3 45.3 %all-to-all-done.4 = bf16[16,50,2048]{2,1,0:T(8,128)(2,1)} async-done(((bf16[16,50,2048]{2,1,0:T(8,128)(2,1)}), bf16[16,50,2048]{2,1,0:T(8,128)(2,1)}, u32[]{:S(2)}, u32[]{:S(2)}) %all-to-all-start.4) | async-done | bytes 3276832 | tf_op jit(solution)/shard_map/all_to_all | solution.py:118
  441.7 3.2 reshape.96
  444.8 3.8 fusion.2
  (40 shorter events, 0.7 us)
Async XLA Ops:
  6.5 3.9 copy-start.3
  6.5 4.2 copy-start.4
  6.5 44.2 %all-to-all-start.1 = ((bf16[4,256,704]{1,2,0:T(8,128)(2,1)}), bf16[4,256,704]{1,2,0:T(8,128)(2,1)S(1)}, u32[]{:S(2)}, u32[]{:S(2)}) async-start(bf16[4,256,704]{1,2,0:T(8,128)(2,1)} %param.21), calls=%async_computation.1 | async-start | bytes 2883584 | tf_op jit(solution)/shard_map/all_to_all | solution.py:55
  11.4 43.9 %collective-permute-start = (f32[16,128,128]{2,1,0:T(8,128)S(1)}, f32[16,128,128]{2,1,0:T(8,128)}, u32[]{:S(2)}, u32[]{:S(2)}) collective-permute-start(f32[16,128,128]{2,1,0:T(8,128)S(1)} %fusion.16), channel_id=1, source_target_pairs={{0,4},{4,8},{8,12},{12,16},{16,20},{20,24},{24,28},{1,5},{5,9},{9,... | collective-permute-start | bytes 3145736 | tf_op jit(solution)/shard_map/ppermute | solution.py:18
  50.7 6.9 %copy-start.1 = (bf16[4,256,704]{1,2,0:T(8,128)(2,1)}, bf16[4,256,704]{1,2,0:T(8,128)(2,1)S(1)}, u32[]{:S(2)}) copy-start(bf16[4,256,704]{1,2,0:T(8,128)(2,1)S(1)} %all-to-all-done.1) | copy-start | bytes 4325380
  50.7 10.7 %copy-start.9 = (s32[1,128,6]{1,0,2:T(1,128)S(1)}, s32[1,128,6]{1,0,2:T(1,128)}, u32[]{:S(2)}) copy-start(s32[1,128,6]{1,0,2:T(1,128)} %param.19) | copy-start | bytes 9220
  50.7 50.7 %all-to-all-start.3 = ((bf16[4,704,256]{2,1,0:T(8,128)(2,1)}), bf16[4,704,256]{2,1,0:T(8,128)(2,1)}, u32[]{:S(2)}, u32[]{:S(2)}) async-start(bf16[4,704,256]{2,1,0:T(8,128)(2,1)} %param.23), calls=%async_computation.3 | async-start | bytes 2883584 | tf_op jit(solution)/shard_map/all_to_all | solution.py:55
  55.2 157.9 %all-gather.7.cloned.1.call-start = ((), (), s32[]{:S(2)}) async-start(), calls=%async_computation.5 | async-start | bytes 4325376 | tf_op jit(solution)/shard_map/all_gather | solution.py:56
  57.7 35.3 %collective-permute-start.1 = (f32[16,128,128]{2,1,0:T(8,128)}, f32[16,128,128]{2,1,0:T(8,128)}, u32[]{:S(2)}, u32[]{:S(2)}) collective-permute-start(f32[16,128,128]{2,1,0:T(8,128)} %add.59), channel_id=1, source_target_pairs={{0,8},{4,12},{8,16},{12,20},{16,24},{20,28},{1,9},{5,13},{9,17},{1... | collective-permute-start | bytes 3145736 | tf_op jit(solution)/shard_map/ppermute | solution.py:18
  61.5 35.6 %copy-start.5 = (bf16[1,128,2048]{2,1,0:T(8,128)(2,1)S(1)}, bf16[1,128,2048]{2,1,0:T(8,128)(2,1)}, u32[]{:S(2)}) copy-start(bf16[1,128,2048]{2,1,0:T(8,128)(2,1)} %param.12) | copy-start | bytes 1572868
  95.6 40.1 %collective-permute-start.2 = (f32[16,128,128]{2,1,0:T(8,128)}, f32[16,128,128]{2,1,0:T(8,128)}, u32[]{:S(2)}, u32[]{:S(2)}) collective-permute-start(f32[16,128,128]{2,1,0:T(8,128)} %add.60), channel_id=1, source_target_pairs={{0,16},{4,20},{8,24},{12,28},{1,17},{5,21},{9,25},{13,29},{2,18},{... | collective-permute-start | bytes 3145736 | tf_op jit(solution)/shard_map/ppermute | solution.py:18
  101.4 34.4 %copy-start.2 = (f32[128,16,128]{0,2,1:T(8,128)S(1)}, f32[128,16,128]{0,2,1:T(8,128)}, u32[]{:S(2)}) copy-start(f32[128,16,128]{0,2,1:T(8,128)} %convolution_bitcast_fusion) | copy-start | bytes 3145732
  101.4 43.1 %all-to-all-start.2 = ((bf16[4,256,704]{1,2,0:T(8,128)(2,1)}), bf16[4,256,704]{1,2,0:T(8,128)(2,1)}, u32[]{:S(2)}, u32[]{:S(2)}) async-start(bf16[4,256,704]{1,2,0:T(8,128)(2,1)} %param.22), calls=%async_computation.2 | async-start | bytes 2883584 | tf_op jit(solution)/shard_map/all_to_all | solution.py:55
  138.7 1.0 copy-start.6
  138.7 1.0 copy-start.7
  138.9 1.9 copy-start.8
  139.9 0.8 copy-start
  144.5 219.8 %all-to-all-start = ((bf16[16,50,2048]{2,1,0:T(8,128)(2,1)}), bf16[16,50,2048]{2,1,0:T(8,128)(2,1)}, u32[]{:S(2)}, u32[]{:S(2)}) async-start(bf16[16,50,2048]{2,1,0:T(8,128)(2,1)} %reshape.90), calls=%async_computation | async-start | bytes 7340032 | tf_op jit(solution)/shard_map/all_to_all | solution.py:108
  211.6 74.8 %all-gather.11.cloned.1.call-start = ((), (), s32[]{:S(2)}) async-start(), calls=%async_computation.7 | async-start | bytes 4325376 | tf_op jit(solution)/shard_map/all_gather | solution.py:56
  212.3 148.2 %all-gather.9.cloned.1.call-start = ((), (), s32[]{:S(2)}) async-start(), calls=%async_computation.6 | async-start | bytes 4325376 | tf_op jit(solution)/shard_map/all_gather | solution.py:56
  389.3 6.0 %copy-start.10 = (f32[1,128,6]{1,0,2:T(1,128)S(1)}, f32[1,128,6]{1,0,2:T(1,128)}, u32[]{:S(2)}) copy-start(f32[1,128,6]{1,0,2:T(1,128)} %param.20) | copy-start | bytes 9220
  389.3 52.4 %all-to-all-start.4 = ((bf16[16,50,2048]{2,1,0:T(8,128)(2,1)}), bf16[16,50,2048]{2,1,0:T(8,128)(2,1)}, u32[]{:S(2)}, u32[]{:S(2)}) async-start(bf16[16,50,2048]{2,1,0:T(8,128)(2,1)} %reshape.95), calls=%async_computation.4 | async-start | bytes 7340032 | tf_op jit(solution)/shard_map/all_to_all | solution.py:118
Sparse Core Ops, SparseCore 0:
  99.7 75.2 all-gather.6
  214.0 72.3 all-gather.10
  287.9 72.5 all-gather.8

commit v19 on v16

--- a/solution.py
+++ b/solution.py
@@ -15,8 +15,10 @@
     total = array
     shift = 1
     while shift < count:
-        moved = lax.ppermute(total, axis, [(i, i + shift) for i in range(count - shift)])
-        total = total + moved
+        moved = lax.ppermute(
+            total.astype(jnp.bfloat16), axis, [(i, i + shift) for i in range(count - shift)]
+        )
+        total = total + moved.astype(jnp.float32)
         shift *= 2
     return total - array
 

time: 448 us -> 413 us (0.922)
  starting transfers between devices: 103 us -> 37.8 us
  waiting for transfers between devices: 264 us -> 285 us
    all_to_all x1, starting transfers between devices: 73.9 us -> 9.23 us  [shards(): arrived = lax.all_to_all(outgoing, group, 0, 0, tiled=True)]
    all_gather x3, waiting for transfers between devices: 131 us -> 190 us  [collect(): return lax.all_gather(mine, 'seq_hi', axis=0, tiled=False)]
    ppermute x3, waiting for transfers between devices: 51.3 us -> 21.4 us  [carried_in(): lax.ppermute(total.astype(jnp.bfloat16), axis, [(i, i + shift) for i in r...]
    all_to_all x3, waiting for transfers between devices: 35.4 us -> 27.5 us  [collect(): mine = lax.all_to_all(weight, 'seq_lo', 0, 0, tiled=False)]
    add x2 -> x0, other arithmetic: 4.97 us -> none  [carried_in(): total = total + moved]
  transfers between devices with their start and end apart: 11 -> 11, of which waited for: 6 -> 8; matrix products, arithmetic and copies ran while one was open for 8% -> 11% of each run, Pallas kernels for 0% -> 0%
where the time goes in v19:
time: 413 us; the launch traced here: 409 us
  waiting for transfers between devices  285 us (69%)
  starting transfers between devices  37.8 us (9%)
  local copies, waits for them, and re-layouts  30.5 us (7%)
  matrix products  29.3 us (7%)
  between operations  13.4 us (3%)
  other arithmetic  12.6 us (3%)
    all_gather x3, waiting for transfers between devices, collect(): return lax.all_gather(mine, 'seq_hi', axis=0, tiled=False)  190 us
    all_to_all x1, waiting for transfers between devices, shards(): returned = lax.all_to_all(expert_rows, group, 0, 0, tiled=True)  45.3 us
    all_to_all x3, waiting for transfers between devices, collect(): mine = lax.all_to_all(weight, 'seq_lo', 0, 0, tiled=False)  27.5 us
    ppermute x3, waiting for transfers between devices, carried_in(): lax.ppermute(total.astype(jnp.bfloat16), axis, [(i, i + shift) for i in r...  21.4 us
    all_to_all x3, starting transfers between devices, collect(): mine = lax.all_to_all(weight, 'seq_lo', 0, 0, tiled=False)  13.1 us
    dot_general x1, matrix products, shards(): jnp.einsum('rh,abhd->rabd', hidden, whole_down, preferred_element_type=jn...  11.1 us
    all_to_all x1, starting transfers between devices, shards(): arrived = lax.all_to_all(outgoing, group, 0, 0, tiled=True)  9.23 us
    ppermute x3, starting transfers between devices, carried_in(): lax.ppermute(total.astype(jnp.bfloat16), axis, [(i, i + shift) for i in r...  9.2 us
  transfers between devices with their start and end apart: 11, of which 8 were waited for; matrix products, arithmetic and copies ran while one was open for 11% of the time, Pallas kernels for 0%

profile of v19, /device:TPU:16, one launch (start us, length us, event | category | flops | bytes accessed | tf_op | source)
XLA Modules:
  0.0 408.7 jit_solution(9580520239785523287)
XLA Ops:
  6.5 3.9 all-to-all-start.1
  10.4 0.3 copy.70
  10.8 1.3 fusion.32
  12.2 4.1 collective-permute-start
  16.2 23.3 %all-to-all-done.1 = bf16[4,256,704]{1,2,0:T(8,128)(2,1)S(1)} async-done(((bf16[4,256,704]{1,2,0:T(8,128)(2,1)}), bf16[4,256,704]{1,2,0:T(8,128)(2,1)S(1)}, u32[]{:S(2)}, u32[]{:S(2)}) %all-to-all-start.1) | async-done | bytes 1441824 | tf_op jit(solution)/shard_map/all_to_all | solution.py:57
  39.5 4.3 %all-to-all-start.2 = ((bf16[4,256,704]{1,2,0:T(8,128)(2,1)}), bf16[4,256,704]{1,2,0:T(8,128)(2,1)}, u32[]{:S(2)}, u32[]{:S(2)}) async-start(bf16[4,256,704]{1,2,0:T(8,128)(2,1)} %param.22), calls=%async_computation.2 | async-start | bytes 2883584 | tf_op jit(solution)/shard_map/all_to_all | solution.py:57
  43.9 2.0 fusion.13
  45.8 3.9 collective-permute-start.1
  49.7 0.7 copy.59
  50.4 1.0 eq.42
  51.4 1.0 eq.38
  52.4 0.6 fusion.29
  53.0 4.1 %reduce-window.6 = s32[16,6,128]{2,0,1:T(8,128)} reduce-window(s32[16,6,128]{2,0,1:T(8,128)} %fusion.29, s32[]{:T(128)} %constant.8.clone.1), window={size=1x1x128 pad=0_0x0_0x127_0}, to_apply=%region_1.2 | reduce-window | flops 1560576 | bytes 98308 | tf_op jit(solution)/shard_map/reduce-window
  57.1 1.0 slice_reduce_fusion
  58.2 12.1 %collective-permute-done.1 = bf16[16,128,128]{2,1,0:T(8,128)(2,1)} collective-permute-done((bf16[16,128,128]{2,1,0:T(8,128)(2,1)}, bf16[16,128,128]{2,1,0:T(8,128)(2,1)}, u32[]{:S(2)}, u32[]{:S(2)}) %collective-permute-start.1) | collective-permute-done | bytes 524320 | tf_op jit(solution)/shard_map/ppermute | solution.py:18
  70.3 2.2 fusion.14
  72.5 1.3 collective-permute-start.2
  73.8 0.9 fusion.28
  75.0 0.8 bitcast_add_fusion.2
  75.9 0.4 fusion
  76.3 4.9 %all-to-all-start.3 = ((bf16[4,704,256]{2,1,0:T(8,128)(2,1)}), bf16[4,704,256]{2,1,0:T(8,128)(2,1)}, u32[]{:S(2)}, u32[]{:S(2)}) async-start(bf16[4,704,256]{2,1,0:T(8,128)(2,1)} %param.23), calls=%async_computation.3 | async-start | bytes 2883584 | tf_op jit(solution)/shard_map/all_to_all | solution.py:57
  81.3 9.3 %collective-permute-done.2 = bf16[16,128,128]{2,1,0:T(8,128)(2,1)} collective-permute-done((bf16[16,128,128]{2,1,0:T(8,128)(2,1)}, bf16[16,128,128]{2,1,0:T(8,128)(2,1)}, u32[]{:S(2)}, u32[]{:S(2)}) %collective-permute-start.2) | collective-permute-done | bytes 524320 | tf_op jit(solution)/shard_map/ppermute | solution.py:18
  90.5 3.9 convolution_bitcast_fusion.1
  94.4 2.1 multiply_reduce_fusion
  96.6 0.3 copy.58
  97.0 0.6 copy-done.5
  97.9 0.6 copy-done
  98.5 1.1 convolution_convert_fusion
  99.6 2.7 reshape.87
  102.3 4.2 %all-to-all-done.3 = bf16[4,704,256]{2,1,0:T(8,128)(2,1)} async-done(((bf16[4,704,256]{2,1,0:T(8,128)(2,1)}), bf16[4,704,256]{2,1,0:T(8,128)(2,1)}, u32[]{:S(2)}, u32[]{:S(2)}) %all-to-all-start.3) | async-done | bytes 1441824 | tf_op jit(solution)/shard_map/all_to_all | solution.py:57
  106.5 9.2 %all-to-all-start = ((bf16[16,50,2048]{2,1,0:T(8,128)(2,1)}), bf16[16,50,2048]{2,1,0:T(8,128)(2,1)}, u32[]{:S(2)}, u32[]{:S(2)}) async-start(bf16[16,50,2048]{2,1,0:T(8,128)(2,1)} %reshape.87), calls=%async_computation | async-start | bytes 7340032 | tf_op jit(solution)/shard_map/all_to_all | solution.py:110
  115.8 0.7 all-gather.9.cloned.1.call-update
  116.7 0.5 all-gather.11.cloned.1.call-update
  117.2 57.8 %all-gather.7.cloned.1.call-done = bf16[8,256,704]{1,2,0:T(8,128)(2,1)} async-done(((bf16[4,256,704]{1,2,0:T(8,128)(2,1)}), bf16[8,256,704]{1,2,0:T(8,128)(2,1)}) %all-gather.7.cloned.1.call-update) | async-done | bytes 2883600 | tf_op jit(solution)/shard_map/all_gather | solution.py:58
  175.0 3.8 copy.72
  178.8 70.6 %all-gather.9.cloned.1.call-done = bf16[8,256,704]{1,2,0:T(8,128)(2,1)} async-done(((bf16[4,256,704]{1,2,0:T(8,128)(2,1)}), bf16[8,256,704]{1,2,0:T(8,128)(2,1)}) %all-gather.9.cloned.1.call-update) | async-done | bytes 2883600 | tf_op jit(solution)/shard_map/all_gather | solution.py:58
  249.4 3.8 copy.73
  253.2 3.2 reshape.88
  256.4 6.0 %fusion.37 = f32[800,704]{1,0:T(8,128)} fusion(bf16[800,2048]{1,0:T(8,128)(2,1)S(1)} %reshape.88, bf16[2048,704]{0,1:T(8,128)(2,1)} %bitcast.74), kind=kOutput, calls=%fused_computation.57 | convolution fusion | flops 2306867200 | bytes 8413184 | tf_op jit(solution)/shard_map/dot_general | solution.py:112
  262.4 61.4 %all-gather.11.cloned.1.call-done = bf16[8,704,256]{2,1,0:T(8,128)(2,1)} async-done(((bf16[4,704,256]{2,1,0:T(8,128)(2,1)}), bf16[8,704,256]{2,1,0:T(8,128)(2,1)}) %all-gather.11.cloned.1.call-update) | async-done | bytes 2883600 | tf_op jit(solution)/shard_map/all_gather | solution.py:58
  323.8 11.1 %convolution_convert_fusion.1 = bf16[800,2,4,256]{3,0,2,1:T(8,128)(2,1)} fusion(bf16[2,4,704,256]{3,2,1,0:T(8,128)(2,1)} %bitcast.79, bf16[800,2048]{1,0:T(8,128)(2,1)S(1)} %reshape.88, bf16[2048,704]{0,1:T(8,128)(2,1)} %bitcast.73, f32[800,704]{1,0:T(8,128)} %fusion.37), kind=kOutput, calls=%fused_computation.8 | convolution fusion | flops 4618188800 | bytes 14573568 | tf_op jit(solution)/shard_map/rh,abhd->rabd/dot_general | solution.py:115
  334.9 4.5 %copy.66 = bf16[800,2,4,256]{3,2,1,0:T(4,128)(2,1)S(1)} copy(bf16[800,2,4,256]{3,0,2,1:T(8,128)(2,1)} %convolution_convert_fusion.1) | data formatting | bytes 6553600 | tf_op jit(solution)/shard_map/convert_element_type | solution.py:117
  339.4 3.4 reshape.91
  342.8 6.0 %all-to-all-start.4 = ((bf16[16,50,2048]{2,1,0:T(8,128)(2,1)}), bf16[16,50,2048]{2,1,0:T(8,128)(2,1)}, u32[]{:S(2)}, u32[]{:S(2)}) async-start(bf16[16,50,2048]{2,1,0:T(8,128)(2,1)} %reshape.91), calls=%async_computation.4 | async-start | bytes 7340032 | tf_op jit(solution)/shard_map/all_to_all | solution.py:119
  348.8 1.0 select_reduce_fusion
  349.8 45.3 %all-to-all-done.4 = bf16[16,50,2048]{2,1,0:T(8,128)(2,1)} async-done(((bf16[16,50,2048]{2,1,0:T(8,128)(2,1)}), bf16[16,50,2048]{2,1,0:T(8,128)(2,1)}, u32[]{:S(2)}, u32[]{:S(2)}) %all-to-all-start.4) | async-done | bytes 3276832 | tf_op jit(solution)/shard_map/all_to_all | solution.py:119
  395.2 3.2 reshape.92
  398.4 3.8 fusion.2
  (37 shorter events, 1.2 us)
Async XLA Ops:
  6.5 3.9 copy-start.2
  6.5 4.2 %copy-start.3 = (bf16[1,128,2048]{2,1,0:T(8,128)(2,1)S(1)}, bf16[1,128,2048]{2,1,0:T(8,128)(2,1)}, u32[]{:S(2)}) copy-start(bf16[1,128,2048]{2,1,0:T(8,128)(2,1)} %param.13) | copy-start | bytes 1572868
  6.5 33.0 %all-to-all-start.1 = ((bf16[4,256,704]{1,2,0:T(8,128)(2,1)}), bf16[4,256,704]{1,2,0:T(8,128)(2,1)S(1)}, u32[]{:S(2)}, u32[]{:S(2)}) async-start(bf16[4,256,704]{1,2,0:T(8,128)(2,1)} %param.21), calls=%async_computation.1 | async-start | bytes 2883584 | tf_op jit(solution)/shard_map/all_to_all | solution.py:57
  12.2 37.5 %copy-start.8 = (s32[1,128,6]{1,0,2:T(1,128)S(1)}, s32[1,128,6]{1,0,2:T(1,128)}, u32[]{:S(2)}) copy-start(s32[1,128,6]{1,0,2:T(1,128)} %param.19) | copy-start | bytes 9220
  12.2 31.7 %collective-permute-start = (bf16[16,128,128]{2,1,0:T(8,128)(2,1)}, bf16[16,128,128]{2,1,0:T(8,128)(2,1)}, u32[]{:S(2)}, u32[]{:S(2)}) collective-permute-start(bf16[16,128,128]{2,1,0:T(8,128)(2,1)} %get-tuple-element.5), channel_id=1, source_target_pairs={{0,4},{4,8},{8,12},{12,16},{16,20},{20,24},{24,28},{1,5},{5,9},{9,... | collective-permute-start | bytes 1572872 | tf_op jit(solution)/shard_map/ppermute | solution.py:18
  39.5 33.0 %copy-start.1 = (bf16[4,256,704]{1,2,0:T(8,128)(2,1)}, bf16[4,256,704]{1,2,0:T(8,128)(2,1)S(1)}, u32[]{:S(2)}) copy-start(bf16[4,256,704]{1,2,0:T(8,128)(2,1)S(1)} %all-to-all-done.1) | copy-start | bytes 4325380
  39.5 36.8 %all-to-all-start.2 = ((bf16[4,256,704]{1,2,0:T(8,128)(2,1)}), bf16[4,256,704]{1,2,0:T(8,128)(2,1)}, u32[]{:S(2)}, u32[]{:S(2)}) async-start(bf16[4,256,704]{1,2,0:T(8,128)(2,1)} %param.22), calls=%async_computation.2 | async-start | bytes 2883584 | tf_op jit(solution)/shard_map/all_to_all | solution.py:57
  45.8 24.5 %collective-permute-start.1 = (bf16[16,128,128]{2,1,0:T(8,128)(2,1)}, bf16[16,128,128]{2,1,0:T(8,128)(2,1)}, u32[]{:S(2)}, u32[]{:S(2)}) collective-permute-start(bf16[16,128,128]{2,1,0:T(8,128)(2,1)} %fusion.13), channel_id=1, source_target_pairs={{0,8},{4,12},{8,16},{12,20},{16,24},{20,28},{1,9},{5,13},{9,17},{1... | collective-permute-start | bytes 1572872 | tf_op jit(solution)/shard_map/ppermute | solution.py:18
  58.2 16.5 %copy-start.4 = (bf16[1,128,2048]{2,1,0:T(8,128)(2,1)S(1)}, bf16[1,128,2048]{2,1,0:T(8,128)(2,1)}, u32[]{:S(2)}) copy-start(bf16[1,128,2048]{2,1,0:T(8,128)(2,1)} %param.12) | copy-start | bytes 1572868
  72.5 18.0 %collective-permute-start.2 = (bf16[16,128,128]{2,1,0:T(8,128)(2,1)}, bf16[16,128,128]{2,1,0:T(8,128)(2,1)}, u32[]{:S(2)}, u32[]{:S(2)}) collective-permute-start(bf16[16,128,128]{2,1,0:T(8,128)(2,1)} %fusion.14), channel_id=1, source_target_pairs={{0,16},{4,20},{8,24},{12,28},{1,17},{5,21},{9,25},{13,29},{2,18},{... | collective-permute-start | bytes 1572872 | tf_op jit(solution)/shard_map/ppermute | solution.py:18
  76.3 30.1 %all-to-all-start.3 = ((bf16[4,704,256]{2,1,0:T(8,128)(2,1)}), bf16[4,704,256]{2,1,0:T(8,128)(2,1)}, u32[]{:S(2)}, u32[]{:S(2)}) async-start(bf16[4,704,256]{2,1,0:T(8,128)(2,1)} %param.23), calls=%async_computation.3 | async-start | bytes 2883584 | tf_op jit(solution)/shard_map/all_to_all | solution.py:57
  81.3 93.7 %all-gather.7.cloned.1.call-start = ((), (), s32[]{:S(2)}) async-start(), calls=%async_computation.5 | async-start | bytes 4325376 | tf_op jit(solution)/shard_map/all_gather | solution.py:58
  96.5 1.0 copy-start.5
  96.5 1.0 copy-start.6
  96.6 1.9 copy-start.7
  97.7 0.8 copy-start
  106.5 146.7 %all-to-all-start = ((bf16[16,50,2048]{2,1,0:T(8,128)(2,1)}), bf16[16,50,2048]{2,1,0:T(8,128)(2,1)}, u32[]{:S(2)}, u32[]{:S(2)}) async-start(bf16[16,50,2048]{2,1,0:T(8,128)(2,1)} %reshape.87), calls=%async_computation | async-start | bytes 7340032 | tf_op jit(solution)/shard_map/all_to_all | solution.py:110
  115.7 133.7 %all-gather.9.cloned.1.call-start = ((), (), s32[]{:S(2)}) async-start(), calls=%async_computation.6 | async-start | bytes 4325376 | tf_op jit(solution)/shard_map/all_gather | solution.py:58
  116.5 207.3 %all-gather.11.cloned.1.call-start = ((), (), s32[]{:S(2)}) async-start(), calls=%async_computation.7 | async-start | bytes 4325376 | tf_op jit(solution)/shard_map/all_gather | solution.py:58
  342.8 6.0 %copy-start.9 = (f32[1,128,6]{1,0,2:T(1,128)S(1)}, f32[1,128,6]{1,0,2:T(1,128)}, u32[]{:S(2)}) copy-start(f32[1,128,6]{1,0,2:T(1,128)} %param.20) | copy-start | bytes 9220
  342.8 52.4 %all-to-all-start.4 = ((bf16[16,50,2048]{2,1,0:T(8,128)(2,1)}), bf16[16,50,2048]{2,1,0:T(8,128)(2,1)}, u32[]{:S(2)}, u32[]{:S(2)}) async-start(bf16[16,50,2048]{2,1,0:T(8,128)(2,1)} %reshape.91), calls=%async_computation.4 | async-start | bytes 7340032 | tf_op jit(solution)/shard_map/all_to_all | solution.py:119
Sparse Core Ops, SparseCore 0:
  94.5 80.4 all-gather.6
  176.5 72.7 all-gather.8
  250.9 72.7 all-gather.10

commit v20 on v19

--- a/solution.py
+++ b/solution.py
@@ -11,7 +11,7 @@
 CAP = 50
 
 
-def carried_in(array, axis, count):
+def scanned(array, axis, count):
     total = array
     shift = 1
     while shift < count:
@@ -20,7 +20,26 @@
         )
         total = total + moved.astype(jnp.float32)
         shift *= 2
-    return total - array
+    return total
+
+
+def summed(array, axis, count):
+    total = array
+    shift = 1
+    while shift < count:
+        moved = lax.ppermute(
+            total.astype(jnp.bfloat16), axis, [(i, i ^ shift) for i in range(count)]
+        )
+        total = total + moved.astype(jnp.float32)
+        shift *= 2
+    return total
+
+
+def carried_in(array, n_hi, n_lo):
+    within = scanned(array, "seq_lo", n_lo) - array
+    group_total = summed(array, "seq_lo", n_lo)
+    before = scanned(group_total, "seq_hi", n_hi) - group_total
+    return within + before
 
 
 def route_slots(block_routes):
@@ -35,7 +54,7 @@
     return gate_sum / (1.0 + jnp.exp(-gate_sum)) * up_sum
 
 
-def make_shards(n_seq):
+def make_shards(n_seq, n_lo):
     seq = ("seq_hi", "seq_lo")
     group = ("ep", "seq_lo")
 
@@ -70,7 +89,7 @@
         local_state = jnp.einsum(
             "thd,the->hde", key_heads, value_heads, preferred_element_type=jnp.float32
         )
-        earlier = carried_in(local_state, seq, n_seq)
+        earlier = carried_in(local_state, n_seq // n_lo, n_lo)
         state_before = state_start[0] + earlier
         causal = (
             jnp.arange(tokens, dtype=jnp.int32)[:, None]
@@ -153,6 +172,6 @@
         split_names += list(seq) if name == "seq" else [name]
     split = Mesh(mesh.devices.reshape(shape), tuple(split_names))
     return jax.shard_map(
-        make_shards(n_seq), mesh=split, in_specs=placed, out_specs=P("ep", seq, None),
+        make_shards(n_seq, n_lo), mesh=split, in_specs=placed, out_specs=P("ep", seq, None),
         check_vma=False,
     )

time: 413 us -> 416 us (level)
  starting transfers between devices: 37.8 us -> 47.3 us
  waiting for transfers between devices: 285 us -> 278 us
    all_to_all x3, waiting for transfers between devices: 27.5 us -> 16.6 us  [collect(): mine = lax.all_to_all(weight, 'seq_lo', 0, 0, tiled=False)]
    all_to_all x3, starting transfers between devices: 13.1 us -> 18.3 us  [collect(): mine = lax.all_to_all(weight, 'seq_lo', 0, 0, tiled=False)]
    ppermute x3 -> x5, waiting for transfers between devices: 21.4 us -> 25.8 us  [the longest x3 15.8 us: scanned(): lax.ppermute(total.astype(jnp.bfloat16), axis, [(i, i + shift) for i in r...]
    ppermute x3 -> x5, starting transfers between devices: 9.2 us -> 12.5 us  [the longest x3 9.53 us: scanned(): lax.ppermute(total.astype(jnp.bfloat16), axis, [(i, i + shift) for i in r...]
  transfers between devices with their start and end apart: 11 -> 13, of which waited for: 8 -> 10; matrix products, arithmetic and copies ran while one was open for 11% -> 11% of each run, Pallas kernels for 0% -> 0%
where the time goes in v20:
time: 416 us; the launch traced here: 411 us
  waiting for transfers between devices  278 us (67%)
  starting transfers between devices  47.3 us (11%)
  local copies, waits for them, and re-layouts  30.5 us (7%)
  matrix products  29.7 us (7%)
  between operations  13.4 us (3%)
  other arithmetic  12.3 us (3%)
    all_gather x3, waiting for transfers between devices, collect(): return lax.all_gather(mine, 'seq_hi', axis=0, tiled=False)  189 us
    all_to_all x1, waiting for transfers between devices, shards(): returned = lax.all_to_all(expert_rows, group, 0, 0, tiled=True)  45.4 us
    all_to_all x3, starting transfers between devices, collect(): mine = lax.all_to_all(weight, 'seq_lo', 0, 0, tiled=False)  18.3 us
    all_to_all x3, waiting for transfers between devices, collect(): mine = lax.all_to_all(weight, 'seq_lo', 0, 0, tiled=False)  16.6 us
    ppermute x3, waiting for transfers between devices, scanned(): lax.ppermute(total.astype(jnp.bfloat16), axis, [(i, i + shift) for i in r...  15.8 us
    dot_general x1, matrix products, shards(): jnp.einsum('rh,abhd->rabd', hidden, whole_down, preferred_element_type=jn...  11.1 us
    all_to_all x1, starting transfers between devices, shards(): arrived = lax.all_to_all(outgoing, group, 0, 0, tiled=True)  10.4 us
    ppermute x2, waiting for transfers between devices, summed(): lax.ppermute(total.astype(jnp.bfloat16), axis, [(i, i ^ shift) for i in r...  10 us
  transfers between devices with their start and end apart: 13, of which 10 were waited for; matrix products, arithmetic and copies ran while one was open for 11% of the time, Pallas kernels for 0%

profile of v20, /device:TPU:16, one launch (start us, length us, event | category | flops | bytes accessed | tf_op | source)
XLA Modules:
  0.0 411.5 jit_solution(2359308294322903128)
XLA Ops:
  6.5 3.9 all-to-all-start.1
  10.8 1.3 fusion.38
  12.2 2.0 collective-permute-start.2
  14.2 15.1 %all-to-all-done.1 = bf16[4,256,704]{1,2,0:T(8,128)(2,1)S(1)} async-done(((bf16[4,256,704]{1,2,0:T(8,128)(2,1)}), bf16[4,256,704]{1,2,0:T(8,128)(2,1)S(1)}, u32[]{:S(2)}, u32[]{:S(2)}) %all-to-all-start.1) | async-done | bytes 1441824 | tf_op jit(solution)/shard_map/all_to_all | solution.py:76
  29.3 4.3 %all-to-all-start.2 = ((bf16[4,256,704]{1,2,0:T(8,128)(2,1)}), bf16[4,256,704]{1,2,0:T(8,128)(2,1)}, u32[]{:S(2)}, u32[]{:S(2)}) async-start(bf16[4,256,704]{1,2,0:T(8,128)(2,1)} %param.22), calls=%async_computation.2 | async-start | bytes 2883584 | tf_op jit(solution)/shard_map/all_to_all | solution.py:76
  33.7 4.7 %collective-permute-start = (bf16[16,128,128]{2,1,0:T(8,128)(2,1)}, bf16[16,128,128]{2,1,0:T(8,128)(2,1)}, u32[]{:S(2)}, u32[]{:S(2)}) collective-permute-start(bf16[16,128,128]{2,1,0:T(8,128)(2,1)} %get-tuple-element.7), channel_id=1, source_target_pairs={{0,4},{4,8},{8,12},{1,5},{5,9},{9,13},{2,6},{6,10},{10,14},{3,7},{... | collective-permute-start | bytes 1572872 | tf_op jit(solution)/shard_map/ppermute | solution.py:18
  38.4 10.0 %collective-permute-done.2 = bf16[16,128,128]{2,1,0:T(8,128)(2,1)} collective-permute-done((bf16[16,128,128]{2,1,0:T(8,128)(2,1)}, bf16[16,128,128]{2,1,0:T(8,128)(2,1)}, u32[]{:S(2)}, u32[]{:S(2)}) %collective-permute-start.2) | collective-permute-done | bytes 524320 | tf_op jit(solution)/shard_map/ppermute | solution.py:30
  48.4 2.0 fusion.19
  50.4 0.9 collective-permute-start.3
  51.3 0.7 copy.59
  52.0 1.0 eq.42
  53.0 1.0 eq.38
  54.0 0.6 fusion.35
  54.6 4.1 %reduce-window.6 = s32[16,6,128]{2,0,1:T(8,128)} reduce-window(s32[16,6,128]{2,0,1:T(8,128)} %fusion.35, s32[]{:T(128)} %constant.8.clone.1), window={size=1x1x128 pad=0_0x0_0x127_0}, to_apply=%region_1.2 | reduce-window | flops 1560576 | bytes 98308 | tf_op jit(solution)/shard_map/reduce-window
  58.7 1.0 slice_reduce_fusion
  59.8 4.3 %collective-permute-done = bf16[16,128,128]{2,1,0:T(8,128)(2,1)} collective-permute-done((bf16[16,128,128]{2,1,0:T(8,128)(2,1)}, bf16[16,128,128]{2,1,0:T(8,128)(2,1)}, u32[]{:S(2)}, u32[]{:S(2)}) %collective-permute-start) | collective-permute-done | bytes 524320 | tf_op jit(solution)/shard_map/ppermute | solution.py:18
  64.1 2.7 fusion.18
  66.8 3.5 collective-permute-start.1
  70.4 1.3 collective-permute-start.4
  72.1 0.8 bitcast_add_fusion
  73.4 10.1 %all-to-all-start.3 = ((bf16[4,704,256]{2,1,0:T(8,128)(2,1)}), bf16[4,704,256]{2,1,0:T(8,128)(2,1)}, u32[]{:S(2)}, u32[]{:S(2)}) async-start(bf16[4,704,256]{2,1,0:T(8,128)(2,1)} %param.23), calls=%async_computation.3 | async-start | bytes 2883584 | tf_op jit(solution)/shard_map/all_to_all | solution.py:76
  83.5 8.3 %collective-permute-done.1 = bf16[16,128,128]{2,1,0:T(8,128)(2,1)S(1)} collective-permute-done((bf16[16,128,128]{2,1,0:T(8,128)(2,1)}, bf16[16,128,128]{2,1,0:T(8,128)(2,1)S(1)}, u32[]{:S(2)}, u32[]{:S(2)}) %collective-permute-start.1) | collective-permute-done | bytes 524320 | tf_op jit(solution)/shard_map/ppermute | solution.py:18
  91.8 3.2 collective-permute-done.4
  95.0 4.2 %convolution_bitcast_fusion.1 = f32[128,16,128]{0,2,1:T(8,128)} fusion(f32[1,16,128,128]{3,2,1,0:T(8,128)} %param.16, bf16[16,128,128]{2,1,0:T(8,128)(2,1)} %collective-permute-done.4, f32[16,128,128]{2,1,0:T(8,128)S(1)} %get-tuple-element.8, bf16[16,128,128]{2,1,0:T(8,128)(2,1)S(1)} %collective-permute-done.1, ...), kind=kOutput, calls=%fused_computation.16 | convolution fusion | flops 406323200 | bytes 6291456 | tf_op jit(solution)/shard_map/thd,hde->the/dot_general | solution.py:105
  99.3 2.1 multiply_reduce_fusion
  101.9 0.6 copy-done.5
  102.8 0.6 copy-done
  103.4 1.1 convolution_convert_fusion
  104.5 2.7 reshape.87
  107.2 1.4 all-to-all-done.3
  108.6 10.4 %all-to-all-start = ((bf16[16,50,2048]{2,1,0:T(8,128)(2,1)}), bf16[16,50,2048]{2,1,0:T(8,128)(2,1)}, u32[]{:S(2)}, u32[]{:S(2)}) async-start(bf16[16,50,2048]{2,1,0:T(8,128)(2,1)} %reshape.87), calls=%async_computation | async-start | bytes 7340032 | tf_op jit(solution)/shard_map/all_to_all | solution.py:129
  119.0 0.7 all-gather.9.cloned.1.call-update
  119.9 0.5 all-gather.11.cloned.1.call-update
  120.4 57.3 %all-gather.7.cloned.1.call-done = bf16[8,256,704]{1,2,0:T(8,128)(2,1)} async-done(((bf16[4,256,704]{1,2,0:T(8,128)(2,1)}), bf16[8,256,704]{1,2,0:T(8,128)(2,1)}) %all-gather.7.cloned.1.call-update) | async-done | bytes 2883600 | tf_op jit(solution)/shard_map/all_gather | solution.py:77
  177.7 3.8 copy.72
  181.5 70.6 %all-gather.9.cloned.1.call-done = bf16[8,256,704]{1,2,0:T(8,128)(2,1)} async-done(((bf16[4,256,704]{1,2,0:T(8,128)(2,1)}), bf16[8,256,704]{1,2,0:T(8,128)(2,1)}) %all-gather.9.cloned.1.call-update) | async-done | bytes 2883600 | tf_op jit(solution)/shard_map/all_gather | solution.py:77
  252.1 3.9 copy.73
  256.0 3.2 reshape.88
  259.1 6.0 %fusion.43 = f32[800,704]{1,0:T(8,128)} fusion(bf16[800,2048]{1,0:T(8,128)(2,1)S(1)} %reshape.88, bf16[2048,704]{0,1:T(8,128)(2,1)} %bitcast.76), kind=kOutput, calls=%fused_computation.63 | convolution fusion | flops 2306867200 | bytes 8413184 | tf_op jit(solution)/shard_map/dot_general | solution.py:131
  265.1 61.4 %all-gather.11.cloned.1.call-done = bf16[8,704,256]{2,1,0:T(8,128)(2,1)} async-done(((bf16[4,704,256]{2,1,0:T(8,128)(2,1)}), bf16[8,704,256]{2,1,0:T(8,128)(2,1)}) %all-gather.11.cloned.1.call-update) | async-done | bytes 2883600 | tf_op jit(solution)/shard_map/all_gather | solution.py:77
  326.5 11.1 %convolution_convert_fusion.1 = bf16[800,2,4,256]{3,0,2,1:T(8,128)(2,1)} fusion(bf16[2,4,704,256]{3,2,1,0:T(8,128)(2,1)} %bitcast.81, bf16[800,2048]{1,0:T(8,128)(2,1)S(1)} %reshape.88, bf16[2048,704]{0,1:T(8,128)(2,1)} %bitcast.75, f32[800,704]{1,0:T(8,128)} %fusion.43), kind=kOutput, calls=%fused_computation.8 | convolution fusion | flops 4618188800 | bytes 14573568 | tf_op jit(solution)/shard_map/rh,abhd->rabd/dot_general | solution.py:134
  337.6 4.5 %copy.66 = bf16[800,2,4,256]{3,2,1,0:T(4,128)(2,1)S(1)} copy(bf16[800,2,4,256]{3,0,2,1:T(8,128)(2,1)} %convolution_convert_fusion.1) | data formatting | bytes 6553600 | tf_op jit(solution)/shard_map/convert_element_type | solution.py:136
  342.1 3.5 reshape.91
  345.6 5.9 %all-to-all-start.4 = ((bf16[16,50,2048]{2,1,0:T(8,128)(2,1)}), bf16[16,50,2048]{2,1,0:T(8,128)(2,1)}, u32[]{:S(2)}, u32[]{:S(2)}) async-start(bf16[16,50,2048]{2,1,0:T(8,128)(2,1)} %reshape.91), calls=%async_computation.4 | async-start | bytes 7340032 | tf_op jit(solution)/shard_map/all_to_all | solution.py:138
  351.5 1.0 select_reduce_fusion
  352.6 45.4 %all-to-all-done.4 = bf16[16,50,2048]{2,1,0:T(8,128)(2,1)} async-done(((bf16[16,50,2048]{2,1,0:T(8,128)(2,1)}), bf16[16,50,2048]{2,1,0:T(8,128)(2,1)}, u32[]{:S(2)}, u32[]{:S(2)}) %all-to-all-start.4) | async-done | bytes 3276832 | tf_op jit(solution)/shard_map/all_to_all | solution.py:138
  397.9 3.2 reshape.92
  401.1 3.8 fusion.2
  (43 shorter events, 2.3 us)
Async XLA Ops:
  6.5 3.9 copy-start.2
  6.5 4.2 %copy-start.3 = (bf16[1,128,2048]{2,1,0:T(8,128)(2,1)S(1)}, bf16[1,128,2048]{2,1,0:T(8,128)(2,1)}, u32[]{:S(2)}) copy-start(bf16[1,128,2048]{2,1,0:T(8,128)(2,1)} %param.13) | copy-start | bytes 1572868
  6.5 22.8 %all-to-all-start.1 = ((bf16[4,256,704]{1,2,0:T(8,128)(2,1)}), bf16[4,256,704]{1,2,0:T(8,128)(2,1)S(1)}, u32[]{:S(2)}, u32[]{:S(2)}) async-start(bf16[4,256,704]{1,2,0:T(8,128)(2,1)} %param.21), calls=%async_computation.1 | async-start | bytes 2883584 | tf_op jit(solution)/shard_map/all_to_all | solution.py:76
  12.2 39.1 %copy-start.9 = (s32[1,128,6]{1,0,2:T(1,128)S(1)}, s32[1,128,6]{1,0,2:T(1,128)}, u32[]{:S(2)}) copy-start(s32[1,128,6]{1,0,2:T(1,128)} %param.19) | copy-start | bytes 9220
  12.2 36.2 %collective-permute-start.2 = (bf16[16,128,128]{2,1,0:T(8,128)(2,1)}, bf16[16,128,128]{2,1,0:T(8,128)(2,1)}, u32[]{:S(2)}, u32[]{:S(2)}) collective-permute-start(bf16[16,128,128]{2,1,0:T(8,128)(2,1)} %get-tuple-element.7), channel_id=1, source_target_pairs={{0,4},{4,0},{8,12},{12,8},{1,5},{5,1},{9,13},{13,9},{2,6},{6,2},{1... | collective-permute-start | bytes 1572872 | tf_op jit(solution)/shard_map/ppermute | solution.py:30
  29.3 37.5 %copy-start.1 = (bf16[4,256,704]{1,2,0:T(8,128)(2,1)}, bf16[4,256,704]{1,2,0:T(8,128)(2,1)S(1)}, u32[]{:S(2)}) copy-start(bf16[4,256,704]{1,2,0:T(8,128)(2,1)S(1)} %all-to-all-done.1) | copy-start | bytes 4325380
  29.3 44.1 %all-to-all-start.2 = ((bf16[4,256,704]{1,2,0:T(8,128)(2,1)}), bf16[4,256,704]{1,2,0:T(8,128)(2,1)}, u32[]{:S(2)}, u32[]{:S(2)}) async-start(bf16[4,256,704]{1,2,0:T(8,128)(2,1)} %param.22), calls=%async_computation.2 | async-start | bytes 2883584 | tf_op jit(solution)/shard_map/all_to_all | solution.py:76
  33.7 30.5 %collective-permute-start = (bf16[16,128,128]{2,1,0:T(8,128)(2,1)}, bf16[16,128,128]{2,1,0:T(8,128)(2,1)}, u32[]{:S(2)}, u32[]{:S(2)}) collective-permute-start(bf16[16,128,128]{2,1,0:T(8,128)(2,1)} %get-tuple-element.7), channel_id=1, source_target_pairs={{0,4},{4,8},{8,12},{1,5},{5,9},{9,13},{2,6},{6,10},{10,14},{3,7},{... | collective-permute-start | bytes 1572872 | tf_op jit(solution)/shard_map/ppermute | solution.py:18
  50.4 13.7 %collective-permute-start.3 = (bf16[16,128,128]{2,1,0:T(8,128)(2,1)}, bf16[16,128,128]{2,1,0:T(8,128)(2,1)}, u32[]{:S(2)}, u32[]{:S(2)}) collective-permute-start(bf16[16,128,128]{2,1,0:T(8,128)(2,1)} %fusion.19), channel_id=1, source_target_pairs={{0,8},{4,12},{8,0},{12,4},{1,9},{5,13},{9,1},{13,5},{2,10},{6,14},... | collective-permute-start | bytes 1572872 | tf_op jit(solution)/shard_map/ppermute | solution.py:30
  59.8 11.9 %copy-start.6 = (s32[16,6,128]{2,0,1:T(8,128)S(1)}, s32[16,6,128]{2,0,1:T(8,128)}, u32[]{:S(2)}) copy-start(s32[16,6,128]{2,0,1:T(8,128)} %reduce-window.6) | copy-start | bytes 147460
  59.8 12.0 %copy-start.4 = (bf16[1,128,2048]{2,1,0:T(8,128)(2,1)S(1)}, bf16[1,128,2048]{2,1,0:T(8,128)(2,1)}, u32[]{:S(2)}) copy-start(bf16[1,128,2048]{2,1,0:T(8,128)(2,1)} %param.12) | copy-start | bytes 1572868
  66.8 25.0 %collective-permute-start.1 = (bf16[16,128,128]{2,1,0:T(8,128)(2,1)}, bf16[16,128,128]{2,1,0:T(8,128)(2,1)S(1)}, u32[]{:S(2)}, u32[]{:S(2)}) collective-permute-start(bf16[16,128,128]{2,1,0:T(8,128)(2,1)} %get-tuple-element.5), channel_id=1, source_target_pairs={{0,8},{4,12},{1,9},{5,13},{2,10},{6,14},{3,11},{7,15},{16,24},{20,... | collective-permute-start | bytes 1572872 | tf_op jit(solution)/shard_map/ppermute | solution.py:18
  70.4 24.6 %collective-permute-start.4 = (bf16[16,128,128]{2,1,0:T(8,128)(2,1)}, bf16[16,128,128]{2,1,0:T(8,128)(2,1)}, u32[]{:S(2)}, u32[]{:S(2)}) collective-permute-start(bf16[16,128,128]{2,1,0:T(8,128)(2,1)} %get-tuple-element.6), channel_id=1, source_target_pairs={{0,16},{1,17},{2,18},{3,19},{4,20},{5,21},{6,22},{7,23},{8,24},{9,... | collective-permute-start | bytes 1572872 | tf_op jit(solution)/shard_map/ppermute | solution.py:18
  73.4 35.1 %all-to-all-start.3 = ((bf16[4,704,256]{2,1,0:T(8,128)(2,1)}), bf16[4,704,256]{2,1,0:T(8,128)(2,1)}, u32[]{:S(2)}, u32[]{:S(2)}) async-start(bf16[4,704,256]{2,1,0:T(8,128)(2,1)} %param.23), calls=%async_computation.3 | async-start | bytes 2883584 | tf_op jit(solution)/shard_map/all_to_all | solution.py:76
  83.5 94.2 %all-gather.7.cloned.1.call-start = ((), (), s32[]{:S(2)}) async-start(), calls=%async_computation.5 | async-start | bytes 4325376 | tf_op jit(solution)/shard_map/all_gather | solution.py:77
  101.4 1.0 copy-start.5
  101.4 1.0 copy-start.7
  101.5 1.9 copy-start.8
  102.6 0.8 copy-start
  108.6 147.4 %all-to-all-start = ((bf16[16,50,2048]{2,1,0:T(8,128)(2,1)}), bf16[16,50,2048]{2,1,0:T(8,128)(2,1)}, u32[]{:S(2)}, u32[]{:S(2)}) async-start(bf16[16,50,2048]{2,1,0:T(8,128)(2,1)} %reshape.87), calls=%async_computation | async-start | bytes 7340032 | tf_op jit(solution)/shard_map/all_to_all | solution.py:129
  118.9 133.2 %all-gather.9.cloned.1.call-start = ((), (), s32[]{:S(2)}) async-start(), calls=%async_computation.6 | async-start | bytes 4325376 | tf_op jit(solution)/shard_map/all_gather | solution.py:77
  119.7 206.8 %all-gather.11.cloned.1.call-start = ((), (), s32[]{:S(2)}) async-start(), calls=%async_computation.7 | async-start | bytes 4325376 | tf_op jit(solution)/shard_map/all_gather | solution.py:77
  345.6 6.0 %copy-start.10 = (f32[1,128,6]{1,0,2:T(1,128)S(1)}, f32[1,128,6]{1,0,2:T(1,128)}, u32[]{:S(2)}) copy-start(f32[1,128,6]{1,0,2:T(1,128)} %param.20) | copy-start | bytes 9220
  345.6 52.4 %all-to-all-start.4 = ((bf16[16,50,2048]{2,1,0:T(8,128)(2,1)}), bf16[16,50,2048]{2,1,0:T(8,128)(2,1)}, u32[]{:S(2)}, u32[]{:S(2)}) async-start(bf16[16,50,2048]{2,1,0:T(8,128)(2,1)} %reshape.91), calls=%async_computation.4 | async-start | bytes 7340032 | tf_op jit(solution)/shard_map/all_to_all | solution.py:138
Sparse Core Ops, SparseCore 0:
  99.4 78.2 all-gather.6
  179.3 72.7 all-gather.8
  253.6 72.7 all-gather.10

commit v21 on v19

--- a/solution.py
+++ b/solution.py
@@ -59,7 +59,8 @@
 
         whole_gate = collect(gate_weight)
         whole_up = collect(up_weight)
-        whole_down = collect(down_weight)
+        down_mine = lax.all_to_all(down_weight, "seq_lo", 0, 0, tiled=False)
+        whole_down = lax.all_gather(down_mine, "seq_hi", axis=0, tiled=False)
         whole_gate = whole_gate.reshape(-1, whole_gate.shape[-1])
         whole_up = whole_up.reshape(-1, whole_up.shape[-1])
 
@@ -112,9 +113,24 @@
         gate_sum = jnp.dot(arrived, whole_gate, preferred_element_type=jnp.float32)
         up_sum = jnp.dot(arrived, whole_up, preferred_element_type=jnp.float32)
         hidden = silu_gate(gate_sum, up_sum).astype(jnp.bfloat16)
-        expert_rows = jnp.einsum(
-            "rh,abhd->rabd", hidden, whole_down, preferred_element_type=jnp.float32
-        ).astype(jnp.bfloat16)
+        if whole_down.shape[0] == 2:
+            place = lax.axis_index("seq_hi")
+            other = lax.dynamic_index_in_dim(whole_down, 1 - place, 0, False)
+            own_rows = jnp.einsum(
+                "rh,bhd->rbd", hidden, down_mine, preferred_element_type=jnp.float32
+            )
+            other_rows = jnp.einsum(
+                "rh,bhd->rbd", hidden, other, preferred_element_type=jnp.float32
+            )
+            expert_rows = jnp.where(
+                place == 0,
+                jnp.stack([own_rows, other_rows], axis=1),
+                jnp.stack([other_rows, own_rows], axis=1),
+            ).astype(jnp.bfloat16)
+        else:
+            expert_rows = jnp.einsum(
+                "rh,abhd->rabd", hidden, whole_down, preferred_element_type=jnp.float32
+            ).astype(jnp.bfloat16)
         expert_rows = expert_rows.reshape(EXPERTS, CAP, D)
         returned = lax.all_to_all(expert_rows, group, 0, 0, tiled=True)
         combine = jnp.sum(jnp.where(routed, route_gates[0][:, :, None], 0.0), axis=1)

time: 413 us -> 409 us (level)
  waiting for transfers between devices: 285 us -> 291 us
    all_gather x3 -> x2, waiting for transfers between devices: 190 us -> 131 us  [collect(): return lax.all_gather(mine, 'seq_hi', axis=0, tiled=False)]
    all_gather x0 -> x1, waiting for transfers between devices: none -> 58.7 us  [shards(): whole_down = lax.all_gather(down_mine, 'seq_hi', axis=0, tiled=False)]
    ppermute x3, waiting for transfers between devices: 21.4 us -> 28 us  [carried_in(): lax.ppermute(total.astype(jnp.bfloat16), axis, [(i, i + shift) for i in r...]
    all_to_all x0 -> x1, starting transfers between devices: none -> 4.91 us  [shards(): down_mine = lax.all_to_all(down_weight, 'seq_lo', 0, 0, tiled=False)]
    all_to_all x3 -> x2, starting transfers between devices: 13.1 us -> 8.35 us  [collect(): mine = lax.all_to_all(weight, 'seq_lo', 0, 0, tiled=False)]
    all_to_all x3 -> x2, waiting for transfers between devices: 27.5 us -> 23.4 us  [collect(): mine = lax.all_to_all(weight, 'seq_lo', 0, 0, tiled=False)]
    dot_general x1 -> x3, matrix products: 11.1 us -> 10 us  [the longest x1 3.96 us: shards(): up_sum = jnp.dot(arrived, whole_up, preferred_element_type=jnp.float32)]
  transfers between devices with their start and end apart: 11 -> 11, of which waited for: 8 -> 8; matrix products, arithmetic and copies ran while one was open for 11% -> 10% of each run, Pallas kernels for 0% -> 0%
where the time goes in v21:
time: 409 us; the launch traced here: 405 us
  waiting for transfers between devices  291 us (71%)
  starting transfers between devices  38.2 us (9%)
  matrix products  26.7 us (7%)
  local copies, waits for them, and re-layouts  26.6 us (7%)
  between operations  13.5 us (3%)
  other arithmetic  8.47 us (2%)
    all_gather x2, waiting for transfers between devices, collect(): return lax.all_gather(mine, 'seq_hi', axis=0, tiled=False)  131 us
    all_gather x1, waiting for transfers between devices, shards(): whole_down = lax.all_gather(down_mine, 'seq_hi', axis=0, tiled=False)  58.7 us
    all_to_all x1, waiting for transfers between devices, shards(): returned = lax.all_to_all(expert_rows, group, 0, 0, tiled=True)  45.4 us
    ppermute x3, waiting for transfers between devices, carried_in(): lax.ppermute(total.astype(jnp.bfloat16), axis, [(i, i + shift) for i in r...  28 us
    all_to_all x2, waiting for transfers between devices, collect(): mine = lax.all_to_all(weight, 'seq_lo', 0, 0, tiled=False)  23.4 us
    all_to_all x1, starting transfers between devices, shards(): arrived = lax.all_to_all(outgoing, group, 0, 0, tiled=True)  9.64 us
    ppermute x3, starting transfers between devices, carried_in(): lax.ppermute(total.astype(jnp.bfloat16), axis, [(i, i + shift) for i in r...  9.07 us
    all_to_all x2, starting transfers between devices, collect(): mine = lax.all_to_all(weight, 'seq_lo', 0, 0, tiled=False)  8.35 us
  transfers between devices with their start and end apart: 11, of which 8 were waited for; matrix products, arithmetic and copies ran while one was open for 10% of the time, Pallas kernels for 0%

profile of v21, /device:TPU:16, one launch (start us, length us, event | category | flops | bytes accessed | tf_op | source)
XLA Modules:
  0.0 404.7 jit_solution(15464071692914527808)
XLA Ops:
  6.5 3.9 all-to-all-start.1
  10.4 0.3 copy.69
  10.8 1.3 fusion.35
  12.2 3.9 collective-permute-start
  16.1 23.4 %all-to-all-done.1 = bf16[4,256,704]{1,2,0:T(8,128)(2,1)S(1)} async-done(((bf16[4,256,704]{1,2,0:T(8,128)(2,1)}), bf16[4,256,704]{1,2,0:T(8,128)(2,1)S(1)}, u32[]{:S(2)}, u32[]{:S(2)}) %all-to-all-start.1) | async-done | bytes 1441824 | tf_op jit(solution)/shard_map/all_to_all | solution.py:57
  39.5 4.5 %all-to-all-start.2 = ((bf16[4,256,704]{1,2,0:T(8,128)(2,1)}), bf16[4,256,704]{1,2,0:T(8,128)(2,1)}, u32[]{:S(2)}, u32[]{:S(2)}) async-start(bf16[4,256,704]{1,2,0:T(8,128)(2,1)} %param.22), calls=%async_computation.2 | async-start | bytes 2883584 | tf_op jit(solution)/shard_map/all_to_all | solution.py:57
  44.0 2.0 fusion.16
  46.0 3.9 collective-permute-start.1
  50.3 1.7 reduce-window.6
  52.0 0.3 slice_reduce_fusion
  52.2 18.2 %collective-permute-done.1 = bf16[16,128,128]{2,1,0:T(8,128)(2,1)} collective-permute-done((bf16[16,128,128]{2,1,0:T(8,128)(2,1)}, bf16[16,128,128]{2,1,0:T(8,128)(2,1)}, u32[]{:S(2)}, u32[]{:S(2)}) %collective-permute-start.1) | collective-permute-done | bytes 524320 | tf_op jit(solution)/shard_map/ppermute | solution.py:18
  70.4 2.2 fusion.17
  72.6 1.3 collective-permute-start.2
  74.0 1.1 copy.74
  75.4 0.4 fusion.1
  75.8 4.9 %all-to-all-start.3 = ((bf16[4,704,256]{2,1,0:T(8,128)(2,1)}), bf16[4,704,256]{2,1,0:T(8,128)(2,1)}, u32[]{:S(2)}, u32[]{:S(2)}) async-start(bf16[4,704,256]{2,1,0:T(8,128)(2,1)} %param.23), calls=%async_computation.3 | async-start | bytes 2883584 | tf_op jit(solution)/shard_map/all_to_all | solution.py:62
  80.8 9.8 %collective-permute-done.2 = bf16[16,128,128]{2,1,0:T(8,128)(2,1)S(1)} collective-permute-done((bf16[16,128,128]{2,1,0:T(8,128)(2,1)}, bf16[16,128,128]{2,1,0:T(8,128)(2,1)S(1)}, u32[]{:S(2)}, u32[]{:S(2)}) %collective-permute-start.2) | collective-permute-done | bytes 524320 | tf_op jit(solution)/shard_map/ppermute | solution.py:18
  90.5 3.7 convolution_bitcast_fusion.3
  94.2 2.1 multiply_reduce_fusion
  96.4 0.3 copy.58
  96.8 0.2 copy-done.6
  97.0 0.5 copy-done.5
  97.8 0.6 copy-done
  98.4 1.1 convolution_convert_fusion
  99.5 2.7 reshape.90
  102.2 3.8 all-to-all-done.3
  106.0 9.6 %all-to-all-start = ((bf16[16,50,2048]{2,1,0:T(8,128)(2,1)}), bf16[16,50,2048]{2,1,0:T(8,128)(2,1)}, u32[]{:S(2)}, u32[]{:S(2)}) async-start(bf16[16,50,2048]{2,1,0:T(8,128)(2,1)} %reshape.90), calls=%async_computation | async-start | bytes 7340032 | tf_op jit(solution)/shard_map/all_to_all | solution.py:111
  115.7 0.7 all-gather.9.cloned.1.call-update
  116.4 0.2 all-gather.11.cloned.1.call-start
  116.6 0.5 all-gather.11.cloned.1.call-update
  117.1 61.1 %all-gather.7.cloned.1.call-done = bf16[8,256,704]{1,2,0:T(8,128)(2,1)} async-done(((bf16[4,256,704]{1,2,0:T(8,128)(2,1)}), bf16[8,256,704]{1,2,0:T(8,128)(2,1)}) %all-gather.7.cloned.1.call-update) | async-done | bytes 2883600 | tf_op jit(solution)/shard_map/all_gather | solution.py:58
  178.3 3.8 copy.71
  182.0 69.8 %all-gather.9.cloned.1.call-done = bf16[8,256,704]{1,2,0:T(8,128)(2,1)} async-done(((bf16[4,256,704]{1,2,0:T(8,128)(2,1)}), bf16[8,256,704]{1,2,0:T(8,128)(2,1)}) %all-gather.9.cloned.1.call-update) | async-done | bytes 2883600 | tf_op jit(solution)/shard_map/all_gather | solution.py:58
  251.8 3.8 copy.72
  255.6 3.2 reshape.91
  258.8 4.7 %fusion.40 = f32[800,704]{1,0:T(8,128)S(1)} fusion(bf16[800,2048]{1,0:T(8,128)(2,1)S(1)} %reshape.91, bf16[2048,704]{0,1:T(8,128)(2,1)} %bitcast.78), kind=kOutput, calls=%fused_computation.62 | convolution fusion | flops 2306867200 | bytes 8413184 | tf_op jit(solution)/shard_map/dot_general | solution.py:113
  263.5 4.0 fusion.6
  267.5 58.7 %all-gather.11.cloned.1.call-done = bf16[8,704,256]{2,1,0:T(8,128)(2,1)} async-done(((bf16[4,704,256]{2,1,0:T(8,128)(2,1)}), bf16[8,704,256]{2,1,0:T(8,128)(2,1)}) %all-gather.11.cloned.1.call-update) | async-done | bytes 2883600 | tf_op jit(solution)/shard_map/all_gather | solution.py:63
  326.2 3.3 convolution_bitcast_fusion
  329.5 2.8 convolution_bitcast_fusion.1
  332.3 0.6 fusion
  332.8 2.5 copy.66
  335.4 3.4 convert_element_type.76
  338.8 6.0 %all-to-all-start.4 = ((bf16[16,50,2048]{2,1,0:T(8,128)(2,1)}), bf16[16,50,2048]{2,1,0:T(8,128)(2,1)}, u32[]{:S(2)}, u32[]{:S(2)}) async-start(bf16[16,50,2048]{2,1,0:T(8,128)(2,1)} %convert_element_type.76), calls=%async_computation.4 | async-start | bytes 7340032 | tf_op jit(solution)/shard_map/all_to_all | solution.py:135
  344.8 1.0 select_reduce_fusion
  345.8 45.4 %all-to-all-done.4 = bf16[16,50,2048]{2,1,0:T(8,128)(2,1)} async-done(((bf16[16,50,2048]{2,1,0:T(8,128)(2,1)}), bf16[16,50,2048]{2,1,0:T(8,128)(2,1)}, u32[]{:S(2)}, u32[]{:S(2)}) %all-to-all-start.4) | async-done | bytes 3276832 | tf_op jit(solution)/shard_map/all_to_all | solution.py:135
  391.2 3.2 reshape.94
  394.4 3.8 fusion.3
  (42 shorter events, 1.4 us)
Async XLA Ops:
  6.5 3.9 copy-start.3
  6.5 4.2 %copy-start.4 = (bf16[1,128,2048]{2,1,0:T(8,128)(2,1)S(1)}, bf16[1,128,2048]{2,1,0:T(8,128)(2,1)}, u32[]{:S(2)}) copy-start(bf16[1,128,2048]{2,1,0:T(8,128)(2,1)} %param.13) | copy-start | bytes 1572868
  6.5 33.0 %all-to-all-start.1 = ((bf16[4,256,704]{1,2,0:T(8,128)(2,1)}), bf16[4,256,704]{1,2,0:T(8,128)(2,1)S(1)}, u32[]{:S(2)}, u32[]{:S(2)}) async-start(bf16[4,256,704]{1,2,0:T(8,128)(2,1)} %param.21), calls=%async_computation.1 | async-start | bytes 2883584 | tf_op jit(solution)/shard_map/all_to_all | solution.py:57
  12.2 31.8 %collective-permute-start = (bf16[16,128,128]{2,1,0:T(8,128)(2,1)}, bf16[16,128,128]{2,1,0:T(8,128)(2,1)}, u32[]{:S(2)}, u32[]{:S(2)}) collective-permute-start(bf16[16,128,128]{2,1,0:T(8,128)(2,1)} %get-tuple-element.5), channel_id=1, source_target_pairs={{0,4},{4,8},{8,12},{12,16},{16,20},{20,24},{24,28},{1,5},{5,9},{9,... | collective-permute-start | bytes 1572872 | tf_op jit(solution)/shard_map/ppermute | solution.py:18
  39.5 6.5 %copy-start.1 = (bf16[4,256,704]{1,2,0:T(8,128)(2,1)}, bf16[4,256,704]{1,2,0:T(8,128)(2,1)S(1)}, u32[]{:S(2)}) copy-start(bf16[4,256,704]{1,2,0:T(8,128)(2,1)S(1)} %all-to-all-done.1) | copy-start | bytes 4325380
  39.5 10.3 %copy-start.8 = (s32[1,128,6]{1,0,2:T(1,128)S(1)}, s32[1,128,6]{1,0,2:T(1,128)}, u32[]{:S(2)}) copy-start(s32[1,128,6]{1,0,2:T(1,128)} %param.19) | copy-start | bytes 9220
  39.5 36.3 %all-to-all-start.2 = ((bf16[4,256,704]{1,2,0:T(8,128)(2,1)}), bf16[4,256,704]{1,2,0:T(8,128)(2,1)}, u32[]{:S(2)}, u32[]{:S(2)}) async-start(bf16[4,256,704]{1,2,0:T(8,128)(2,1)} %param.22), calls=%async_computation.2 | async-start | bytes 2883584 | tf_op jit(solution)/shard_map/all_to_all | solution.py:57
  46.0 24.5 %collective-permute-start.1 = (bf16[16,128,128]{2,1,0:T(8,128)(2,1)}, bf16[16,128,128]{2,1,0:T(8,128)(2,1)}, u32[]{:S(2)}, u32[]{:S(2)}) collective-permute-start(bf16[16,128,128]{2,1,0:T(8,128)(2,1)} %fusion.16), channel_id=1, source_target_pairs={{0,8},{4,12},{8,16},{12,20},{16,24},{20,28},{1,9},{5,13},{9,17},{1... | collective-permute-start | bytes 1572872 | tf_op jit(solution)/shard_map/ppermute | solution.py:18
  72.6 17.9 %collective-permute-start.2 = (bf16[16,128,128]{2,1,0:T(8,128)(2,1)}, bf16[16,128,128]{2,1,0:T(8,128)(2,1)S(1)}, u32[]{:S(2)}, u32[]{:S(2)}) collective-permute-start(bf16[16,128,128]{2,1,0:T(8,128)(2,1)} %fusion.17), channel_id=1, source_target_pairs={{0,16},{4,20},{8,24},{12,28},{1,17},{5,21},{9,25},{13,29},{2,18},{... | collective-permute-start | bytes 1572872 | tf_op jit(solution)/shard_map/ppermute | solution.py:18
  75.8 30.1 %all-to-all-start.3 = ((bf16[4,704,256]{2,1,0:T(8,128)(2,1)}), bf16[4,704,256]{2,1,0:T(8,128)(2,1)}, u32[]{:S(2)}, u32[]{:S(2)}) async-start(bf16[4,704,256]{2,1,0:T(8,128)(2,1)} %param.23), calls=%async_computation.3 | async-start | bytes 2883584 | tf_op jit(solution)/shard_map/all_to_all | solution.py:62
  80.8 97.5 %all-gather.7.cloned.1.call-start = ((), (), s32[]{:S(2)}) async-start(), calls=%async_computation.5 | async-start | bytes 4325376 | tf_op jit(solution)/shard_map/all_gather | solution.py:58
  96.3 0.7 copy-start.6
  96.4 1.0 copy-start.5
  96.8 1.6 copy-start.7
  97.6 0.8 copy-start
  106.0 149.6 %all-to-all-start = ((bf16[16,50,2048]{2,1,0:T(8,128)(2,1)}), bf16[16,50,2048]{2,1,0:T(8,128)(2,1)}, u32[]{:S(2)}, u32[]{:S(2)}) async-start(bf16[16,50,2048]{2,1,0:T(8,128)(2,1)} %reshape.90), calls=%async_computation | async-start | bytes 7340032 | tf_op jit(solution)/shard_map/all_to_all | solution.py:111
  115.6 136.1 %all-gather.9.cloned.1.call-start = ((), (), s32[]{:S(2)}) async-start(), calls=%async_computation.6 | async-start | bytes 4325376 | tf_op jit(solution)/shard_map/all_gather | solution.py:58
  116.4 209.8 %all-gather.11.cloned.1.call-start = ((), (), s32[]{:S(2)}) async-start(), calls=%async_computation.7 | async-start | bytes 4325376 | tf_op jit(solution)/shard_map/all_gather | solution.py:63
  258.8 4.7 %copy-start.2 = (bf16[8,88,8,256]{3,2,0,1:T(8,128)(2,1)S(1)}, bf16[8,88,8,256]{3,2,0,1:T(8,128)(2,1)}, u32[]{:S(2)}) copy-start(bf16[8,88,8,256]{3,2,0,1:T(8,128)(2,1)} %copy.72) | copy-start | bytes 8650756
  326.2 3.3 copy-start.10
  338.8 6.0 %copy-start.9 = (f32[1,128,6]{1,0,2:T(1,128)S(1)}, f32[1,128,6]{1,0,2:T(1,128)}, u32[]{:S(2)}) copy-start(f32[1,128,6]{1,0,2:T(1,128)} %param.20) | copy-start | bytes 9220
  338.8 52.4 %all-to-all-start.4 = ((bf16[16,50,2048]{2,1,0:T(8,128)(2,1)}), bf16[16,50,2048]{2,1,0:T(8,128)(2,1)}, u32[]{:S(2)}, u32[]{:S(2)}) async-start(bf16[16,50,2048]{2,1,0:T(8,128)(2,1)} %convert_element_type.76), calls=%async_computation.4 | async-start | bytes 7340032 | tf_op jit(solution)/shard_map/all_to_all | solution.py:135
Sparse Core Ops, SparseCore 0:
  96.9 81.2 all-gather.6
  179.8 71.9 all-gather.8
  253.3 72.7 all-gather.10

commit v22 on v21

--- a/solution.py
+++ b/solution.py
@@ -118,21 +118,27 @@
             other = lax.dynamic_index_in_dim(whole_down, 1 - place, 0, False)
             own_rows = jnp.einsum(
                 "rh,bhd->rbd", hidden, down_mine, preferred_element_type=jnp.float32
-            )
+            ).astype(jnp.bfloat16)
             other_rows = jnp.einsum(
                 "rh,bhd->rbd", hidden, other, preferred_element_type=jnp.float32
+            ).astype(jnp.bfloat16)
+            own_back = lax.all_to_all(
+                own_rows.reshape(EXPERTS, CAP, -1), group, 0, 0, tiled=True
             )
-            expert_rows = jnp.where(
+            other_back = lax.all_to_all(
+                other_rows.reshape(EXPERTS, CAP, -1), group, 0, 0, tiled=True
+            )
+            returned = jnp.where(
                 place == 0,
-                jnp.stack([own_rows, other_rows], axis=1),
-                jnp.stack([other_rows, own_rows], axis=1),
-            ).astype(jnp.bfloat16)
+                jnp.concatenate([own_back, other_back], axis=2),
+                jnp.concatenate([other_back, own_back], axis=2),
+            )
         else:
             expert_rows = jnp.einsum(
                 "rh,abhd->rabd", hidden, whole_down, preferred_element_type=jnp.float32
             ).astype(jnp.bfloat16)
-        expert_rows = expert_rows.reshape(EXPERTS, CAP, D)
-        returned = lax.all_to_all(expert_rows, group, 0, 0, tiled=True)
+            expert_rows = expert_rows.reshape(EXPERTS, CAP, D)
+            returned = lax.all_to_all(expert_rows, group, 0, 0, tiled=True)
         combine = jnp.sum(jnp.where(routed, route_gates[0][:, :, None], 0.0), axis=1)
         expert_mix = jnp.dot(
             combine,

time: 409 us -> 409 us (level)
  waiting for transfers between devices: 291 us -> 286 us
  starting transfers between devices: 38.2 us -> 42.8 us
    all_to_all x1 -> x2, waiting for transfers between devices: 45.4 us -> 40.5 us  [the longest x1 22.3 us: shards(): lax.all_to_all(own_rows.reshape(EXPERTS, CAP, -1), group, 0, 0, tiled=True)]
    all_to_all x1 -> x2, starting transfers between devices: 5.95 us -> 10.5 us  [the longest x1 5.89 us: shards(): lax.all_to_all(other_rows.reshape(EXPERTS, CAP, -1), group, 0, 0, tiled=T...]
  transfers between devices with their start and end apart: 11 -> 12, of which waited for: 8 -> 9; matrix products, arithmetic and copies ran while one was open for 10% -> 12% of each run, Pallas kernels for 0% -> 0%
where the time goes in v22:
time: 409 us; the launch traced here: 405 us
  waiting for transfers between devices  286 us (70%)
  starting transfers between devices  42.8 us (10%)
  matrix products  27.8 us (7%)
  local copies, waits for them, and re-layouts  27 us (7%)
  between operations  13.5 us (3%)
  other arithmetic  7.91 us (2%)
    all_gather x2, waiting for transfers between devices, collect(): return lax.all_gather(mine, 'seq_hi', axis=0, tiled=False)  131 us
    all_gather x1, waiting for transfers between devices, shards(): whole_down = lax.all_gather(down_mine, 'seq_hi', axis=0, tiled=False)  58.7 us
    ppermute x3, waiting for transfers between devices, carried_in(): lax.ppermute(total.astype(jnp.bfloat16), axis, [(i, i + shift) for i in r...  28 us
    all_to_all x2, waiting for transfers between devices, collect(): mine = lax.all_to_all(weight, 'seq_lo', 0, 0, tiled=False)  23.4 us
    all_to_all x1, waiting for transfers between devices, shards(): lax.all_to_all(own_rows.reshape(EXPERTS, CAP, -1), group, 0, 0, tiled=True)  22.3 us
    all_to_all x1, waiting for transfers between devices, shards(): lax.all_to_all(other_rows.reshape(EXPERTS, CAP, -1), group, 0, 0, tiled=T...  18.1 us
    all_to_all x1, starting transfers between devices, shards(): arrived = lax.all_to_all(outgoing, group, 0, 0, tiled=True)  9.65 us
    ppermute x3, starting transfers between devices, carried_in(): lax.ppermute(total.astype(jnp.bfloat16), axis, [(i, i + shift) for i in r...  9.07 us
  transfers between devices with their start and end apart: 12, of which 9 were waited for; matrix products, arithmetic and copies ran while one was open for 12% of the time, Pallas kernels for 0%

profile of v22, /device:TPU:16, one launch (start us, length us, event | category | flops | bytes accessed | tf_op | source)
XLA Modules:
  0.0 405.5 jit_solution(7538869452626658260)
XLA Ops:
  6.5 3.9 all-to-all-start.1
  10.8 1.3 fusion.43
  12.2 3.9 collective-permute-start
  16.1 23.4 %all-to-all-done.1 = bf16[4,256,704]{1,2,0:T(8,128)(2,1)S(1)} async-done(((bf16[4,256,704]{1,2,0:T(8,128)(2,1)}), bf16[4,256,704]{1,2,0:T(8,128)(2,1)S(1)}, u32[]{:S(2)}, u32[]{:S(2)}) %all-to-all-start.1) | async-done | bytes 1441824 | tf_op jit(solution)/shard_map/all_to_all | solution.py:57
  39.5 4.5 %all-to-all-start.2 = ((bf16[4,256,704]{1,2,0:T(8,128)(2,1)}), bf16[4,256,704]{1,2,0:T(8,128)(2,1)}, u32[]{:S(2)}, u32[]{:S(2)}) async-start(bf16[4,256,704]{1,2,0:T(8,128)(2,1)} %param.22), calls=%async_computation.2 | async-start | bytes 2883584 | tf_op jit(solution)/shard_map/all_to_all | solution.py:57
  44.0 2.0 fusion.23
  46.0 3.9 collective-permute-start.1
  50.3 1.7 reduce-window.6
  52.3 18.2 %collective-permute-done.1 = bf16[16,128,128]{2,1,0:T(8,128)(2,1)} collective-permute-done((bf16[16,128,128]{2,1,0:T(8,128)(2,1)}, bf16[16,128,128]{2,1,0:T(8,128)(2,1)}, u32[]{:S(2)}, u32[]{:S(2)}) %collective-permute-start.1) | collective-permute-done | bytes 524320 | tf_op jit(solution)/shard_map/ppermute | solution.py:18
  70.5 2.2 fusion.24
  72.6 1.3 collective-permute-start.2
  74.0 1.1 copy.77
  75.4 0.4 fusion.7
  75.9 4.9 %all-to-all-start.3 = ((bf16[4,704,256]{2,1,0:T(8,128)(2,1)}), bf16[4,704,256]{2,1,0:T(8,128)(2,1)}, u32[]{:S(2)}, u32[]{:S(2)}) async-start(bf16[4,704,256]{2,1,0:T(8,128)(2,1)} %param.23), calls=%async_computation.3 | async-start | bytes 2883584 | tf_op jit(solution)/shard_map/all_to_all | solution.py:62
  80.8 9.8 %collective-permute-done.2 = bf16[16,128,128]{2,1,0:T(8,128)(2,1)S(1)} collective-permute-done((bf16[16,128,128]{2,1,0:T(8,128)(2,1)}, bf16[16,128,128]{2,1,0:T(8,128)(2,1)S(1)}, u32[]{:S(2)}, u32[]{:S(2)}) %collective-permute-start.2) | collective-permute-done | bytes 524320 | tf_op jit(solution)/shard_map/ppermute | solution.py:18
  90.5 3.7 convolution_bitcast_fusion.1
  94.2 2.1 multiply_reduce_fusion
  96.5 0.3 copy.60
  97.0 0.5 copy-done.6
  97.8 0.6 copy-done.1
  98.4 1.1 convolution_convert_fusion
  99.5 2.7 reshape.92
  102.2 3.8 all-to-all-done.3
  106.0 9.6 %all-to-all-start = ((bf16[16,50,2048]{2,1,0:T(8,128)(2,1)}), bf16[16,50,2048]{2,1,0:T(8,128)(2,1)}, u32[]{:S(2)}, u32[]{:S(2)}) async-start(bf16[16,50,2048]{2,1,0:T(8,128)(2,1)} %reshape.92), calls=%async_computation | async-start | bytes 7340032 | tf_op jit(solution)/shard_map/all_to_all | solution.py:111
  115.7 0.7 all-gather.9.cloned.1.call-update
  116.6 0.5 all-gather.11.cloned.1.call-update
  117.2 61.1 %all-gather.7.cloned.1.call-done = bf16[8,256,704]{1,2,0:T(8,128)(2,1)} async-done(((bf16[4,256,704]{1,2,0:T(8,128)(2,1)}), bf16[8,256,704]{1,2,0:T(8,128)(2,1)}) %all-gather.7.cloned.1.call-update) | async-done | bytes 2883600 | tf_op jit(solution)/shard_map/all_gather | solution.py:58
  178.3 3.8 copy.74
  182.1 69.8 %all-gather.9.cloned.1.call-done = bf16[8,256,704]{1,2,0:T(8,128)(2,1)} async-done(((bf16[4,256,704]{1,2,0:T(8,128)(2,1)}), bf16[8,256,704]{1,2,0:T(8,128)(2,1)}) %all-gather.9.cloned.1.call-update) | async-done | bytes 2883600 | tf_op jit(solution)/shard_map/all_gather | solution.py:58
  251.8 3.8 copy.75
  255.7 3.2 reshape.93
  258.9 4.7 %fusion.48 = f32[800,704]{1,0:T(8,128)S(1)} fusion(bf16[800,2048]{1,0:T(8,128)(2,1)S(1)} %reshape.93, bf16[2048,704]{0,1:T(8,128)(2,1)} %bitcast.73), kind=kOutput, calls=%fused_computation.69 | convolution fusion | flops 2306867200 | bytes 8413184 | tf_op jit(solution)/shard_map/dot_general | solution.py:113
  263.6 4.0 fusion.13
  267.6 58.7 %all-gather.11.cloned.1.call-done = bf16[8,704,256]{2,1,0:T(8,128)(2,1)} async-done(((bf16[4,704,256]{2,1,0:T(8,128)(2,1)}), bf16[8,704,256]{2,1,0:T(8,128)(2,1)}) %all-gather.11.cloned.1.call-update) | async-done | bytes 2883600 | tf_op jit(solution)/shard_map/all_gather | solution.py:63
  326.2 3.2 convolution_convert_fusion.1
  329.4 1.3 copy.69
  330.7 2.0 reshape.97
  332.7 5.9 %all-to-all-start.5 = ((bf16[16,50,1024]{2,1,0:T(8,128)(2,1)}), bf16[16,50,1024]{2,1,0:T(8,128)(2,1)S(1)}, u32[]{:S(2)}, u32[]{:S(2)}) async-start(bf16[16,50,1024]{2,1,0:T(8,128)(2,1)} %reshape.97), calls=%async_computation.5 | async-start | bytes 3670016 | tf_op jit(solution)/shard_map/all_to_all | solution.py:128
  338.6 2.8 convolution_convert_fusion.2
  341.4 1.3 copy.68
  342.7 2.0 reshape.96
  344.7 18.1 %all-to-all-done.5 = bf16[16,50,1024]{2,1,0:T(8,128)(2,1)S(1)} async-done(((bf16[16,50,1024]{2,1,0:T(8,128)(2,1)}), bf16[16,50,1024]{2,1,0:T(8,128)(2,1)S(1)}, u32[]{:S(2)}, u32[]{:S(2)}) %all-to-all-start.5) | async-done | bytes 1638432 | tf_op jit(solution)/shard_map/all_to_all | solution.py:128
  362.8 4.6 %all-to-all-start.4 = ((bf16[16,50,1024]{2,1,0:T(8,128)(2,1)}), bf16[16,50,1024]{2,1,0:T(8,128)(2,1)}, u32[]{:S(2)}, u32[]{:S(2)}) async-start(bf16[16,50,1024]{2,1,0:T(8,128)(2,1)} %reshape.96), calls=%async_computation.4 | async-start | bytes 3670016 | tf_op jit(solution)/shard_map/all_to_all | solution.py:125
  367.5 1.0 select_reduce_fusion
  368.5 0.5 concatenate.13
  369.0 22.3 %all-to-all-done.4 = bf16[16,50,1024]{2,1,0:T(8,128)(2,1)} async-done(((bf16[16,50,1024]{2,1,0:T(8,128)(2,1)}), bf16[16,50,1024]{2,1,0:T(8,128)(2,1)}, u32[]{:S(2)}, u32[]{:S(2)}) %all-to-all-start.4) | async-done | bytes 1638432 | tf_op jit(solution)/shard_map/all_to_all | solution.py:125
  391.3 2.6 concatenate.12
  393.9 5.0 %fusion.10 = bf16[1,128,2048]{2,1,0:T(8,128)(2,1)} fusion(f32[128,800]{0,1:T(8,128)S(1)} %copy-done.7, bf16[800,1024]{1,0:T(8,128)(2,1)S(1)} %concatenate.13, bf16[800,1024]{1,0:T(8,128)(2,1)} %concatenate.12, pred[]{:T(512)S(6)} %eq.52, bf16[128,2048]{1,0:T(8,128)(2,1)S(1)} %copy-done.2), kind=kOutput, calls=%fused_computation.15 | convolution fusion | flops 2532114432 | bytes 4734977 | tf_op jit(solution)/shard_map/dot_general | solution.py:143
  (50 shorter events, 2.3 us)
Async XLA Ops:
  6.5 3.9 copy-start.4
  6.5 4.2 %copy-start.5 = (bf16[1,128,2048]{2,1,0:T(8,128)(2,1)S(1)}, bf16[1,128,2048]{2,1,0:T(8,128)(2,1)}, u32[]{:S(2)}) copy-start(bf16[1,128,2048]{2,1,0:T(8,128)(2,1)} %param.13) | copy-start | bytes 1572868
  6.5 33.0 %all-to-all-start.1 = ((bf16[4,256,704]{1,2,0:T(8,128)(2,1)}), bf16[4,256,704]{1,2,0:T(8,128)(2,1)S(1)}, u32[]{:S(2)}, u32[]{:S(2)}) async-start(bf16[4,256,704]{1,2,0:T(8,128)(2,1)} %param.21), calls=%async_computation.1 | async-start | bytes 2883584 | tf_op jit(solution)/shard_map/all_to_all | solution.py:57
  12.2 31.8 %collective-permute-start = (bf16[16,128,128]{2,1,0:T(8,128)(2,1)}, bf16[16,128,128]{2,1,0:T(8,128)(2,1)}, u32[]{:S(2)}, u32[]{:S(2)}) collective-permute-start(bf16[16,128,128]{2,1,0:T(8,128)(2,1)} %get-tuple-element.5), channel_id=1, source_target_pairs={{0,4},{4,8},{8,12},{12,16},{16,20},{20,24},{24,28},{1,5},{5,9},{9,... | collective-permute-start | bytes 1572872 | tf_op jit(solution)/shard_map/ppermute | solution.py:18
  39.5 6.5 %copy-start = (bf16[4,256,704]{1,2,0:T(8,128)(2,1)}, bf16[4,256,704]{1,2,0:T(8,128)(2,1)S(1)}, u32[]{:S(2)}) copy-start(bf16[4,256,704]{1,2,0:T(8,128)(2,1)S(1)} %all-to-all-done.1) | copy-start | bytes 4325380
  39.5 10.3 %copy-start.10 = (s32[1,128,6]{1,0,2:T(1,128)S(1)}, s32[1,128,6]{1,0,2:T(1,128)}, u32[]{:S(2)}) copy-start(s32[1,128,6]{1,0,2:T(1,128)} %param.19) | copy-start | bytes 9220
  39.5 36.3 %all-to-all-start.2 = ((bf16[4,256,704]{1,2,0:T(8,128)(2,1)}), bf16[4,256,704]{1,2,0:T(8,128)(2,1)}, u32[]{:S(2)}, u32[]{:S(2)}) async-start(bf16[4,256,704]{1,2,0:T(8,128)(2,1)} %param.22), calls=%async_computation.2 | async-start | bytes 2883584 | tf_op jit(solution)/shard_map/all_to_all | solution.py:57
  46.0 24.5 %collective-permute-start.1 = (bf16[16,128,128]{2,1,0:T(8,128)(2,1)}, bf16[16,128,128]{2,1,0:T(8,128)(2,1)}, u32[]{:S(2)}, u32[]{:S(2)}) collective-permute-start(bf16[16,128,128]{2,1,0:T(8,128)(2,1)} %fusion.23), channel_id=1, source_target_pairs={{0,8},{4,12},{8,16},{12,20},{16,24},{20,28},{1,9},{5,13},{9,17},{1... | collective-permute-start | bytes 1572872 | tf_op jit(solution)/shard_map/ppermute | solution.py:18
  72.6 17.9 %collective-permute-start.2 = (bf16[16,128,128]{2,1,0:T(8,128)(2,1)}, bf16[16,128,128]{2,1,0:T(8,128)(2,1)S(1)}, u32[]{:S(2)}, u32[]{:S(2)}) collective-permute-start(bf16[16,128,128]{2,1,0:T(8,128)(2,1)} %fusion.24), channel_id=1, source_target_pairs={{0,16},{4,20},{8,24},{12,28},{1,17},{5,21},{9,25},{13,29},{2,18},{... | collective-permute-start | bytes 1572872 | tf_op jit(solution)/shard_map/ppermute | solution.py:18
  75.9 30.1 %all-to-all-start.3 = ((bf16[4,704,256]{2,1,0:T(8,128)(2,1)}), bf16[4,704,256]{2,1,0:T(8,128)(2,1)}, u32[]{:S(2)}, u32[]{:S(2)}) async-start(bf16[4,704,256]{2,1,0:T(8,128)(2,1)} %param.23), calls=%async_computation.3 | async-start | bytes 2883584 | tf_op jit(solution)/shard_map/all_to_all | solution.py:62
  80.8 97.5 %all-gather.7.cloned.1.call-start = ((), (), s32[]{:S(2)}) async-start(), calls=%async_computation.6 | async-start | bytes 4325376 | tf_op jit(solution)/shard_map/all_gather | solution.py:58
  96.3 0.7 copy-start.8
  96.5 1.0 copy-start.6
  96.8 1.6 copy-start.9
  97.6 0.8 copy-start.1
  106.0 149.7 %all-to-all-start = ((bf16[16,50,2048]{2,1,0:T(8,128)(2,1)}), bf16[16,50,2048]{2,1,0:T(8,128)(2,1)}, u32[]{:S(2)}, u32[]{:S(2)}) async-start(bf16[16,50,2048]{2,1,0:T(8,128)(2,1)} %reshape.92), calls=%async_computation | async-start | bytes 7340032 | tf_op jit(solution)/shard_map/all_to_all | solution.py:111
  115.7 136.2 %all-gather.9.cloned.1.call-start = ((), (), s32[]{:S(2)}) async-start(), calls=%async_computation.7 | async-start | bytes 4325376 | tf_op jit(solution)/shard_map/all_gather | solution.py:58
  116.4 209.8 %all-gather.11.cloned.1.call-start = ((), (), s32[]{:S(2)}) async-start(), calls=%async_computation.8 | async-start | bytes 4325376 | tf_op jit(solution)/shard_map/all_gather | solution.py:63
  258.9 4.7 %copy-start.3 = (bf16[8,88,8,256]{3,2,0,1:T(8,128)(2,1)S(1)}, bf16[8,88,8,256]{3,2,0,1:T(8,128)(2,1)}, u32[]{:S(2)}) copy-start(bf16[8,88,8,256]{3,2,0,1:T(8,128)(2,1)} %copy.75) | copy-start | bytes 8650756
  332.7 5.9 %copy-start.12 = (bf16[800,704,1]{1,0,2:T(8,128)(2,1)S(1)}, bf16[800,704,1]{1,0,2:T(8,128)(2,1)}, u32[]{:S(2)}) copy-start(bf16[800,704,1]{1,0,2:T(8,128)(2,1)} %fusion.13) | copy-start | bytes 3379204
  332.7 30.1 %all-to-all-start.5 = ((bf16[16,50,1024]{2,1,0:T(8,128)(2,1)}), bf16[16,50,1024]{2,1,0:T(8,128)(2,1)S(1)}, u32[]{:S(2)}, u32[]{:S(2)}) async-start(bf16[16,50,1024]{2,1,0:T(8,128)(2,1)} %reshape.97), calls=%async_computation.5 | async-start | bytes 3670016 | tf_op jit(solution)/shard_map/all_to_all | solution.py:128
  344.6 22.8 %copy-start.11 = (f32[1,128,6]{1,0,2:T(1,128)S(1)}, f32[1,128,6]{1,0,2:T(1,128)}, u32[]{:S(2)}) copy-start(f32[1,128,6]{1,0,2:T(1,128)} %param.20) | copy-start | bytes 9220
  362.8 28.5 %all-to-all-start.4 = ((bf16[16,50,1024]{2,1,0:T(8,128)(2,1)}), bf16[16,50,1024]{2,1,0:T(8,128)(2,1)}, u32[]{:S(2)}, u32[]{:S(2)}) async-start(bf16[16,50,1024]{2,1,0:T(8,128)(2,1)} %reshape.96), calls=%async_computation.4 | async-start | bytes 3670016 | tf_op jit(solution)/shard_map/all_to_all | solution.py:125
  369.0 24.9 %copy-start.2 = (bf16[128,2048]{1,0:T(8,128)(2,1)S(1)}, bf16[128,2048]{1,0:T(8,128)(2,1)}, u32[]{:S(2)}) copy-start(bf16[128,2048]{1,0:T(8,128)(2,1)} %copy-done.1) | copy-start | bytes 1572868
  369.0 24.9 %copy-start.7 = (f32[128,800]{0,1:T(8,128)S(1)}, f32[128,800]{0,1:T(8,128)}, u32[]{:S(2)}) copy-start(f32[128,800]{0,1:T(8,128)} %select_reduce_fusion) | copy-start | bytes 1228804
Sparse Core Ops, SparseCore 0:
  97.0 81.2 all-gather.6
  179.8 71.9 all-gather.8
  253.4 72.8 all-gather.10
